TPU v7x, 128 devices: a whole 4x4x4 slice. The times are simulated.
128 devices in a mesh: wide: 32 (over y, x, z_lo), narrow: 4 (over z_hi, core).
Axes of the slice: x: 4, y: 4, z: 4 (z_hi: 2, z_lo: 2; z = z_hi * 2 + z_lo), core: 2. Of those that a mesh axis runs over, the one named last changes fastest.
Arguments:
- hidden: bfloat16 [4096, 2048], P('wide'), may hold values from -6 to 6
- attn_gain: bfloat16 [2048], replicated, may hold values from 0.099609375 to 1.8984375
- q_weight: bfloat16 [2048, 3072], P('wide', 'narrow'), may hold values from -0.125 to 0.125
- kva_weight: bfloat16 [2048, 576], P('wide'), may hold values from -0.125 to 0.125
- kv_gain: bfloat16 [512], replicated, may hold values from 0.099609375 to 1.8984375
- kvb_weight: bfloat16 [512, 4096], P('wide', 'narrow'), may hold values from -0.25 to 0.25
- o_weight: bfloat16 [2048, 2048], P('narrow', 'wide'), may hold values from -12 to 12
- cache: bfloat16 [8, 20480, 576], P(None, 'wide'), as said below
- lengths: int32 [8], replicated, may hold values from 2 to 20480, as said below
Outputs:
- attn_out: bfloat16 [4096, 2048], P('wide')
Inputs may be any that keep to these rules, and one draw needn't show every extreme that they name: `lengths`: each request has at most 20480 cached positions; one request of every draw has exactly 20480. `cache`: each cached row holds a stored latent (first 512 entries) and a rotated key (last 64); rows at or past a request's length are never read.
All inputs are finite; a program needn't handle non-finite values.
Results may differ from a plain program's by a relative error of at most 0.02.
Values may be sent and summed in bfloat16 or wider, within the bound.
No kernel may reach another device: no remote copies, remote signals or barrier semaphores. Data moves between devices by JAX's collectives and lax.ppermute only.
A program may use at most 128 MiB of HBM per device.

v0:
```python
import jax
import jax.numpy as jnp
from jax import lax
from jax.sharding import PartitionSpec as P

NOPE = 128
ROPE = 64
VDIM = 128
LAT = 512
SPAN = 512


eps = 1e-06
score_scale = 1.0 / 13.856406460551018


def rotate(values, positions):
    half_size = values.shape[-1] // 2
    frequency = 10000.0 ** (-jnp.arange(half_size, dtype=jnp.float32) / half_size)
    angles = positions.astype(jnp.float32)[..., None] * frequency
    lower_half = values[..., :half_size]
    upper_half = values[..., half_size:]
    cosine = jnp.cos(angles)
    sine_part = jnp.sin(angles)
    return jnp.concatenate(
        [
            lower_half * cosine - upper_half * sine_part,
            lower_half * sine_part + upper_half * cosine,
        ],
        axis=-1,
    )


def scaled_norm(values, gain):
    return (
        values
        * lax.rsqrt(jnp.mean(values * values, axis=-1, keepdims=True) + eps)
        * gain.astype(jnp.float32)
    )


def absorb(nope_part, key_maps):
    return jnp.einsum(
        "thc,lhc->thl", nope_part, key_maps, preferred_element_type=jnp.float32
    ).astype(jnp.bfloat16)


def project_values(mixed, value_maps):
    upper_part = mixed.astype(jnp.bfloat16)
    lower_part = (mixed - upper_part.astype(jnp.float32)).astype(jnp.bfloat16)
    first_term = jnp.einsum(
        "qhc,chv->qhv", upper_part, value_maps, preferred_element_type=jnp.float32
    )
    second_term = jnp.einsum(
        "qhc,chv->qhv", lower_part, value_maps, preferred_element_type=jnp.float32
    )
    return first_term + second_term


def attend(block_queries, key_rows, live_mask, value_maps):
    scores = (
        jnp.einsum("qhc,kc->qhk", block_queries, key_rows, preferred_element_type=jnp.float32)
        * score_scale
    )
    live_rows = live_mask[:, None, :]
    row_peak = jnp.max(jnp.where(live_rows, scores, -1e30), axis=-1)
    weights = jnp.where(live_rows, jnp.exp(scores - row_peak[..., None]), 0.0)
    row_total = jnp.sum(weights, axis=-1)
    mixed = jnp.einsum(
        "qhk,kc->qhc",
        weights.astype(jnp.bfloat16),
        key_rows[:, :LAT],
        preferred_element_type=jnp.float32,
    )
    return (row_peak, row_total, project_values(mixed, value_maps))


def skipped(block_queries, key_rows, live_mask, value_maps):
    rows_here = block_queries.shape[0]
    heads_here = block_queries.shape[1]
    return (
        jnp.full((rows_here, heads_here), -1e30, jnp.float32),
        jnp.zeros((rows_here, heads_here), jnp.float32),
        jnp.zeros((rows_here, heads_here, value_maps.shape[2]), jnp.float32),
    )


def merge_parts(first, second):
    joint_peak = jnp.maximum(first[0], second[0])
    first_factor = jnp.exp(first[0] - joint_peak)
    second_factor = jnp.exp(second[0] - joint_peak)
    joint_total = first_factor * first[1] + second_factor * second[1]
    joint_value = first_factor[..., None] * first[2] + second_factor[..., None] * second[2]
    return (joint_peak, joint_total, joint_value)


def per_device(
    hidden, attn_gain, q_weight, kva_weight, kv_gain, kvb_weight, o_weight, cache, lengths
):
    wide_count = lax.axis_size("wide")
    wide_place = lax.axis_index("wide")
    tok_rows = hidden.shape[0]
    requests = lengths.shape[0]
    cache_rows = cache.shape[1]
    heads_here = q_weight.shape[1] // (NOPE + ROPE)
    q_full, kva_full, kvb_full, o_full = (
        lax.all_gather(q_weight, "wide", axis=0, tiled=True),
        lax.all_gather(kva_weight, "wide", axis=0, tiled=True),
        lax.all_gather(kvb_weight, "wide", axis=0, tiled=True),
        lax.all_gather(o_weight, "wide", axis=1, tiled=True),
    )
    normed = scaled_norm(hidden.astype(jnp.float32), attn_gain).astype(jnp.bfloat16)
    query_rows = jnp.dot(normed, q_full, preferred_element_type=jnp.float32).astype(jnp.bfloat16)
    query_rows = query_rows.reshape(tok_rows, heads_here, NOPE + ROPE)
    compressed = jnp.dot(normed, kva_full, preferred_element_type=jnp.float32)
    first_token = wide_place * tok_rows
    token_ids = first_token + jnp.arange(tok_rows, dtype=jnp.int32)
    request_of = token_ids // SPAN
    request_ids = jnp.arange(requests, dtype=jnp.int32)
    own_length = jnp.sum(
        jnp.where(request_of[:, None] == request_ids[None, :], lengths[None, :], 0), axis=1
    )
    positions = own_length + token_ids % SPAN
    own_keys = jnp.concatenate(
        [
            scaled_norm(compressed[:, :LAT], kv_gain).astype(jnp.bfloat16),
            rotate(compressed[:, LAT:], positions).astype(jnp.bfloat16),
        ],
        axis=1,
    )
    q_nope = query_rows[..., :NOPE]
    q_rope = rotate(query_rows[..., NOPE:].astype(jnp.float32), positions[:, None]).astype(
        jnp.bfloat16
    )
    kvb_heads = kvb_full.reshape(LAT, heads_here, NOPE + VDIM)
    key_maps = kvb_heads[..., :NOPE]
    value_maps = kvb_heads[..., NOPE:]
    outgoing = jnp.concatenate([absorb(q_nope, key_maps), q_rope], axis=-1).reshape(
        tok_rows, heads_here * (LAT + ROPE)
    )
    own_request = first_token // SPAN
    gathered = lax.all_gather(outgoing, "wide", axis=0, tiled=True)
    total_tokens = gathered.shape[0]
    queries = gathered.reshape(total_tokens, heads_here, LAT + ROPE)
    blocks = [cache[request] for request in range(requests)]
    starts = [wide_place * cache_rows for request in range(requests)]
    cache_slots = jnp.arange(cache_rows, dtype=jnp.int32)
    peaks_list = []
    totals_list = []
    values_list = []
    for request in range(requests):
        length_now = lengths[request]
        cache_live = starts[request] + cache_slots < length_now
        live_mask = jnp.broadcast_to(cache_live[None, :], (SPAN, cache_rows))
        block_live = starts[request] < length_now
        block_queries = queries[request * SPAN : (request + 1) * SPAN]
        row_peak, row_total, row_value = lax.cond(
            block_live, attend, skipped, block_queries, blocks[request], live_mask, value_maps
        )
        peaks_list.append(row_peak)
        totals_list.append(row_total)
        values_list.append(row_value)
    peak_all = jnp.concatenate(peaks_list, axis=0)
    total_all = jnp.concatenate(totals_list, axis=0)
    value_all = jnp.concatenate(values_list, axis=0)
    start_row = own_request * SPAN
    own_slots = first_token % SPAN + jnp.arange(tok_rows, dtype=jnp.int32)
    causal = own_slots[None, :] <= jnp.arange(SPAN, dtype=jnp.int32)[:, None]
    own_queries = lax.dynamic_slice_in_dim(queries, start_row, SPAN, 0)
    own_part = attend(own_queries, own_keys, causal, value_maps)
    old_part = (
        lax.dynamic_slice_in_dim(peak_all, start_row, SPAN, 0),
        lax.dynamic_slice_in_dim(total_all, start_row, SPAN, 0),
        lax.dynamic_slice_in_dim(value_all, start_row, SPAN, 0),
    )
    joint = merge_parts(old_part, own_part)
    peak_all = lax.dynamic_update_slice_in_dim(peak_all, joint[0], start_row, 0)
    total_all = lax.dynamic_update_slice_in_dim(total_all, joint[1], start_row, 0)
    value_all = lax.dynamic_update_slice_in_dim(value_all, joint[2], start_row, 0)
    got_peak, got_total, got_value = (
        lax.all_to_all(
            peak_all[None].astype(jnp.bfloat16), "wide", split_axis=1, concat_axis=0, tiled=True
        ).astype(jnp.float32),
        lax.all_to_all(
            total_all[None].astype(jnp.bfloat16), "wide", split_axis=1, concat_axis=0, tiled=True
        ).astype(jnp.float32),
        lax.all_to_all(
            value_all.reshape(1, total_tokens, heads_here * VDIM).astype(jnp.bfloat16),
            "wide",
            split_axis=1,
            concat_axis=0,
            tiled=True,
        ).astype(jnp.float32),
    )
    peak_value = jnp.max(got_peak, axis=0)
    factor = jnp.exp(got_peak - peak_value[None])
    denominator = jnp.sum(factor * got_total, axis=0)
    numerator = jnp.sum(
        factor[..., None] * got_value.reshape(wide_count, tok_rows, heads_here, VDIM), axis=0
    )
    context = (
        (numerator / denominator[..., None])
        .astype(jnp.bfloat16)
        .reshape(tok_rows, heads_here * VDIM)
    )
    partial_out = jnp.dot(context, o_full, preferred_element_type=jnp.float32)
    summed = lax.psum(partial_out.astype(jnp.bfloat16), "narrow")
    return summed


def solution(mesh):
    in_specs = (
        P("wide", None),
        P(),
        P("wide", "narrow"),
        P("wide", None),
        P(),
        P("wide", "narrow"),
        P("narrow", "wide"),
        P(None, "wide", None),
        P(),
    )
    out_specs = P("wide", None)
    return jax.shard_map(
        per_device, mesh=mesh, in_specs=in_specs, out_specs=out_specs, check_vma=False
    )
```

profile of v0, /device:TPU:1, one launch (start us, length us, event | category | flops | bytes accessed | tf_op | source)
XLA Modules:
  0.0 1511.4 jit_solution(1036586615018934695)
XLA Ops:
  11.5 128.7 %all-gather.8.cloned.1.call-done = bf16[512,1024]{1,0:T(8,128)(2,1)} async-done(((bf16[16,1024]{1,0:T(8,128)(2,1)}), bf16[512,1024]{1,0:T(8,128)(2,1)}) %all-gather.8.cloned.1.call-update) | async-done | bytes 1048592 | tf_op jit(solution)/shard_map/all_gather | solution.py:109
  141.7 155.5 %all-gather.12.cloned.1.call-done = bf16[2048,576]{1,0:T(8,128)(2,1)} async-done(((bf16[64,576]{1,0:T(8,128)(2,1)}), bf16[2048,576]{1,0:T(8,128)(2,1)}) %all-gather.12.cloned.1.call-update) | async-done | bytes 2359312 | tf_op jit(solution)/shard_map/all_gather | solution.py:108
  300.7 154.1 %all-gather.6.cloned.1.call-done = bf16[2048,768]{1,0:T(8,128)(2,1)} async-done(((bf16[64,768]{1,0:T(8,128)(2,1)}), bf16[2048,768]{1,0:T(8,128)(2,1)}) %all-gather.6.cloned.1.call-update) | async-done | bytes 3145744 | tf_op jit(solution)/shard_map/all_gather | solution.py:107
  465.4 456.9 %all-gather.10.cloned.1.call-done = bf16[4096,2304]{0,1:T(8,128)(2,1)} async-done(((bf16[128,2304]{0,1:T(8,128)(2,1)}), bf16[4096,2304]{0,1:T(8,128)(2,1)}) %all-gather.10.cloned.1.call-update) | async-done | bytes 18874384 | tf_op jit(solution)/shard_map/all_gather | solution.py:142
  927.7 19.3 %conditional.8 = (f32[512,4]{0,1:T(4,128)}, f32[512,4]{0,1:T(4,128)S(1)}, f32[512,4,128]{0,2,1:T(8,128)S(1)}) conditional(s32[]{:T(128)} %convert_element_type.237, () %tuple.69, (s32[]{:T(128)}, s32[1,640]{1,0:T(1,128)S(1)}, bf16[4096,2304]{0,1:T(8,128)(2,1)}, bf16[8,640,576]{1,2,0:T(8,128)(2,1)}, bf16[512,4,128]{0,2,1:T(8,128)(2,1)S(1)}) %tuple.70), branch_computations={%region_2.3_spmd, %region_3.6_spmd} | conditional | flops 3408916992 | bytes 65557944 | solution.py:157
  930.4 4.8 select_reduce_fusion
  943.7 3.3 fusion.1
  947.7 20.3 %conditional.9 = (f32[512,4]{0,1:T(4,128)}, f32[512,4]{0,1:T(4,128)S(1)}, f32[512,4,128]{0,2,1:T(8,128)}) conditional(s32[]{:T(128)} %convert_element_type.246, () %tuple.71, (s32[]{:T(128)}, s32[1,640]{1,0:T(1,128)S(1)}, bf16[4096,2304]{0,1:T(8,128)(2,1)}, bf16[8,640,576]{1,2,0:T(8,128)(2,1)}, bf16[512,4,128]{0,2,1:T(8,128)(2,1)S(1)}) %tuple.72), branch_computations={%region_6.7_spmd, %region_7.10_spmd} | conditional | flops 3408916992 | bytes 65557944 | solution.py:157
  950.4 4.8 select_reduce_fusion.1
  964.7 3.2 fusion.20
  968.7 20.2 %conditional.10 = (f32[512,4]{0,1:T(4,128)}, f32[512,4]{0,1:T(4,128)S(1)}, f32[512,4,128]{0,2,1:T(8,128)}) conditional(s32[]{:T(128)} %convert_element_type.247, () %tuple.73, (s32[]{:T(128)}, s32[1,640]{1,0:T(1,128)S(1)}, bf16[4096,2304]{0,1:T(8,128)(2,1)}, bf16[8,640,576]{1,2,0:T(8,128)(2,1)}, bf16[512,4,128]{0,2,1:T(8,128)(2,1)S(1)}) %tuple.74), branch_computations={%region_10.11_spmd, %region_11.14_spmd} | conditional | flops 3408916992 | bytes 65557944 | solution.py:157
  971.3 4.8 select_reduce_fusion.2
  985.6 3.2 fusion.39
  989.6 20.5 %conditional.11 = (f32[512,4]{0,1:T(4,128)}, f32[512,4]{0,1:T(4,128)S(1)}, f32[512,4,128]{0,2,1:T(8,128)}) conditional(s32[]{:T(128)} %convert_element_type.248, () %tuple.75, (s32[]{:T(128)}, s32[1,640]{1,0:T(1,128)S(1)}, bf16[4096,2304]{0,1:T(8,128)(2,1)}, bf16[8,640,576]{1,2,0:T(8,128)(2,1)}, bf16[512,4,128]{0,2,1:T(8,128)(2,1)S(1)}) %tuple.76), branch_computations={%region_14.15_spmd, %region_15.18_spmd} | conditional | flops 3408916992 | bytes 65557944 | solution.py:157
  992.5 4.8 select_reduce_fusion.3
  1006.8 3.2 fusion.58
  1010.8 20.2 %conditional.12 = (f32[512,4]{0,1:T(4,128)}, f32[512,4]{0,1:T(4,128)S(1)}, f32[512,4,128]{0,2,1:T(8,128)}) conditional(s32[]{:T(128)} %convert_element_type.249, () %tuple.77, (s32[]{:T(128)}, s32[1,640]{1,0:T(1,128)S(1)}, bf16[4096,2304]{0,1:T(8,128)(2,1)}, bf16[8,640,576]{1,2,0:T(8,128)(2,1)}, bf16[512,4,128]{0,2,1:T(8,128)(2,1)S(1)}) %tuple.78), branch_computations={%region_18.19_spmd, %region_19.22_spmd} | conditional | flops 3408916992 | bytes 65557944 | solution.py:157
  1013.4 4.8 select_reduce_fusion.4
  1027.8 3.2 fusion.77
  1031.7 20.2 %conditional.13 = (f32[512,4]{0,1:T(4,128)}, f32[512,4]{0,1:T(4,128)S(1)}, f32[512,4,128]{0,2,1:T(8,128)}) conditional(s32[]{:T(128)} %convert_element_type.250, () %tuple.79, (s32[]{:T(128)}, s32[1,640]{1,0:T(1,128)S(1)}, bf16[4096,2304]{0,1:T(8,128)(2,1)}, bf16[8,640,576]{1,2,0:T(8,128)(2,1)}, bf16[512,4,128]{0,2,1:T(8,128)(2,1)S(1)}) %tuple.80), branch_computations={%region_22.23_spmd, %region_23.26_spmd} | conditional | flops 3408916992 | bytes 65557944 | solution.py:157
  1034.3 4.9 select_reduce_fusion.5
  1048.6 3.2 fusion.96
  1052.6 20.2 %conditional.14 = (f32[512,4]{0,1:T(4,128)}, f32[512,4]{0,1:T(4,128)S(1)}, f32[512,4,128]{0,2,1:T(8,128)}) conditional(s32[]{:T(128)} %convert_element_type.251, () %tuple.81, (s32[]{:T(128)}, s32[1,640]{1,0:T(1,128)S(1)}, bf16[4096,2304]{0,1:T(8,128)(2,1)}, bf16[8,640,576]{1,2,0:T(8,128)(2,1)}, bf16[512,4,128]{0,2,1:T(8,128)(2,1)S(1)}) %tuple.82), branch_computations={%region_26.27_spmd, %region_27.30_spmd} | conditional | flops 3408916992 | bytes 65557944 | solution.py:157
  1055.2 4.8 select_reduce_fusion.6
  1069.6 3.2 fusion.115
  1073.5 20.7 %conditional.15 = (f32[512,4]{0,1:T(4,128)}, f32[512,4]{0,1:T(4,128)S(1)}, f32[512,4,128]{0,2,1:T(8,128)}) conditional(s32[]{:T(128)} %convert_element_type.252, () %tuple.83, (s32[]{:T(128)}, s32[1,640]{1,0:T(1,128)S(1)}, bf16[4096,2304]{0,1:T(8,128)(2,1)}, bf16[8,640,576]{1,2,0:T(8,128)(2,1)}, bf16[512,4,128]{0,2,1:T(8,128)(2,1)S(1)}) %tuple.84), branch_computations={%region_30.31_spmd, %region_31.34_spmd} | conditional | flops 3408916992 | bytes 65557944 | solution.py:157
  1076.5 4.8 select_reduce_fusion.7
  1099.8 4.4 convert_bitcast_fusion.2
  1104.9 24.4 %reduce.23 = bf16[4096,4]{1,0:T(8,128)(2,1)} reduce(bf16[4096,1,4]{2,1,0:T(2,128)(2,1)} %convert_bitcast_fusion.2, bf16[]{:T(256)} %broadcast.452), dimensions={1}, to_apply=%convert_bitcast_fusion.2.reduce_sub_computation | reduce | bytes 65538
  1129.3 3.7 reshape.363
  1133.0 4.1 all-to-all-start
  1138.0 4.9 convert_bitcast_fusion.1
  1160.9 24.4 %reduce.22 = bf16[4096,4]{1,0:T(8,128)(2,1)} reduce(bf16[4096,1,4]{2,1,0:T(2,128)(2,1)} %convert_bitcast_fusion.1, bf16[]{:T(256)} %broadcast.452), dimensions={1}, to_apply=%convert_bitcast_fusion.1.reduce_sub_computation | reduce | bytes 65538
  1185.3 3.7 reshape.365
  1189.0 8.1 all-to-all-start.2
  1197.2 5.8 fusion.159
  1202.9 6.0 convert_element_type.261
  1208.9 18.9 %copy.254 = bf16[1,4096,512]{2,0,1:T(2,128)(2,1)} copy(bf16[1,4096,512]{1,2,0:T(8,128)(2,1)} %bitcast.201) | data formatting | bytes 8388608 | tf_op jit(solution)/shard_map/convert_element_type | solution.py:188
  1227.8 28.5 %reduce.21 = bf16[4096,512]{1,0:T(8,128)(2,1)} reduce(bf16[4096,1,512]{2,1,0:T(2,128)(2,1)} %bitcast.198, bf16[]{:T(256)} %broadcast.452), dimensions={1}, to_apply=%bitcast.143.reduce_sub_computation | reduce | bytes 8388610
  1256.3 7.8 reshape.361
  1264.1 7.9 all-to-all-start.1
  1282.3 44.2 %all-to-all-done.1 = bf16[32,2,32768]{2,1,0:T(2,128)(2,1)} async-done(((bf16[32,2,32768]{2,1,0:T(2,128)(2,1)}), bf16[32,2,32768]{2,1,0:T(2,128)(2,1)}, u32[]{:S(2)}, u32[]{:S(2)}) %all-to-all-start.1) | async-done | bytes 4194336 | tf_op jit(solution)/shard_map/all_to_all | solution.py:187
  1326.4 19.8 %reshape.362 = bf16[4096,1,512]{2,1,0:T(2,128)(2,1)} reshape(bf16[32,2,32768]{2,1,0:T(2,128)(2,1)} %all-to-all-done.1) | data formatting | bytes 8388608
  1346.2 10.8 bitcast_convert_fusion
  1357.0 8.0 copy.255
  1365.0 5.4 multiply_reduce_fusion
  1370.5 65.5 %all-gather.14.cloned.1.call-done = bf16[512,2048]{0,1:T(8,128)(2,1)} async-done(((bf16[512,64]{0,1:T(8,128)(2,1)}), bf16[512,2048]{0,1:T(8,128)(2,1)}) %all-gather.14.cloned.1.call-update) | async-done | bytes 2097168 | tf_op jit(solution)/shard_map/all_gather | solution.py:110
  1439.2 63.3 %all-reduce.2.cloned.1.call-done = bf16[128,2048]{1,0:T(8,128)(2,1)} async-done(((bf16[128,2048]{1,0:T(8,128)(2,1)}), bf16[128,2048]{1,0:T(8,128)(2,1)}) %all-reduce.2.cloned.1.call-update) | async-done | bytes 524304 | tf_op jit(solution)/shard_map/psum | solution.py:207
  (171 shorter events, 163.7 us)
Async XLA Ops:
  6.5 448.2 %copy-start.9 = (bf16[128,2048]{1,0:T(8,128)(2,1)S(1)}, bf16[128,2048]{1,0:T(8,128)(2,1)}, u32[]{:S(2)}) copy-start(bf16[128,2048]{1,0:T(8,128)(2,1)} %param.25) | copy-start | bytes 1572868
  6.5 133.7 %all-gather.8.cloned.1.call-start = ((), (), s32[]{:S(2)}) async-start(), calls=%async_computation.4 | async-start | bytes 1081344 | tf_op jit(solution)/shard_map/all_gather | solution.py:109
  7.3 290.0 %all-gather.12.cloned.1.call-start = ((), (), s32[]{:S(2)}) async-start(), calls=%async_computation.6 | async-start | bytes 2703360 | tf_op jit(solution)/shard_map/all_gather | solution.py:108
  8.0 446.7 %all-gather.6.cloned.1.call-start = ((), (), s32[]{:S(2)}) async-start(), calls=%async_computation.3 | async-start | bytes 3244032 | tf_op jit(solution)/shard_map/all_gather | solution.py:107
  8.7 913.6 %all-gather.10.cloned.1.call-start = ((), (), s32[]{:S(2)}) async-start(), calls=%async_computation.5 | async-start | bytes 19464192 | tf_op jit(solution)/shard_map/all_gather | solution.py:142
  300.6 158.8 %copy-start.10 = (s32[8]{0:T(128)S(1)}, s32[8]{0:T(128)}, u32[]{:S(2)}) copy-start(s32[8]{0:T(128)} %param.33) | copy-start | bytes 100
  300.7 164.3 %copy-start.11 = (bf16[512]{0:T(512)(128)(2,1)S(1)}, bf16[512]{0:T(512)(128)(2,1)}, u32[]{:S(2)}) copy-start(bf16[512]{0:T(512)(128)(2,1)} %param.29) | copy-start | bytes 3076
  935.2 4.5 copy-start.1
  955.2 4.5 copy-start.2
  976.2 4.5 copy-start.3
  997.4 4.5 copy-start.4
  1018.2 4.5 copy-start.5
  1039.2 4.5 copy-start.6
  1060.1 4.5 copy-start.7
  1081.3 4.5 copy-start.8
  1133.0 56.0 %all-to-all-start = ((bf16[32,2,256]{2,1,0:T(2,128)(2,1)}), bf16[32,2,256]{2,1,0:T(2,128)(2,1)S(1)}, u32[]{:S(2)}, u32[]{:S(2)}) async-start(bf16[32,2,256]{2,1,0:T(2,128)(2,1)} %reshape.363), calls=%async_computation | async-start | bytes 65536 | tf_op jit(solution)/shard_map/all_to_all | solution.py:181
  1137.2 6.7 copy-start
  1189.0 75.1 %all-to-all-start.2 = ((bf16[32,2,256]{2,1,0:T(2,128)(2,1)}), bf16[32,2,256]{2,1,0:T(2,128)(2,1)S(1)}, u32[]{:S(2)}, u32[]{:S(2)}) async-start(bf16[32,2,256]{2,1,0:T(2,128)(2,1)} %reshape.365), calls=%async_computation.2 | async-start | bytes 65536 | tf_op jit(solution)/shard_map/all_to_all | solution.py:184
  1264.1 62.3 %all-to-all-start.1 = ((bf16[32,2,32768]{2,1,0:T(2,128)(2,1)}), bf16[32,2,32768]{2,1,0:T(2,128)(2,1)}, u32[]{:S(2)}, u32[]{:S(2)}) async-start(bf16[32,2,32768]{2,1,0:T(2,128)(2,1)} %reshape.361), calls=%async_computation.1 | async-start | bytes 8388608 | tf_op jit(solution)/shard_map/all_to_all | solution.py:187
  1272.0 164.0 %all-gather.14.cloned.1.call-start = ((), (), s32[]{:S(2)}) async-start(), calls=%async_computation.7 | async-start | bytes 2162688 | tf_op jit(solution)/shard_map/all_gather | solution.py:110
  1272.5 229.9 %all-reduce.2.cloned.1.call-start = ((), (), s32[]{:S(2)}) async-start(), calls=%async_computation.8 | async-start | bytes 1048576 | tf_op jit(solution)/shard_map/psum | solution.py:207
Sparse Core Ops, SparseCore 0:
  9.0 131.2 all-gather.7
  141.9 155.3 all-gather.11
  298.9 155.8 all-gather.5
  459.4 462.8 all-gather.9
  1274.1 161.7 all-gather.13
  1439.3 63.0 all-reduce.1
where the time goes:
time: 1520 us; the launch traced here: 1510 us
  waiting for transfers between devices  1070 us (70%)
  local copies, waits for them, and re-layouts  154 us (10%)
  other arithmetic  144 us (9%)
  matrix products  101 us (7%)
  starting transfers between devices  20.3 us (1%)
  between operations  19 us (1%)
    all_gather x1, waiting for transfers between devices, per_device(): gathered = lax.all_gather(outgoing, 'wide', axis=0, tiled=True)  457 us
    all_gather x1, waiting for transfers between devices, per_device(): lax.all_gather(kva_weight, 'wide', axis=0, tiled=True)  156 us
    all_gather x1, waiting for transfers between devices, per_device(): lax.all_gather(q_weight, 'wide', axis=0, tiled=True)  154 us
    all_gather x1, waiting for transfers between devices, per_device(): lax.all_gather(kvb_weight, 'wide', axis=0, tiled=True)  129 us
    unnamed x6, other arithmetic  86.7 us
    all_gather x1, waiting for transfers between devices, per_device(): lax.all_gather(o_weight, 'wide', axis=1, tiled=True)  65.5 us
    psum x1, waiting for transfers between devices, per_device(): summed = lax.psum(partial_out.astype(jnp.bfloat16), 'narrow')  63.3 us
    unnamed x37, local copies, waits for them, and re-layouts  63 us
  transfers between devices with their start and end apart: 9, of which 7 were waited for; matrix products, arithmetic and copies ran while one was open for 12% of the time, Pallas kernels for 0%

commit v1 on v0

--- a/solution.py
+++ b/solution.py
@@ -39,6 +39,12 @@
     )
 
 
+def gather_axis(x, axis_name):
+    count = lax.axis_size(axis_name)
+    spread = jnp.broadcast_to(x[None], (count,) + x.shape)
+    return lax.all_to_all(spread, axis_name, split_axis=0, concat_axis=0, tiled=True)
+
+
 def absorb(nope_part, key_maps):
     return jnp.einsum(
         "thc,lhc->thl", nope_part, key_maps, preferred_element_type=jnp.float32
@@ -64,6 +70,7 @@
     )
     live_rows = live_mask[:, None, :]
     row_peak = jnp.max(jnp.where(live_rows, scores, -1e30), axis=-1)
+    row_peak = row_peak.astype(jnp.bfloat16).astype(jnp.float32)
     weights = jnp.where(live_rows, jnp.exp(scores - row_peak[..., None]), 0.0)
     row_total = jnp.sum(weights, axis=-1)
     mixed = jnp.einsum(
@@ -103,15 +110,23 @@
     requests = lengths.shape[0]
     cache_rows = cache.shape[1]
     heads_here = q_weight.shape[1] // (NOPE + ROPE)
-    q_full, kva_full, kvb_full, o_full = (
-        lax.all_gather(q_weight, "wide", axis=0, tiled=True),
-        lax.all_gather(kva_weight, "wide", axis=0, tiled=True),
-        lax.all_gather(kvb_weight, "wide", axis=0, tiled=True),
-        lax.all_gather(o_weight, "wide", axis=1, tiled=True),
-    )
+    q_cols = q_weight.shape[1]
+    kva_cols = kva_weight.shape[1]
+    kvb_cols = kvb_weight.shape[1]
+    q_size = q_weight.size
+    kva_size = kva_weight.size
+    packed = jnp.concatenate(
+        [q_weight.reshape(-1), kva_weight.reshape(-1), kvb_weight.reshape(-1)]
+    )
+    got_weights = gather_axis(packed, "wide")
+    q_full = got_weights[:, :q_size].reshape(-1, q_cols)
+    kva_full = got_weights[:, q_size : q_size + kva_size].reshape(-1, kva_cols)
+    kvb_full = got_weights[:, q_size + kva_size :].reshape(-1, kvb_cols)
+    o_got = gather_axis(o_weight, "wide")
+    o_full = jnp.transpose(o_got, (1, 0, 2)).reshape(o_weight.shape[0], -1)
+
     normed = scaled_norm(hidden.astype(jnp.float32), attn_gain).astype(jnp.bfloat16)
     query_rows = jnp.dot(normed, q_full, preferred_element_type=jnp.float32).astype(jnp.bfloat16)
-    query_rows = query_rows.reshape(tok_rows, heads_here, NOPE + ROPE)
     compressed = jnp.dot(normed, kva_full, preferred_element_type=jnp.float32)
     first_token = wide_place * tok_rows
     token_ids = first_token + jnp.arange(tok_rows, dtype=jnp.int32)
@@ -128,31 +143,36 @@
         ],
         axis=1,
     )
-    q_nope = query_rows[..., :NOPE]
-    q_rope = rotate(query_rows[..., NOPE:].astype(jnp.float32), positions[:, None]).astype(
-        jnp.bfloat16
-    )
+
+    raw_all = gather_axis(query_rows, "wide")
+    total_tokens = raw_all.shape[0] * tok_rows
+    raw_all = raw_all.reshape(total_tokens, heads_here, NOPE + ROPE)
+    all_ids = jnp.arange(total_tokens, dtype=jnp.int32)
+    all_request = all_ids // SPAN
+    all_length = jnp.sum(
+        jnp.where(all_request[:, None] == request_ids[None, :], lengths[None, :], 0), axis=1
+    )
+    all_positions = all_length + all_ids % SPAN
     kvb_heads = kvb_full.reshape(LAT, heads_here, NOPE + VDIM)
     key_maps = kvb_heads[..., :NOPE]
     value_maps = kvb_heads[..., NOPE:]
-    outgoing = jnp.concatenate([absorb(q_nope, key_maps), q_rope], axis=-1).reshape(
-        tok_rows, heads_here * (LAT + ROPE)
-    )
+    q_rope = rotate(raw_all[..., NOPE:].astype(jnp.float32), all_positions[:, None]).astype(
+        jnp.bfloat16
+    )
+    queries = jnp.concatenate([absorb(raw_all[..., :NOPE], key_maps), q_rope], axis=-1)
+
     own_request = first_token // SPAN
-    gathered = lax.all_gather(outgoing, "wide", axis=0, tiled=True)
-    total_tokens = gathered.shape[0]
-    queries = gathered.reshape(total_tokens, heads_here, LAT + ROPE)
     blocks = [cache[request] for request in range(requests)]
-    starts = [wide_place * cache_rows for request in range(requests)]
+    start = wide_place * cache_rows
     cache_slots = jnp.arange(cache_rows, dtype=jnp.int32)
     peaks_list = []
     totals_list = []
     values_list = []
     for request in range(requests):
         length_now = lengths[request]
-        cache_live = starts[request] + cache_slots < length_now
+        cache_live = start + cache_slots < length_now
         live_mask = jnp.broadcast_to(cache_live[None, :], (SPAN, cache_rows))
-        block_live = starts[request] < length_now
+        block_live = start < length_now
         block_queries = queries[request * SPAN : (request + 1) * SPAN]
         row_peak, row_total, row_value = lax.cond(
             block_live, attend, skipped, block_queries, blocks[request], live_mask, value_maps
@@ -174,38 +194,46 @@
         lax.dynamic_slice_in_dim(value_all, start_row, SPAN, 0),
     )
     joint = merge_parts(old_part, own_part)
-    peak_all = lax.dynamic_update_slice_in_dim(peak_all, joint[0], start_row, 0)
-    total_all = lax.dynamic_update_slice_in_dim(total_all, joint[1], start_row, 0)
-    value_all = lax.dynamic_update_slice_in_dim(value_all, joint[2], start_row, 0)
-    got_peak, got_total, got_value = (
-        lax.all_to_all(
-            peak_all[None].astype(jnp.bfloat16), "wide", split_axis=1, concat_axis=0, tiled=True
-        ).astype(jnp.float32),
-        lax.all_to_all(
-            total_all[None].astype(jnp.bfloat16), "wide", split_axis=1, concat_axis=0, tiled=True
-        ).astype(jnp.float32),
-        lax.all_to_all(
-            value_all.reshape(1, total_tokens, heads_here * VDIM).astype(jnp.bfloat16),
-            "wide",
-            split_axis=1,
-            concat_axis=0,
-            tiled=True,
-        ).astype(jnp.float32),
-    )
+    joint_peak = joint[0].astype(jnp.bfloat16).astype(jnp.float32)
+    shift = jnp.exp(joint[0] - joint_peak)
+    peak_all = lax.dynamic_update_slice_in_dim(peak_all, joint_peak, start_row, 0)
+    total_all = lax.dynamic_update_slice_in_dim(total_all, joint[1] * shift, start_row, 0)
+    value_all = lax.dynamic_update_slice_in_dim(
+        value_all, joint[2] * shift[..., None], start_row, 0
+    )
+    stats = jnp.concatenate([peak_all, total_all], axis=1).astype(jnp.bfloat16)
+    got_stats = lax.all_to_all(
+        stats.reshape(wide_count, tok_rows, 2 * heads_here), "wide", 0, 0, tiled=True
+    ).astype(jnp.float32)
+    got_value = lax.all_to_all(
+        value_all.astype(jnp.bfloat16).reshape(wide_count, tok_rows, heads_here, VDIM),
+        "wide",
+        0,
+        0,
+        tiled=True,
+    ).astype(jnp.float32)
+    got_peak = got_stats[..., :heads_here]
+    got_total = got_stats[..., heads_here:]
     peak_value = jnp.max(got_peak, axis=0)
     factor = jnp.exp(got_peak - peak_value[None])
     denominator = jnp.sum(factor * got_total, axis=0)
-    numerator = jnp.sum(
-        factor[..., None] * got_value.reshape(wide_count, tok_rows, heads_here, VDIM), axis=0
-    )
+    numerator = jnp.sum(factor[..., None] * got_value, axis=0)
     context = (
         (numerator / denominator[..., None])
         .astype(jnp.bfloat16)
         .reshape(tok_rows, heads_here * VDIM)
     )
     partial_out = jnp.dot(context, o_full, preferred_element_type=jnp.float32)
-    summed = lax.psum(partial_out.astype(jnp.bfloat16), "narrow")
-    return summed
+    narrow_count = lax.axis_size("narrow")
+    out_cols = partial_out.shape[1]
+    pieces = jnp.transpose(
+        partial_out.astype(jnp.bfloat16).reshape(tok_rows, narrow_count, out_cols // narrow_count),
+        (1, 0, 2),
+    )
+    got_pieces = lax.all_to_all(pieces, "narrow", 0, 0, tiled=True)
+    mine = jnp.sum(got_pieces.astype(jnp.float32), axis=0).astype(jnp.bfloat16)
+    all_pieces = gather_axis(mine, "narrow")
+    return jnp.transpose(all_pieces, (1, 0, 2)).reshape(tok_rows, out_cols)
 
 
 def solution(mesh):

time: 1520 us -> 650 us (0.43)
  waiting for transfers between devices: 1070 us -> 179 us
  blocking collectives: 0 us -> 86.7 us
  other arithmetic: 144 us -> 96.4 us
    all_gather x5 -> x0, waiting for transfers between devices: 961 us -> none  [the longest x1 457 us: per_device(): gathered = lax.all_gather(outgoing, 'wide', axis=0, tiled=True)]
    all_to_all x3 -> x4, waiting for transfers between devices: 44.2 us -> 179 us  [the longest x3 179 us: gather_axis(): lax.all_to_all(spread, axis_name, split_axis=0, concat_axis=0, tiled=True)]
    unnamed x6 -> x0, other arithmetic: 86.7 us -> none
    all_to_all x0 -> x3, blocking collectives: none -> 86.7 us  [the longest x1 55.9 us: per_device(): lax.all_to_all(value_all.astype(jnp.bfloat16).reshape(wide_count, tok_row...]
    psum x1 -> x0, waiting for transfers between devices: 63.3 us -> none  [per_device(): summed = lax.psum(partial_out.astype(jnp.bfloat16), 'narrow')]
    broadcast_in_dim x1, other arithmetic: 0.02 us -> 42.8 us  [gather_axis(): spread = jnp.broadcast_to(x[None], (count,) + x.shape)]
    convert_element_type x2 -> x0, local copies, waits for them, and re-layouts: 26.9 us -> none  [the longest x1 18.9 us: per_device(): value_all.reshape(1, total_tokens, heads_here * VDIM).astype(jnp.bfloat16)]
    reshape x0 -> x7, local copies, waits for them, and re-layouts: none -> 21.4 us  [the longest x1 10.3 us: per_device(): raw_all = raw_all.reshape(total_tokens, heads_here, NOPE + ROPE)]
  transfers between devices with their start and end apart: 9 -> 4, of which waited for: 7 -> 3; matrix products, arithmetic and copies ran while one was open for 12% -> 6% of each run, Pallas kernels for 0% -> 0%
where the time goes in v1:
time: 650 us; the launch traced here: 641 us
  waiting for transfers between devices  179 us (28%)
  local copies, waits for them, and re-layouts  143 us (22%)
  matrix products  99.2 us (15%)
  other arithmetic  96.4 us (15%)
  blocking collectives  86.7 us (13%)
  starting transfers between devices  29.3 us (5%)
    all_to_all x3, waiting for transfers between devices, gather_axis(): lax.all_to_all(spread, axis_name, split_axis=0, concat_axis=0, tiled=True)  179 us
    all_to_all x1, blocking collectives, per_device(): lax.all_to_all(value_all.astype(jnp.bfloat16).reshape(wide_count, tok_row...  55.9 us
    unnamed x42, local copies, waits for them, and re-layouts  53.8 us
    broadcast_in_dim x1, other arithmetic, gather_axis(): spread = jnp.broadcast_to(x[None], (count,) + x.shape)  42.8 us
    dot_general x9, matrix products, attend(): jnp.einsum('qhc,kc->qhk', block_queries, key_rows, preferred_element_type...  42.1 us
    all_to_all x3, starting transfers between devices, gather_axis(): lax.all_to_all(spread, axis_name, split_axis=0, concat_axis=0, tiled=True)  25.4 us
    broadcast_in_dim x5, local copies, waits for them, and re-layouts, gather_axis(): spread = jnp.broadcast_to(x[None], (count,) + x.shape)  19.2 us
    dot_general x9, matrix products, attend(): jnp.einsum('qhk,kc->qhc', weights.astype(jnp.bfloat16), key_rows[:, :LAT]...  19.2 us
  transfers between devices with their start and end apart: 4, of which 3 were waited for; matrix products, arithmetic and copies ran while one was open for 6% of the time, Pallas kernels for 0%

profile of v1, /device:TPU:1, one launch (start us, length us, event | category | flops | bytes accessed | tf_op | source)
XLA Modules:
  0.0 641.1 jit_solution(7006646920720835009)
XLA Ops:
  2.8 13.0 %broadcast_in_dim.223 = bf16[32,1,102400]{2,1,0:T(2,128)(2,1)} broadcast(bf16[102400]{0:T(1024)(128)(2,1)S(1)} %pad_maximum_fusion.1), dimensions={2} | broadcast | bytes 6758400 | tf_op jit(solution)/shard_map/broadcast_in_dim | solution.py:44
  16.3 42.8 %reduce.17 = bf16[32,102400]{1,0:T(8,128)(2,1)} reduce(bf16[32,1,102400]{2,1,0:T(2,128)(2,1)} %broadcast_in_dim.223, bf16[]{:T(256)} %broadcast.463), dimensions={1}, to_apply=%broadcast_in_dim.223.reduce_sub_computation | reduce | bytes 13107202 | tf_op jit(solution)/shard_map/broadcast_in_dim | solution.py:44
  59.1 9.0 %reshape.364 = bf16[32,2,51200]{2,1,0:T(2,128)(2,1)} reshape(bf16[32,102400]{1,0:T(8,128)(2,1)} %reduce.17) | data formatting | bytes 13107200
  68.2 9.7 %all-to-all-start = ((bf16[32,2,51200]{2,1,0:T(2,128)(2,1)}), bf16[32,2,51200]{2,1,0:T(2,128)(2,1)}, u32[]{:S(2)}, u32[]{:S(2)}) async-start(bf16[32,2,51200]{2,1,0:T(2,128)(2,1)} %reshape.364), calls=%async_computation | async-start | bytes 13107200 | tf_op jit(solution)/shard_map/all_to_all | solution.py:45
  78.1 92.2 %all-to-all-done = bf16[32,2,51200]{2,1,0:T(2,128)(2,1)} async-done(((bf16[32,2,51200]{2,1,0:T(2,128)(2,1)}), bf16[32,2,51200]{2,1,0:T(2,128)(2,1)}, u32[]{:S(2)}, u32[]{:S(2)}) %all-to-all-start) | async-done | bytes 6553632 | tf_op jit(solution)/shard_map/all_to_all | solution.py:45
  170.3 22.0 %reshape.365 = bf16[32,1,102400]{2,1,0:T(2,128)(2,1)} reshape(bf16[32,2,51200]{2,1,0:T(2,128)(2,1)} %all-to-all-done) | data formatting | bytes 13107200
  192.2 14.6 %copy.257 = bf16[32,1,102400]{2,0,1:T(8,128)(2,1)} copy(bf16[32,1,102400]{2,1,0:T(2,128)(2,1)} %reshape.365) | data formatting | bytes 13107200
  206.8 3.8 slice.189
  210.6 3.4 reshape.331
  215.8 4.1 broadcast_in_dim.224
  219.9 10.2 %all-to-all-start.1 = ((bf16[32,128,768]{1,2,0:T(8,128)(2,1)}), bf16[32,128,768]{1,2,0:T(8,128)(2,1)}, u32[]{:S(2)}, u32[]{:S(2)}) async-start(bf16[32,128,768]{1,2,0:T(8,128)(2,1)} %broadcast_in_dim.224), calls=%async_computation.1 | async-start | bytes 12582912 | tf_op jit(solution)/shard_map/all_to_all | solution.py:45
  236.1 2.8 multiply_cosine_fusion
  240.2 3.3 slice.195
  245.7 4.5 reshape.333
  252.9 62.5 %all-to-all-done.1 = bf16[32,128,768]{1,2,0:T(8,128)(2,1)} async-done(((bf16[32,128,768]{1,2,0:T(8,128)(2,1)}), bf16[32,128,768]{1,2,0:T(8,128)(2,1)}, u32[]{:S(2)}, u32[]{:S(2)}) %all-to-all-start.1) | async-done | bytes 6291488 | tf_op jit(solution)/shard_map/all_to_all | solution.py:45
  315.4 9.5 %copy.173 = bf16[32,128,768]{1,0,2:T(8,128)(2,1)} copy(bf16[32,128,768]{1,2,0:T(8,128)(2,1)} %all-to-all-done.1) | data formatting | bytes 12582912 | tf_op jit(solution)/shard_map/all_to_all | solution.py:45
  324.9 10.3 %reshape.332 = bf16[4096,4,192]{0,2,1:T(8,128)(2,1)} reshape(bf16[32,128,768]{1,0,2:T(8,128)(2,1)} %copy.173) | data formatting | bytes 12582912 | tf_op jit(solution)/shard_map/reshape | solution.py:149
  335.2 4.2 slice_convert_fusion
  339.4 10.5 %convert_bitcast_fusion = bf16[4096,4,512]{0,2,1:T(8,128)(2,1)} fusion(bf16[4096,4,192]{0,2,1:T(8,128)(2,1)} %reshape.332, bf16[512,4,128]{2,1,0:T(4,128)(2,1)S(1)} %copy-done.3), kind=kOutput, calls=%fused_computation.209 | convolution fusion | flops 2155872256 | bytes 21495808 | tf_op jit(solution)/shard_map/thc,lhc->thl/dot_general | solution.py:49
  349.9 2.9 subtract_convert_fusion.50
  352.8 18.8 %pad_maximum_fusion = bf16[4096,4,576]{0,2,1:T(8,128)(2,1)} fusion(bf16[4096,4,32]{0,2,1:T(8,128)(2,1)S(1)} %get-tuple-element.405, bf16[4096,4,32]{0,2,1:T(8,128)(2,1)S(1)} %get-tuple-element.404, bf16[4096,4,512]{0,2,1:T(8,128)(2,1)} %convert_bitcast_fusion), kind=kLoop, calls=%fused_computation.208 | loop fusion | flops 56623104 | bytes 37748736 | tf_op jit(solution)/shard_map/concatenate | solution.py:162
  374.1 2.8 fusion.181
  376.9 12.2 %conditional.8 = (f32[512,4]{0,1:T(4,128)S(1)}, f32[512,4]{0,1:T(4,128)S(1)}, f32[512,4,128]{0,2,1:T(8,128)S(1)}) conditional(s32[]{:T(128)} %convert_element_type.338, () %tuple.69, (s32[]{:T(128)}, s32[1,640]{1,0:T(1,128)S(1)}, bf16[4096,4,576]{0,2,1:T(8,128)(2,1)}, bf16[8,640,576]{1,2,0:T(8,128)(2,1)}, bf16[512,4,128]{0,2,1:T(8,128)(2,1)S(1)}) %tuple.70), branch_computations={%region_2.3_spmd, %region_3.6_spmd} | conditional | flops 3408919040 | bytes 39941588 | solution.py:177
  377.6 5.0 select_reduce_fusion
  389.1 14.6 %conditional.9 = (f32[512,4]{0,1:T(4,128)S(1)}, f32[512,4]{0,1:T(4,128)S(1)}, f32[512,4,128]{0,2,1:T(8,128)S(1)}) conditional(s32[]{:T(128)} %convert_element_type.347, () %tuple.71, (s32[]{:T(128)}, s32[1,640]{1,0:T(1,128)S(1)}, bf16[4096,4,576]{0,2,1:T(8,128)(2,1)}, bf16[8,640,576]{1,2,0:T(8,128)(2,1)}, bf16[512,4,128]{0,2,1:T(8,128)(2,1)S(1)}) %tuple.72), branch_computations={%region_6.7_spmd, %region_7.10_spmd} | conditional | flops 3408919040 | bytes 39941588 | solution.py:177
  389.8 5.0 select_reduce_fusion.1
  403.7 15.4 %conditional.10 = (f32[512,4]{0,1:T(4,128)S(1)}, f32[512,4]{0,1:T(4,128)S(1)}, f32[512,4,128]{0,2,1:T(8,128)}) conditional(s32[]{:T(128)} %convert_element_type.348, () %tuple.73, (s32[]{:T(128)}, s32[1,640]{1,0:T(1,128)S(1)}, bf16[4096,4,576]{0,2,1:T(8,128)(2,1)}, bf16[8,640,576]{1,2,0:T(8,128)(2,1)}, bf16[512,4,128]{0,2,1:T(8,128)(2,1)S(1)}) %tuple.74), branch_computations={%region_10.11_spmd, %region_11.14_spmd} | conditional | flops 3408919040 | bytes 39941588 | solution.py:177
  404.4 5.0 select_reduce_fusion.2
  419.1 15.8 %conditional.11 = (f32[512,4]{0,1:T(4,128)S(1)}, f32[512,4]{0,1:T(4,128)S(1)}, f32[512,4,128]{0,2,1:T(8,128)}) conditional(s32[]{:T(128)} %convert_element_type.349, () %tuple.75, (s32[]{:T(128)}, s32[1,640]{1,0:T(1,128)S(1)}, bf16[4096,4,576]{0,2,1:T(8,128)(2,1)}, bf16[8,640,576]{1,2,0:T(8,128)(2,1)}, bf16[512,4,128]{0,2,1:T(8,128)(2,1)S(1)}) %tuple.76), branch_computations={%region_14.15_spmd, %region_15.18_spmd} | conditional | flops 3408919040 | bytes 39941588 | solution.py:177
  420.1 5.0 select_reduce_fusion.3
  432.3 2.6 copy.235
  434.9 15.5 %conditional.12 = (f32[512,4]{0,1:T(4,128)S(1)}, f32[512,4]{0,1:T(4,128)S(1)}, f32[512,4,128]{0,2,1:T(8,128)}) conditional(s32[]{:T(128)} %convert_element_type.350, () %tuple.77, (s32[]{:T(128)}, s32[1,640]{1,0:T(1,128)S(1)}, bf16[4096,4,576]{0,2,1:T(8,128)(2,1)}, bf16[8,640,576]{1,2,0:T(8,128)(2,1)}, bf16[512,4,128]{0,2,1:T(8,128)(2,1)S(1)}) %tuple.78), branch_computations={%region_18.19_spmd, %region_19.22_spmd} | conditional | flops 3408919040 | bytes 39941588 | solution.py:177
  435.7 5.0 select_reduce_fusion.4
  450.4 15.6 %conditional.13 = (f32[512,4]{0,1:T(4,128)S(1)}, f32[512,4]{0,1:T(4,128)S(1)}, f32[512,4,128]{0,2,1:T(8,128)}) conditional(s32[]{:T(128)} %convert_element_type.351, () %tuple.79, (s32[]{:T(128)}, s32[1,640]{1,0:T(1,128)S(1)}, bf16[4096,4,576]{0,2,1:T(8,128)(2,1)}, bf16[8,640,576]{1,2,0:T(8,128)(2,1)}, bf16[512,4,128]{0,2,1:T(8,128)(2,1)S(1)}) %tuple.80), branch_computations={%region_22.23_spmd, %region_23.26_spmd} | conditional | flops 3408919040 | bytes 39941588 | solution.py:177
  451.3 5.0 select_reduce_fusion.5
  466.0 15.5 %conditional.14 = (f32[512,4]{0,1:T(4,128)S(1)}, f32[512,4]{0,1:T(4,128)S(1)}, f32[512,4,128]{0,2,1:T(8,128)}) conditional(s32[]{:T(128)} %convert_element_type.352, () %tuple.81, (s32[]{:T(128)}, s32[1,640]{1,0:T(1,128)S(1)}, bf16[4096,4,576]{0,2,1:T(8,128)(2,1)}, bf16[8,640,576]{1,2,0:T(8,128)(2,1)}, bf16[512,4,128]{0,2,1:T(8,128)(2,1)S(1)}) %tuple.82), branch_computations={%region_26.27_spmd, %region_27.30_spmd} | conditional | flops 3408919040 | bytes 39941588 | solution.py:177
  466.8 5.0 select_reduce_fusion.6
  481.5 15.6 %conditional.15 = (f32[512,4]{0,1:T(4,128)S(1)}, f32[512,4]{0,1:T(4,128)S(1)}, f32[512,4,128]{0,2,1:T(8,128)}) conditional(s32[]{:T(128)} %convert_element_type.353, () %tuple.83, (s32[]{:T(128)}, s32[1,640]{1,0:T(1,128)S(1)}, bf16[4096,4,576]{0,2,1:T(8,128)(2,1)}, bf16[8,640,576]{1,2,0:T(8,128)(2,1)}, bf16[512,4,128]{0,2,1:T(8,128)(2,1)S(1)}) %tuple.84), branch_computations={%region_30.31_spmd, %region_31.34_spmd} | conditional | flops 3408919040 | bytes 39941588 | solution.py:177
  482.4 5.0 select_reduce_fusion.7
  498.0 3.9 all-to-all-start.2
  501.9 3.0 fusion.177
  514.3 3.1 copy_bitcast_fusion.1
  517.4 55.9 %all_to_all.39 = bf16[32,128,4,128]{1,3,2,0:T(8,128)(2,1)} all-to-all(bf16[32,128,4,128]{1,3,2,0:T(8,128)(2,1)} %copy_bitcast_fusion.1), channel_id=1, replica_groups=mesh['wide'=32,'narrow'=4] {'wide'}, dimensions={0} | all-to-all | bytes 8388608 | tf_op jit(solution)/shard_map/all_to_all | solution.py:208
  574.9 5.6 all-to-all-start.4
  580.6 3.2 multiply_reduce_fusion
  583.8 24.1 %all-to-all-done.4 = bf16[32,512,64]{1,2,0:T(8,128)(2,1)S(1)} async-done(((bf16[32,512,64]{1,2,0:T(8,128)(2,1)}), bf16[32,512,64]{1,2,0:T(8,128)(2,1)S(1)}, u32[]{:S(2)}, u32[]{:S(2)}) %all-to-all-start.4) | async-done | bytes 2097184 | tf_op jit(solution)/shard_map/all_to_all | solution.py:45
  608.8 18.1 %all_to_all.40 = bf16[4,128,512]{2,1,0:T(8,128)(2,1)S(1)} all-to-all(bf16[4,128,512]{2,1,0:T(8,128)(2,1)S(1)} %bitcast.180), channel_id=1, replica_groups=mesh['wide'=32,'narrow'=4] {'narrow'}, dimensions={0} | all-to-all | bytes 1048576 | tf_op jit(solution)/shard_map/all_to_all | solution.py:233
  627.0 12.7 %all_to_all.41 = bf16[4,128,512]{2,1,0:T(8,128)(2,1)S(1)} all-to-all(bf16[4,128,512]{2,1,0:T(8,128)(2,1)S(1)} %broadcast_in_dim.233), channel_id=1, replica_groups=mesh['wide'=32,'narrow'=4] {'narrow'}, dimensions={0} | all-to-all | bytes 1048576 | tf_op jit(solution)/shard_map/all_to_all | solution.py:45
  (187 shorter events, 105.1 us)
Async XLA Ops:
  68.2 9.7 %copy-start.22 = (bf16[2048]{0:T(1024)(128)(2,1)S(1)}, bf16[2048]{0:T(1024)(128)(2,1)}, u32[]{:S(2)}) copy-start(bf16[2048]{0:T(1024)(128)(2,1)} %param.26) | copy-start | bytes 12292
  68.2 9.7 %copy-start.1 = (bf16[128,2048]{1,0:T(8,128)(2,1)S(1)}, bf16[128,2048]{1,0:T(8,128)(2,1)}, u32[]{:S(2)}) copy-start(bf16[128,2048]{1,0:T(8,128)(2,1)} %param.25) | copy-start | bytes 1572868
  68.2 102.1 %all-to-all-start = ((bf16[32,2,51200]{2,1,0:T(2,128)(2,1)}), bf16[32,2,51200]{2,1,0:T(2,128)(2,1)}, u32[]{:S(2)}, u32[]{:S(2)}) async-start(bf16[32,2,51200]{2,1,0:T(2,128)(2,1)} %reshape.364), calls=%async_computation | async-start | bytes 13107200 | tf_op jit(solution)/shard_map/all_to_all | solution.py:45
  219.9 10.2 %copy-start.23 = (bf16[512]{0:T(512)(128)(2,1)S(1)}, bf16[512]{0:T(512)(128)(2,1)}, u32[]{:S(2)}) copy-start(bf16[512]{0:T(512)(128)(2,1)} %param.29) | copy-start | bytes 3076
  219.9 10.2 %copy-start.21 = (s32[8]{0:T(128)S(1)}, s32[8]{0:T(128)}, u32[]{:S(2)}) copy-start(s32[8]{0:T(128)} %param.33) | copy-start | bytes 100
  219.9 95.5 %all-to-all-start.1 = ((bf16[32,128,768]{1,2,0:T(8,128)(2,1)}), bf16[32,128,768]{1,2,0:T(8,128)(2,1)}, u32[]{:S(2)}, u32[]{:S(2)}) async-start(bf16[32,128,768]{1,2,0:T(8,128)(2,1)} %broadcast_in_dim.224), calls=%async_computation.1 | async-start | bytes 12582912 | tf_op jit(solution)/shard_map/all_to_all | solution.py:45
  335.2 4.2 copy-start.3
  339.4 10.5 %copy-start.2 = (f32[4096,32]{0,1:T(8,128)S(1)}, f32[4096,32]{0,1:T(8,128)}, u32[]{:S(2)}) copy-start(f32[4096,32]{0,1:T(8,128)} %get-tuple-element.410) | copy-start | bytes 1572868
  382.6 4.7 copy-start.18
  388.0 1.1 copy-start.19
  394.8 4.7 copy-start.4
  400.2 3.3 copy-start.5
  409.4 4.7 copy-start.6
  414.8 4.3 copy-start.7
  425.1 4.7 copy-start.8
  430.5 4.4 copy-start.9
  440.7 4.7 copy-start.10
  446.1 4.3 copy-start.11
  456.3 4.7 copy-start.12
  461.7 4.3 copy-start.13
  471.8 4.7 copy-start.14
  477.3 4.3 copy-start.15
  487.4 4.7 copy-start.16
  492.8 4.4 copy-start.17
  498.0 19.4 %all-to-all-start.2 = ((bf16[32,128,8]{1,2,0:T(8,128)(2,1)}), bf16[32,128,8]{1,2,0:T(8,128)(2,1)S(1)}, u32[]{:S(2)}, u32[]{:S(2)}) async-start(bf16[32,128,8]{1,2,0:T(8,128)(2,1)} %pad_maximum_fusion.2), calls=%async_computation.2 | async-start | bytes 131072 | tf_op jit(solution)/shard_map/all_to_all | solution.py:205
  506.4 6.9 %copy-start = (f32[512,4,512]{2,0,1:T(8,128)S(1)}, f32[512,4,512]{2,0,1:T(8,128)}, u32[]{:S(2)}) copy-start(f32[512,4,512]{2,0,1:T(8,128)} %fusion.181) | copy-start | bytes 12582916
  517.4 55.9 %copy-start.20 = (bf16[512,64]{0,1:T(8,128)(2,1)S(1)}, bf16[512,64]{0,1:T(8,128)(2,1)}, u32[]{:S(2)}) copy-start(bf16[512,64]{0,1:T(8,128)(2,1)} %param.31) | copy-start | bytes 196612
  574.9 33.0 %all-to-all-start.4 = ((bf16[32,512,64]{1,2,0:T(8,128)(2,1)}), bf16[32,512,64]{1,2,0:T(8,128)(2,1)S(1)}, u32[]{:S(2)}, u32[]{:S(2)}) async-start(bf16[32,512,64]{1,2,0:T(8,128)(2,1)} %broadcast_in_dim.232), calls=%async_computation.4 | async-start | bytes 4194304 | tf_op jit(solution)/shard_map/all_to_all | solution.py:45

commit v2 on v1

--- a/solution.py
+++ b/solution.py
@@ -110,32 +110,28 @@
     requests = lengths.shape[0]
     cache_rows = cache.shape[1]
     heads_here = q_weight.shape[1] // (NOPE + ROPE)
+    narrow_count = lax.axis_size("narrow")
+    narrow_place = lax.axis_index("narrow")
     q_cols = q_weight.shape[1]
     kva_cols = kva_weight.shape[1]
-    kvb_cols = kvb_weight.shape[1]
-    q_size = q_weight.size
-    kva_size = kva_weight.size
-    packed = jnp.concatenate(
-        [q_weight.reshape(-1), kva_weight.reshape(-1), kvb_weight.reshape(-1)]
-    )
+    kva_part = kva_cols // narrow_count
+    kva_mine = lax.dynamic_slice_in_dim(kva_weight, narrow_place * kva_part, kva_part, 1)
+    packed = jnp.concatenate([q_weight, kva_mine], axis=1)
     got_weights = gather_axis(packed, "wide")
-    q_full = got_weights[:, :q_size].reshape(-1, q_cols)
-    kva_full = got_weights[:, q_size : q_size + kva_size].reshape(-1, kva_cols)
-    kvb_full = got_weights[:, q_size + kva_size :].reshape(-1, kvb_cols)
+    proj_full = got_weights.reshape(-1, q_cols + kva_part)
+    kvb_full = gather_axis(kvb_weight, "wide").reshape(-1, kvb_weight.shape[1])
     o_got = gather_axis(o_weight, "wide")
-    o_full = jnp.transpose(o_got, (1, 0, 2)).reshape(o_weight.shape[0], -1)
 
     normed = scaled_norm(hidden.astype(jnp.float32), attn_gain).astype(jnp.bfloat16)
-    query_rows = jnp.dot(normed, q_full, preferred_element_type=jnp.float32).astype(jnp.bfloat16)
-    compressed = jnp.dot(normed, kva_full, preferred_element_type=jnp.float32)
+    projected = jnp.dot(normed, proj_full, preferred_element_type=jnp.float32)
+    query_rows = projected[:, :q_cols].astype(jnp.bfloat16)
+    compressed_part = projected[:, q_cols:]
+    compressed = jnp.transpose(gather_axis(compressed_part, "narrow"), (1, 0, 2)).reshape(
+        tok_rows, kva_cols
+    )
     first_token = wide_place * tok_rows
     token_ids = first_token + jnp.arange(tok_rows, dtype=jnp.int32)
-    request_of = token_ids // SPAN
-    request_ids = jnp.arange(requests, dtype=jnp.int32)
-    own_length = jnp.sum(
-        jnp.where(request_of[:, None] == request_ids[None, :], lengths[None, :], 0), axis=1
-    )
-    positions = own_length + token_ids % SPAN
+    positions = lengths[token_ids // SPAN] + token_ids % SPAN
     own_keys = jnp.concatenate(
         [
             scaled_norm(compressed[:, :LAT], kv_gain).astype(jnp.bfloat16),
@@ -144,22 +140,26 @@
         axis=1,
     )
 
-    raw_all = gather_axis(query_rows, "wide")
+    query_heads = query_rows.reshape(tok_rows, heads_here, NOPE + ROPE)
+    outgoing = jnp.concatenate(
+        [
+            query_heads[..., :NOPE].reshape(tok_rows, heads_here * NOPE),
+            query_heads[..., NOPE:].reshape(tok_rows, heads_here * ROPE),
+        ],
+        axis=1,
+    )
+    raw_all = gather_axis(outgoing, "wide")
     total_tokens = raw_all.shape[0] * tok_rows
-    raw_all = raw_all.reshape(total_tokens, heads_here, NOPE + ROPE)
+    raw_all = raw_all.reshape(total_tokens, heads_here * (NOPE + ROPE))
     all_ids = jnp.arange(total_tokens, dtype=jnp.int32)
-    all_request = all_ids // SPAN
-    all_length = jnp.sum(
-        jnp.where(all_request[:, None] == request_ids[None, :], lengths[None, :], 0), axis=1
-    )
-    all_positions = all_length + all_ids % SPAN
+    all_positions = lengths[all_ids // SPAN] + all_ids % SPAN
     kvb_heads = kvb_full.reshape(LAT, heads_here, NOPE + VDIM)
     key_maps = kvb_heads[..., :NOPE]
     value_maps = kvb_heads[..., NOPE:]
-    q_rope = rotate(raw_all[..., NOPE:].astype(jnp.float32), all_positions[:, None]).astype(
-        jnp.bfloat16
-    )
-    queries = jnp.concatenate([absorb(raw_all[..., :NOPE], key_maps), q_rope], axis=-1)
+    nope_all = raw_all[:, : heads_here * NOPE].reshape(total_tokens, heads_here, NOPE)
+    rope_all = raw_all[:, heads_here * NOPE :].reshape(total_tokens, heads_here, ROPE)
+    q_rope = rotate(rope_all.astype(jnp.float32), all_positions[:, None]).astype(jnp.bfloat16)
+    queries = jnp.concatenate([absorb(nope_all, key_maps), q_rope], axis=-1)
 
     own_request = first_token // SPAN
     blocks = [cache[request] for request in range(requests)]
@@ -223,8 +223,9 @@
         .astype(jnp.bfloat16)
         .reshape(tok_rows, heads_here * VDIM)
     )
-    partial_out = jnp.dot(context, o_full, preferred_element_type=jnp.float32)
-    narrow_count = lax.axis_size("narrow")
+    partial_out = jnp.einsum(
+        "tk,wkc->twc", context, o_got, preferred_element_type=jnp.float32
+    ).reshape(tok_rows, -1)
     out_cols = partial_out.shape[1]
     pieces = jnp.transpose(
         partial_out.astype(jnp.bfloat16).reshape(tok_rows, narrow_count, out_cols // narrow_count),

time: 650 us -> 507 us (0.78)
  local copies, waits for them, and re-layouts: 143 us -> 48 us
  waiting for transfers between devices: 179 us -> 108 us
  blocking collectives: 86.7 us -> 149 us
  other arithmetic: 96.4 us -> 65.5 us
    all_to_all x3 -> x4, waiting for transfers between devices: 179 us -> 108 us  [gather_axis(): lax.all_to_all(spread, axis_name, split_axis=0, concat_axis=0, tiled=True)]
    all_to_all x1 -> x2, blocking collectives: 12.7 us -> 72.5 us  [gather_axis(): lax.all_to_all(spread, axis_name, split_axis=0, concat_axis=0, tiled=True)]
    broadcast_in_dim x1 -> x0, other arithmetic: 42.8 us -> none  [gather_axis(): spread = jnp.broadcast_to(x[None], (count,) + x.shape)]
    unnamed x42 -> x56, local copies, waits for them, and re-layouts: 53.8 us -> 16.3 us
    cond x40 -> x32, local copies, waits for them, and re-layouts: 17.4 us -> 0.1 us  [the longest x8 17.3 us: per_device(): lax.cond(block_live, attend, skipped, block_queries, blocks[request], liv...]
    reshape x5 -> x2, local copies, waits for them, and re-layouts: 20.3 us -> 5.97 us  [the longest x1 3.7 us: per_device(): raw_all = raw_all.reshape(total_tokens, heads_here * (NOPE + ROPE))]
    broadcast_in_dim x5 -> x6, local copies, waits for them, and re-layouts: 19.2 us -> 8.03 us  [gather_axis(): spread = jnp.broadcast_to(x[None], (count,) + x.shape)]
    all_to_all x2 -> x1, local copies, waits for them, and re-layouts: 9.75 us -> 0.27 us  [gather_axis(): lax.all_to_all(spread, axis_name, split_axis=0, concat_axis=0, tiled=True)]
  transfers between devices with their start and end apart: 4 -> 5, of which waited for: 3 -> 4; matrix products, arithmetic and copies ran while one was open for 6% -> 9% of each run, Pallas kernels for 0% -> 0%
where the time goes in v2:
time: 507 us; the launch traced here: 502 us
  blocking collectives  149 us (29%)
  waiting for transfers between devices  108 us (21%)
  matrix products  94.7 us (19%)
  other arithmetic  65.5 us (13%)
  local copies, waits for them, and re-layouts  48 us (9%)
  starting transfers between devices  27.4 us (5%)
  between operations  6.09 us (1%)
    all_to_all x4, waiting for transfers between devices, gather_axis(): lax.all_to_all(spread, axis_name, split_axis=0, concat_axis=0, tiled=True)  108 us
    all_to_all x2, blocking collectives, gather_axis(): lax.all_to_all(spread, axis_name, split_axis=0, concat_axis=0, tiled=True)  72.5 us
    all_to_all x1, blocking collectives, per_device(): lax.all_to_all(value_all.astype(jnp.bfloat16).reshape(wide_count, tok_row...  57.2 us
    dot_general x9, matrix products, attend(): jnp.einsum('qhc,kc->qhk', block_queries, key_rows, preferred_element_type...  42.1 us
    all_to_all x4, starting transfers between devices, gather_axis(): lax.all_to_all(spread, axis_name, split_axis=0, concat_axis=0, tiled=True)  20.8 us
    all_to_all x1, blocking collectives, per_device(): got_pieces = lax.all_to_all(pieces, 'narrow', 0, 0, tiled=True)  19.6 us
    dot_general x9, matrix products, attend(): jnp.einsum('qhk,kc->qhc', weights.astype(jnp.bfloat16), key_rows[:, :LAT]...  19.2 us
    concatenate x1, other arithmetic, per_device(): queries = jnp.concatenate([absorb(nope_all, key_maps), q_rope], axis=-1)  18.8 us
  transfers between devices with their start and end apart: 5, of which 4 were waited for; matrix products, arithmetic and copies ran while one was open for 9% of the time, Pallas kernels for 0%

profile of v2, /device:TPU:1, one launch (start us, length us, event | category | flops | bytes accessed | tf_op | source)
XLA Modules:
  0.0 501.8 jit_solution(2565257822281021568)
XLA Ops:
  2.4 59.8 %all_to_all.45 = bf16[32,64,912]{2,1,0:T(8,128)(2,1)} all-to-all(bf16[32,64,912]{2,1,0:T(8,128)(2,1)S(1)} %broadcast_in_dim.207), channel_id=1, replica_groups=mesh['wide'=32,'narrow'=4] {'wide'}, dimensions={0} | all-to-all | bytes 7471104 | tf_op jit(solution)/shard_map/all_to_all | solution.py:45
  63.4 3.9 all-to-all-start.2
  67.5 3.9 fusion.182
  71.5 11.8 %all-to-all-done.2 = bf16[32,16,1024]{2,1,0:T(8,128)(2,1)S(1)} async-done(((bf16[32,16,1024]{2,1,0:T(8,128)(2,1)}), bf16[32,16,1024]{2,1,0:T(8,128)(2,1)S(1)}, u32[]{:S(2)}, u32[]{:S(2)}) %all-to-all-start.2) | async-done | bytes 1048608 | tf_op jit(solution)/shard_map/all_to_all | solution.py:45
  84.0 7.7 %all-to-all-start.3 = ((f32[4,128,144]{1,2,0:T(8,128)}), f32[4,128,144]{1,2,0:T(8,128)S(1)}, u32[]{:S(2)}, u32[]{:S(2)}) async-start(f32[4,128,144]{1,2,0:T(8,128)} %broadcast_in_dim.211), calls=%async_computation.3 | async-start | bytes 589824 | tf_op jit(solution)/shard_map/all_to_all | solution.py:45
  91.7 6.8 %all-to-all-done.3 = f32[4,128,144]{1,2,0:T(8,128)S(1)} async-done(((f32[4,128,144]{1,2,0:T(8,128)}), f32[4,128,144]{1,2,0:T(8,128)S(1)}, u32[]{:S(2)}, u32[]{:S(2)}) %all-to-all-start.3) | async-done | bytes 294944 | tf_op jit(solution)/shard_map/all_to_all | solution.py:45
  98.6 4.1 broadcast_in_dim.208
  102.6 5.0 %all-to-all-start.1 = ((bf16[32,128,768]{1,2,0:T(8,128)(2,1)}), bf16[32,128,768]{1,2,0:T(8,128)(2,1)}, u32[]{:S(2)}, u32[]{:S(2)}) async-start(bf16[32,128,768]{1,2,0:T(8,128)(2,1)} %broadcast_in_dim.208), calls=%async_computation.1 | async-start | bytes 12582912 | tf_op jit(solution)/shard_map/all_to_all | solution.py:45
  114.0 5.0 fusion.214
  119.0 4.3 compare_select_fusion.1
  124.1 2.8 multiply_cosine_fusion
  128.5 67.0 %all-to-all-done.1 = bf16[32,128,768]{1,2,0:T(8,128)(2,1)} async-done(((bf16[32,128,768]{1,2,0:T(8,128)(2,1)}), bf16[32,128,768]{1,2,0:T(8,128)(2,1)}, u32[]{:S(2)}, u32[]{:S(2)}) %all-to-all-start.1) | async-done | bytes 6291488 | tf_op jit(solution)/shard_map/all_to_all | solution.py:45
  195.5 3.7 copy_bitcast_fusion
  201.6 2.4 convert.32
  204.0 10.3 %convert_bitcast_fusion = bf16[4096,4,512]{0,2,1:T(8,128)(2,1)} fusion(bf16[4096,4,128]{0,2,1:T(8,128)(2,1)} %bitcast.195, bf16[512,4,128]{2,1,0:T(4,128)(2,1)S(1)} %get-tuple-element.239), kind=kOutput, calls=%fused_computation.209 | convolution fusion | flops 2155872256 | bytes 21495808 | tf_op jit(solution)/shard_map/thc,lhc->thl/dot_general | solution.py:49
  214.3 3.0 subtract_convert_fusion.50
  217.4 18.8 %pad_maximum_fusion = bf16[4096,4,576]{0,2,1:T(8,128)(2,1)} fusion(bf16[4096,4,32]{0,2,1:T(8,128)(2,1)S(1)} %get-tuple-element.237, bf16[4096,4,32]{0,2,1:T(8,128)(2,1)S(1)} %get-tuple-element.236, bf16[4096,4,512]{0,2,1:T(8,128)(2,1)} %convert_bitcast_fusion), kind=kLoop, calls=%fused_computation.208 | loop fusion | flops 56623104 | bytes 37748736 | tf_op jit(solution)/shard_map/concatenate | solution.py:162
  236.1 2.3 select_reduce_fusion.8
  238.5 2.8 fusion.180
  241.6 11.9 %conditional.8 = (f32[512,4]{0,1:T(4,128)S(1)}, f32[512,4]{0,1:T(4,128)S(1)}, f32[512,4,128]{2,0,1:T(8,128)S(1)}) conditional(s32[]{:T(128)} %convert_element_type.339, () %tuple.69, (s32[]{:T(128)}, s32[1,640]{1,0:T(1,128)S(1)}, bf16[4096,4,576]{0,2,1:T(8,128)(2,1)}, bf16[8,640,576]{1,2,0:T(8,128)(2,1)}, bf16[512,4,128]{2,0,1:T(8,128)(2,1)S(1)}) %tuple.70), branch_computations={%region_1.2_spmd, %region_2.5_spmd} | conditional | flops 3408919040 | bytes 37844436 | solution.py:177
  242.3 5.0 select_reduce_fusion
  254.5 2.9 fusion.176
  257.4 12.0 %conditional.9 = (f32[512,4]{0,1:T(4,128)S(1)}, f32[512,4]{0,1:T(4,128)S(1)}, f32[512,4,128]{2,0,1:T(8,128)S(1)}) conditional(s32[]{:T(128)} %convert_element_type.348, () %tuple.71, (s32[]{:T(128)}, s32[1,640]{1,0:T(1,128)S(1)}, bf16[4096,4,576]{0,2,1:T(8,128)(2,1)}, bf16[8,640,576]{1,2,0:T(8,128)(2,1)}, bf16[512,4,128]{2,0,1:T(8,128)(2,1)S(1)}) %tuple.72), branch_computations={%region_5.6_spmd, %region_6.9_spmd} | conditional | flops 3408919040 | bytes 37844436 | solution.py:177
  258.3 5.0 select_reduce_fusion.1
  269.5 12.2 %conditional.10 = (f32[512,4]{0,1:T(4,128)S(1)}, f32[512,4]{0,1:T(4,128)S(1)}, f32[512,4,128]{2,0,1:T(8,128)S(1)}) conditional(s32[]{:T(128)} %convert_element_type.349, () %tuple.73, (s32[]{:T(128)}, s32[1,640]{1,0:T(1,128)S(1)}, bf16[4096,4,576]{0,2,1:T(8,128)(2,1)}, bf16[8,640,576]{1,2,0:T(8,128)(2,1)}, bf16[512,4,128]{2,0,1:T(8,128)(2,1)S(1)}) %tuple.74), branch_computations={%region_9.10_spmd, %region_10.13_spmd} | conditional | flops 3408919040 | bytes 37844436 | solution.py:177
  270.5 5.0 select_reduce_fusion.2
  282.6 12.3 %conditional.11 = (f32[512,4]{0,1:T(4,128)S(1)}, f32[512,4]{0,1:T(4,128)S(1)}, f32[512,4,128]{2,0,1:T(8,128)S(1)}) conditional(s32[]{:T(128)} %convert_element_type.350, () %tuple.75, (s32[]{:T(128)}, s32[1,640]{1,0:T(1,128)S(1)}, bf16[4096,4,576]{0,2,1:T(8,128)(2,1)}, bf16[8,640,576]{1,2,0:T(8,128)(2,1)}, ...), branch_computations={%region_13.14_spmd, %region_14.17_spmd} | conditional | flops 3408919040 | bytes 37844436 | solution.py:177
  283.8 5.0 select_reduce_fusion.3
  295.9 11.9 %conditional.12 = (f32[512,4]{0,1:T(4,128)S(1)}, f32[512,4]{0,1:T(4,128)S(1)}, f32[512,4,128]{2,0,1:T(8,128)S(1)}) conditional(s32[]{:T(128)} %convert_element_type.351, () %tuple.77, (s32[]{:T(128)}, s32[1,640]{1,0:T(1,128)S(1)}, bf16[4096,4,576]{0,2,1:T(8,128)(2,1)}, bf16[8,640,576]{1,2,0:T(8,128)(2,1)}, ...), branch_computations={%region_17.18_spmd, %region_18.21_spmd} | conditional | flops 3408919040 | bytes 37844436 | solution.py:177
  296.7 5.0 select_reduce_fusion.4
  308.8 12.1 %conditional.13 = (f32[512,4]{0,1:T(4,128)S(1)}, f32[512,4]{0,1:T(4,128)S(1)}, f32[512,4,128]{2,0,1:T(8,128)S(1)}) conditional(s32[]{:T(128)} %convert_element_type.352, () %tuple.79, (s32[]{:T(128)}, s32[1,640]{1,0:T(1,128)S(1)}, bf16[4096,4,576]{0,2,1:T(8,128)(2,1)}, bf16[8,640,576]{1,2,0:T(8,128)(2,1)}, ...), branch_computations={%region_21.22_spmd, %region_22.25_spmd} | conditional | flops 3408919040 | bytes 37844436 | solution.py:177
  309.7 5.0 select_reduce_fusion.5
  321.9 12.0 %conditional.14 = (f32[512,4]{0,1:T(4,128)S(1)}, f32[512,4]{0,1:T(4,128)S(1)}, f32[512,4,128]{2,0,1:T(8,128)S(1)}) conditional(s32[]{:T(128)} %convert_element_type.353, () %tuple.81, (s32[]{:T(128)}, s32[1,640]{1,0:T(1,128)S(1)}, bf16[4096,4,576]{0,2,1:T(8,128)(2,1)}, bf16[8,640,576]{1,2,0:T(8,128)(2,1)}, ...), branch_computations={%region_25.26_spmd, %region_26.29_spmd} | conditional | flops 3408919040 | bytes 37844436 | solution.py:177
  322.7 5.0 select_reduce_fusion.6
  334.9 13.1 %conditional.15 = (f32[512,4]{0,1:T(4,128)S(1)}, f32[512,4]{0,1:T(4,128)S(1)}, f32[512,4,128]{2,0,1:T(8,128)}) conditional(s32[]{:T(128)} %convert_element_type.354, () %tuple.83, (s32[]{:T(128)}, s32[1,640]{1,0:T(1,128)S(1)}, bf16[4096,4,576]{0,2,1:T(8,128)(2,1)}, bf16[8,640,576]{1,2,0:T(8,128)(2,1)}, bf16[512,4,128]{2,0,1:T(8,128)(2,1)S(1)}) %tuple.84), branch_computations={%region_29.30_spmd, %region_30.33_spmd} | conditional | flops 3408919040 | bytes 37844436 | solution.py:177
  335.8 5.0 select_reduce_fusion.7
  348.8 6.5 %all-to-all-start.4 = ((bf16[32,128,8]{1,2,0:T(8,128)(2,1)}), bf16[32,128,8]{1,2,0:T(8,128)(2,1)S(1)}, u32[]{:S(2)}, u32[]{:S(2)}) async-start(bf16[32,128,8]{1,2,0:T(8,128)(2,1)} %pad_maximum_fusion.3), calls=%async_computation.4 | async-start | bytes 131072 | tf_op jit(solution)/shard_map/all_to_all | solution.py:205
  356.4 2.5 constant_dynamic-update-slice_fusion.21
  359.0 2.5 constant_dynamic-update-slice_fusion.20
  364.7 2.3 constant_dynamic-update-slice_fusion.16
  367.0 2.9 fusion.171
  369.9 3.9 convert_element_type.367
  376.1 57.2 %all_to_all.46 = bf16[32,128,4,128]{3,1,2,0:T(8,128)(2,1)} all-to-all(bf16[32,128,4,128]{3,1,2,0:T(8,128)(2,1)} %copy.95), channel_id=1, replica_groups=mesh['wide'=32,'narrow'=4] {'wide'}, dimensions={0} | all-to-all | bytes 8388608 | tf_op jit(solution)/shard_map/all_to_all | solution.py:208
  434.8 4.2 all-to-all-start.6
  439.2 4.5 multiply_reduce_fusion
  443.9 22.9 %all-to-all-done.6 = bf16[32,512,64]{1,2,0:T(8,128)(2,1)S(1)} async-done(((bf16[32,512,64]{1,2,0:T(8,128)(2,1)}), bf16[32,512,64]{1,2,0:T(8,128)(2,1)S(1)}, u32[]{:S(2)}, u32[]{:S(2)}) %all-to-all-start.6) | async-done | bytes 2097184 | tf_op jit(solution)/shard_map/all_to_all | solution.py:45
  467.6 19.6 %all_to_all.47 = bf16[4,128,512]{2,1,0:T(8,128)(2,1)S(1)} all-to-all(bf16[4,128,512]{2,1,0:T(8,128)(2,1)S(1)} %bitcast.201), channel_id=1, replica_groups=mesh['wide'=32,'narrow'=4] {'narrow'}, dimensions={0} | all-to-all | bytes 1048576 | tf_op jit(solution)/shard_map/all_to_all | solution.py:234
  487.3 12.7 %all_to_all.48 = bf16[4,128,512]{2,1,0:T(8,128)(2,1)S(1)} all-to-all(bf16[4,128,512]{2,1,0:T(8,128)(2,1)S(1)} %broadcast_in_dim.215), channel_id=1, replica_groups=mesh['wide'=32,'narrow'=4] {'narrow'}, dimensions={0} | all-to-all | bytes 1048576 | tf_op jit(solution)/shard_map/all_to_all | solution.py:45
  (194 shorter events, 83.6 us)
Async XLA Ops:
  0.0 0.9 copy-start
  2.4 59.8 %copy-start.29 = (bf16[16,1024]{1,0:T(8,128)(2,1)S(1)}, bf16[16,1024]{1,0:T(8,128)(2,1)}, u32[]{:S(2)}) copy-start(bf16[16,1024]{1,0:T(8,128)(2,1)} %param.30) | copy-start | bytes 98308
  2.4 64.9 %copy-start.31 = (bf16[2048]{0:T(1024)(128)(2,1)S(1)}, bf16[2048]{0:T(1024)(128)(2,1)}, u32[]{:S(2)}) copy-start(bf16[2048]{0:T(1024)(128)(2,1)} %param.26) | copy-start | bytes 12292
  2.4 64.9 %copy-start.11 = (bf16[128,2048]{1,0:T(8,128)(2,1)S(1)}, bf16[128,2048]{1,0:T(8,128)(2,1)}, u32[]{:S(2)}) copy-start(bf16[128,2048]{1,0:T(8,128)(2,1)} %param.25) | copy-start | bytes 1572868
  63.4 19.9 %all-to-all-start.2 = ((bf16[32,16,1024]{2,1,0:T(8,128)(2,1)}), bf16[32,16,1024]{2,1,0:T(8,128)(2,1)S(1)}, u32[]{:S(2)}, u32[]{:S(2)}) async-start(bf16[32,16,1024]{2,1,0:T(8,128)(2,1)} %broadcast_in_dim.209), calls=%async_computation.2 | async-start | bytes 2097152 | tf_op jit(solution)/shard_map/all_to_all | solution.py:45
  84.0 14.6 %all-to-all-start.3 = ((f32[4,128,144]{1,2,0:T(8,128)}), f32[4,128,144]{1,2,0:T(8,128)S(1)}, u32[]{:S(2)}, u32[]{:S(2)}) async-start(f32[4,128,144]{1,2,0:T(8,128)} %broadcast_in_dim.211), calls=%async_computation.3 | async-start | bytes 589824 | tf_op jit(solution)/shard_map/all_to_all | solution.py:45
  102.6 5.1 %copy-start.30 = (s32[8]{0:T(128)S(1)}, s32[8]{0:T(128)}, u32[]{:S(2)}) copy-start(s32[8]{0:T(128)} %param.33) | copy-start | bytes 100
  102.6 10.8 %copy-start.32 = (bf16[512]{0:T(512)(128)(2,1)S(1)}, bf16[512]{0:T(512)(128)(2,1)}, u32[]{:S(2)}) copy-start(bf16[512]{0:T(512)(128)(2,1)} %param.29) | copy-start | bytes 3076
  102.6 92.9 %all-to-all-start.1 = ((bf16[32,128,768]{1,2,0:T(8,128)(2,1)}), bf16[32,128,768]{1,2,0:T(8,128)(2,1)}, u32[]{:S(2)}, u32[]{:S(2)}) async-start(bf16[32,128,768]{1,2,0:T(8,128)(2,1)} %broadcast_in_dim.208), calls=%async_computation.1 | async-start | bytes 12582912 | tf_op jit(solution)/shard_map/all_to_all | solution.py:45
  247.3 4.7 copy-start.26
  252.7 0.8 copy-start.27
  263.3 4.7 copy-start.12
  268.7 0.8 copy-start.13
  275.5 4.7 copy-start.14
  280.9 0.8 copy-start.15
  281.7 1.0 copy-start.3
  288.7 4.7 copy-start.16
  294.2 0.7 copy-start.17
  294.9 1.0 copy-start.4
  301.6 4.7 copy-start.18
  307.1 0.7 copy-start.19
  307.8 1.0 copy-start.5
  314.7 4.7 copy-start.20
  320.1 0.7 copy-start.21
  320.9 1.0 copy-start.7
  327.7 4.7 copy-start.22
  333.1 0.8 copy-start.23
  333.9 1.0 copy-start.9
  340.8 4.7 copy-start.24
  346.2 1.8 copy-start.25
  348.8 27.3 %all-to-all-start.4 = ((bf16[32,128,8]{1,2,0:T(8,128)(2,1)}), bf16[32,128,8]{1,2,0:T(8,128)(2,1)S(1)}, u32[]{:S(2)}, u32[]{:S(2)}) async-start(bf16[32,128,8]{1,2,0:T(8,128)(2,1)} %pad_maximum_fusion.3), calls=%async_computation.4 | async-start | bytes 131072 | tf_op jit(solution)/shard_map/all_to_all | solution.py:205
  355.3 6.1 %copy-start.6 = (f32[512,4,128]{2,0,1:T(8,128)S(1)}, f32[512,4,128]{2,0,1:T(8,128)}, u32[]{:S(2)}) copy-start(f32[512,4,128]{2,0,1:T(8,128)} %copy-done.5) | copy-start | bytes 3145732
  355.3 7.2 %copy-start.8 = (f32[512,4,128]{2,0,1:T(8,128)S(1)}, f32[512,4,128]{2,0,1:T(8,128)}, u32[]{:S(2)}) copy-start(f32[512,4,128]{2,0,1:T(8,128)} %copy-done.7) | copy-start | bytes 3145732
  355.4 8.3 %copy-start.10 = (f32[512,4,128]{2,0,1:T(8,128)S(1)}, f32[512,4,128]{2,0,1:T(8,128)}, u32[]{:S(2)}) copy-start(f32[512,4,128]{2,0,1:T(8,128)} %copy-done.9) | copy-start | bytes 3145732
  359.0 8.0 %copy-start.2 = (f32[512,4,512]{2,0,1:T(8,128)S(1)}, f32[512,4,512]{2,0,1:T(8,128)}, u32[]{:S(2)}) copy-start(f32[512,4,512]{2,0,1:T(8,128)} %fusion.180) | copy-start | bytes 12582916
  376.1 57.2 %copy-start.28 = (bf16[512,64]{0,1:T(8,128)(2,1)S(1)}, bf16[512,64]{0,1:T(8,128)(2,1)}, u32[]{:S(2)}) copy-start(bf16[512,64]{0,1:T(8,128)(2,1)} %param.31) | copy-start | bytes 196612
  434.8 31.9 %all-to-all-start.6 = ((bf16[32,512,64]{1,2,0:T(8,128)(2,1)}), bf16[32,512,64]{1,2,0:T(8,128)(2,1)S(1)}, u32[]{:S(2)}, u32[]{:S(2)}) async-start(bf16[32,512,64]{1,2,0:T(8,128)(2,1)} %broadcast_in_dim.214), calls=%async_computation.6 | async-start | bytes 4194304 | tf_op jit(solution)/shard_map/all_to_all | solution.py:45
  439.1 62.2 %copy-start.1 = (bf16[64,576]{1,0:T(8,128)(2,1)S(1)}, bf16[64,576]{1,0:T(8,128)(2,1)}, u32[]{:S(2)}) copy-start(bf16[64,576]{1,0:T(8,128)(2,1)} %param.28) | copy-start | bytes 221188

commit v3 on v2

--- a/solution.py
+++ b/solution.py
@@ -2,6 +2,8 @@
 import jax.numpy as jnp
 from jax import lax
 from jax.sharding import PartitionSpec as P
+from jax.experimental import pallas as pl
+from jax.experimental.pallas import tpu as pltpu
 
 NOPE = 128
 ROPE = 64
@@ -70,7 +72,6 @@
     )
     live_rows = live_mask[:, None, :]
     row_peak = jnp.max(jnp.where(live_rows, scores, -1e30), axis=-1)
-    row_peak = row_peak.astype(jnp.bfloat16).astype(jnp.float32)
     weights = jnp.where(live_rows, jnp.exp(scores - row_peak[..., None]), 0.0)
     row_total = jnp.sum(weights, axis=-1)
     mixed = jnp.einsum(
@@ -90,6 +91,74 @@
         jnp.zeros((rows_here, heads_here), jnp.float32),
         jnp.zeros((rows_here, heads_here, value_maps.shape[2]), jnp.float32),
     )
+
+
+def cache_kernel(lens_ref, base_ref, lat_ref, rope_ref, kv_ref, vm_ref, peak_ref, total_ref, value_ref):
+    length_now = lens_ref[pl.program_id(0)]
+    base = base_ref[0]
+    live_block = base < length_now
+
+    @pl.when(live_block)
+    def _():
+        keys = kv_ref[0]
+        key_lat = keys[:, :LAT]
+        key_rope = keys[:, LAT:]
+        nt = (((1,), (1,)), ((), ()))
+        scores = (
+            lax.dot_general(lat_ref[0], key_lat, nt, preferred_element_type=jnp.float32)
+            + lax.dot_general(rope_ref[0], key_rope, nt, preferred_element_type=jnp.float32)
+        ) * score_scale
+        slots = base + lax.broadcasted_iota(jnp.int32, scores.shape, 1)
+        live = slots < length_now
+        peak = jnp.max(jnp.where(live, scores, -1e30), axis=-1, keepdims=True)
+        weights = jnp.where(live, jnp.exp(scores - peak), 0.0)
+        peak_ref[0] = peak
+        total_ref[0] = jnp.sum(weights, axis=-1, keepdims=True)
+        mixed = jnp.dot(weights.astype(jnp.bfloat16), key_lat, preferred_element_type=jnp.float32)
+        value_map = vm_ref[0]
+        upper_part = mixed.astype(jnp.bfloat16)
+        lower_part = (mixed - upper_part.astype(jnp.float32)).astype(jnp.bfloat16)
+        value_ref[0] = jnp.dot(upper_part, value_map, preferred_element_type=jnp.float32) + jnp.dot(
+            lower_part, value_map, preferred_element_type=jnp.float32
+        )
+
+    @pl.when(jnp.logical_not(live_block))
+    def _():
+        peak_ref[...] = jnp.full(peak_ref.shape, -1e30, jnp.float32)
+        total_ref[...] = jnp.zeros(total_ref.shape, jnp.float32)
+        value_ref[...] = jnp.zeros(value_ref.shape, jnp.float32)
+
+
+def cache_attention(lengths, base, lat_hm, rope_hm, cache, value_hm):
+    heads_here, total_tokens, _ = lat_hm.shape
+    requests, cache_rows, width = cache.shape
+    span = total_tokens // requests
+    vdim = value_hm.shape[2]
+    grid_spec = pltpu.PrefetchScalarGridSpec(
+        num_scalar_prefetch=2,
+        grid=(requests, heads_here),
+        in_specs=[
+            pl.BlockSpec((1, span, LAT), lambda r, h, lens, b: (h, r, 0)),
+            pl.BlockSpec((1, span, ROPE), lambda r, h, lens, b: (h, r, 0)),
+            pl.BlockSpec((1, cache_rows, width), lambda r, h, lens, b: (r, 0, 0)),
+            pl.BlockSpec((1, LAT, vdim), lambda r, h, lens, b: (h, 0, 0)),
+        ],
+        out_specs=[
+            pl.BlockSpec((1, span, 1), lambda r, h, lens, b: (h, r, 0)),
+            pl.BlockSpec((1, span, 1), lambda r, h, lens, b: (h, r, 0)),
+            pl.BlockSpec((1, span, vdim), lambda r, h, lens, b: (h, r, 0)),
+        ],
+    )
+    return pl.pallas_call(
+        cache_kernel,
+        grid_spec=grid_spec,
+        out_shape=[
+            jax.ShapeDtypeStruct((heads_here, total_tokens, 1), jnp.float32),
+            jax.ShapeDtypeStruct((heads_here, total_tokens, 1), jnp.float32),
+            jax.ShapeDtypeStruct((heads_here, total_tokens, vdim), jnp.float32),
+        ],
+        compiler_params=pltpu.CompilerParams(dimension_semantics=("arbitrary", "arbitrary")),
+    )(lengths, base, lat_hm, rope_hm, cache, value_hm)
 
 
 def merge_parts(first, second):
@@ -159,70 +228,70 @@
     nope_all = raw_all[:, : heads_here * NOPE].reshape(total_tokens, heads_here, NOPE)
     rope_all = raw_all[:, heads_here * NOPE :].reshape(total_tokens, heads_here, ROPE)
     q_rope = rotate(rope_all.astype(jnp.float32), all_positions[:, None]).astype(jnp.bfloat16)
-    queries = jnp.concatenate([absorb(nope_all, key_maps), q_rope], axis=-1)
+    lat_hm = jnp.einsum(
+        "thc,lhc->htl", nope_all, key_maps, preferred_element_type=jnp.float32
+    ).astype(jnp.bfloat16)
+    rope_hm = jnp.transpose(q_rope, (1, 0, 2))
+    value_hm = jnp.transpose(value_maps, (1, 0, 2))
+
+    base = (wide_place * cache_rows).reshape(1).astype(jnp.int32)
+    peak_hm, total_hm, value_out = cache_attention(lengths, base, lat_hm, rope_hm, cache, value_hm)
+    peak_hm = peak_hm[..., 0]
+    total_hm = total_hm[..., 0]
 
     own_request = first_token // SPAN
-    blocks = [cache[request] for request in range(requests)]
-    start = wide_place * cache_rows
-    cache_slots = jnp.arange(cache_rows, dtype=jnp.int32)
-    peaks_list = []
-    totals_list = []
-    values_list = []
-    for request in range(requests):
-        length_now = lengths[request]
-        cache_live = start + cache_slots < length_now
-        live_mask = jnp.broadcast_to(cache_live[None, :], (SPAN, cache_rows))
-        block_live = start < length_now
-        block_queries = queries[request * SPAN : (request + 1) * SPAN]
-        row_peak, row_total, row_value = lax.cond(
-            block_live, attend, skipped, block_queries, blocks[request], live_mask, value_maps
-        )
-        peaks_list.append(row_peak)
-        totals_list.append(row_total)
-        values_list.append(row_value)
-    peak_all = jnp.concatenate(peaks_list, axis=0)
-    total_all = jnp.concatenate(totals_list, axis=0)
-    value_all = jnp.concatenate(values_list, axis=0)
     start_row = own_request * SPAN
     own_slots = first_token % SPAN + jnp.arange(tok_rows, dtype=jnp.int32)
     causal = own_slots[None, :] <= jnp.arange(SPAN, dtype=jnp.int32)[:, None]
-    own_queries = lax.dynamic_slice_in_dim(queries, start_row, SPAN, 0)
-    own_part = attend(own_queries, own_keys, causal, value_maps)
+    own_lat = lax.dynamic_slice_in_dim(lat_hm, start_row, SPAN, 1)
+    own_rope = lax.dynamic_slice_in_dim(rope_hm, start_row, SPAN, 1)
+    own_scores = (
+        jnp.einsum("hqc,kc->hqk", own_lat, own_keys[:, :LAT], preferred_element_type=jnp.float32)
+        + jnp.einsum("hqc,kc->hqk", own_rope, own_keys[:, LAT:], preferred_element_type=jnp.float32)
+    ) * score_scale
+    own_live = causal[None]
+    own_peak = jnp.max(jnp.where(own_live, own_scores, -1e30), axis=-1)
+    own_weights = jnp.where(own_live, jnp.exp(own_scores - own_peak[..., None]), 0.0)
+    own_total = jnp.sum(own_weights, axis=-1)
+    own_mixed = jnp.einsum(
+        "hqk,kc->hqc", own_weights.astype(jnp.bfloat16), own_keys[:, :LAT],
+        preferred_element_type=jnp.float32,
+    )
+    own_upper = own_mixed.astype(jnp.bfloat16)
+    own_lower = (own_mixed - own_upper.astype(jnp.float32)).astype(jnp.bfloat16)
+    own_value = jnp.einsum(
+        "hqc,hcv->hqv", own_upper, value_hm, preferred_element_type=jnp.float32
+    ) + jnp.einsum("hqc,hcv->hqv", own_lower, value_hm, preferred_element_type=jnp.float32)
     old_part = (
-        lax.dynamic_slice_in_dim(peak_all, start_row, SPAN, 0),
-        lax.dynamic_slice_in_dim(total_all, start_row, SPAN, 0),
-        lax.dynamic_slice_in_dim(value_all, start_row, SPAN, 0),
-    )
-    joint = merge_parts(old_part, own_part)
-    joint_peak = joint[0].astype(jnp.bfloat16).astype(jnp.float32)
-    shift = jnp.exp(joint[0] - joint_peak)
-    peak_all = lax.dynamic_update_slice_in_dim(peak_all, joint_peak, start_row, 0)
-    total_all = lax.dynamic_update_slice_in_dim(total_all, joint[1] * shift, start_row, 0)
-    value_all = lax.dynamic_update_slice_in_dim(
-        value_all, joint[2] * shift[..., None], start_row, 0
-    )
-    stats = jnp.concatenate([peak_all, total_all], axis=1).astype(jnp.bfloat16)
+        lax.dynamic_slice_in_dim(peak_hm, start_row, SPAN, 1),
+        lax.dynamic_slice_in_dim(total_hm, start_row, SPAN, 1),
+        lax.dynamic_slice_in_dim(value_out, start_row, SPAN, 1),
+    )
+    joint = merge_parts(old_part, (own_peak, own_total, own_value))
+    peak_hm = lax.dynamic_update_slice_in_dim(peak_hm, joint[0], start_row, 1)
+    total_hm = lax.dynamic_update_slice_in_dim(total_hm, joint[1], start_row, 1)
+    value_out = lax.dynamic_update_slice_in_dim(value_out, joint[2], start_row, 1)
+
+    stats = jnp.stack([peak_hm, total_hm], axis=0).astype(jnp.bfloat16)
     got_stats = lax.all_to_all(
-        stats.reshape(wide_count, tok_rows, 2 * heads_here), "wide", 0, 0, tiled=True
+        stats.reshape(2, heads_here, wide_count, tok_rows), "wide", 2, 2, tiled=True
     ).astype(jnp.float32)
     got_value = lax.all_to_all(
-        value_all.astype(jnp.bfloat16).reshape(wide_count, tok_rows, heads_here, VDIM),
+        value_out.astype(jnp.bfloat16).reshape(heads_here, wide_count, tok_rows, VDIM),
         "wide",
-        0,
-        0,
+        1,
+        1,
         tiled=True,
     ).astype(jnp.float32)
-    got_peak = got_stats[..., :heads_here]
-    got_total = got_stats[..., heads_here:]
-    peak_value = jnp.max(got_peak, axis=0)
-    factor = jnp.exp(got_peak - peak_value[None])
-    denominator = jnp.sum(factor * got_total, axis=0)
-    numerator = jnp.sum(factor[..., None] * got_value, axis=0)
-    context = (
-        (numerator / denominator[..., None])
-        .astype(jnp.bfloat16)
-        .reshape(tok_rows, heads_here * VDIM)
-    )
+    got_peak = got_stats[0]
+    got_total = got_stats[1]
+    peak_value = jnp.max(got_peak, axis=1)
+    factor = jnp.exp(got_peak - peak_value[:, None])
+    denominator = jnp.sum(factor * got_total, axis=1)
+    numerator = jnp.sum(factor[..., None] * got_value, axis=1)
+    context = jnp.transpose(
+        (numerator / denominator[..., None]).astype(jnp.bfloat16), (1, 0, 2)
+    ).reshape(tok_rows, heads_here * VDIM)
     partial_out = jnp.einsum(
         "tk,wkc->twc", context, o_got, preferred_element_type=jnp.float32
     ).reshape(tok_rows, -1)

time: 507 us -> 482 us (0.951)
  Pallas kernels: 0 us -> 77.8 us
  matrix products: 94.7 us -> 27 us
  waiting for transfers between devices: 108 us -> 95.3 us
  other arithmetic: 65.5 us -> 53.1 us
  between operations: 6.09 us -> 0.4 us
    pallas_call x0 -> x1, Pallas kernels: none -> 77.8 us  [cache_attention(): pl.pallas_call(cache_kernel, grid_spec=grid_spec, out_shape=[jax.ShapeDty...]
    dot_general x37 -> x6, matrix products: 90 us -> 22.3 us  [the longest x1 10.6 us: per_device(): jnp.einsum('thc,lhc->htl', nope_all, key_maps, preferred_element_type=jnp...]
    concatenate x4 -> x0, other arithmetic: 19.5 us -> none  [the longest x1 18.8 us: per_device(): queries = jnp.concatenate([absorb(nope_all, key_maps), q_rope], axis=-1)]
    all_to_all x4, waiting for transfers between devices: 108 us -> 95.3 us  [gather_axis(): lax.all_to_all(spread, axis_name, split_axis=0, concat_axis=0, tiled=True)]
    reduce_sum x11 -> x3, other arithmetic: 16.2 us -> 4.7 us  [the longest x1 4.42 us: per_device(): numerator = jnp.sum(factor[..., None] * got_value, axis=1)]
    pallas_call x0 -> x2, other arithmetic: none -> 11.3 us  [cache_attention(): pl.pallas_call(cache_kernel, grid_spec=grid_spec, out_shape=[jax.ShapeDty...]
    squeeze x8 -> x0, local copies, waits for them, and re-layouts: 9.47 us -> none  [per_device(): blocks = [cache[request] for request in range(requests)]]
    unnamed x56 -> x28, local copies, waits for them, and re-layouts: 16.3 us -> 23.2 us
  transfers between devices with their start and end apart: 5 -> 5, of which waited for: 4 -> 4; matrix products, arithmetic and copies ran while one was open for 9% -> 11% of each run, Pallas kernels for 0% -> 0%
where the time goes in v3:
time: 482 us; the launch traced here: 479 us
  blocking collectives  149 us (31%)
  waiting for transfers between devices  95.3 us (20%)
  Pallas kernels  77.8 us (16%)
  other arithmetic  53.1 us (11%)
  local copies, waits for them, and re-layouts  49 us (10%)
  starting transfers between devices  27.3 us (6%)
  matrix products  27 us (6%)
    all_to_all x4, waiting for transfers between devices, gather_axis(): lax.all_to_all(spread, axis_name, split_axis=0, concat_axis=0, tiled=True)  95.3 us
    pallas_call x1, Pallas kernels, cache_attention(): pl.pallas_call(cache_kernel, grid_spec=grid_spec, out_shape=[jax.ShapeDty...  77.8 us
    all_to_all x2, blocking collectives, gather_axis(): lax.all_to_all(spread, axis_name, split_axis=0, concat_axis=0, tiled=True)  72.5 us
    all_to_all x1, blocking collectives, per_device(): lax.all_to_all(value_out.astype(jnp.bfloat16).reshape(heads_here, wide_co...  57.2 us
    unnamed x28, local copies, waits for them, and re-layouts  23.2 us
    all_to_all x4, starting transfers between devices, gather_axis(): lax.all_to_all(spread, axis_name, split_axis=0, concat_axis=0, tiled=True)  20.8 us
    all_to_all x1, blocking collectives, per_device(): got_pieces = lax.all_to_all(pieces, 'narrow', 0, 0, tiled=True)  19.5 us
    pallas_call x2, other arithmetic, cache_attention(): pl.pallas_call(cache_kernel, grid_spec=grid_spec, out_shape=[jax.ShapeDty...  11.3 us
  transfers between devices with their start and end apart: 5, of which 4 were waited for; matrix products, arithmetic and copies ran while one was open for 11% of the time, Pallas kernels for 0%

profile of v3, /device:TPU:1, one launch (start us, length us, event | category | flops | bytes accessed | tf_op | source)
XLA Modules:
  0.0 479.3 jit_solution(16149095972432146823)
XLA Ops:
  0.0 0.9 copy-done
  1.0 0.9 pad_maximum_fusion.1
  2.4 59.8 %all_to_all.45 = bf16[32,64,912]{2,1,0:T(8,128)(2,1)} all-to-all(bf16[32,64,912]{2,1,0:T(8,128)(2,1)S(1)} %broadcast_in_dim.26), channel_id=1, replica_groups=mesh['wide'=32,'narrow'=4] {'wide'}, dimensions={0} | all-to-all | bytes 7471104 | tf_op jit(solution)/shard_map/all_to_all | solution.py:47
  62.3 1.1 broadcast_in_dim.28
  63.4 3.9 all-to-all-start.2
  67.5 3.9 fusion.28
  71.5 11.8 %all-to-all-done.2 = bf16[32,16,1024]{2,1,0:T(8,128)(2,1)S(1)} async-done(((bf16[32,16,1024]{2,1,0:T(8,128)(2,1)}), bf16[32,16,1024]{2,1,0:T(8,128)(2,1)S(1)}, u32[]{:S(2)}, u32[]{:S(2)}) %all-to-all-start.2) | async-done | bytes 1048608 | tf_op jit(solution)/shard_map/all_to_all | solution.py:47
  83.3 0.8 broadcast_in_dim.30
  84.0 7.7 %all-to-all-start.3 = ((f32[4,128,144]{1,2,0:T(8,128)}), f32[4,128,144]{1,2,0:T(8,128)S(1)}, u32[]{:S(2)}, u32[]{:S(2)}) async-start(f32[4,128,144]{1,2,0:T(8,128)} %broadcast_in_dim.30), calls=%async_computation.3 | async-start | bytes 589824 | tf_op jit(solution)/shard_map/all_to_all | solution.py:47
  91.8 6.8 %all-to-all-done.3 = f32[4,128,144]{1,2,0:T(8,128)S(1)} async-done(((f32[4,128,144]{1,2,0:T(8,128)}), f32[4,128,144]{1,2,0:T(8,128)S(1)}, u32[]{:S(2)}, u32[]{:S(2)}) %all-to-all-start.3) | async-done | bytes 294944 | tf_op jit(solution)/shard_map/all_to_all | solution.py:47
  98.6 4.1 broadcast_in_dim.27
  102.7 5.0 %all-to-all-start.1 = ((bf16[32,128,768]{1,2,0:T(8,128)(2,1)}), bf16[32,128,768]{1,2,0:T(8,128)(2,1)}, u32[]{:S(2)}, u32[]{:S(2)}) async-start(bf16[32,128,768]{1,2,0:T(8,128)(2,1)} %broadcast_in_dim.27), calls=%async_computation.1 | async-start | bytes 12582912 | tf_op jit(solution)/shard_map/all_to_all | solution.py:47
  107.8 8.6 %copy.88.kv_ref = bf16[8,640,576]{2,1,0:T(8,128)(2,1)} copy(bf16[8,640,576]{1,2,0:T(8,128)(2,1)} %param.16) | data formatting | bytes 11796480 | tf_op args[7]
  117.1 5.0 %fusion.71 = f32[128]{0:T(128)S(1)} fusion(s32[]{:T(128)} %bitcast.8, s32[]{:T(128)} %bitcast.9, s32[]{:T(128)} %bitcast.10, s32[]{:T(128)} %bitcast.11, s32[]{:T(128)} %bitcast.12, s32[]{:T(128)} %bitcast.14, s32[]{:T(128)} %bitcast.13, s32[]{:T(128)} %bitcast.7, s32[]{:T(128)S(6)} %mul.197), kind=kLoop, calls=%fused_computation.135 | loop fusion | flops 6016 | bytes 548 | tf_op jit(solution)/shard_map/convert_element_type | solution.py:22
  122.1 4.4 compare_select_fusion.1
  127.3 9.2 %multiply_cosine_fusion = (f32[4096,32]{1,0:T(8,128)S(1)}, f32[4096,32]{1,0:T(8,128)}) fusion(f32[32]{0:T(128)S(1)} %multiply_power_fusion, f32[4096]{0:T(1024)S(1)} %fusion.53), kind=kLoop, calls=%fused_computation.10 | loop fusion | flops 131072 | bytes 1065088 | tf_op jit(solution)/shard_map/cos | solution.py:25
  136.5 2.6 reshape_reshape.3
  139.1 1.6 fusion.76
  140.7 0.9 copy.127
  141.8 53.8 %all-to-all-done.1 = bf16[32,128,768]{1,2,0:T(8,128)(2,1)} async-done(((bf16[32,128,768]{1,2,0:T(8,128)(2,1)}), bf16[32,128,768]{1,2,0:T(8,128)(2,1)}, u32[]{:S(2)}, u32[]{:S(2)}) %all-to-all-start.1) | async-done | bytes 6291488 | tf_op jit(solution)/shard_map/all_to_all | solution.py:47
  195.6 3.7 copy_bitcast_fusion
  199.4 2.3 slice.85
  201.7 2.5 fusion.75
  204.2 6.2 %copy.113 = f32[4096,4,32]{2,0,1:T(8,128)} copy(f32[4096,4,32]{0,2,1:T(8,128)} %get-tuple-element.18) | data formatting | bytes 4194304
  210.4 6.2 %copy.114 = f32[4096,4,32]{2,0,1:T(8,128)} copy(f32[4096,4,32]{0,2,1:T(8,128)} %get-tuple-element.19) | data formatting | bytes 4194304
  216.7 10.6 %convolution_convert_fusion.lat_ref = bf16[4,4096,512]{2,1,0:T(8,128)(2,1)} fusion(bf16[4096,4,128]{0,2,1:T(8,128)(2,1)} %bitcast.143, bf16[512,4,128]{2,1,0:T(4,128)(2,1)S(1)} %get-tuple-element.21), kind=kOutput, calls=%fused_computation | convolution fusion | flops 2155872256 | bytes 21495808 | tf_op jit(solution)/shard_map/thc,lhc->htl/dot_general | solution.py:231
  227.3 5.1 %subtract_convert_fusion = (bf16[4096,4,32]{2,0,1:T(8,128)(2,1)S(1)}, bf16[4096,4,32]{2,0,1:T(8,128)(2,1)S(1)}) fusion(f32[4096,4,32]{2,0,1:T(8,128)} %copy.114, f32[4096,4,32]{2,0,1:T(8,128)S(1)} %bitcast.139, f32[4096,32]{1,0:T(8,128)} %get-tuple-element.25, f32[4096,32]{1,0:T(8,128)S(1)} %get-tuple-element.24), kind=kLoop, calls=%fused_computation.3 | loop fusion | flops 4194304 | bytes 7340032 | tf_op jit(solution)/shard_map/convert.8
  232.4 3.7 maximum_bitcast_fusion.rope_ref
  236.6 2.6 select_reduce_fusion
  239.4 2.8 fusion.26
  242.5 77.8 %shard_map.91 = (f32[4,4096,1]{2,1,0:T(8,128)}, f32[4,4096,1]{2,1,0:T(8,128)}, f32[4,4096,128]{2,1,0:T(8,128)}) custom-call(s32[8]{0:T(128)} %lens_ref.1, s32[1]{0:T(128)} %bitcast.base_ref, bf16[4,4096,512]{2,1,0:T(8,128)(2,1)} %convolution_convert_fusion.lat_ref, bf16[4,4096,64]{2,1,0:T(8,128)(2,1)} %maximum_bitcast_fusion.rope_ref, ...), custom_call_target="tpu_custom_call" | custom-call | tf_op jit(solution)/shard_map/pallas_call | solution.py:152
  320.3 5.6 %reduce.3 = bf16[4,4096]{1,0:T(4,128)(2,1)S(1)} reduce(f32[4,4096,1]{2,1,0:T(8,128)} %get-tuple-element.8, f32[]{:T(128)} %constant.133), dimensions={2}, to_apply=%get-tuple-element.8.reduce_sub_computation | reduce | bytes 98308 | tf_op jit(solution)/shard_map/pallas_call | solution.py:152
  325.9 5.6 %reduce.5 = bf16[4,4096]{1,0:T(4,128)(2,1)S(1)} reduce(f32[4,4096,1]{2,1,0:T(8,128)} %get-tuple-element.9, f32[]{:T(128)} %constant.133), dimensions={2}, to_apply=%get-tuple-element.9.reduce_sub_computation | reduce | bytes 98308 | tf_op jit(solution)/shard_map/pallas_call | solution.py:152
  331.6 2.7 fusion.17
  335.0 6.5 %all-to-all-start.4 = ((bf16[2,4,32,128]{3,1,0,2:T(4,128)(2,1)}), bf16[2,4,32,128]{3,1,0,2:T(4,128)(2,1)S(1)}, u32[]{:S(2)}, u32[]{:S(2)}) async-start(bf16[2,4,32,128]{3,1,0,2:T(4,128)(2,1)} %pad_maximum_fusion.2), calls=%async_computation.4 | async-start | bytes 131072 | tf_op jit(solution)/shard_map/all_to_all | solution.py:276
  341.6 3.1 fusion.21
  345.0 2.8 fusion.12
  347.8 3.9 convert_element_type.90
  351.7 2.3 copy.98
  354.0 57.2 %all_to_all.46 = bf16[4,32,128,128]{3,2,0,1:T(8,128)(2,1)} all-to-all(bf16[4,32,128,128]{3,2,0,1:T(8,128)(2,1)} %copy.98), channel_id=1, replica_groups=mesh['wide'=32,'narrow'=4] {'wide'}, dimensions={1} | all-to-all | bytes 8388608 | tf_op jit(solution)/shard_map/all_to_all | solution.py:279
  411.2 1.6 broadcast_in_dim.33
  412.8 4.2 all-to-all-start.6
  417.1 4.4 multiply_reduce_fusion
  421.8 22.9 %all-to-all-done.6 = bf16[32,512,64]{1,2,0:T(8,128)(2,1)S(1)} async-done(((bf16[32,512,64]{1,2,0:T(8,128)(2,1)}), bf16[32,512,64]{1,2,0:T(8,128)(2,1)S(1)}, u32[]{:S(2)}, u32[]{:S(2)}) %all-to-all-start.6) | async-done | bytes 2097184 | tf_op jit(solution)/shard_map/all_to_all | solution.py:47
  444.7 0.8 convolution_convert_fusion.1
  445.6 19.5 %all_to_all.47 = bf16[4,128,512]{2,1,0:T(8,128)(2,1)S(1)} all-to-all(bf16[4,128,512]{2,1,0:T(8,128)(2,1)S(1)} %bitcast.150), channel_id=1, replica_groups=mesh['wide'=32,'narrow'=4] {'narrow'}, dimensions={0} | all-to-all | bytes 1048576 | tf_op jit(solution)/shard_map/all_to_all | solution.py:303
  465.3 12.7 %all_to_all.48 = bf16[4,128,512]{2,1,0:T(8,128)(2,1)S(1)} all-to-all(bf16[4,128,512]{2,1,0:T(8,128)(2,1)S(1)} %broadcast_in_dim.34), channel_id=1, replica_groups=mesh['wide'=32,'narrow'=4] {'narrow'}, dimensions={0} | all-to-all | bytes 1048576 | tf_op jit(solution)/shard_map/all_to_all | solution.py:47
  478.2 1.0 copy.103
  (61 shorter events, 5.8 us)
Async XLA Ops:
  0.0 0.9 copy-start
  2.4 59.8 %copy-start.7 = (bf16[16,1024]{1,0:T(8,128)(2,1)S(1)}, bf16[16,1024]{1,0:T(8,128)(2,1)}, u32[]{:S(2)}) copy-start(bf16[16,1024]{1,0:T(8,128)(2,1)} %param.14) | copy-start | bytes 98308
  2.4 64.9 %copy-start.8 = (bf16[2048]{0:T(1024)(128)(2,1)S(1)}, bf16[2048]{0:T(1024)(128)(2,1)}, u32[]{:S(2)}) copy-start(bf16[2048]{0:T(1024)(128)(2,1)} %param.10) | copy-start | bytes 12292
  2.4 64.9 %copy-start.4 = (bf16[128,2048]{1,0:T(8,128)(2,1)S(1)}, bf16[128,2048]{1,0:T(8,128)(2,1)}, u32[]{:S(2)}) copy-start(bf16[128,2048]{1,0:T(8,128)(2,1)} %param.9) | copy-start | bytes 1572868
  63.4 19.9 %all-to-all-start.2 = ((bf16[32,16,1024]{2,1,0:T(8,128)(2,1)}), bf16[32,16,1024]{2,1,0:T(8,128)(2,1)S(1)}, u32[]{:S(2)}, u32[]{:S(2)}) async-start(bf16[32,16,1024]{2,1,0:T(8,128)(2,1)} %broadcast_in_dim.28), calls=%async_computation.2 | async-start | bytes 2097152 | tf_op jit(solution)/shard_map/all_to_all | solution.py:47
  83.3 19.4 %copy-start.3 = (bf16[32,16,1024]{2,1,0:T(8,128)(2,1)}, bf16[32,16,1024]{2,1,0:T(8,128)(2,1)S(1)}, u32[]{:S(2)}) copy-start(bf16[32,16,1024]{2,1,0:T(8,128)(2,1)S(1)} %all-to-all-done.2) | copy-start | bytes 3145732
  84.0 14.6 %all-to-all-start.3 = ((f32[4,128,144]{1,2,0:T(8,128)}), f32[4,128,144]{1,2,0:T(8,128)S(1)}, u32[]{:S(2)}, u32[]{:S(2)}) async-start(f32[4,128,144]{1,2,0:T(8,128)} %broadcast_in_dim.30), calls=%async_computation.3 | async-start | bytes 589824 | tf_op jit(solution)/shard_map/all_to_all | solution.py:47
  102.7 5.1 %copy-start.9 = (bf16[512]{0:T(512)(128)(2,1)S(1)}, bf16[512]{0:T(512)(128)(2,1)}, u32[]{:S(2)}) copy-start(bf16[512]{0:T(512)(128)(2,1)} %param.13) | copy-start | bytes 3076
  102.7 92.9 %all-to-all-start.1 = ((bf16[32,128,768]{1,2,0:T(8,128)(2,1)}), bf16[32,128,768]{1,2,0:T(8,128)(2,1)}, u32[]{:S(2)}, u32[]{:S(2)}) async-start(bf16[32,128,768]{1,2,0:T(8,128)(2,1)} %broadcast_in_dim.27), calls=%async_computation.1 | async-start | bytes 12582912 | tf_op jit(solution)/shard_map/all_to_all | solution.py:47
  107.8 8.7 %copy-start.6 = (s32[8]{0:T(128)S(1)}, s32[8]{0:T(128)}, u32[]{:S(2)}) copy-start(s32[8]{0:T(128)} %lens_ref.1) | copy-start | bytes 100
  216.7 10.6 %slice-start = ((s8[8388608]{0:T(1024)(128)(4,1)}), s8[4194304]{0:T(1024)(128)(4,1)S(1)}, s32[]{:S(2)}) async-start(s8[8388608]{0:T(1024)(128)(4,1)} %bitcast.138), calls=%async_computation.9 | async-start | bytes 8388608
  216.7 10.6 %slice-start.1 = ((s8[8388608]{0:T(1024)(128)(4,1)}), s8[4194304]{0:T(1024)(128)(4,1)S(1)}, s32[]{:S(2)}) async-start(s8[8388608]{0:T(1024)(128)(4,1)} %bitcast.138), calls=%async_computation.10 | async-start | bytes 8388608
  335.0 19.0 %all-to-all-start.4 = ((bf16[2,4,32,128]{3,1,0,2:T(4,128)(2,1)}), bf16[2,4,32,128]{3,1,0,2:T(4,128)(2,1)S(1)}, u32[]{:S(2)}, u32[]{:S(2)}) async-start(bf16[2,4,32,128]{3,1,0,2:T(4,128)(2,1)} %pad_maximum_fusion.2), calls=%async_computation.4 | async-start | bytes 131072 | tf_op jit(solution)/shard_map/all_to_all | solution.py:276
  341.6 3.5 copy-start.2
  354.0 57.2 %copy-start.5 = (bf16[512,64]{0,1:T(8,128)(2,1)S(1)}, bf16[512,64]{0,1:T(8,128)(2,1)}, u32[]{:S(2)}) copy-start(bf16[512,64]{0,1:T(8,128)(2,1)} %param.15) | copy-start | bytes 196612
  412.8 31.9 %all-to-all-start.6 = ((bf16[32,512,64]{1,2,0:T(8,128)(2,1)}), bf16[32,512,64]{1,2,0:T(8,128)(2,1)S(1)}, u32[]{:S(2)}, u32[]{:S(2)}) async-start(bf16[32,512,64]{1,2,0:T(8,128)(2,1)} %broadcast_in_dim.33), calls=%async_computation.6 | async-start | bytes 4194304 | tf_op jit(solution)/shard_map/all_to_all | solution.py:47
  444.7 34.5 %copy-start.1 = (bf16[64,576]{1,0:T(8,128)(2,1)S(1)}, bf16[64,576]{1,0:T(8,128)(2,1)}, u32[]{:S(2)}) copy-start(bf16[64,576]{1,0:T(8,128)(2,1)} %param.12) | copy-start | bytes 221188

commit v4 on v3

--- a/solution.py
+++ b/solution.py
@@ -93,60 +93,79 @@
     )
 
 
-def cache_kernel(lens_ref, base_ref, lat_ref, rope_ref, kv_ref, vm_ref, peak_ref, total_ref, value_ref):
+def cache_kernel(
+    lens_ref, base_ref, nope_ref, rope_ref, kv_ref, km_ref, vm_ref, peak_ref, total_ref, value_ref
+):
     length_now = lens_ref[pl.program_id(0)]
     base = base_ref[0]
-    live_block = base < length_now
-
-    @pl.when(live_block)
-    def _():
+    cache_rows = kv_ref.shape[1]
+    nt = (((1,), (1,)), ((), ()))
+
+    def compute(masked):
         keys = kv_ref[0]
         key_lat = keys[:, :LAT]
         key_rope = keys[:, LAT:]
-        nt = (((1,), (1,)), ((), ()))
+        q_lat = lax.dot_general(
+            nope_ref[...], km_ref[...], nt, preferred_element_type=jnp.float32
+        ).astype(jnp.bfloat16)
         scores = (
-            lax.dot_general(lat_ref[0], key_lat, nt, preferred_element_type=jnp.float32)
+            lax.dot_general(q_lat, key_lat, nt, preferred_element_type=jnp.float32)
             + lax.dot_general(rope_ref[0], key_rope, nt, preferred_element_type=jnp.float32)
         ) * score_scale
-        slots = base + lax.broadcasted_iota(jnp.int32, scores.shape, 1)
-        live = slots < length_now
-        peak = jnp.max(jnp.where(live, scores, -1e30), axis=-1, keepdims=True)
-        weights = jnp.where(live, jnp.exp(scores - peak), 0.0)
+        if masked:
+            slots = base + lax.broadcasted_iota(jnp.int32, scores.shape, 1)
+            live = slots < length_now
+            peak = jnp.max(jnp.where(live, scores, -1e30), axis=-1, keepdims=True)
+            weights = jnp.where(live, jnp.exp(scores - peak), 0.0)
+        else:
+            peak = jnp.max(scores, axis=-1, keepdims=True)
+            weights = jnp.exp(scores - peak)
         peak_ref[0] = peak
         total_ref[0] = jnp.sum(weights, axis=-1, keepdims=True)
         mixed = jnp.dot(weights.astype(jnp.bfloat16), key_lat, preferred_element_type=jnp.float32)
-        value_map = vm_ref[0]
+        value_map = vm_ref[...]
         upper_part = mixed.astype(jnp.bfloat16)
         lower_part = (mixed - upper_part.astype(jnp.float32)).astype(jnp.bfloat16)
         value_ref[0] = jnp.dot(upper_part, value_map, preferred_element_type=jnp.float32) + jnp.dot(
             lower_part, value_map, preferred_element_type=jnp.float32
         )
 
-    @pl.when(jnp.logical_not(live_block))
+    whole_live = base + cache_rows <= length_now
+    part_live = jnp.logical_and(base < length_now, jnp.logical_not(whole_live))
+
+    @pl.when(whole_live)
+    def _():
+        compute(False)
+
+    @pl.when(part_live)
+    def _():
+        compute(True)
+
+    @pl.when(base >= length_now)
     def _():
         peak_ref[...] = jnp.full(peak_ref.shape, -1e30, jnp.float32)
         total_ref[...] = jnp.zeros(total_ref.shape, jnp.float32)
         value_ref[...] = jnp.zeros(value_ref.shape, jnp.float32)
 
 
-def cache_attention(lengths, base, lat_hm, rope_hm, cache, value_hm):
-    heads_here, total_tokens, _ = lat_hm.shape
+def cache_attention(lengths, base, nope_rows, rope_hm, cache, kvb_full):
+    heads_here, total_tokens, _ = rope_hm.shape
     requests, cache_rows, width = cache.shape
     span = total_tokens // requests
-    vdim = value_hm.shape[2]
     grid_spec = pltpu.PrefetchScalarGridSpec(
         num_scalar_prefetch=2,
         grid=(requests, heads_here),
         in_specs=[
-            pl.BlockSpec((1, span, LAT), lambda r, h, lens, b: (h, r, 0)),
+            pl.BlockSpec((span, NOPE), lambda r, h, lens, b: (r, h)),
             pl.BlockSpec((1, span, ROPE), lambda r, h, lens, b: (h, r, 0)),
             pl.BlockSpec((1, cache_rows, width), lambda r, h, lens, b: (r, 0, 0)),
-            pl.BlockSpec((1, LAT, vdim), lambda r, h, lens, b: (h, 0, 0)),
+            pl.BlockSpec((LAT, NOPE), lambda r, h, lens, b: (0, 2 * h)),
+            pl.BlockSpec((LAT, VDIM), lambda r, h, lens, b: (0, 2 * h + 1)),
         ],
         out_specs=[
             pl.BlockSpec((1, span, 1), lambda r, h, lens, b: (h, r, 0)),
             pl.BlockSpec((1, span, 1), lambda r, h, lens, b: (h, r, 0)),
-            pl.BlockSpec((1, span, vdim), lambda r, h, lens, b: (h, r, 0)),
+            pl.BlockSpec((1, span, VDIM), lambda r, h, lens, b: (h, r, 0)),
         ],
     )
     return pl.pallas_call(
@@ -155,11 +174,10 @@
         out_shape=[
             jax.ShapeDtypeStruct((heads_here, total_tokens, 1), jnp.float32),
             jax.ShapeDtypeStruct((heads_here, total_tokens, 1), jnp.float32),
-            jax.ShapeDtypeStruct((heads_here, total_tokens, vdim), jnp.float32),
+            jax.ShapeDtypeStruct((heads_here, total_tokens, VDIM), jnp.float32),
         ],
         compiler_params=pltpu.CompilerParams(dimension_semantics=("arbitrary", "arbitrary")),
-    )(lengths, base, lat_hm, rope_hm, cache, value_hm)
-
+    )(lengths, base, nope_rows, rope_hm, cache, kvb_full, kvb_full)
 
 def merge_parts(first, second):
     joint_peak = jnp.maximum(first[0], second[0])
@@ -228,14 +246,12 @@
     nope_all = raw_all[:, : heads_here * NOPE].reshape(total_tokens, heads_here, NOPE)
     rope_all = raw_all[:, heads_here * NOPE :].reshape(total_tokens, heads_here, ROPE)
     q_rope = rotate(rope_all.astype(jnp.float32), all_positions[:, None]).astype(jnp.bfloat16)
-    lat_hm = jnp.einsum(
-        "thc,lhc->htl", nope_all, key_maps, preferred_element_type=jnp.float32
-    ).astype(jnp.bfloat16)
     rope_hm = jnp.transpose(q_rope, (1, 0, 2))
-    value_hm = jnp.transpose(value_maps, (1, 0, 2))
 
     base = (wide_place * cache_rows).reshape(1).astype(jnp.int32)
-    peak_hm, total_hm, value_out = cache_attention(lengths, base, lat_hm, rope_hm, cache, value_hm)
+    peak_hm, total_hm, value_out = cache_attention(
+        lengths, base, raw_all, rope_hm, cache, kvb_full
+    )
     peak_hm = peak_hm[..., 0]
     total_hm = total_hm[..., 0]
 
@@ -243,7 +259,12 @@
     start_row = own_request * SPAN
     own_slots = first_token % SPAN + jnp.arange(tok_rows, dtype=jnp.int32)
     causal = own_slots[None, :] <= jnp.arange(SPAN, dtype=jnp.int32)[:, None]
-    own_lat = lax.dynamic_slice_in_dim(lat_hm, start_row, SPAN, 1)
+    own_lat = jnp.einsum(
+        "thc,lhc->htl",
+        lax.dynamic_slice_in_dim(nope_all, start_row, SPAN, 0),
+        key_maps,
+        preferred_element_type=jnp.float32,
+    ).astype(jnp.bfloat16)
     own_rope = lax.dynamic_slice_in_dim(rope_hm, start_row, SPAN, 1)
     own_scores = (
         jnp.einsum("hqc,kc->hqk", own_lat, own_keys[:, :LAT], preferred_element_type=jnp.float32)
@@ -260,8 +281,8 @@
     own_upper = own_mixed.astype(jnp.bfloat16)
     own_lower = (own_mixed - own_upper.astype(jnp.float32)).astype(jnp.bfloat16)
     own_value = jnp.einsum(
-        "hqc,hcv->hqv", own_upper, value_hm, preferred_element_type=jnp.float32
-    ) + jnp.einsum("hqc,hcv->hqv", own_lower, value_hm, preferred_element_type=jnp.float32)
+        "hqc,chv->hqv", own_upper, value_maps, preferred_element_type=jnp.float32
+    ) + jnp.einsum("hqc,chv->hqv", own_lower, value_maps, preferred_element_type=jnp.float32)
     old_part = (
         lax.dynamic_slice_in_dim(peak_hm, start_row, SPAN, 1),
         lax.dynamic_slice_in_dim(total_hm, start_row, SPAN, 1),

time: 482 us -> 494 us (1.025)
  local copies, waits for them, and re-layouts: 49 us -> 62.8 us
  matrix products: 27 us -> 16.3 us
  other arithmetic: 53.1 us -> 59.4 us
    dot_general x3 -> x2, matrix products: 16.5 us -> 5.82 us  [the longest x1 3.06 us: per_device(): jnp.einsum('hqc,chv->hqv', own_upper, value_maps, preferred_element_type=...]
    convert_element_type x0 -> x1, local copies, waits for them, and re-layouts: none -> 5.62 us  [per_device(): rope_all.astype(jnp.float32)]
    unnamed x28 -> x25, local copies, waits for them, and re-layouts: 23.2 us -> 22.8 us
where the time goes in v4:
time: 494 us; the launch traced here: 493 us
  blocking collectives  149 us (30%)
  waiting for transfers between devices  96.3 us (19%)
  Pallas kernels  81 us (16%)
  local copies, waits for them, and re-layouts  62.8 us (13%)
  other arithmetic  59.4 us (12%)
  starting transfers between devices  27.6 us (6%)
  matrix products  16.3 us (3%)
    all_to_all x4, waiting for transfers between devices, gather_axis(): lax.all_to_all(spread, axis_name, split_axis=0, concat_axis=0, tiled=True)  96.3 us
    pallas_call x1, Pallas kernels, cache_attention(): pl.pallas_call(cache_kernel, grid_spec=grid_spec, out_shape=[jax.ShapeDty...  81 us
    all_to_all x2, blocking collectives, gather_axis(): lax.all_to_all(spread, axis_name, split_axis=0, concat_axis=0, tiled=True)  72.5 us
    all_to_all x1, blocking collectives, per_device(): lax.all_to_all(value_out.astype(jnp.bfloat16).reshape(heads_here, wide_co...  57.2 us
    unnamed x25, local copies, waits for them, and re-layouts  22.8 us
    all_to_all x4, starting transfers between devices, gather_axis(): lax.all_to_all(spread, axis_name, split_axis=0, concat_axis=0, tiled=True)  21.1 us
    all_to_all x1, blocking collectives, per_device(): got_pieces = lax.all_to_all(pieces, 'narrow', 0, 0, tiled=True)  19.5 us
    pallas_call x2, other arithmetic, cache_attention(): pl.pallas_call(cache_kernel, grid_spec=grid_spec, out_shape=[jax.ShapeDty...  11.3 us
  transfers between devices with their start and end apart: 5, of which 4 were waited for; matrix products, arithmetic and copies ran while one was open for 11% of the time, Pallas kernels for 0%

profile of v4, /device:TPU:1, one launch (start us, length us, event | category | flops | bytes accessed | tf_op | source)
XLA Modules:
  0.0 493.0 jit_solution(6353287722780751393)
XLA Ops:
  0.0 0.9 copy-done
  1.0 0.9 pad_maximum_fusion.1
  2.4 59.8 %all_to_all.45 = bf16[32,64,912]{2,1,0:T(8,128)(2,1)} all-to-all(bf16[32,64,912]{2,1,0:T(8,128)(2,1)S(1)} %broadcast_in_dim.26), channel_id=1, replica_groups=mesh['wide'=32,'narrow'=4] {'wide'}, dimensions={0} | all-to-all | bytes 7471104 | tf_op jit(solution)/shard_map/all_to_all | solution.py:47
  62.3 1.1 broadcast_in_dim.28
  63.4 3.9 all-to-all-start.2
  67.5 3.9 fusion.30
  71.5 11.8 %all-to-all-done.2 = bf16[32,16,1024]{2,1,0:T(8,128)(2,1)S(1)} async-done(((bf16[32,16,1024]{2,1,0:T(8,128)(2,1)}), bf16[32,16,1024]{2,1,0:T(8,128)(2,1)S(1)}, u32[]{:S(2)}, u32[]{:S(2)}) %all-to-all-start.2) | async-done | bytes 1048608 | tf_op jit(solution)/shard_map/all_to_all | solution.py:47
  84.0 7.7 %all-to-all-start.3 = ((f32[4,128,144]{1,2,0:T(8,128)}), f32[4,128,144]{1,2,0:T(8,128)S(1)}, u32[]{:S(2)}, u32[]{:S(2)}) async-start(f32[4,128,144]{1,2,0:T(8,128)} %broadcast_in_dim.30), calls=%async_computation.3 | async-start | bytes 589824 | tf_op jit(solution)/shard_map/all_to_all | solution.py:47
  92.0 6.6 %all-to-all-done.3 = f32[4,128,144]{1,2,0:T(8,128)S(1)} async-done(((f32[4,128,144]{1,2,0:T(8,128)}), f32[4,128,144]{1,2,0:T(8,128)S(1)}, u32[]{:S(2)}, u32[]{:S(2)}) %all-to-all-start.3) | async-done | bytes 294944 | tf_op jit(solution)/shard_map/all_to_all | solution.py:47
  98.6 3.4 broadcast_in_dim.27
  102.0 5.0 %all-to-all-start.1 = ((bf16[32,128,768]{2,1,0:T(8,128)(2,1)}), bf16[32,128,768]{2,1,0:T(8,128)(2,1)}, u32[]{:S(2)}, u32[]{:S(2)}) async-start(bf16[32,128,768]{2,1,0:T(8,128)(2,1)} %broadcast_in_dim.27), calls=%async_computation.1 | async-start | bytes 12582912 | tf_op jit(solution)/shard_map/all_to_all | solution.py:47
  107.1 8.5 %copy.96.kv_ref = bf16[8,640,576]{2,1,0:T(8,128)(2,1)} copy(bf16[8,640,576]{1,2,0:T(8,128)(2,1)} %param.16) | data formatting | bytes 11796480 | tf_op args[7]
  116.3 5.0 %fusion.77 = f32[128]{0:T(128)S(1)} fusion(s32[]{:T(128)} %bitcast.8, s32[]{:T(128)} %bitcast.9, s32[]{:T(128)} %bitcast.10, s32[]{:T(128)} %bitcast.11, s32[]{:T(128)} %bitcast.12, s32[]{:T(128)} %bitcast.14, s32[]{:T(128)} %bitcast.13, s32[]{:T(128)} %bitcast.7, s32[]{:T(128)S(6)} %mul.197), kind=kLoop, calls=%fused_computation.137 | loop fusion | flops 6016 | bytes 548 | tf_op jit(solution)/shard_map/convert_element_type | solution.py:22
  121.3 4.4 compare_select_fusion.1
  126.5 9.2 %multiply_cosine_fusion = (f32[4096,32]{1,0:T(8,128)S(1)}, f32[4096,32]{1,0:T(8,128)}) fusion(f32[32]{0:T(128)S(1)} %multiply_power_fusion, f32[4096]{0:T(1024)S(1)} %fusion.60), kind=kLoop, calls=%fused_computation.8 | loop fusion | flops 131072 | bytes 1065088 | tf_op jit(solution)/shard_map/cos | solution.py:25
  135.7 1.6 reshape_reshape.3
  137.3 2.4 fusion.82
  139.9 55.0 %all-to-all-done.1 = bf16[32,128,768]{2,1,0:T(8,128)(2,1)} async-done(((bf16[32,128,768]{2,1,0:T(8,128)(2,1)}), bf16[32,128,768]{2,1,0:T(8,128)(2,1)}, u32[]{:S(2)}, u32[]{:S(2)}) %all-to-all-start.1) | async-done | bytes 6291488 | tf_op jit(solution)/shard_map/all_to_all | solution.py:47
  194.9 3.8 slice_convert_fusion
  198.7 4.4 slice.88
  203.1 5.6 %copy.93 = f32[4096,256]{0,1:T(8,128)} copy(f32[4096,256]{1,0:T(8,128)} %slice_convert_fusion) | data formatting | bytes 8388608 | tf_op jit(solution)/shard_map/convert_element_type | solution.py:248
  208.7 4.6 fusion.81
  213.3 6.2 %copy.122 = f32[4096,4,32]{2,0,1:T(8,128)} copy(f32[4096,4,32]{0,2,1:T(8,128)} %get-tuple-element.18) | data formatting | bytes 4194304
  219.6 6.2 %copy.123 = f32[4096,4,32]{2,0,1:T(8,128)} copy(f32[4096,4,32]{0,2,1:T(8,128)} %get-tuple-element.19) | data formatting | bytes 4194304
  225.8 6.9 %reshape.390 = bf16[4096,4,128]{2,1,0:T(4,128)(2,1)} reshape(bf16[4096,512]{1,0:T(8,128)(2,1)} %slice.88) | data formatting | bytes 8388608 | tf_op jit(solution)/shard_map/reshape | solution.py:246
  232.7 2.1 constant_dynamic-slice_fusion
  234.8 7.5 %subtract_convert_fusion = (bf16[4096,4,32]{2,0,1:T(8,128)(2,1)S(1)}, bf16[4096,4,32]{2,0,1:T(8,128)(2,1)S(1)}) fusion(f32[4096,4,32]{2,0,1:T(8,128)} %copy.123, f32[4096,4,32]{2,0,1:T(8,128)} %copy.122, f32[4096,32]{1,0:T(8,128)} %get-tuple-element.25, f32[4096,32]{1,0:T(8,128)S(1)} %get-tuple-element.24), kind=kLoop, calls=%fused_computation.2 | loop fusion | flops 4194304 | bytes 7340032 | tf_op jit(solution)/shard_map/convert.8
  242.3 3.6 maximum_bitcast_fusion.rope_ref
  247.0 2.4 select_reduce_fusion
  249.6 2.8 fusion.28
  252.8 81.0 %shard_map.91 = (f32[4,4096,1]{2,1,0:T(8,128)}, f32[4,4096,1]{2,1,0:T(8,128)}, f32[4,4096,128]{2,1,0:T(8,128)}) custom-call(s32[8]{0:T(128)} %lens_ref.1, s32[1]{0:T(128)} %bitcast.base_ref, bf16[4096,768]{1,0:T(8,128)(2,1)} %bitcast.5.nope_ref, bf16[4,4096,64]{2,1,0:T(8,128)(2,1)} %maximum_bitcast_fusion.rope_ref, bf16[8,640,576]{2,1,0:T(8,128)(2,1)} %copy.96.kv_ref, ...), custom_call_target="tpu_custom_call" | custom-call | tf_op jit(solution)/shard_map/pallas_call | solution.py:171
  333.8 5.6 %reduce.3 = bf16[4,4096]{1,0:T(4,128)(2,1)S(1)} reduce(f32[4,4096,1]{2,1,0:T(8,128)} %get-tuple-element.8, f32[]{:T(128)} %constant.133), dimensions={2}, to_apply=%get-tuple-element.8.reduce_sub_computation | reduce | bytes 98308 | tf_op jit(solution)/shard_map/pallas_call | solution.py:171
  339.4 5.6 %reduce.5 = bf16[4,4096]{1,0:T(4,128)(2,1)S(1)} reduce(f32[4,4096,1]{2,1,0:T(8,128)} %get-tuple-element.9, f32[]{:T(128)} %constant.133), dimensions={2}, to_apply=%get-tuple-element.9.reduce_sub_computation | reduce | bytes 98308 | tf_op jit(solution)/shard_map/pallas_call | solution.py:171
  345.0 2.7 fusion.19
  348.5 6.5 %all-to-all-start.4 = ((bf16[2,4,32,128]{3,1,0,2:T(4,128)(2,1)}), bf16[2,4,32,128]{3,1,0,2:T(4,128)(2,1)S(1)}, u32[]{:S(2)}, u32[]{:S(2)}) async-start(bf16[2,4,32,128]{3,1,0,2:T(4,128)(2,1)} %pad_maximum_fusion.2), calls=%async_computation.4 | async-start | bytes 131072 | tf_op jit(solution)/shard_map/all_to_all | solution.py:297
  355.1 3.1 fusion.23
  358.5 2.8 fusion.14
  361.3 3.9 convert_element_type.90
  365.2 2.3 copy.109
  367.5 57.2 %all_to_all.46 = bf16[4,32,128,128]{3,2,0,1:T(8,128)(2,1)} all-to-all(bf16[4,32,128,128]{3,2,0,1:T(8,128)(2,1)} %copy.109), channel_id=1, replica_groups=mesh['wide'=32,'narrow'=4] {'wide'}, dimensions={1} | all-to-all | bytes 8388608 | tf_op jit(solution)/shard_map/all_to_all | solution.py:300
  424.7 1.6 broadcast_in_dim.33
  426.3 4.4 all-to-all-start.6
  430.8 4.4 multiply_reduce_fusion
  435.5 22.9 %all-to-all-done.6 = bf16[32,512,64]{1,2,0:T(8,128)(2,1)S(1)} async-done(((bf16[32,512,64]{1,2,0:T(8,128)(2,1)}), bf16[32,512,64]{1,2,0:T(8,128)(2,1)S(1)}, u32[]{:S(2)}, u32[]{:S(2)}) %all-to-all-start.6) | async-done | bytes 2097184 | tf_op jit(solution)/shard_map/all_to_all | solution.py:47
  458.4 0.8 convolution_convert_fusion
  459.3 19.5 %all_to_all.47 = bf16[4,128,512]{2,1,0:T(8,128)(2,1)S(1)} all-to-all(bf16[4,128,512]{2,1,0:T(8,128)(2,1)S(1)} %bitcast.137), channel_id=1, replica_groups=mesh['wide'=32,'narrow'=4] {'narrow'}, dimensions={0} | all-to-all | bytes 1048576 | tf_op jit(solution)/shard_map/all_to_all | solution.py:324
  479.0 12.7 %all_to_all.48 = bf16[4,128,512]{2,1,0:T(8,128)(2,1)S(1)} all-to-all(bf16[4,128,512]{2,1,0:T(8,128)(2,1)S(1)} %broadcast_in_dim.34), channel_id=1, replica_groups=mesh['wide'=32,'narrow'=4] {'narrow'}, dimensions={0} | all-to-all | bytes 1048576 | tf_op jit(solution)/shard_map/all_to_all | solution.py:47
  492.0 1.0 copy.114
  (60 shorter events, 7.2 us)
Async XLA Ops:
  0.0 0.9 copy-start
  2.4 59.8 %copy-start.8 = (bf16[16,1024]{1,0:T(8,128)(2,1)S(1)}, bf16[16,1024]{1,0:T(8,128)(2,1)}, u32[]{:S(2)}) copy-start(bf16[16,1024]{1,0:T(8,128)(2,1)} %param.14) | copy-start | bytes 98308
  2.4 64.9 %copy-start.9 = (bf16[2048]{0:T(1024)(128)(2,1)S(1)}, bf16[2048]{0:T(1024)(128)(2,1)}, u32[]{:S(2)}) copy-start(bf16[2048]{0:T(1024)(128)(2,1)} %param.10) | copy-start | bytes 12292
  2.4 64.9 %copy-start.4 = (bf16[128,2048]{1,0:T(8,128)(2,1)S(1)}, bf16[128,2048]{1,0:T(8,128)(2,1)}, u32[]{:S(2)}) copy-start(bf16[128,2048]{1,0:T(8,128)(2,1)} %param.9) | copy-start | bytes 1572868
  63.4 19.9 %all-to-all-start.2 = ((bf16[32,16,1024]{2,1,0:T(8,128)(2,1)}), bf16[32,16,1024]{2,1,0:T(8,128)(2,1)S(1)}, u32[]{:S(2)}, u32[]{:S(2)}) async-start(bf16[32,16,1024]{2,1,0:T(8,128)(2,1)} %broadcast_in_dim.28), calls=%async_computation.2 | async-start | bytes 2097152 | tf_op jit(solution)/shard_map/all_to_all | solution.py:47
  83.3 52.5 %copy-start.3 = (bf16[32,16,1024]{2,1,0:T(8,128)(2,1)}, bf16[32,16,1024]{2,1,0:T(8,128)(2,1)S(1)}, u32[]{:S(2)}) copy-start(bf16[32,16,1024]{2,1,0:T(8,128)(2,1)S(1)} %all-to-all-done.2) | copy-start | bytes 3145732
  84.0 14.6 %all-to-all-start.3 = ((f32[4,128,144]{1,2,0:T(8,128)}), f32[4,128,144]{1,2,0:T(8,128)S(1)}, u32[]{:S(2)}, u32[]{:S(2)}) async-start(f32[4,128,144]{1,2,0:T(8,128)} %broadcast_in_dim.30), calls=%async_computation.3 | async-start | bytes 589824 | tf_op jit(solution)/shard_map/all_to_all | solution.py:47
  102.0 5.1 %copy-start.10 = (bf16[512]{0:T(512)(128)(2,1)S(1)}, bf16[512]{0:T(512)(128)(2,1)}, u32[]{:S(2)}) copy-start(bf16[512]{0:T(512)(128)(2,1)} %param.13) | copy-start | bytes 3076
  102.0 92.9 %all-to-all-start.1 = ((bf16[32,128,768]{2,1,0:T(8,128)(2,1)}), bf16[32,128,768]{2,1,0:T(8,128)(2,1)}, u32[]{:S(2)}, u32[]{:S(2)}) async-start(bf16[32,128,768]{2,1,0:T(8,128)(2,1)} %broadcast_in_dim.27), calls=%async_computation.1 | async-start | bytes 12582912 | tf_op jit(solution)/shard_map/all_to_all | solution.py:47
  107.1 8.5 %copy-start.7 = (s32[8]{0:T(128)S(1)}, s32[8]{0:T(128)}, u32[]{:S(2)}) copy-start(s32[8]{0:T(128)} %lens_ref.1) | copy-start | bytes 100
  245.9 1.0 copy-start.5
  348.5 19.0 %all-to-all-start.4 = ((bf16[2,4,32,128]{3,1,0,2:T(4,128)(2,1)}), bf16[2,4,32,128]{3,1,0,2:T(4,128)(2,1)S(1)}, u32[]{:S(2)}, u32[]{:S(2)}) async-start(bf16[2,4,32,128]{3,1,0,2:T(4,128)(2,1)} %pad_maximum_fusion.2), calls=%async_computation.4 | async-start | bytes 131072 | tf_op jit(solution)/shard_map/all_to_all | solution.py:297
  355.0 3.5 copy-start.2
  367.5 57.2 %copy-start.6 = (bf16[512,64]{0,1:T(8,128)(2,1)S(1)}, bf16[512,64]{0,1:T(8,128)(2,1)}, u32[]{:S(2)}) copy-start(bf16[512,64]{0,1:T(8,128)(2,1)} %param.15) | copy-start | bytes 196612
  426.3 32.2 %all-to-all-start.6 = ((bf16[32,512,64]{1,2,0:T(8,128)(2,1)}), bf16[32,512,64]{1,2,0:T(8,128)(2,1)S(1)}, u32[]{:S(2)}, u32[]{:S(2)}) async-start(bf16[32,512,64]{1,2,0:T(8,128)(2,1)} %broadcast_in_dim.33), calls=%async_computation.6 | async-start | bytes 4194304 | tf_op jit(solution)/shard_map/all_to_all | solution.py:47
  458.4 34.6 %copy-start.1 = (bf16[64,576]{1,0:T(8,128)(2,1)S(1)}, bf16[64,576]{1,0:T(8,128)(2,1)}, u32[]{:S(2)}) copy-start(bf16[64,576]{1,0:T(8,128)(2,1)} %param.12) | copy-start | bytes 221188

commit v5 on v3

--- a/solution.py
+++ b/solution.py
@@ -188,8 +188,12 @@
     packed = jnp.concatenate([q_weight, kva_mine], axis=1)
     got_weights = gather_axis(packed, "wide")
     proj_full = got_weights.reshape(-1, q_cols + kva_part)
-    kvb_full = gather_axis(kvb_weight, "wide").reshape(-1, kvb_weight.shape[1])
-    o_got = gather_axis(o_weight, "wide")
+    kvb_rows, kvb_cols = kvb_weight.shape
+    o_rows, o_cols = o_weight.shape
+    late = jnp.concatenate([kvb_weight, o_weight.reshape(-1, kvb_cols)], axis=0)
+    late_got = lax.all_gather(late, "wide", axis=0, tiled=False)
+    kvb_full = late_got[:, :kvb_rows].reshape(-1, kvb_cols)
+    o_got = late_got[:, kvb_rows:].reshape(wide_count, o_rows, o_cols)
 
     normed = scaled_norm(hidden.astype(jnp.float32), attn_gain).astype(jnp.bfloat16)
     projected = jnp.dot(normed, proj_full, preferred_element_type=jnp.float32)

time: 482 us -> 543 us (1.13)
  waiting for transfers between devices: 95.3 us -> 214 us
  blocking collectives: 149 us -> 51.3 us
  between operations: 0.4 us -> 13.8 us
  local copies, waits for them, and re-layouts: 49 us -> 62.2 us
  starting transfers between devices: 27.3 us -> 40.2 us
    all_gather x0 -> x1, waiting for transfers between devices: none -> 119 us  [per_device(): late_got = lax.all_gather(late, 'wide', axis=0, tiled=False)]
    all_to_all x2 -> x1, blocking collectives: 72.5 us -> 12.7 us  [gather_axis(): lax.all_to_all(spread, axis_name, split_axis=0, concat_axis=0, tiled=True)]
    all_to_all x1 -> x0, blocking collectives: 57.2 us -> none  [per_device(): lax.all_to_all(value_out.astype(jnp.bfloat16).reshape(heads_here, wide_co...]
    all_to_all x4 -> x3, waiting for transfers between devices: 95.3 us -> 69.8 us  [gather_axis(): lax.all_to_all(spread, axis_name, split_axis=0, concat_axis=0, tiled=True)]
    all_to_all x0 -> x1, waiting for transfers between devices: none -> 25 us  [per_device(): lax.all_to_all(value_out.astype(jnp.bfloat16).reshape(heads_here, wide_co...]
    all_to_all x1, blocking collectives: 19.5 us -> 38.6 us  [per_device(): got_pieces = lax.all_to_all(pieces, 'narrow', 0, 0, tiled=True)]
    all_to_all x0 -> x1, starting transfers between devices: none -> 8.15 us  [per_device(): lax.all_to_all(value_out.astype(jnp.bfloat16).reshape(heads_here, wide_co...]
    all_to_all x4 -> x3, starting transfers between devices: 20.8 us -> 28.1 us  [gather_axis(): lax.all_to_all(spread, axis_name, split_axis=0, concat_axis=0, tiled=True)]
  transfers between devices with their start and end apart: 5 -> 6, of which waited for: 4 -> 4; matrix products, arithmetic and copies ran while one was open for 11% -> 13% of each run, Pallas kernels for 0% -> 0%
where the time goes in v5:
time: 543 us; the launch traced here: 541 us
  waiting for transfers between devices  214 us (39%)
  Pallas kernels  77.8 us (14%)
  local copies, waits for them, and re-layouts  62.2 us (11%)
  other arithmetic  56.3 us (10%)
  blocking collectives  51.3 us (9%)
  starting transfers between devices  40.2 us (7%)
  matrix products  25.5 us (5%)
  between operations  13.8 us (3%)
    all_gather x1, waiting for transfers between devices, per_device(): late_got = lax.all_gather(late, 'wide', axis=0, tiled=False)  119 us
    pallas_call x1, Pallas kernels, cache_attention(): pl.pallas_call(cache_kernel, grid_spec=grid_spec, out_shape=[jax.ShapeDty...  77.8 us
    all_to_all x3, waiting for transfers between devices, gather_axis(): lax.all_to_all(spread, axis_name, split_axis=0, concat_axis=0, tiled=True)  69.8 us
    all_to_all x1, blocking collectives, per_device(): got_pieces = lax.all_to_all(pieces, 'narrow', 0, 0, tiled=True)  38.6 us
    all_to_all x3, starting transfers between devices, gather_axis(): lax.all_to_all(spread, axis_name, split_axis=0, concat_axis=0, tiled=True)  28.1 us
    unnamed x29, local copies, waits for them, and re-layouts  26.8 us
    all_to_all x1, waiting for transfers between devices, per_device(): lax.all_to_all(value_out.astype(jnp.bfloat16).reshape(heads_here, wide_co...  25 us
    all_to_all x1, blocking collectives, gather_axis(): lax.all_to_all(spread, axis_name, split_axis=0, concat_axis=0, tiled=True)  12.7 us
  transfers between devices with their start and end apart: 6, of which 4 were waited for; matrix products, arithmetic and copies ran while one was open for 13% of the time, Pallas kernels for 0%

profile of v5, /device:TPU:1, one launch (start us, length us, event | category | flops | bytes accessed | tf_op | source)
XLA Modules:
  0.0 541.2 jit_solution(14109884253437226517)
XLA Ops:
  6.5 0.9 copy-done
  7.5 0.9 pad_maximum_fusion.1
  8.4 2.5 broadcast_in_dim.22
  10.9 9.5 %all-to-all-start = ((bf16[32,64,912]{2,1,0:T(8,128)(2,1)}), bf16[32,64,912]{2,1,0:T(8,128)(2,1)}, u32[]{:S(2)}, u32[]{:S(2)}) async-start(bf16[32,64,912]{2,1,0:T(8,128)(2,1)} %broadcast_in_dim.22), calls=%async_computation | async-start | bytes 8388608 | tf_op jit(solution)/shard_map/all_to_all | solution.py:47
  21.7 58.4 %all-to-all-done = bf16[32,64,912]{2,1,0:T(8,128)(2,1)} async-done(((bf16[32,64,912]{2,1,0:T(8,128)(2,1)}), bf16[32,64,912]{2,1,0:T(8,128)(2,1)}, u32[]{:S(2)}, u32[]{:S(2)}) %all-to-all-start) | async-done | bytes 3735584 | tf_op jit(solution)/shard_map/all_to_all | solution.py:47
  80.0 3.9 fusion.28
  84.7 6.7 %all-to-all-start.2 = ((f32[4,128,144]{1,2,0:T(8,128)}), f32[4,128,144]{1,2,0:T(8,128)S(1)}, u32[]{:S(2)}, u32[]{:S(2)}) async-start(f32[4,128,144]{1,2,0:T(8,128)} %broadcast_in_dim.25), calls=%async_computation.2 | async-start | bytes 589824 | tf_op jit(solution)/shard_map/all_to_all | solution.py:47
  91.5 11.4 %all-to-all-done.2 = f32[4,128,144]{1,2,0:T(8,128)S(1)} async-done(((f32[4,128,144]{1,2,0:T(8,128)}), f32[4,128,144]{1,2,0:T(8,128)S(1)}, u32[]{:S(2)}, u32[]{:S(2)}) %all-to-all-start.2) | async-done | bytes 294944 | tf_op jit(solution)/shard_map/all_to_all | solution.py:47
  102.9 4.1 broadcast_in_dim.23
  107.0 11.9 %all-to-all-start.1 = ((bf16[32,128,768]{1,2,0:T(8,128)(2,1)}), bf16[32,128,768]{1,2,0:T(8,128)(2,1)}, u32[]{:S(2)}, u32[]{:S(2)}) async-start(bf16[32,128,768]{1,2,0:T(8,128)(2,1)} %broadcast_in_dim.23), calls=%async_computation.1 | async-start | bytes 12582912 | tf_op jit(solution)/shard_map/all_to_all | solution.py:47
  119.0 8.6 %copy.96.kv_ref = bf16[8,640,576]{2,1,0:T(8,128)(2,1)} copy(bf16[8,640,576]{1,2,0:T(8,128)(2,1)} %param.16) | data formatting | bytes 11796480 | tf_op args[7]
  128.4 5.1 fusion.71
  133.4 4.4 compare_select_fusion.1
  138.6 9.2 %multiply_cosine_fusion = (f32[4096,32]{1,0:T(8,128)S(1)}, f32[4096,32]{1,0:T(8,128)}) fusion(f32[32]{0:T(128)S(1)} %multiply_power_fusion, f32[4096]{0:T(1024)S(1)} %fusion.53), kind=kLoop, calls=%fused_computation.10 | loop fusion | flops 131072 | bytes 1065088 | tf_op jit(solution)/shard_map/cos | solution.py:25
  148.1 119.3 %all-gather.3.cloned.1.call-done = bf16[1536,1024]{1,0:T(8,128)(2,1)} async-done(((bf16[48,1024]{1,0:T(8,128)(2,1)}), bf16[1536,1024]{1,0:T(8,128)(2,1)}) %all-gather.3.cloned.1.call-update) | async-done | bytes 3145744 | tf_op jit(solution)/shard_map/all_gather | solution.py:194
  267.4 2.3 slice.94
  269.7 2.6 reshape_reshape.3
  272.3 2.4 fusion.76
  274.7 0.8 copy-done.4
  275.5 0.9 copy.136
  276.4 3.7 copy_bitcast_fusion
  280.3 2.5 copy-done.3
  282.8 2.5 fusion.75
  285.3 6.2 %copy.122 = f32[4096,4,32]{2,0,1:T(8,128)} copy(f32[4096,4,32]{0,2,1:T(8,128)} %get-tuple-element.18) | data formatting | bytes 4194304
  291.6 6.2 %copy.123 = f32[4096,4,32]{2,0,1:T(8,128)} copy(f32[4096,4,32]{0,2,1:T(8,128)} %get-tuple-element.19) | data formatting | bytes 4194304
  297.8 7.5 %subtract_convert_fusion = (bf16[4096,4,32]{2,0,1:T(8,128)(2,1)S(1)}, bf16[4096,4,32]{2,0,1:T(8,128)(2,1)S(1)}) fusion(f32[4096,4,32]{2,0,1:T(8,128)} %copy.123, f32[4096,4,32]{2,0,1:T(8,128)} %copy.122, f32[4096,32]{1,0:T(8,128)} %get-tuple-element.25, f32[4096,32]{1,0:T(8,128)S(1)} %get-tuple-element.24), kind=kLoop, calls=%fused_computation.3 | loop fusion | flops 4194304 | bytes 7340032 | tf_op jit(solution)/shard_map/convert.8
  305.3 3.7 maximum_bitcast_fusion.rope_ref
  309.0 9.1 %convolution_convert_fusion.lat_ref = bf16[4,4096,512]{2,1,0:T(8,128)(2,1)} fusion(bf16[4096,4,128]{0,2,1:T(8,128)(2,1)S(1)} %bitcast.138, bf16[512,4,128]{2,1,0:T(4,128)(2,1)} %get-tuple-element.21), kind=kOutput, calls=%fused_computation | convolution fusion | flops 2155872256 | bytes 21495808 | tf_op jit(solution)/shard_map/thc,lhc->htl/dot_general | solution.py:235
  318.6 2.5 select_reduce_fusion
  321.4 2.8 fusion.26
  324.2 77.8 %shard_map.91 = (f32[4,4096,1]{2,1,0:T(8,128)}, f32[4,4096,1]{2,1,0:T(8,128)}, f32[4,4096,128]{2,1,0:T(8,128)}) custom-call(s32[8]{0:T(128)} %lens_ref.1, s32[1]{0:T(128)} %bitcast.base_ref, bf16[4,4096,512]{2,1,0:T(8,128)(2,1)} %convolution_convert_fusion.lat_ref, bf16[4,4096,64]{2,1,0:T(8,128)(2,1)} %maximum_bitcast_fusion.rope_ref, ...), custom_call_target="tpu_custom_call" | custom-call | tf_op jit(solution)/shard_map/pallas_call | solution.py:152
  401.9 5.6 %reduce.3 = bf16[4,4096]{1,0:T(4,128)(2,1)S(1)} reduce(f32[4,4096,1]{2,1,0:T(8,128)} %get-tuple-element.8, f32[]{:T(128)} %constant.133), dimensions={2}, to_apply=%get-tuple-element.8.reduce_sub_computation | reduce | bytes 98308 | tf_op jit(solution)/shard_map/pallas_call | solution.py:152
  407.6 5.6 %reduce.5 = bf16[4,4096]{1,0:T(4,128)(2,1)S(1)} reduce(f32[4,4096,1]{2,1,0:T(8,128)} %get-tuple-element.9, f32[]{:T(128)} %constant.133), dimensions={2}, to_apply=%get-tuple-element.9.reduce_sub_computation | reduce | bytes 98308 | tf_op jit(solution)/shard_map/pallas_call | solution.py:152
  413.6 2.7 fusion.17
  417.0 3.9 all-to-all-start.3
  420.9 3.1 fusion.21
  424.4 2.8 fusion.12
  427.1 3.9 convert_element_type.90
  431.0 2.3 copy.106
  433.3 8.2 %all-to-all-start.4 = ((bf16[4,32,128,128]{3,2,0,1:T(8,128)(2,1)}), bf16[4,32,128,128]{3,2,0,1:T(8,128)(2,1)}, u32[]{:S(2)}, u32[]{:S(2)}) async-start(bf16[4,32,128,128]{3,2,0,1:T(8,128)(2,1)} %copy.106), calls=%async_computation.4 | async-start | bytes 8388608 | tf_op jit(solution)/shard_map/all_to_all | solution.py:283
  441.5 1.8 slice.106
  443.3 4.0 reshape.395
  447.3 3.5 copy.109
  451.0 25.0 %all-to-all-done.4 = bf16[4,32,128,128]{3,2,0,1:T(8,128)(2,1)} async-done(((bf16[4,32,128,128]{3,2,0,1:T(8,128)(2,1)}), bf16[4,32,128,128]{3,2,0,1:T(8,128)(2,1)}, u32[]{:S(2)}, u32[]{:S(2)}) %all-to-all-start.4) | async-done | bytes 4194336 | tf_op jit(solution)/shard_map/all_to_all | solution.py:283
  476.0 4.4 multiply_reduce_fusion
  481.6 38.6 %all_to_all.35 = bf16[4,128,512]{2,1,0:T(8,128)(2,1)S(1)} all-to-all(bf16[4,128,512]{2,1,0:T(8,128)(2,1)S(1)} %bitcast.150), channel_id=1, replica_groups=mesh['wide'=32,'narrow'=4] {'narrow'}, dimensions={0} | all-to-all | bytes 1048576 | tf_op jit(solution)/shard_map/all_to_all | solution.py:307
  520.3 12.7 %all_to_all.36 = bf16[4,128,512]{2,1,0:T(8,128)(2,1)S(1)} all-to-all(bf16[4,128,512]{2,1,0:T(8,128)(2,1)S(1)} %broadcast_in_dim.28), channel_id=1, replica_groups=mesh['wide'=32,'narrow'=4] {'narrow'}, dimensions={0} | all-to-all | bytes 1048576 | tf_op jit(solution)/shard_map/all_to_all | solution.py:47
  533.3 1.0 copy.112
  (67 shorter events, 7.8 us)
Async XLA Ops:
  6.5 0.9 copy-start
  10.9 9.6 %copy-start.7 = (bf16[512,64]{0,1:T(8,128)(2,1)S(1)}, bf16[512,64]{0,1:T(8,128)(2,1)}, u32[]{:S(2)}) copy-start(bf16[512,64]{0,1:T(8,128)(2,1)} %param.15) | copy-start | bytes 196612
  10.9 9.8 %copy-start.9 = (bf16[16,1024]{1,0:T(8,128)(2,1)S(1)}, bf16[16,1024]{1,0:T(8,128)(2,1)}, u32[]{:S(2)}) copy-start(bf16[16,1024]{1,0:T(8,128)(2,1)} %param.14) | copy-start | bytes 98308
  10.9 10.5 %copy-start.10 = (bf16[2048]{0:T(1024)(128)(2,1)S(1)}, bf16[2048]{0:T(1024)(128)(2,1)}, u32[]{:S(2)}) copy-start(bf16[2048]{0:T(1024)(128)(2,1)} %param.10) | copy-start | bytes 12292
  10.9 10.5 %copy-start.6 = (bf16[128,2048]{1,0:T(8,128)(2,1)S(1)}, bf16[128,2048]{1,0:T(8,128)(2,1)}, u32[]{:S(2)}) copy-start(bf16[128,2048]{1,0:T(8,128)(2,1)} %param.9) | copy-start | bytes 1572868
  10.9 69.1 %all-to-all-start = ((bf16[32,64,912]{2,1,0:T(8,128)(2,1)}), bf16[32,64,912]{2,1,0:T(8,128)(2,1)}, u32[]{:S(2)}, u32[]{:S(2)}) async-start(bf16[32,64,912]{2,1,0:T(8,128)(2,1)} %broadcast_in_dim.22), calls=%async_computation | async-start | bytes 8388608 | tf_op jit(solution)/shard_map/all_to_all | solution.py:47
  20.4 247.0 %all-gather.3.cloned.1.call-start = ((), (), s32[]{:S(2)}) async-start(), calls=%async_computation.7 | async-start | bytes 3244032 | tf_op jit(solution)/shard_map/all_gather | solution.py:194
  84.7 18.2 %all-to-all-start.2 = ((f32[4,128,144]{1,2,0:T(8,128)}), f32[4,128,144]{1,2,0:T(8,128)S(1)}, u32[]{:S(2)}, u32[]{:S(2)}) async-start(f32[4,128,144]{1,2,0:T(8,128)} %broadcast_in_dim.25), calls=%async_computation.2 | async-start | bytes 589824 | tf_op jit(solution)/shard_map/all_to_all | solution.py:47
  107.0 12.0 %copy-start.11 = (bf16[512]{0:T(512)(128)(2,1)S(1)}, bf16[512]{0:T(512)(128)(2,1)}, u32[]{:S(2)}) copy-start(bf16[512]{0:T(512)(128)(2,1)} %param.13) | copy-start | bytes 3076
  107.0 169.4 %all-to-all-start.1 = ((bf16[32,128,768]{1,2,0:T(8,128)(2,1)}), bf16[32,128,768]{1,2,0:T(8,128)(2,1)}, u32[]{:S(2)}, u32[]{:S(2)}) async-start(bf16[32,128,768]{1,2,0:T(8,128)(2,1)} %broadcast_in_dim.23), calls=%async_computation.1 | async-start | bytes 12582912 | tf_op jit(solution)/shard_map/all_to_all | solution.py:47
  119.0 8.7 %copy-start.8 = (s32[8]{0:T(128)S(1)}, s32[8]{0:T(128)}, u32[]{:S(2)}) copy-start(s32[8]{0:T(128)} %lens_ref.1) | copy-start | bytes 100
  274.7 0.8 copy-start.4
  280.1 2.7 copy-start.3
  305.3 3.7 slice-start
  413.2 7.7 %copy-start.5 = (bf16[512,4,128]{2,1,0:T(4,128)(2,1)S(1)}, bf16[512,4,128]{2,1,0:T(4,128)(2,1)}, u32[]{:S(2)}) copy-start(bf16[512,4,128]{2,1,0:T(4,128)(2,1)} %copy-done.4) | copy-start | bytes 1572868
  417.0 16.3 %all-to-all-start.3 = ((bf16[2,4,32,128]{3,1,0,2:T(4,128)(2,1)}), bf16[2,4,32,128]{3,1,0,2:T(4,128)(2,1)S(1)}, u32[]{:S(2)}, u32[]{:S(2)}) async-start(bf16[2,4,32,128]{3,1,0,2:T(4,128)(2,1)} %pad_maximum_fusion.3), calls=%async_computation.3 | async-start | bytes 131072 | tf_op jit(solution)/shard_map/all_to_all | solution.py:280
  420.9 3.5 copy-start.2
  433.3 42.7 %all-to-all-start.4 = ((bf16[4,32,128,128]{3,2,0,1:T(8,128)(2,1)}), bf16[4,32,128,128]{3,2,0,1:T(8,128)(2,1)}, u32[]{:S(2)}, u32[]{:S(2)}) async-start(bf16[4,32,128,128]{3,2,0,1:T(8,128)(2,1)} %copy.106), calls=%async_computation.4 | async-start | bytes 8388608 | tf_op jit(solution)/shard_map/all_to_all | solution.py:283
  480.8 53.6 %copy-start.1 = (bf16[64,576]{1,0:T(8,128)(2,1)S(1)}, bf16[64,576]{1,0:T(8,128)(2,1)}, u32[]{:S(2)}) copy-start(bf16[64,576]{1,0:T(8,128)(2,1)} %param.12) | copy-start | bytes 221188
Sparse Core Ops, SparseCore 0:
  22.9 244.4 all-gather.2

commit v6 on v3

--- a/solution.py
+++ b/solution.py
@@ -189,7 +189,7 @@
     got_weights = gather_axis(packed, "wide")
     proj_full = got_weights.reshape(-1, q_cols + kva_part)
     kvb_full = gather_axis(kvb_weight, "wide").reshape(-1, kvb_weight.shape[1])
-    o_got = gather_axis(o_weight, "wide")
+    o_got = lax.all_gather(o_weight, "wide", axis=0, tiled=False)
 
     normed = scaled_norm(hidden.astype(jnp.float32), attn_gain).astype(jnp.bfloat16)
     projected = jnp.dot(normed, proj_full, preferred_element_type=jnp.float32)

time: 482 us -> 478 us (level)
  blocking collectives: 149 us -> 90.3 us
  waiting for transfers between devices: 95.3 us -> 131 us
  between operations: 0.4 us -> 13.8 us
    all_to_all x1 -> x0, blocking collectives: 57.2 us -> none  [per_device(): lax.all_to_all(value_out.astype(jnp.bfloat16).reshape(heads_here, wide_co...]
    all_to_all x0 -> x1, waiting for transfers between devices: none -> 50.3 us  [per_device(): lax.all_to_all(value_out.astype(jnp.bfloat16).reshape(heads_here, wide_co...]
    all_to_all x4 -> x3, waiting for transfers between devices: 95.3 us -> 79.7 us  [gather_axis(): lax.all_to_all(spread, axis_name, split_axis=0, concat_axis=0, tiled=True)]
    all_to_all x0 -> x1, starting transfers between devices: none -> 8.15 us  [per_device(): lax.all_to_all(value_out.astype(jnp.bfloat16).reshape(heads_here, wide_co...]
    all_to_all x4 -> x3, starting transfers between devices: 20.8 us -> 16.6 us  [gather_axis(): lax.all_to_all(spread, axis_name, split_axis=0, concat_axis=0, tiled=True)]
    unnamed x28 -> x27, local copies, waits for them, and re-layouts: 23.2 us -> 25.6 us
  transfers between devices with their start and end apart: 5 -> 6, of which waited for: 4 -> 4; matrix products, arithmetic and copies ran while one was open for 11% -> 24% of each run, Pallas kernels for 0% -> 16%
where the time goes in v6:
time: 478 us; the launch traced here: 472 us
  waiting for transfers between devices  131 us (27%)
  blocking collectives  90.3 us (19%)
  Pallas kernels  77.8 us (16%)
  other arithmetic  53.2 us (11%)
  local copies, waits for them, and re-layouts  51 us (11%)
  starting transfers between devices  28.7 us (6%)
  matrix products  27 us (6%)
  between operations  13.8 us (3%)
    all_to_all x3, waiting for transfers between devices, gather_axis(): lax.all_to_all(spread, axis_name, split_axis=0, concat_axis=0, tiled=True)  79.7 us
    pallas_call x1, Pallas kernels, cache_attention(): pl.pallas_call(cache_kernel, grid_spec=grid_spec, out_shape=[jax.ShapeDty...  77.8 us
    all_to_all x2, blocking collectives, gather_axis(): lax.all_to_all(spread, axis_name, split_axis=0, concat_axis=0, tiled=True)  72.5 us
    all_to_all x1, waiting for transfers between devices, per_device(): lax.all_to_all(value_out.astype(jnp.bfloat16).reshape(heads_here, wide_co...  50.3 us
    unnamed x27, local copies, waits for them, and re-layouts  25.6 us
    all_to_all x1, blocking collectives, per_device(): got_pieces = lax.all_to_all(pieces, 'narrow', 0, 0, tiled=True)  17.8 us
    all_to_all x3, starting transfers between devices, gather_axis(): lax.all_to_all(spread, axis_name, split_axis=0, concat_axis=0, tiled=True)  16.6 us
    pallas_call x2, other arithmetic, cache_attention(): pl.pallas_call(cache_kernel, grid_spec=grid_spec, out_shape=[jax.ShapeDty...  11.3 us
  transfers between devices with their start and end apart: 6, of which 4 were waited for; matrix products, arithmetic and copies ran while one was open for 24% of the time, Pallas kernels for 16%

profile of v6, /device:TPU:1, one launch (start us, length us, event | category | flops | bytes accessed | tf_op | source)
XLA Modules:
  0.0 472.5 jit_solution(13049738093019029878)
XLA Ops:
  6.5 0.9 copy-done
  7.5 0.9 pad_maximum_fusion.1
  9.0 59.8 %all_to_all.40 = bf16[32,64,912]{2,1,0:T(8,128)(2,1)} all-to-all(bf16[32,64,912]{2,1,0:T(8,128)(2,1)S(1)} %broadcast_in_dim.24), channel_id=1, replica_groups=mesh['wide'=32,'narrow'=4] {'wide'}, dimensions={0} | all-to-all | bytes 7471104 | tf_op jit(solution)/shard_map/all_to_all | solution.py:47
  68.8 1.1 broadcast_in_dim.26
  69.9 3.9 all-to-all-start.2
  74.1 3.9 fusion.28
  78.0 11.8 %all-to-all-done.2 = bf16[32,16,1024]{2,1,0:T(8,128)(2,1)S(1)} async-done(((bf16[32,16,1024]{2,1,0:T(8,128)(2,1)}), bf16[32,16,1024]{2,1,0:T(8,128)(2,1)S(1)}, u32[]{:S(2)}, u32[]{:S(2)}) %all-to-all-start.2) | async-done | bytes 1048608 | tf_op jit(solution)/shard_map/all_to_all | solution.py:47
  89.8 0.8 broadcast_in_dim.28
  90.6 7.7 %all-to-all-start.3 = ((f32[4,128,144]{1,2,0:T(8,128)}), f32[4,128,144]{1,2,0:T(8,128)S(1)}, u32[]{:S(2)}, u32[]{:S(2)}) async-start(f32[4,128,144]{1,2,0:T(8,128)} %broadcast_in_dim.28), calls=%async_computation.3 | async-start | bytes 589824 | tf_op jit(solution)/shard_map/all_to_all | solution.py:47
  98.3 6.8 %all-to-all-done.3 = f32[4,128,144]{1,2,0:T(8,128)S(1)} async-done(((f32[4,128,144]{1,2,0:T(8,128)}), f32[4,128,144]{1,2,0:T(8,128)S(1)}, u32[]{:S(2)}, u32[]{:S(2)}) %all-to-all-start.3) | async-done | bytes 294944 | tf_op jit(solution)/shard_map/all_to_all | solution.py:47
  105.1 4.1 broadcast_in_dim.25
  109.2 5.0 %all-to-all-start.1 = ((bf16[32,128,768]{1,2,0:T(8,128)(2,1)}), bf16[32,128,768]{1,2,0:T(8,128)(2,1)}, u32[]{:S(2)}, u32[]{:S(2)}) async-start(bf16[32,128,768]{1,2,0:T(8,128)(2,1)} %broadcast_in_dim.25), calls=%async_computation.1 | async-start | bytes 12582912 | tf_op jit(solution)/shard_map/all_to_all | solution.py:47
  115.1 8.6 %copy.90.kv_ref = bf16[8,640,576]{2,1,0:T(8,128)(2,1)} copy(bf16[8,640,576]{1,2,0:T(8,128)(2,1)} %param.16) | data formatting | bytes 11796480 | tf_op args[7]
  124.4 5.0 %fusion.71 = f32[128]{0:T(128)S(1)} fusion(s32[]{:T(128)} %bitcast.8, s32[]{:T(128)} %bitcast.9, s32[]{:T(128)} %bitcast.10, s32[]{:T(128)} %bitcast.11, s32[]{:T(128)} %bitcast.12, s32[]{:T(128)} %bitcast.14, s32[]{:T(128)} %bitcast.13, s32[]{:T(128)} %bitcast.7, s32[]{:T(128)S(6)} %mul.197), kind=kLoop, calls=%fused_computation.135 | loop fusion | flops 6016 | bytes 548 | tf_op jit(solution)/shard_map/convert_element_type | solution.py:22
  129.4 4.4 compare_select_fusion.1
  134.6 9.2 %multiply_cosine_fusion = (f32[4096,32]{1,0:T(8,128)S(1)}, f32[4096,32]{1,0:T(8,128)}) fusion(f32[32]{0:T(128)S(1)} %multiply_power_fusion, f32[4096]{0:T(1024)S(1)} %fusion.53), kind=kLoop, calls=%fused_computation.10 | loop fusion | flops 131072 | bytes 1065088 | tf_op jit(solution)/shard_map/cos | solution.py:25
  143.7 2.6 reshape_reshape.3
  146.4 1.6 fusion.76
  148.0 0.9 copy.131
  149.1 61.0 %all-to-all-done.1 = bf16[32,128,768]{1,2,0:T(8,128)(2,1)} async-done(((bf16[32,128,768]{1,2,0:T(8,128)(2,1)}), bf16[32,128,768]{1,2,0:T(8,128)(2,1)}, u32[]{:S(2)}, u32[]{:S(2)}) %all-to-all-start.1) | async-done | bytes 6291488 | tf_op jit(solution)/shard_map/all_to_all | solution.py:47
  210.1 3.7 copy_bitcast_fusion
  214.0 2.3 slice.85
  216.3 2.5 fusion.75
  218.7 6.2 %copy.116 = f32[4096,4,32]{2,0,1:T(8,128)} copy(f32[4096,4,32]{0,2,1:T(8,128)} %get-tuple-element.18) | data formatting | bytes 4194304
  224.9 6.3 %copy.117 = f32[4096,4,32]{2,0,1:T(8,128)} copy(f32[4096,4,32]{0,2,1:T(8,128)} %get-tuple-element.19) | data formatting | bytes 4194304
  231.2 10.6 %convolution_convert_fusion.lat_ref = bf16[4,4096,512]{2,1,0:T(8,128)(2,1)} fusion(bf16[4096,4,128]{0,2,1:T(8,128)(2,1)} %bitcast.147, bf16[512,4,128]{2,1,0:T(4,128)(2,1)S(1)} %get-tuple-element.21), kind=kOutput, calls=%fused_computation | convolution fusion | flops 2155872256 | bytes 21495808 | tf_op jit(solution)/shard_map/thc,lhc->htl/dot_general | solution.py:231
  241.8 5.2 %subtract_convert_fusion = (bf16[4096,4,32]{2,0,1:T(8,128)(2,1)S(1)}, bf16[4096,4,32]{2,0,1:T(8,128)(2,1)S(1)}) fusion(f32[4096,4,32]{2,0,1:T(8,128)} %copy.117, f32[4096,4,32]{2,0,1:T(8,128)S(1)} %bitcast.143, f32[4096,32]{1,0:T(8,128)} %get-tuple-element.25, f32[4096,32]{1,0:T(8,128)S(1)} %get-tuple-element.24), kind=kLoop, calls=%fused_computation.3 | loop fusion | flops 4194304 | bytes 7340032 | tf_op jit(solution)/shard_map/convert.8
  247.0 3.7 maximum_bitcast_fusion.rope_ref
  251.2 2.6 select_reduce_fusion
  254.0 2.8 fusion.26
  257.1 77.8 %shard_map.91 = (f32[4,4096,1]{2,1,0:T(8,128)}, f32[4,4096,1]{2,1,0:T(8,128)}, f32[4,4096,128]{2,1,0:T(8,128)}) custom-call(s32[8]{0:T(128)} %lens_ref.1, s32[1]{0:T(128)} %bitcast.base_ref, bf16[4,4096,512]{2,1,0:T(8,128)(2,1)} %convolution_convert_fusion.lat_ref, bf16[4,4096,64]{2,1,0:T(8,128)(2,1)} %maximum_bitcast_fusion.rope_ref, ...), custom_call_target="tpu_custom_call" | custom-call | tf_op jit(solution)/shard_map/pallas_call | solution.py:152
  334.9 5.6 %reduce.3 = bf16[4,4096]{1,0:T(4,128)(2,1)S(1)} reduce(f32[4,4096,1]{2,1,0:T(8,128)} %get-tuple-element.8, f32[]{:T(128)} %constant.133), dimensions={2}, to_apply=%get-tuple-element.8.reduce_sub_computation | reduce | bytes 98308 | tf_op jit(solution)/shard_map/pallas_call | solution.py:152
  340.5 5.6 %reduce.5 = bf16[4,4096]{1,0:T(4,128)(2,1)S(1)} reduce(f32[4,4096,1]{2,1,0:T(8,128)} %get-tuple-element.9, f32[]{:T(128)} %constant.133), dimensions={2}, to_apply=%get-tuple-element.9.reduce_sub_computation | reduce | bytes 98308 | tf_op jit(solution)/shard_map/pallas_call | solution.py:152
  346.2 2.7 fusion.17
  349.6 3.9 all-to-all-start.4
  353.5 3.0 fusion.21
  356.9 2.8 fusion.12
  359.7 3.9 convert_element_type.90
  363.6 2.3 copy.100
  365.9 8.2 %all-to-all-start.5 = ((bf16[4,32,128,128]{3,2,0,1:T(8,128)(2,1)}), bf16[4,32,128,128]{3,2,0,1:T(8,128)(2,1)}, u32[]{:S(2)}, u32[]{:S(2)}) async-start(bf16[4,32,128,128]{3,2,0,1:T(8,128)(2,1)} %copy.100), calls=%async_computation.5 | async-start | bytes 8388608 | tf_op jit(solution)/shard_map/all_to_all | solution.py:279
  374.1 2.4 copy.122
  376.5 1.2 copy.103
  377.8 50.3 %all-to-all-done.5 = bf16[4,32,128,128]{3,2,0,1:T(8,128)(2,1)} async-done(((bf16[4,32,128,128]{3,2,0,1:T(8,128)(2,1)}), bf16[4,32,128,128]{3,2,0,1:T(8,128)(2,1)}, u32[]{:S(2)}, u32[]{:S(2)}) %all-to-all-start.5) | async-done | bytes 4194336 | tf_op jit(solution)/shard_map/all_to_all | solution.py:279
  428.1 4.4 multiply_reduce_fusion
  432.8 0.8 convolution_convert_fusion.1
  433.7 17.8 %all_to_all.41 = bf16[4,128,512]{2,1,0:T(8,128)(2,1)S(1)} all-to-all(bf16[4,128,512]{2,1,0:T(8,128)(2,1)S(1)} %bitcast.156), channel_id=1, replica_groups=mesh['wide'=32,'narrow'=4] {'narrow'}, dimensions={0} | all-to-all | bytes 1048576 | tf_op jit(solution)/shard_map/all_to_all | solution.py:303
  451.6 12.7 %all_to_all.42 = bf16[4,128,512]{2,1,0:T(8,128)(2,1)S(1)} all-to-all(bf16[4,128,512]{2,1,0:T(8,128)(2,1)S(1)} %broadcast_in_dim.31), channel_id=1, replica_groups=mesh['wide'=32,'narrow'=4] {'narrow'}, dimensions={0} | all-to-all | bytes 1048576 | tf_op jit(solution)/shard_map/all_to_all | solution.py:47
  464.6 1.0 copy.106
  (62 shorter events, 6.6 us)
Async XLA Ops:
  6.5 0.9 copy-start
  8.9 59.8 %copy-start.6 = (bf16[16,1024]{1,0:T(8,128)(2,1)S(1)}, bf16[16,1024]{1,0:T(8,128)(2,1)}, u32[]{:S(2)}) copy-start(bf16[16,1024]{1,0:T(8,128)(2,1)} %param.14) | copy-start | bytes 98308
  9.0 64.9 %copy-start.7 = (bf16[2048]{0:T(1024)(128)(2,1)S(1)}, bf16[2048]{0:T(1024)(128)(2,1)}, u32[]{:S(2)}) copy-start(bf16[2048]{0:T(1024)(128)(2,1)} %param.10) | copy-start | bytes 12292
  9.0 64.9 %copy-start.4 = (bf16[128,2048]{1,0:T(8,128)(2,1)S(1)}, bf16[128,2048]{1,0:T(8,128)(2,1)}, u32[]{:S(2)}) copy-start(bf16[128,2048]{1,0:T(8,128)(2,1)} %param.9) | copy-start | bytes 1572868
  69.9 19.9 %all-to-all-start.2 = ((bf16[32,16,1024]{2,1,0:T(8,128)(2,1)}), bf16[32,16,1024]{2,1,0:T(8,128)(2,1)S(1)}, u32[]{:S(2)}, u32[]{:S(2)}) async-start(bf16[32,16,1024]{2,1,0:T(8,128)(2,1)} %broadcast_in_dim.26), calls=%async_computation.2 | async-start | bytes 2097152 | tf_op jit(solution)/shard_map/all_to_all | solution.py:47
  89.8 19.4 %copy-start.3 = (bf16[32,16,1024]{2,1,0:T(8,128)(2,1)}, bf16[32,16,1024]{2,1,0:T(8,128)(2,1)S(1)}, u32[]{:S(2)}) copy-start(bf16[32,16,1024]{2,1,0:T(8,128)(2,1)S(1)} %all-to-all-done.2) | copy-start | bytes 3145732
  90.6 14.6 %all-to-all-start.3 = ((f32[4,128,144]{1,2,0:T(8,128)}), f32[4,128,144]{1,2,0:T(8,128)S(1)}, u32[]{:S(2)}, u32[]{:S(2)}) async-start(f32[4,128,144]{1,2,0:T(8,128)} %broadcast_in_dim.28), calls=%async_computation.3 | async-start | bytes 589824 | tf_op jit(solution)/shard_map/all_to_all | solution.py:47
  109.2 5.8 %copy-start.8 = (bf16[512]{0:T(512)(128)(2,1)S(1)}, bf16[512]{0:T(512)(128)(2,1)}, u32[]{:S(2)}) copy-start(bf16[512]{0:T(512)(128)(2,1)} %param.13) | copy-start | bytes 3076
  109.2 100.9 %all-to-all-start.1 = ((bf16[32,128,768]{1,2,0:T(8,128)(2,1)}), bf16[32,128,768]{1,2,0:T(8,128)(2,1)}, u32[]{:S(2)}, u32[]{:S(2)}) async-start(bf16[32,128,768]{1,2,0:T(8,128)(2,1)} %broadcast_in_dim.25), calls=%async_computation.1 | async-start | bytes 12582912 | tf_op jit(solution)/shard_map/all_to_all | solution.py:47
  114.3 259.8 %all-gather.3.cloned.1.call-start = ((), (), s32[]{:S(2)}) async-start(), calls=%async_computation.8 | async-start | bytes 2162688 | tf_op jit(solution)/shard_map/all_gather | solution.py:192
  115.0 8.7 %copy-start.5 = (s32[8]{0:T(128)S(1)}, s32[8]{0:T(128)}, u32[]{:S(2)}) copy-start(s32[8]{0:T(128)} %lens_ref.1) | copy-start | bytes 100
  231.2 10.6 %slice-start = ((s8[8388608]{0:T(1024)(128)(4,1)}), s8[4194304]{0:T(1024)(128)(4,1)S(1)}, s32[]{:S(2)}) async-start(s8[8388608]{0:T(1024)(128)(4,1)} %bitcast.142), calls=%async_computation.9 | async-start | bytes 8388608
  231.2 10.6 %slice-start.1 = ((s8[8388608]{0:T(1024)(128)(4,1)}), s8[4194304]{0:T(1024)(128)(4,1)S(1)}, s32[]{:S(2)}) async-start(s8[8388608]{0:T(1024)(128)(4,1)} %bitcast.142), calls=%async_computation.10 | async-start | bytes 8388608
  349.6 16.3 %all-to-all-start.4 = ((bf16[2,4,32,128]{3,1,0,2:T(4,128)(2,1)}), bf16[2,4,32,128]{3,1,0,2:T(4,128)(2,1)S(1)}, u32[]{:S(2)}, u32[]{:S(2)}) async-start(bf16[2,4,32,128]{3,1,0,2:T(4,128)(2,1)} %pad_maximum_fusion.2), calls=%async_computation.4 | async-start | bytes 131072 | tf_op jit(solution)/shard_map/all_to_all | solution.py:276
  353.5 3.5 copy-start.2
  365.9 62.2 %all-to-all-start.5 = ((bf16[4,32,128,128]{3,2,0,1:T(8,128)(2,1)}), bf16[4,32,128,128]{3,2,0,1:T(8,128)(2,1)}, u32[]{:S(2)}, u32[]{:S(2)}) async-start(bf16[4,32,128,128]{3,2,0,1:T(8,128)(2,1)} %copy.100), calls=%async_computation.5 | async-start | bytes 8388608 | tf_op jit(solution)/shard_map/all_to_all | solution.py:279
  432.8 32.8 %copy-start.1 = (bf16[64,576]{1,0:T(8,128)(2,1)S(1)}, bf16[64,576]{1,0:T(8,128)(2,1)}, u32[]{:S(2)}) copy-start(bf16[64,576]{1,0:T(8,128)(2,1)} %param.12) | copy-start | bytes 221188
Sparse Core Ops, SparseCore 0:
  116.7 188.8 all-gather.2

commit v7 on v6

--- a/solution.py
+++ b/solution.py
@@ -93,7 +93,7 @@
     )
 
 
-def cache_kernel(lens_ref, base_ref, lat_ref, rope_ref, kv_ref, vm_ref, peak_ref, total_ref, value_ref):
+def cache_kernel(lens_ref, base_ref, lat_ref, rope_ref, kv_ref, vm_ref, stats_ref, value_ref):
     length_now = lens_ref[pl.program_id(0)]
     base = base_ref[0]
     live_block = base < length_now
@@ -112,8 +112,9 @@
         live = slots < length_now
         peak = jnp.max(jnp.where(live, scores, -1e30), axis=-1, keepdims=True)
         weights = jnp.where(live, jnp.exp(scores - peak), 0.0)
-        peak_ref[0] = peak
-        total_ref[0] = jnp.sum(weights, axis=-1, keepdims=True)
+        total = jnp.sum(weights, axis=-1, keepdims=True)
+        lane = lax.broadcasted_iota(jnp.int32, stats_ref.shape[1:], 1)
+        stats_ref[0] = jnp.where(lane == 0, peak, total)
         mixed = jnp.dot(weights.astype(jnp.bfloat16), key_lat, preferred_element_type=jnp.float32)
         value_map = vm_ref[0]
         upper_part = mixed.astype(jnp.bfloat16)
@@ -124,8 +125,8 @@
 
     @pl.when(jnp.logical_not(live_block))
     def _():
-        peak_ref[...] = jnp.full(peak_ref.shape, -1e30, jnp.float32)
-        total_ref[...] = jnp.zeros(total_ref.shape, jnp.float32)
+        lane = lax.broadcasted_iota(jnp.int32, stats_ref.shape, 2)
+        stats_ref[...] = jnp.where(lane == 0, -1e30, 0.0).astype(jnp.float32)
         value_ref[...] = jnp.zeros(value_ref.shape, jnp.float32)
 
 
@@ -144,8 +145,7 @@
             pl.BlockSpec((1, LAT, vdim), lambda r, h, lens, b: (h, 0, 0)),
         ],
         out_specs=[
-            pl.BlockSpec((1, span, 1), lambda r, h, lens, b: (h, r, 0)),
-            pl.BlockSpec((1, span, 1), lambda r, h, lens, b: (h, r, 0)),
+            pl.BlockSpec((1, span, 128), lambda r, h, lens, b: (h, r, 0)),
             pl.BlockSpec((1, span, vdim), lambda r, h, lens, b: (h, r, 0)),
         ],
     )
@@ -153,8 +153,7 @@
         cache_kernel,
         grid_spec=grid_spec,
         out_shape=[
-            jax.ShapeDtypeStruct((heads_here, total_tokens, 1), jnp.float32),
-            jax.ShapeDtypeStruct((heads_here, total_tokens, 1), jnp.float32),
+            jax.ShapeDtypeStruct((heads_here, total_tokens, 128), jnp.float32),
             jax.ShapeDtypeStruct((heads_here, total_tokens, vdim), jnp.float32),
         ],
         compiler_params=pltpu.CompilerParams(dimension_semantics=("arbitrary", "arbitrary")),
@@ -210,34 +209,34 @@
     )
 
     query_heads = query_rows.reshape(tok_rows, heads_here, NOPE + ROPE)
+    own_rope_q = rotate(query_heads[..., NOPE:].astype(jnp.float32), positions[:, None]).astype(
+        jnp.bfloat16
+    )
     outgoing = jnp.concatenate(
         [
             query_heads[..., :NOPE].reshape(tok_rows, heads_here * NOPE),
-            query_heads[..., NOPE:].reshape(tok_rows, heads_here * ROPE),
+            own_rope_q.reshape(tok_rows, heads_here * ROPE),
         ],
         axis=1,
     )
     raw_all = gather_axis(outgoing, "wide")
     total_tokens = raw_all.shape[0] * tok_rows
     raw_all = raw_all.reshape(total_tokens, heads_here * (NOPE + ROPE))
-    all_ids = jnp.arange(total_tokens, dtype=jnp.int32)
-    all_positions = lengths[all_ids // SPAN] + all_ids % SPAN
     kvb_heads = kvb_full.reshape(LAT, heads_here, NOPE + VDIM)
     key_maps = kvb_heads[..., :NOPE]
     value_maps = kvb_heads[..., NOPE:]
     nope_all = raw_all[:, : heads_here * NOPE].reshape(total_tokens, heads_here, NOPE)
     rope_all = raw_all[:, heads_here * NOPE :].reshape(total_tokens, heads_here, ROPE)
-    q_rope = rotate(rope_all.astype(jnp.float32), all_positions[:, None]).astype(jnp.bfloat16)
     lat_hm = jnp.einsum(
         "thc,lhc->htl", nope_all, key_maps, preferred_element_type=jnp.float32
     ).astype(jnp.bfloat16)
-    rope_hm = jnp.transpose(q_rope, (1, 0, 2))
+    rope_hm = jnp.transpose(rope_all, (1, 0, 2))
     value_hm = jnp.transpose(value_maps, (1, 0, 2))
 
     base = (wide_place * cache_rows).reshape(1).astype(jnp.int32)
-    peak_hm, total_hm, value_out = cache_attention(lengths, base, lat_hm, rope_hm, cache, value_hm)
-    peak_hm = peak_hm[..., 0]
-    total_hm = total_hm[..., 0]
+    stats_hm, value_out = cache_attention(lengths, base, lat_hm, rope_hm, cache, value_hm)
+    peak_hm = stats_hm[..., 0]
+    total_hm = stats_hm[..., 1]
 
     own_request = first_token // SPAN
     start_row = own_request * SPAN

time: 478 us -> 463 us (0.969)
  waiting for transfers between devices: 131 us -> 200 us
  blocking collectives: 90.3 us -> 31.4 us
  other arithmetic: 53.2 us -> 18.6 us
  starting transfers between devices: 28.7 us -> 37.7 us
    all_to_all x3 -> x4, waiting for transfers between devices: 79.7 us -> 151 us  [gather_axis(): lax.all_to_all(spread, axis_name, split_axis=0, concat_axis=0, tiled=True)]
    all_to_all x2 -> x1, blocking collectives: 72.5 us -> 12.7 us  [gather_axis(): lax.all_to_all(spread, axis_name, split_axis=0, concat_axis=0, tiled=True)]
    slice x2 -> x1, local copies, waits for them, and re-layouts: 2.46 us -> 14.6 us  [per_device(): peak_hm = stats_hm[..., 0]]
    pallas_call x2 -> x0, other arithmetic: 11.3 us -> none  [cache_attention(): pl.pallas_call(cache_kernel, grid_spec=grid_spec, out_shape=[jax.ShapeDty...]
    unnamed x27 -> x19, local copies, waits for them, and re-layouts: 25.6 us -> 14.5 us
    cos x1 -> x0, other arithmetic: 9.19 us -> none  [rotate(): cosine = jnp.cos(angles)]
    all_to_all x3 -> x4, starting transfers between devices: 16.6 us -> 25.7 us  [gather_axis(): lax.all_to_all(spread, axis_name, split_axis=0, concat_axis=0, tiled=True)]
    another operation x2, other arithmetic: 5.31 us -> 0.17 us
  transfers between devices with their start and end apart: 6 -> 7, of which waited for: 4 -> 5; matrix products, arithmetic and copies ran while one was open for 24% -> 16% of each run, Pallas kernels for 16% -> 17%
where the time goes in v7:
time: 463 us; the launch traced here: 457 us
  waiting for transfers between devices  200 us (43%)
  Pallas kernels  77.2 us (17%)
  local copies, waits for them, and re-layouts  54.1 us (12%)
  starting transfers between devices  37.7 us (8%)
  blocking collectives  31.4 us (7%)
  matrix products  25 us (5%)
  other arithmetic  18.6 us (4%)
  between operations  13.8 us (3%)
    all_to_all x4, waiting for transfers between devices, gather_axis(): lax.all_to_all(spread, axis_name, split_axis=0, concat_axis=0, tiled=True)  151 us
    pallas_call x1, Pallas kernels, cache_attention(): pl.pallas_call(cache_kernel, grid_spec=grid_spec, out_shape=[jax.ShapeDty...  77.2 us
    all_to_all x1, waiting for transfers between devices, per_device(): lax.all_to_all(value_out.astype(jnp.bfloat16).reshape(heads_here, wide_co...  48.5 us
    all_to_all x4, starting transfers between devices, gather_axis(): lax.all_to_all(spread, axis_name, split_axis=0, concat_axis=0, tiled=True)  25.7 us
    all_to_all x1, blocking collectives, per_device(): got_pieces = lax.all_to_all(pieces, 'narrow', 0, 0, tiled=True)  18.7 us
    slice x1, local copies, waits for them, and re-layouts, per_device(): peak_hm = stats_hm[..., 0]  14.6 us
    unnamed x19, local copies, waits for them, and re-layouts  14.5 us
    all_to_all x1, blocking collectives, gather_axis(): lax.all_to_all(spread, axis_name, split_axis=0, concat_axis=0, tiled=True)  12.7 us
  transfers between devices with their start and end apart: 7, of which 5 were waited for; matrix products, arithmetic and copies ran while one was open for 16% of the time, Pallas kernels for 17%

profile of v7, /device:TPU:1, one launch (start us, length us, event | category | flops | bytes accessed | tf_op | source)
XLA Modules:
  0.0 457.4 jit_solution(8029253874725225100)
XLA Ops:
  6.5 0.9 copy-done
  7.5 0.9 pad_maximum_fusion.1
  8.4 2.5 broadcast_in_dim.24
  10.9 9.5 %all-to-all-start = ((bf16[32,64,912]{2,1,0:T(8,128)(2,1)}), bf16[32,64,912]{2,1,0:T(8,128)(2,1)}, u32[]{:S(2)}, u32[]{:S(2)}) async-start(bf16[32,64,912]{2,1,0:T(8,128)(2,1)} %broadcast_in_dim.24), calls=%async_computation | async-start | bytes 8388608 | tf_op jit(solution)/shard_map/all_to_all | solution.py:47
  20.7 58.9 %all-to-all-done = bf16[32,64,912]{2,1,0:T(8,128)(2,1)} async-done(((bf16[32,64,912]{2,1,0:T(8,128)(2,1)}), bf16[32,64,912]{2,1,0:T(8,128)(2,1)}, u32[]{:S(2)}, u32[]{:S(2)}) %all-to-all-start) | async-done | bytes 3735584 | tf_op jit(solution)/shard_map/all_to_all | solution.py:47
  79.6 3.9 fusion.27
  83.5 0.7 broadcast_in_dim.28
  84.3 6.6 %all-to-all-start.3 = ((f32[4,128,144]{1,2,0:T(8,128)}), f32[4,128,144]{1,2,0:T(8,128)S(1)}, u32[]{:S(2)}, u32[]{:S(2)}) async-start(f32[4,128,144]{1,2,0:T(8,128)} %broadcast_in_dim.28), calls=%async_computation.3 | async-start | bytes 589824 | tf_op jit(solution)/shard_map/all_to_all | solution.py:47
  90.9 0.7 fusion.62
  91.6 6.2 %all-to-all-done.3 = f32[4,128,144]{1,2,0:T(8,128)S(1)} async-done(((f32[4,128,144]{1,2,0:T(8,128)}), f32[4,128,144]{1,2,0:T(8,128)S(1)}, u32[]{:S(2)}, u32[]{:S(2)}) %all-to-all-start.3) | async-done | bytes 294944 | tf_op jit(solution)/shard_map/all_to_all | solution.py:47
  97.8 1.1 broadcast_in_dim.26
  98.9 4.7 %all-to-all-start.2 = ((bf16[32,16,1024]{2,1,0:T(8,128)(2,1)}), bf16[32,16,1024]{2,1,0:T(8,128)(2,1)S(1)}, u32[]{:S(2)}, u32[]{:S(2)}) async-start(bf16[32,16,1024]{2,1,0:T(8,128)(2,1)} %broadcast_in_dim.26), calls=%async_computation.2 | async-start | bytes 2097152 | tf_op jit(solution)/shard_map/all_to_all | solution.py:47
  103.6 5.0 %fusion.57 = f32[128]{0:T(128)S(1)} fusion(s32[]{:T(128)} %bitcast.6, s32[]{:T(128)} %bitcast.7, s32[]{:T(128)} %bitcast.8, s32[]{:T(128)} %bitcast.9, s32[]{:T(128)} %bitcast.10, s32[]{:T(128)} %bitcast.12, s32[]{:T(128)} %bitcast.11, s32[]{:T(128)} %bitcast.5, s32[]{:T(128)S(6)} %mul.182), kind=kLoop, calls=%fused_computation.110 | loop fusion | flops 6016 | bytes 548 | tf_op jit(solution)/shard_map/convert_element_type | solution.py:22
  108.9 11.3 %all-to-all-done.2 = bf16[32,16,1024]{2,1,0:T(8,128)(2,1)S(1)} async-done(((bf16[32,16,1024]{2,1,0:T(8,128)(2,1)}), bf16[32,16,1024]{2,1,0:T(8,128)(2,1)S(1)}, u32[]{:S(2)}, u32[]{:S(2)}) %all-to-all-start.2) | async-done | bytes 1048608 | tf_op jit(solution)/shard_map/all_to_all | solution.py:47
  120.2 4.1 broadcast_in_dim.25
  124.3 4.9 %all-to-all-start.1 = ((bf16[32,128,768]{1,2,0:T(8,128)(2,1)}), bf16[32,128,768]{1,2,0:T(8,128)(2,1)}, u32[]{:S(2)}, u32[]{:S(2)}) async-start(bf16[32,128,768]{1,2,0:T(8,128)(2,1)} %broadcast_in_dim.25), calls=%async_computation.1 | async-start | bytes 12582912 | tf_op jit(solution)/shard_map/all_to_all | solution.py:47
  129.4 0.5 all-gather.3.cloned.1.call-update
  130.0 8.6 %copy.81.kv_ref = bf16[8,640,576]{2,1,0:T(8,128)(2,1)} copy(bf16[8,640,576]{1,2,0:T(8,128)(2,1)} %param.16) | data formatting | bytes 11796480 | tf_op args[7]
  138.7 0.8 reshape_reshape.3
  139.5 0.4 fusion.61
  139.9 0.9 copy.118
  140.8 74.1 %all-to-all-done.1 = bf16[32,128,768]{1,2,0:T(8,128)(2,1)} async-done(((bf16[32,128,768]{1,2,0:T(8,128)(2,1)}), bf16[32,128,768]{1,2,0:T(8,128)(2,1)}, u32[]{:S(2)}, u32[]{:S(2)}) %all-to-all-start.1) | async-done | bytes 6291488 | tf_op jit(solution)/shard_map/all_to_all | solution.py:47
  215.0 3.7 copy_bitcast_fusion
  218.7 2.3 slice.86
  221.1 3.1 copy.79
  224.3 10.5 %convolution_convert_fusion.lat_ref = bf16[4,4096,512]{2,1,0:T(8,128)(2,1)} fusion(bf16[4096,4,128]{0,2,1:T(8,128)(2,1)} %bitcast.141, bf16[512,4,128]{2,1,0:T(4,128)(2,1)S(1)} %get-tuple-element.19), kind=kOutput, calls=%fused_computation | convolution fusion | flops 2155872256 | bytes 21495808 | tf_op jit(solution)/shard_map/thc,lhc->htl/dot_general | solution.py:230
  235.1 2.6 select_reduce_fusion
  237.6 0.8 fusion.25
  238.7 1.8 copy-done.2
  240.5 0.7 fusion.21
  241.2 0.4 copy.86
  241.6 77.2 %shard_map.91 = (f32[4,4096,128]{2,1,0:T(8,128)}, f32[4,4096,128]{2,1,0:T(8,128)}) custom-call(s32[8]{0:T(128)} %lens_ref.1, s32[1]{0:T(128)} %bitcast.base_ref, bf16[4,4096,512]{2,1,0:T(8,128)(2,1)} %convolution_convert_fusion.lat_ref, bf16[4,4096,64]{2,1,0:T(8,128)(2,1)} %bitcast.140, bf16[8,640,576]{2,1,0:T(8,128)(2,1)} %copy.81.kv_ref, ...), custom_call_target="tpu_custom_call" | custom-call | tf_op jit(solution)/shard_map/pallas_call | solution.py:152
  318.8 14.6 %slice_reduce_fusion.1 = (bf16[4,4096]{1,0:T(4,128)(2,1)S(1)}, bf16[4,4096]{1,0:T(4,128)(2,1)S(1)}, f32[4,4096,1]{2,1,0:T(8,128)S(1)}, f32[4,4096,1]{2,1,0:T(8,128)}) fusion(f32[4,4096,128]{2,1,0:T(8,128)} %get-tuple-element.7), kind=kLoop, calls=%fused_computation.115 | loop fusion | bytes 327680 | tf_op jit(solution)/shard_map/slice | solution.py:238
  333.4 2.4 fusion.17
  335.9 0.7 pad_maximum_fusion.3
  336.5 3.9 all-to-all-start.4
  340.4 5.4 %fusion.12 = f32[4,4096,128]{2,1,0:T(8,128)} fusion(f32[4,4096,128]{2,1,0:T(8,128)} %get-tuple-element.8, s32[]{:T(128)S(6)} %select_n.73, f32[4,512,128]{2,1,0:T(8,128)S(1)} %fusion.21, f32[4,512,512]{2,1,0:T(8,128)} %copy-done.2, f32[4,512]{1,0:T(4,128)S(1)} %get-tuple-element.10, f32[4,512]{1,0:T(4,128)S(1)} %get-tuple-element.9, ...), kind=kOutput, calls=%fused_computation.15 | convolution fusion | flops 273678336 | bytes 7880708 | tf_op jit(solution)/shard_map/hqc,hcv->hqv/dot_general | solution.py:263
  345.8 3.9 convert_element_type.88
  349.7 2.3 copy.90
  352.0 7.9 %all-to-all-start.5 = ((bf16[4,32,128,128]{3,2,0,1:T(8,128)(2,1)}), bf16[4,32,128,128]{3,2,0,1:T(8,128)(2,1)}, u32[]{:S(2)}, u32[]{:S(2)}) async-start(bf16[4,32,128,128]{3,2,0,1:T(8,128)(2,1)} %copy.90), calls=%async_computation.5 | async-start | bytes 8388608 | tf_op jit(solution)/shard_map/all_to_all | solution.py:278
  359.9 2.4 copy.109
  362.3 1.2 copy.93
  363.6 48.5 %all-to-all-done.5 = bf16[4,32,128,128]{3,2,0,1:T(8,128)(2,1)} async-done(((bf16[4,32,128,128]{3,2,0,1:T(8,128)(2,1)}), bf16[4,32,128,128]{3,2,0,1:T(8,128)(2,1)}, u32[]{:S(2)}, u32[]{:S(2)}) %all-to-all-start.5) | async-done | bytes 4194336 | tf_op jit(solution)/shard_map/all_to_all | solution.py:278
  412.1 4.4 multiply_reduce_fusion
  416.8 0.8 convolution_convert_fusion.1
  417.7 18.7 %all_to_all.40 = bf16[4,128,512]{2,1,0:T(8,128)(2,1)S(1)} all-to-all(bf16[4,128,512]{2,1,0:T(8,128)(2,1)S(1)} %bitcast.152), channel_id=1, replica_groups=mesh['wide'=32,'narrow'=4] {'narrow'}, dimensions={0} | all-to-all | bytes 1048576 | tf_op jit(solution)/shard_map/all_to_all | solution.py:302
  436.5 12.7 %all_to_all.41 = bf16[4,128,512]{2,1,0:T(8,128)(2,1)S(1)} all-to-all(bf16[4,128,512]{2,1,0:T(8,128)(2,1)S(1)} %broadcast_in_dim.31), channel_id=1, replica_groups=mesh['wide'=32,'narrow'=4] {'narrow'}, dimensions={0} | all-to-all | bytes 1048576 | tf_op jit(solution)/shard_map/all_to_all | solution.py:47
  449.5 1.0 copy.96
  (49 shorter events, 2.6 us)
Async XLA Ops:
  6.5 0.9 copy-start
  10.9 9.5 %copy-start.6 = (bf16[2048]{0:T(1024)(128)(2,1)S(1)}, bf16[2048]{0:T(1024)(128)(2,1)}, u32[]{:S(2)}) copy-start(bf16[2048]{0:T(1024)(128)(2,1)} %param.10) | copy-start | bytes 12292
  10.9 9.5 %copy-start.3 = (bf16[128,2048]{1,0:T(8,128)(2,1)S(1)}, bf16[128,2048]{1,0:T(8,128)(2,1)}, u32[]{:S(2)}) copy-start(bf16[128,2048]{1,0:T(8,128)(2,1)} %param.9) | copy-start | bytes 1572868
  10.9 68.7 %all-to-all-start = ((bf16[32,64,912]{2,1,0:T(8,128)(2,1)}), bf16[32,64,912]{2,1,0:T(8,128)(2,1)}, u32[]{:S(2)}, u32[]{:S(2)}) async-start(bf16[32,64,912]{2,1,0:T(8,128)(2,1)} %broadcast_in_dim.24), calls=%async_computation | async-start | bytes 8388608 | tf_op jit(solution)/shard_map/all_to_all | solution.py:47
  20.4 70.5 %copy-start.4 = (s32[8]{0:T(128)S(1)}, s32[8]{0:T(128)}, u32[]{:S(2)}) copy-start(s32[8]{0:T(128)} %lens_ref.1) | copy-start | bytes 100
  20.4 77.3 %copy-start.5 = (bf16[16,1024]{1,0:T(8,128)(2,1)S(1)}, bf16[16,1024]{1,0:T(8,128)(2,1)}, u32[]{:S(2)}) copy-start(bf16[16,1024]{1,0:T(8,128)(2,1)} %param.14) | copy-start | bytes 98308
  84.3 13.5 %all-to-all-start.3 = ((f32[4,128,144]{1,2,0:T(8,128)}), f32[4,128,144]{1,2,0:T(8,128)S(1)}, u32[]{:S(2)}, u32[]{:S(2)}) async-start(f32[4,128,144]{1,2,0:T(8,128)} %broadcast_in_dim.28), calls=%async_computation.3 | async-start | bytes 589824 | tf_op jit(solution)/shard_map/all_to_all | solution.py:47
  98.9 21.3 %all-to-all-start.2 = ((bf16[32,16,1024]{2,1,0:T(8,128)(2,1)}), bf16[32,16,1024]{2,1,0:T(8,128)(2,1)S(1)}, u32[]{:S(2)}, u32[]{:S(2)}) async-start(bf16[32,16,1024]{2,1,0:T(8,128)(2,1)} %broadcast_in_dim.26), calls=%async_computation.2 | async-start | bytes 2097152 | tf_op jit(solution)/shard_map/all_to_all | solution.py:47
  124.3 90.7 %all-to-all-start.1 = ((bf16[32,128,768]{1,2,0:T(8,128)(2,1)}), bf16[32,128,768]{1,2,0:T(8,128)(2,1)}, u32[]{:S(2)}, u32[]{:S(2)}) async-start(bf16[32,128,768]{1,2,0:T(8,128)(2,1)} %broadcast_in_dim.25), calls=%async_computation.1 | async-start | bytes 12582912 | tf_op jit(solution)/shard_map/all_to_all | solution.py:47
  129.2 230.7 %all-gather.3.cloned.1.call-start = ((), (), s32[]{:S(2)}) async-start(), calls=%async_computation.8 | async-start | bytes 2162688 | tf_op jit(solution)/shard_map/all_gather | solution.py:191
  130.0 8.6 %copy-start.7 = (bf16[512]{0:T(512)(128)(2,1)S(1)}, bf16[512]{0:T(512)(128)(2,1)}, u32[]{:S(2)}) copy-start(bf16[512]{0:T(512)(128)(2,1)} %param.13) | copy-start | bytes 3076
  238.5 2.0 copy-start.2
  336.5 15.5 %all-to-all-start.4 = ((bf16[2,4,32,128]{3,1,0,2:T(4,128)(2,1)}), bf16[2,4,32,128]{3,1,0,2:T(4,128)(2,1)S(1)}, u32[]{:S(2)}, u32[]{:S(2)}) async-start(bf16[2,4,32,128]{3,1,0,2:T(4,128)(2,1)} %pad_maximum_fusion.3), calls=%async_computation.4 | async-start | bytes 131072 | tf_op jit(solution)/shard_map/all_to_all | solution.py:275
  352.0 60.1 %all-to-all-start.5 = ((bf16[4,32,128,128]{3,2,0,1:T(8,128)(2,1)}), bf16[4,32,128,128]{3,2,0,1:T(8,128)(2,1)}, u32[]{:S(2)}, u32[]{:S(2)}) async-start(bf16[4,32,128,128]{3,2,0,1:T(8,128)(2,1)} %copy.90), calls=%async_computation.5 | async-start | bytes 8388608 | tf_op jit(solution)/shard_map/all_to_all | solution.py:278
  416.8 33.7 %copy-start.1 = (bf16[64,576]{1,0:T(8,128)(2,1)S(1)}, bf16[64,576]{1,0:T(8,128)(2,1)}, u32[]{:S(2)}) copy-start(bf16[64,576]{1,0:T(8,128)(2,1)} %param.12) | copy-start | bytes 221188
Sparse Core Ops, SparseCore 0:
  131.7 187.5 all-gather.2

commit v8 on v7

--- a/solution.py
+++ b/solution.py
@@ -113,8 +113,9 @@
         peak = jnp.max(jnp.where(live, scores, -1e30), axis=-1, keepdims=True)
         weights = jnp.where(live, jnp.exp(scores - peak), 0.0)
         total = jnp.sum(weights, axis=-1, keepdims=True)
-        lane = lax.broadcasted_iota(jnp.int32, stats_ref.shape[1:], 1)
-        stats_ref[0] = jnp.where(lane == 0, peak, total)
+        lane = lax.broadcasted_iota(jnp.int32, (peak.shape[0], 128), 1)
+        packed = jnp.where(lane == 0, peak, jnp.where(lane == 1, total, 0.0))
+        stats_ref[0, 0] = jnp.transpose(packed)[: stats_ref.shape[2]]
         mixed = jnp.dot(weights.astype(jnp.bfloat16), key_lat, preferred_element_type=jnp.float32)
         value_map = vm_ref[0]
         upper_part = mixed.astype(jnp.bfloat16)
@@ -125,8 +126,8 @@
 
     @pl.when(jnp.logical_not(live_block))
     def _():
-        lane = lax.broadcasted_iota(jnp.int32, stats_ref.shape, 2)
-        stats_ref[...] = jnp.where(lane == 0, -1e30, 0.0).astype(jnp.float32)
+        row = lax.broadcasted_iota(jnp.int32, stats_ref.shape, 2)
+        stats_ref[...] = jnp.where(row == 0, -1e30, 0.0).astype(jnp.float32)
         value_ref[...] = jnp.zeros(value_ref.shape, jnp.float32)
 
 
@@ -145,7 +146,7 @@
             pl.BlockSpec((1, LAT, vdim), lambda r, h, lens, b: (h, 0, 0)),
         ],
         out_specs=[
-            pl.BlockSpec((1, span, 128), lambda r, h, lens, b: (h, r, 0)),
+            pl.BlockSpec((1, 1, 8, span), lambda r, h, lens, b: (h, r, 0, 0)),
             pl.BlockSpec((1, span, vdim), lambda r, h, lens, b: (h, r, 0)),
         ],
     )
@@ -153,7 +154,7 @@
         cache_kernel,
         grid_spec=grid_spec,
         out_shape=[
-            jax.ShapeDtypeStruct((heads_here, total_tokens, 128), jnp.float32),
+            jax.ShapeDtypeStruct((heads_here, requests, 8, span), jnp.float32),
             jax.ShapeDtypeStruct((heads_here, total_tokens, vdim), jnp.float32),
         ],
         compiler_params=pltpu.CompilerParams(dimension_semantics=("arbitrary", "arbitrary")),
@@ -235,8 +236,8 @@
 
     base = (wide_place * cache_rows).reshape(1).astype(jnp.int32)
     stats_hm, value_out = cache_attention(lengths, base, lat_hm, rope_hm, cache, value_hm)
-    peak_hm = stats_hm[..., 0]
-    total_hm = stats_hm[..., 1]
+    peak_hm = stats_hm[:, :, 0].reshape(heads_here, total_tokens)
+    total_hm = stats_hm[:, :, 1].reshape(heads_here, total_tokens)
 
     own_request = first_token // SPAN
     start_row = own_request * SPAN

time: 463 us -> 448 us (0.968)
  local copies, waits for them, and re-layouts: 54.1 us -> 39.2 us
    slice x1, local copies, waits for them, and re-layouts: 14.6 us -> 1.57 us  [per_device(): total_hm = stats_hm[:, :, 1].reshape(heads_here, total_tokens)]
    unnamed x19 -> x21, local copies, waits for them, and re-layouts: 14.5 us -> 13.1 us
  transfers between devices with their start and end apart: 7 -> 7, of which waited for: 5 -> 5; matrix products, arithmetic and copies ran while one was open for 16% -> 14% of each run, Pallas kernels for 17% -> 17%
where the time goes in v8:
time: 448 us; the launch traced here: 443 us
  waiting for transfers between devices  200 us (45%)
  Pallas kernels  76.9 us (17%)
  local copies, waits for them, and re-layouts  39.2 us (9%)
  starting transfers between devices  38 us (8%)
  blocking collectives  32.4 us (7%)
  matrix products  26.8 us (6%)
  other arithmetic  16.1 us (4%)
  between operations  13.8 us (3%)
    all_to_all x4, waiting for transfers between devices, gather_axis(): lax.all_to_all(spread, axis_name, split_axis=0, concat_axis=0, tiled=True)  151 us
    pallas_call x1, Pallas kernels, cache_attention(): pl.pallas_call(cache_kernel, grid_spec=grid_spec, out_shape=[jax.ShapeDty...  76.9 us
    all_to_all x1, waiting for transfers between devices, per_device(): lax.all_to_all(value_out.astype(jnp.bfloat16).reshape(heads_here, wide_co...  48.5 us
    all_to_all x4, starting transfers between devices, gather_axis(): lax.all_to_all(spread, axis_name, split_axis=0, concat_axis=0, tiled=True)  25.8 us
    all_to_all x1, blocking collectives, per_device(): got_pieces = lax.all_to_all(pieces, 'narrow', 0, 0, tiled=True)  19.7 us
    unnamed x21, local copies, waits for them, and re-layouts  13.1 us
    all_to_all x1, blocking collectives, gather_axis(): lax.all_to_all(spread, axis_name, split_axis=0, concat_axis=0, tiled=True)  12.7 us
    dot_general x1, matrix products, per_device(): jnp.einsum('thc,lhc->htl', nope_all, key_maps, preferred_element_type=jnp...  10.5 us
  transfers between devices with their start and end apart: 7, of which 5 were waited for; matrix products, arithmetic and copies ran while one was open for 14% of the time, Pallas kernels for 17%

profile of v8, /device:TPU:1, one launch (start us, length us, event | category | flops | bytes accessed | tf_op | source)
XLA Modules:
  0.0 442.9 jit_solution(7054974561644903801)
XLA Ops:
  6.5 0.9 copy-done
  7.5 0.9 pad_maximum_fusion.1
  8.4 2.5 broadcast_in_dim.24
  10.9 9.5 %all-to-all-start = ((bf16[32,64,912]{2,1,0:T(8,128)(2,1)}), bf16[32,64,912]{2,1,0:T(8,128)(2,1)}, u32[]{:S(2)}, u32[]{:S(2)}) async-start(bf16[32,64,912]{2,1,0:T(8,128)(2,1)} %broadcast_in_dim.24), calls=%async_computation | async-start | bytes 8388608 | tf_op jit(solution)/shard_map/all_to_all | solution.py:47
  20.7 58.9 %all-to-all-done = bf16[32,64,912]{2,1,0:T(8,128)(2,1)} async-done(((bf16[32,64,912]{2,1,0:T(8,128)(2,1)}), bf16[32,64,912]{2,1,0:T(8,128)(2,1)}, u32[]{:S(2)}, u32[]{:S(2)}) %all-to-all-start) | async-done | bytes 3735584 | tf_op jit(solution)/shard_map/all_to_all | solution.py:47
  79.6 3.9 fusion.23
  83.5 0.7 broadcast_in_dim.28
  84.3 6.6 %all-to-all-start.3 = ((f32[4,128,144]{1,2,0:T(8,128)}), f32[4,128,144]{1,2,0:T(8,128)S(1)}, u32[]{:S(2)}, u32[]{:S(2)}) async-start(f32[4,128,144]{1,2,0:T(8,128)} %broadcast_in_dim.28), calls=%async_computation.3 | async-start | bytes 589824 | tf_op jit(solution)/shard_map/all_to_all | solution.py:47
  90.9 0.7 fusion.53
  91.6 6.2 %all-to-all-done.3 = f32[4,128,144]{1,2,0:T(8,128)S(1)} async-done(((f32[4,128,144]{1,2,0:T(8,128)}), f32[4,128,144]{1,2,0:T(8,128)S(1)}, u32[]{:S(2)}, u32[]{:S(2)}) %all-to-all-start.3) | async-done | bytes 294944 | tf_op jit(solution)/shard_map/all_to_all | solution.py:47
  97.8 1.1 broadcast_in_dim.26
  98.9 4.7 %all-to-all-start.2 = ((bf16[32,16,1024]{2,1,0:T(8,128)(2,1)}), bf16[32,16,1024]{2,1,0:T(8,128)(2,1)S(1)}, u32[]{:S(2)}, u32[]{:S(2)}) async-start(bf16[32,16,1024]{2,1,0:T(8,128)(2,1)} %broadcast_in_dim.26), calls=%async_computation.2 | async-start | bytes 2097152 | tf_op jit(solution)/shard_map/all_to_all | solution.py:47
  103.6 5.0 %fusion.48 = f32[128]{0:T(128)S(1)} fusion(s32[]{:T(128)} %bitcast.6, s32[]{:T(128)} %bitcast.7, s32[]{:T(128)} %bitcast.8, s32[]{:T(128)} %bitcast.9, s32[]{:T(128)} %bitcast.10, s32[]{:T(128)} %bitcast.12, s32[]{:T(128)} %bitcast.11, s32[]{:T(128)} %bitcast.5, s32[]{:T(128)S(6)} %mul.164), kind=kLoop, calls=%fused_computation.99 | loop fusion | flops 6016 | bytes 548 | tf_op jit(solution)/shard_map/convert_element_type | solution.py:22
  108.9 11.3 %all-to-all-done.2 = bf16[32,16,1024]{2,1,0:T(8,128)(2,1)S(1)} async-done(((bf16[32,16,1024]{2,1,0:T(8,128)(2,1)}), bf16[32,16,1024]{2,1,0:T(8,128)(2,1)S(1)}, u32[]{:S(2)}, u32[]{:S(2)}) %all-to-all-start.2) | async-done | bytes 1048608 | tf_op jit(solution)/shard_map/all_to_all | solution.py:47
  120.2 4.1 broadcast_in_dim.25
  124.3 5.0 %all-to-all-start.1 = ((bf16[32,128,768]{1,2,0:T(8,128)(2,1)}), bf16[32,128,768]{1,2,0:T(8,128)(2,1)}, u32[]{:S(2)}, u32[]{:S(2)}) async-start(bf16[32,128,768]{1,2,0:T(8,128)(2,1)} %broadcast_in_dim.25), calls=%async_computation.1 | async-start | bytes 12582912 | tf_op jit(solution)/shard_map/all_to_all | solution.py:47
  129.6 0.5 all-gather.3.cloned.1.call-update
  130.1 8.5 %copy.53.kv_ref = bf16[8,640,576]{2,1,0:T(8,128)(2,1)} copy(bf16[8,640,576]{1,2,0:T(8,128)(2,1)} %param.16) | data formatting | bytes 11796480 | tf_op args[7]
  138.7 0.8 reshape_reshape.3
  139.5 0.4 fusion.52
  139.9 0.9 copy.88
  140.8 74.2 %all-to-all-done.1 = bf16[32,128,768]{1,2,0:T(8,128)(2,1)} async-done(((bf16[32,128,768]{1,2,0:T(8,128)(2,1)}), bf16[32,128,768]{1,2,0:T(8,128)(2,1)}, u32[]{:S(2)}, u32[]{:S(2)}) %all-to-all-start.1) | async-done | bytes 6291488 | tf_op jit(solution)/shard_map/all_to_all | solution.py:47
  215.1 3.7 copy_bitcast_fusion
  218.8 2.2 slice.86
  221.2 3.1 copy.51
  224.3 10.5 %convolution_convert_fusion.lat_ref = bf16[4,4096,512]{2,1,0:T(8,128)(2,1)} fusion(bf16[4096,4,128]{0,2,1:T(8,128)(2,1)} %bitcast.114, bf16[512,4,128]{2,1,0:T(4,128)(2,1)S(1)} %get-tuple-element.17), kind=kOutput, calls=%fused_computation | convolution fusion | flops 2155872256 | bytes 21495808 | tf_op jit(solution)/shard_map/thc,lhc->htl/dot_general | solution.py:231
  234.8 0.3 fusion.32
  235.1 2.5 select_reduce_fusion
  237.9 2.8 fusion.21
  240.7 76.9 %shard_map.91 = (f32[4,8,8,512]{3,2,1,0:T(8,128)}, f32[4,4096,128]{2,1,0:T(8,128)}) custom-call(s32[8]{0:T(128)} %lens_ref.1, s32[1]{0:T(128)} %bitcast.base_ref, bf16[4,4096,512]{2,1,0:T(8,128)(2,1)} %convolution_convert_fusion.lat_ref, bf16[4,4096,64]{2,1,0:T(8,128)(2,1)} %bitcast.113, bf16[8,640,576]{2,1,0:T(8,128)(2,1)} %copy.53.kv_ref, ...), custom_call_target="tpu_custom_call" | custom-call | tf_op jit(solution)/shard_map/pallas_call | solution.py:153
  317.6 1.6 slice_reduce_fusion
  319.4 0.7 pad_maximum_fusion.3
  320.0 3.9 all-to-all-start.4
  323.9 3.1 fusion.17
  327.0 0.4 copy-done.2
  327.4 2.8 fusion.12
  330.2 3.9 convert_element_type.88
  334.1 2.3 copy.58
  336.4 8.1 %all-to-all-start.5 = ((bf16[4,32,128,128]{3,2,0,1:T(8,128)(2,1)}), bf16[4,32,128,128]{3,2,0,1:T(8,128)(2,1)}, u32[]{:S(2)}, u32[]{:S(2)}) async-start(bf16[4,32,128,128]{3,2,0,1:T(8,128)(2,1)} %copy.58), calls=%async_computation.5 | async-start | bytes 8388608 | tf_op jit(solution)/shard_map/all_to_all | solution.py:279
  344.5 2.4 copy.79
  346.8 1.2 copy.61
  348.1 48.5 %all-to-all-done.5 = bf16[4,32,128,128]{3,2,0,1:T(8,128)(2,1)} async-done(((bf16[4,32,128,128]{3,2,0,1:T(8,128)(2,1)}), bf16[4,32,128,128]{3,2,0,1:T(8,128)(2,1)}, u32[]{:S(2)}, u32[]{:S(2)}) %all-to-all-start.5) | async-done | bytes 4194336 | tf_op jit(solution)/shard_map/all_to_all | solution.py:279
  396.6 4.4 multiply_reduce_fusion
  401.4 0.8 convolution_convert_fusion.1
  402.2 19.7 %all_to_all.40 = bf16[4,128,512]{2,1,0:T(8,128)(2,1)S(1)} all-to-all(bf16[4,128,512]{2,1,0:T(8,128)(2,1)S(1)} %bitcast.125), channel_id=1, replica_groups=mesh['wide'=32,'narrow'=4] {'narrow'}, dimensions={0} | all-to-all | bytes 1048576 | tf_op jit(solution)/shard_map/all_to_all | solution.py:303
  422.1 12.7 %all_to_all.41 = bf16[4,128,512]{2,1,0:T(8,128)(2,1)S(1)} all-to-all(bf16[4,128,512]{2,1,0:T(8,128)(2,1)S(1)} %broadcast_in_dim.31), channel_id=1, replica_groups=mesh['wide'=32,'narrow'=4] {'narrow'}, dimensions={0} | all-to-all | bytes 1048576 | tf_op jit(solution)/shard_map/all_to_all | solution.py:47
  434.8 0.3 copy.63
  435.1 1.0 copy.64
  (51 shorter events, 2.1 us)
Async XLA Ops:
  6.5 0.9 copy-start
  10.9 9.5 %copy-start.6 = (bf16[2048]{0:T(1024)(128)(2,1)S(1)}, bf16[2048]{0:T(1024)(128)(2,1)}, u32[]{:S(2)}) copy-start(bf16[2048]{0:T(1024)(128)(2,1)} %param.10) | copy-start | bytes 12292
  10.9 9.5 %copy-start.3 = (bf16[128,2048]{1,0:T(8,128)(2,1)S(1)}, bf16[128,2048]{1,0:T(8,128)(2,1)}, u32[]{:S(2)}) copy-start(bf16[128,2048]{1,0:T(8,128)(2,1)} %param.9) | copy-start | bytes 1572868
  10.9 68.7 %all-to-all-start = ((bf16[32,64,912]{2,1,0:T(8,128)(2,1)}), bf16[32,64,912]{2,1,0:T(8,128)(2,1)}, u32[]{:S(2)}, u32[]{:S(2)}) async-start(bf16[32,64,912]{2,1,0:T(8,128)(2,1)} %broadcast_in_dim.24), calls=%async_computation | async-start | bytes 8388608 | tf_op jit(solution)/shard_map/all_to_all | solution.py:47
  20.4 70.5 %copy-start.4 = (s32[8]{0:T(128)S(1)}, s32[8]{0:T(128)}, u32[]{:S(2)}) copy-start(s32[8]{0:T(128)} %lens_ref.1) | copy-start | bytes 100
  20.4 77.3 %copy-start.5 = (bf16[16,1024]{1,0:T(8,128)(2,1)S(1)}, bf16[16,1024]{1,0:T(8,128)(2,1)}, u32[]{:S(2)}) copy-start(bf16[16,1024]{1,0:T(8,128)(2,1)} %param.14) | copy-start | bytes 98308
  84.3 13.5 %all-to-all-start.3 = ((f32[4,128,144]{1,2,0:T(8,128)}), f32[4,128,144]{1,2,0:T(8,128)S(1)}, u32[]{:S(2)}, u32[]{:S(2)}) async-start(f32[4,128,144]{1,2,0:T(8,128)} %broadcast_in_dim.28), calls=%async_computation.3 | async-start | bytes 589824 | tf_op jit(solution)/shard_map/all_to_all | solution.py:47
  98.9 21.3 %all-to-all-start.2 = ((bf16[32,16,1024]{2,1,0:T(8,128)(2,1)}), bf16[32,16,1024]{2,1,0:T(8,128)(2,1)S(1)}, u32[]{:S(2)}, u32[]{:S(2)}) async-start(bf16[32,16,1024]{2,1,0:T(8,128)(2,1)} %broadcast_in_dim.26), calls=%async_computation.2 | async-start | bytes 2097152 | tf_op jit(solution)/shard_map/all_to_all | solution.py:47
  124.3 5.8 %copy-start.7 = (bf16[512]{0:T(512)(128)(2,1)S(1)}, bf16[512]{0:T(512)(128)(2,1)}, u32[]{:S(2)}) copy-start(bf16[512]{0:T(512)(128)(2,1)} %param.13) | copy-start | bytes 3076
  124.3 90.8 %all-to-all-start.1 = ((bf16[32,128,768]{1,2,0:T(8,128)(2,1)}), bf16[32,128,768]{1,2,0:T(8,128)(2,1)}, u32[]{:S(2)}, u32[]{:S(2)}) async-start(bf16[32,128,768]{1,2,0:T(8,128)(2,1)} %broadcast_in_dim.25), calls=%async_computation.1 | async-start | bytes 12582912 | tf_op jit(solution)/shard_map/all_to_all | solution.py:47
  129.3 215.2 %all-gather.3.cloned.1.call-start = ((), (), s32[]{:S(2)}) async-start(), calls=%async_computation.8 | async-start | bytes 2162688 | tf_op jit(solution)/shard_map/all_gather | solution.py:192
  320.0 16.3 %all-to-all-start.4 = ((bf16[2,4,32,128]{3,1,0,2:T(4,128)(2,1)}), bf16[2,4,32,128]{3,1,0,2:T(4,128)(2,1)S(1)}, u32[]{:S(2)}, u32[]{:S(2)}) async-start(bf16[2,4,32,128]{3,1,0,2:T(4,128)(2,1)} %pad_maximum_fusion.3), calls=%async_computation.4 | async-start | bytes 131072 | tf_op jit(solution)/shard_map/all_to_all | solution.py:276
  323.9 3.5 copy-start.2
  336.4 60.2 %all-to-all-start.5 = ((bf16[4,32,128,128]{3,2,0,1:T(8,128)(2,1)}), bf16[4,32,128,128]{3,2,0,1:T(8,128)(2,1)}, u32[]{:S(2)}, u32[]{:S(2)}) async-start(bf16[4,32,128,128]{3,2,0,1:T(8,128)(2,1)} %copy.58), calls=%async_computation.5 | async-start | bytes 8388608 | tf_op jit(solution)/shard_map/all_to_all | solution.py:279
  401.3 34.7 %copy-start.1 = (bf16[64,576]{1,0:T(8,128)(2,1)S(1)}, bf16[64,576]{1,0:T(8,128)(2,1)}, u32[]{:S(2)}) copy-start(bf16[64,576]{1,0:T(8,128)(2,1)} %param.12) | copy-start | bytes 221188
Sparse Core Ops, SparseCore 0:
  131.8 187.8 all-gather.2

commit v9 on v8

--- a/solution.py
+++ b/solution.py
@@ -93,7 +93,9 @@
     )
 
 
-def cache_kernel(lens_ref, base_ref, lat_ref, rope_ref, kv_ref, vm_ref, stats_ref, value_ref):
+def cache_kernel(
+    lens_ref, base_ref, nope_ref, rope_ref, kv_ref, km_ref, vm_ref, stats_ref, value_ref
+):
     length_now = lens_ref[pl.program_id(0)]
     base = base_ref[0]
     live_block = base < length_now
@@ -104,8 +106,11 @@
         key_lat = keys[:, :LAT]
         key_rope = keys[:, LAT:]
         nt = (((1,), (1,)), ((), ()))
+        q_lat = lax.dot_general(
+            nope_ref[...], km_ref[...], nt, preferred_element_type=jnp.float32
+        ).astype(jnp.bfloat16)
         scores = (
-            lax.dot_general(lat_ref[0], key_lat, nt, preferred_element_type=jnp.float32)
+            lax.dot_general(q_lat, key_lat, nt, preferred_element_type=jnp.float32)
             + lax.dot_general(rope_ref[0], key_rope, nt, preferred_element_type=jnp.float32)
         ) * score_scale
         slots = base + lax.broadcasted_iota(jnp.int32, scores.shape, 1)
@@ -117,7 +122,7 @@
         packed = jnp.where(lane == 0, peak, jnp.where(lane == 1, total, 0.0))
         stats_ref[0, 0] = jnp.transpose(packed)[: stats_ref.shape[2]]
         mixed = jnp.dot(weights.astype(jnp.bfloat16), key_lat, preferred_element_type=jnp.float32)
-        value_map = vm_ref[0]
+        value_map = vm_ref[...]
         upper_part = mixed.astype(jnp.bfloat16)
         lower_part = (mixed - upper_part.astype(jnp.float32)).astype(jnp.bfloat16)
         value_ref[0] = jnp.dot(upper_part, value_map, preferred_element_type=jnp.float32) + jnp.dot(
@@ -131,19 +136,20 @@
         value_ref[...] = jnp.zeros(value_ref.shape, jnp.float32)
 
 
-def cache_attention(lengths, base, lat_hm, rope_hm, cache, value_hm):
-    heads_here, total_tokens, _ = lat_hm.shape
+def cache_attention(lengths, base, nope_rows, rope_hm, cache, kvb_full):
+    heads_here, total_tokens, _ = rope_hm.shape
     requests, cache_rows, width = cache.shape
     span = total_tokens // requests
-    vdim = value_hm.shape[2]
+    vdim = VDIM
     grid_spec = pltpu.PrefetchScalarGridSpec(
         num_scalar_prefetch=2,
         grid=(requests, heads_here),
         in_specs=[
-            pl.BlockSpec((1, span, LAT), lambda r, h, lens, b: (h, r, 0)),
+            pl.BlockSpec((span, NOPE), lambda r, h, lens, b: (r, h)),
             pl.BlockSpec((1, span, ROPE), lambda r, h, lens, b: (h, r, 0)),
             pl.BlockSpec((1, cache_rows, width), lambda r, h, lens, b: (r, 0, 0)),
-            pl.BlockSpec((1, LAT, vdim), lambda r, h, lens, b: (h, 0, 0)),
+            pl.BlockSpec((LAT, NOPE), lambda r, h, lens, b: (0, 2 * h)),
+            pl.BlockSpec((LAT, VDIM), lambda r, h, lens, b: (0, 2 * h + 1)),
         ],
         out_specs=[
             pl.BlockSpec((1, 1, 8, span), lambda r, h, lens, b: (h, r, 0, 0)),
@@ -158,7 +164,7 @@
             jax.ShapeDtypeStruct((heads_here, total_tokens, vdim), jnp.float32),
         ],
         compiler_params=pltpu.CompilerParams(dimension_semantics=("arbitrary", "arbitrary")),
-    )(lengths, base, lat_hm, rope_hm, cache, value_hm)
+    )(lengths, base, nope_rows, rope_hm, cache, kvb_full, kvb_full)
 
 
 def merge_parts(first, second):
@@ -228,14 +234,11 @@
     value_maps = kvb_heads[..., NOPE:]
     nope_all = raw_all[:, : heads_here * NOPE].reshape(total_tokens, heads_here, NOPE)
     rope_all = raw_all[:, heads_here * NOPE :].reshape(total_tokens, heads_here, ROPE)
-    lat_hm = jnp.einsum(
-        "thc,lhc->htl", nope_all, key_maps, preferred_element_type=jnp.float32
-    ).astype(jnp.bfloat16)
     rope_hm = jnp.transpose(rope_all, (1, 0, 2))
     value_hm = jnp.transpose(value_maps, (1, 0, 2))
 
     base = (wide_place * cache_rows).reshape(1).astype(jnp.int32)
-    stats_hm, value_out = cache_attention(lengths, base, lat_hm, rope_hm, cache, value_hm)
+    stats_hm, value_out = cache_attention(lengths, base, raw_all, rope_hm, cache, kvb_full)
     peak_hm = stats_hm[:, :, 0].reshape(heads_here, total_tokens)
     total_hm = stats_hm[:, :, 1].reshape(heads_here, total_tokens)
 
@@ -243,7 +246,12 @@
     start_row = own_request * SPAN
     own_slots = first_token % SPAN + jnp.arange(tok_rows, dtype=jnp.int32)
     causal = own_slots[None, :] <= jnp.arange(SPAN, dtype=jnp.int32)[:, None]
-    own_lat = lax.dynamic_slice_in_dim(lat_hm, start_row, SPAN, 1)
+    own_lat = jnp.einsum(
+        "thc,lhc->htl",
+        lax.dynamic_slice_in_dim(nope_all, start_row, SPAN, 0),
+        key_maps,
+        preferred_element_type=jnp.float32,
+    ).astype(jnp.bfloat16)
     own_rope = lax.dynamic_slice_in_dim(rope_hm, start_row, SPAN, 1)
     own_scores = (
         jnp.einsum("hqc,kc->hqk", own_lat, own_keys[:, :LAT], preferred_element_type=jnp.float32)

time: 448 us -> 454 us (1.013); the launches traced: 443 us -> 455 us
  local copies, waits for them, and re-layouts: 39.2 us -> 51.4 us
  matrix products: 26.8 us -> 17.6 us
  Pallas kernels: 76.9 us -> 81.7 us
    dot_general x1 -> x0, matrix products: 10.5 us -> none  [per_device(): jnp.einsum('thc,lhc->htl', nope_all, key_maps, preferred_element_type=jnp...]
    slice x1 -> x2, local copies, waits for them, and re-layouts: 0.14 us -> 5.96 us  [per_device(): raw_all[:, heads_here * NOPE:].reshape(total_tokens, heads_here, ROPE)]
    pallas_call x1, Pallas kernels: 76.9 us -> 81.7 us  [cache_attention(): pl.pallas_call(cache_kernel, grid_spec=grid_spec, out_shape=[jax.ShapeDty...]
    unnamed x21 -> x22, local copies, waits for them, and re-layouts: 13.1 us -> 12.3 us
  transfers between devices with their start and end apart: 7 -> 7, of which waited for: 5 -> 5; matrix products, arithmetic and copies ran while one was open for 14% -> 14% of each run, Pallas kernels for 17% -> 18%
where the time goes in v9:
time: 454 us; the launch traced here: 455 us
  waiting for transfers between devices  200 us (44%)
  Pallas kernels  81.7 us (18%)
  local copies, waits for them, and re-layouts  51.4 us (11%)
  starting transfers between devices  40.9 us (9%)
  blocking collectives  32.9 us (7%)
  matrix products  17.6 us (4%)
  other arithmetic  16.1 us (4%)
  between operations  13.8 us (3%)
    all_to_all x4, waiting for transfers between devices, gather_axis(): lax.all_to_all(spread, axis_name, split_axis=0, concat_axis=0, tiled=True)  151 us
    pallas_call x1, Pallas kernels, cache_attention(): pl.pallas_call(cache_kernel, grid_spec=grid_spec, out_shape=[jax.ShapeDty...  81.7 us
    all_to_all x1, waiting for transfers between devices, per_device(): lax.all_to_all(value_out.astype(jnp.bfloat16).reshape(heads_here, wide_co...  49.1 us
    all_to_all x4, starting transfers between devices, gather_axis(): lax.all_to_all(spread, axis_name, split_axis=0, concat_axis=0, tiled=True)  25.8 us
    all_to_all x1, blocking collectives, per_device(): got_pieces = lax.all_to_all(pieces, 'narrow', 0, 0, tiled=True)  20.2 us
    all_to_all x1, blocking collectives, gather_axis(): lax.all_to_all(spread, axis_name, split_axis=0, concat_axis=0, tiled=True)  12.7 us
    unnamed x22, local copies, waits for them, and re-layouts  12.3 us
  transfers between devices with their start and end apart: 7, of which 5 were waited for; matrix products, arithmetic and copies ran while one was open for 14% of the time, Pallas kernels for 18%

profile of v9, /device:TPU:1, one launch (start us, length us, event | category | flops | bytes accessed | tf_op | source)
XLA Modules:
  0.0 454.6 jit_solution(13615081527598392598)
XLA Ops:
  6.5 0.9 copy-done
  7.5 0.9 pad_maximum_fusion.1
  8.4 2.5 broadcast_in_dim.24
  10.9 9.5 %all-to-all-start = ((bf16[32,64,912]{2,1,0:T(8,128)(2,1)}), bf16[32,64,912]{2,1,0:T(8,128)(2,1)}, u32[]{:S(2)}, u32[]{:S(2)}) async-start(bf16[32,64,912]{2,1,0:T(8,128)(2,1)} %broadcast_in_dim.24), calls=%async_computation | async-start | bytes 8388608 | tf_op jit(solution)/shard_map/all_to_all | solution.py:47
  20.7 58.9 %all-to-all-done = bf16[32,64,912]{2,1,0:T(8,128)(2,1)} async-done(((bf16[32,64,912]{2,1,0:T(8,128)(2,1)}), bf16[32,64,912]{2,1,0:T(8,128)(2,1)}, u32[]{:S(2)}, u32[]{:S(2)}) %all-to-all-start) | async-done | bytes 3735584 | tf_op jit(solution)/shard_map/all_to_all | solution.py:47
  79.6 3.9 fusion.25
  83.5 0.7 broadcast_in_dim.28
  84.3 6.6 %all-to-all-start.3 = ((f32[4,128,144]{1,2,0:T(8,128)}), f32[4,128,144]{1,2,0:T(8,128)S(1)}, u32[]{:S(2)}, u32[]{:S(2)}) async-start(f32[4,128,144]{1,2,0:T(8,128)} %broadcast_in_dim.28), calls=%async_computation.3 | async-start | bytes 589824 | tf_op jit(solution)/shard_map/all_to_all | solution.py:47
  90.9 0.7 fusion.57
  91.6 6.2 %all-to-all-done.3 = f32[4,128,144]{1,2,0:T(8,128)S(1)} async-done(((f32[4,128,144]{1,2,0:T(8,128)}), f32[4,128,144]{1,2,0:T(8,128)S(1)}, u32[]{:S(2)}, u32[]{:S(2)}) %all-to-all-start.3) | async-done | bytes 294944 | tf_op jit(solution)/shard_map/all_to_all | solution.py:47
  97.8 1.1 broadcast_in_dim.26
  98.9 4.7 %all-to-all-start.2 = ((bf16[32,16,1024]{2,1,0:T(8,128)(2,1)}), bf16[32,16,1024]{2,1,0:T(8,128)(2,1)S(1)}, u32[]{:S(2)}, u32[]{:S(2)}) async-start(bf16[32,16,1024]{2,1,0:T(8,128)(2,1)} %broadcast_in_dim.26), calls=%async_computation.2 | async-start | bytes 2097152 | tf_op jit(solution)/shard_map/all_to_all | solution.py:47
  103.6 5.0 %fusion.52 = f32[128]{0:T(128)S(1)} fusion(s32[]{:T(128)} %bitcast.6, s32[]{:T(128)} %bitcast.7, s32[]{:T(128)} %bitcast.8, s32[]{:T(128)} %bitcast.9, s32[]{:T(128)} %bitcast.10, s32[]{:T(128)} %bitcast.12, s32[]{:T(128)} %bitcast.11, s32[]{:T(128)} %bitcast.5, s32[]{:T(128)S(6)} %mul.164), kind=kLoop, calls=%fused_computation.99 | loop fusion | flops 6016 | bytes 548 | tf_op jit(solution)/shard_map/convert_element_type | solution.py:22
  109.1 11.1 %all-to-all-done.2 = bf16[32,16,1024]{2,1,0:T(8,128)(2,1)S(1)} async-done(((bf16[32,16,1024]{2,1,0:T(8,128)(2,1)}), bf16[32,16,1024]{2,1,0:T(8,128)(2,1)S(1)}, u32[]{:S(2)}, u32[]{:S(2)}) %all-to-all-start.2) | async-done | bytes 1048608 | tf_op jit(solution)/shard_map/all_to_all | solution.py:47
  120.2 3.4 broadcast_in_dim.25
  123.6 5.0 %all-to-all-start.1 = ((bf16[32,128,768]{2,1,0:T(8,128)(2,1)}), bf16[32,128,768]{2,1,0:T(8,128)(2,1)}, u32[]{:S(2)}, u32[]{:S(2)}) async-start(bf16[32,128,768]{2,1,0:T(8,128)(2,1)} %broadcast_in_dim.25), calls=%async_computation.1 | async-start | bytes 12582912 | tf_op jit(solution)/shard_map/all_to_all | solution.py:47
  128.8 0.5 all-gather.3.cloned.1.call-update
  129.4 8.5 %copy.59.kv_ref = bf16[8,640,576]{2,1,0:T(8,128)(2,1)} copy(bf16[8,640,576]{1,2,0:T(8,128)(2,1)} %param.16) | data formatting | bytes 11796480 | tf_op args[7]
  138.0 0.8 reshape_reshape.3
  138.8 1.2 fusion.56
  140.1 74.3 %all-to-all-done.1 = bf16[32,128,768]{2,1,0:T(8,128)(2,1)} async-done(((bf16[32,128,768]{2,1,0:T(8,128)(2,1)}), bf16[32,128,768]{2,1,0:T(8,128)(2,1)}, u32[]{:S(2)}, u32[]{:S(2)}) %all-to-all-start.1) | async-done | bytes 6291488 | tf_op jit(solution)/shard_map/all_to_all | solution.py:47
  214.4 3.0 slice.86
  217.4 4.4 slice.87
  221.8 2.9 copy.57
  224.7 7.0 %reshape.290 = bf16[4096,4,128]{2,1,0:T(4,128)(2,1)} reshape(bf16[4096,512]{1,0:T(8,128)(2,1)} %slice.87) | data formatting | bytes 8388608 | tf_op jit(solution)/shard_map/reshape | solution.py:235
  231.7 3.2 copy.58
  234.9 1.2 constant_dynamic-slice_fusion
  236.1 1.4 fusion.37
  237.6 2.8 select_reduce_fusion
  240.6 2.8 fusion.23
  243.4 81.7 %shard_map.91 = (f32[4,8,8,512]{3,2,1,0:T(8,128)}, f32[4,4096,128]{2,1,0:T(8,128)}) custom-call(s32[8]{0:T(128)} %lens_ref.1, s32[1]{0:T(128)} %bitcast.base_ref, bf16[4096,768]{1,0:T(8,128)(2,1)} %bitcast.15.nope_ref, bf16[4,4096,64]{2,1,0:T(8,128)(2,1)} %bitcast.106, bf16[8,640,576]{2,1,0:T(8,128)(2,1)} %copy.59.kv_ref, bf16[512,1024]{1,0:T(8,128)(2,1)} %bitcast.108, ...), custom_call_target="tpu_custom_call" | custom-call | tf_op jit(solution)/shard_map/pallas_call | solution.py:159
  325.1 1.8 slice_reduce_fusion
  327.0 0.7 pad_maximum_fusion.3
  327.7 6.8 %all-to-all-start.4 = ((bf16[2,4,32,128]{3,1,0,2:T(4,128)(2,1)}), bf16[2,4,32,128]{3,1,0,2:T(4,128)(2,1)S(1)}, u32[]{:S(2)}, u32[]{:S(2)}) async-start(bf16[2,4,32,128]{3,1,0,2:T(4,128)(2,1)} %pad_maximum_fusion.3), calls=%async_computation.4 | async-start | bytes 131072 | tf_op jit(solution)/shard_map/all_to_all | solution.py:284
  334.5 3.0 fusion.19
  337.6 0.4 copy-done.2
  337.9 2.8 fusion.14
  340.7 3.9 convert_element_type.88
  344.7 2.3 copy.67
  346.9 8.1 %all-to-all-start.5 = ((bf16[4,32,128,128]{3,2,0,1:T(8,128)(2,1)}), bf16[4,32,128,128]{3,2,0,1:T(8,128)(2,1)}, u32[]{:S(2)}, u32[]{:S(2)}) async-start(bf16[4,32,128,128]{3,2,0,1:T(8,128)(2,1)} %copy.67), calls=%async_computation.5 | async-start | bytes 8388608 | tf_op jit(solution)/shard_map/all_to_all | solution.py:287
  355.1 2.4 copy.87
  357.4 1.2 copy.70
  358.7 49.1 %all-to-all-done.5 = bf16[4,32,128,128]{3,2,0,1:T(8,128)(2,1)} async-done(((bf16[4,32,128,128]{3,2,0,1:T(8,128)(2,1)}), bf16[4,32,128,128]{3,2,0,1:T(8,128)(2,1)}, u32[]{:S(2)}, u32[]{:S(2)}) %all-to-all-start.5) | async-done | bytes 4194336 | tf_op jit(solution)/shard_map/all_to_all | solution.py:287
  407.8 4.4 multiply_reduce_fusion
  412.5 0.8 convolution_convert_fusion
  413.4 20.2 %all_to_all.40 = bf16[4,128,512]{2,1,0:T(8,128)(2,1)S(1)} all-to-all(bf16[4,128,512]{2,1,0:T(8,128)(2,1)S(1)} %bitcast.119), channel_id=1, replica_groups=mesh['wide'=32,'narrow'=4] {'narrow'}, dimensions={0} | all-to-all | bytes 1048576 | tf_op jit(solution)/shard_map/all_to_all | solution.py:311
  433.8 12.7 %all_to_all.41 = bf16[4,128,512]{2,1,0:T(8,128)(2,1)S(1)} all-to-all(bf16[4,128,512]{2,1,0:T(8,128)(2,1)S(1)} %broadcast_in_dim.31), channel_id=1, replica_groups=mesh['wide'=32,'narrow'=4] {'narrow'}, dimensions={0} | all-to-all | bytes 1048576 | tf_op jit(solution)/shard_map/all_to_all | solution.py:47
  446.8 1.0 copy.73
  (55 shorter events, 2.4 us)
Async XLA Ops:
  6.5 0.9 copy-start
  10.9 9.5 %copy-start.7 = (bf16[2048]{0:T(1024)(128)(2,1)S(1)}, bf16[2048]{0:T(1024)(128)(2,1)}, u32[]{:S(2)}) copy-start(bf16[2048]{0:T(1024)(128)(2,1)} %param.10) | copy-start | bytes 12292
  10.9 9.5 %copy-start.4 = (bf16[128,2048]{1,0:T(8,128)(2,1)S(1)}, bf16[128,2048]{1,0:T(8,128)(2,1)}, u32[]{:S(2)}) copy-start(bf16[128,2048]{1,0:T(8,128)(2,1)} %param.9) | copy-start | bytes 1572868
  10.9 68.7 %all-to-all-start = ((bf16[32,64,912]{2,1,0:T(8,128)(2,1)}), bf16[32,64,912]{2,1,0:T(8,128)(2,1)}, u32[]{:S(2)}, u32[]{:S(2)}) async-start(bf16[32,64,912]{2,1,0:T(8,128)(2,1)} %broadcast_in_dim.24), calls=%async_computation | async-start | bytes 8388608 | tf_op jit(solution)/shard_map/all_to_all | solution.py:47
  20.4 70.5 %copy-start.5 = (s32[8]{0:T(128)S(1)}, s32[8]{0:T(128)}, u32[]{:S(2)}) copy-start(s32[8]{0:T(128)} %lens_ref.1) | copy-start | bytes 100
  20.4 77.3 %copy-start.6 = (bf16[16,1024]{1,0:T(8,128)(2,1)S(1)}, bf16[16,1024]{1,0:T(8,128)(2,1)}, u32[]{:S(2)}) copy-start(bf16[16,1024]{1,0:T(8,128)(2,1)} %param.14) | copy-start | bytes 98308
  84.3 13.5 %all-to-all-start.3 = ((f32[4,128,144]{1,2,0:T(8,128)}), f32[4,128,144]{1,2,0:T(8,128)S(1)}, u32[]{:S(2)}, u32[]{:S(2)}) async-start(f32[4,128,144]{1,2,0:T(8,128)} %broadcast_in_dim.28), calls=%async_computation.3 | async-start | bytes 589824 | tf_op jit(solution)/shard_map/all_to_all | solution.py:47
  98.9 21.3 %all-to-all-start.2 = ((bf16[32,16,1024]{2,1,0:T(8,128)(2,1)}), bf16[32,16,1024]{2,1,0:T(8,128)(2,1)S(1)}, u32[]{:S(2)}, u32[]{:S(2)}) async-start(bf16[32,16,1024]{2,1,0:T(8,128)(2,1)} %broadcast_in_dim.26), calls=%async_computation.2 | async-start | bytes 2097152 | tf_op jit(solution)/shard_map/all_to_all | solution.py:47
  120.2 17.8 %copy-start.3 = (bf16[32,16,1024]{2,1,0:T(8,128)(2,1)}, bf16[32,16,1024]{2,1,0:T(8,128)(2,1)S(1)}, u32[]{:S(2)}) copy-start(bf16[32,16,1024]{2,1,0:T(8,128)(2,1)S(1)} %all-to-all-done.2) | copy-start | bytes 3145732
  123.6 5.8 %copy-start.8 = (bf16[512]{0:T(512)(128)(2,1)S(1)}, bf16[512]{0:T(512)(128)(2,1)}, u32[]{:S(2)}) copy-start(bf16[512]{0:T(512)(128)(2,1)} %param.13) | copy-start | bytes 3076
  123.6 90.8 %all-to-all-start.1 = ((bf16[32,128,768]{2,1,0:T(8,128)(2,1)}), bf16[32,128,768]{2,1,0:T(8,128)(2,1)}, u32[]{:S(2)}, u32[]{:S(2)}) async-start(bf16[32,128,768]{2,1,0:T(8,128)(2,1)} %broadcast_in_dim.25), calls=%async_computation.1 | async-start | bytes 12582912 | tf_op jit(solution)/shard_map/all_to_all | solution.py:47
  128.6 226.4 %all-gather.3.cloned.1.call-start = ((), (), s32[]{:S(2)}) async-start(), calls=%async_computation.8 | async-start | bytes 2162688 | tf_op jit(solution)/shard_map/all_gather | solution.py:198
  327.7 19.2 %all-to-all-start.4 = ((bf16[2,4,32,128]{3,1,0,2:T(4,128)(2,1)}), bf16[2,4,32,128]{3,1,0,2:T(4,128)(2,1)S(1)}, u32[]{:S(2)}, u32[]{:S(2)}) async-start(bf16[2,4,32,128]{3,1,0,2:T(4,128)(2,1)} %pad_maximum_fusion.3), calls=%async_computation.4 | async-start | bytes 131072 | tf_op jit(solution)/shard_map/all_to_all | solution.py:284
  334.5 3.5 copy-start.2
  346.9 60.9 %all-to-all-start.5 = ((bf16[4,32,128,128]{3,2,0,1:T(8,128)(2,1)}), bf16[4,32,128,128]{3,2,0,1:T(8,128)(2,1)}, u32[]{:S(2)}, u32[]{:S(2)}) async-start(bf16[4,32,128,128]{3,2,0,1:T(8,128)(2,1)} %copy.67), calls=%async_computation.5 | async-start | bytes 8388608 | tf_op jit(solution)/shard_map/all_to_all | solution.py:287
  412.5 35.2 %copy-start.1 = (bf16[64,576]{1,0:T(8,128)(2,1)S(1)}, bf16[64,576]{1,0:T(8,128)(2,1)}, u32[]{:S(2)}) copy-start(bf16[64,576]{1,0:T(8,128)(2,1)} %param.12) | copy-start | bytes 221188
Sparse Core Ops, SparseCore 0:
  131.1 187.7 all-gather.2

commit v10 on v8

--- a/solution.py
+++ b/solution.py
@@ -195,12 +195,26 @@
     projected = jnp.dot(normed, proj_full, preferred_element_type=jnp.float32)
     query_rows = projected[:, :q_cols].astype(jnp.bfloat16)
     compressed_part = projected[:, q_cols:]
-    compressed = jnp.transpose(gather_axis(compressed_part, "narrow"), (1, 0, 2)).reshape(
-        tok_rows, kva_cols
-    )
     first_token = wide_place * tok_rows
     token_ids = first_token + jnp.arange(tok_rows, dtype=jnp.int32)
     positions = lengths[token_ids // SPAN] + token_ids % SPAN
+
+    query_heads = query_rows.reshape(tok_rows, heads_here, NOPE + ROPE)
+    own_rope_q = rotate(query_heads[..., NOPE:].astype(jnp.float32), positions[:, None]).astype(
+        jnp.bfloat16
+    )
+    outgoing = jnp.concatenate(
+        [
+            query_heads[..., :NOPE].reshape(tok_rows, heads_here * NOPE),
+            own_rope_q.reshape(tok_rows, heads_here * ROPE),
+        ],
+        axis=1,
+    )
+    raw_all = gather_axis(outgoing, "wide")
+    compressed_part, raw_all = lax.optimization_barrier((compressed_part, raw_all))
+    compressed = jnp.transpose(gather_axis(compressed_part, "narrow"), (1, 0, 2)).reshape(
+        tok_rows, kva_cols
+    )
     own_keys = jnp.concatenate(
         [
             scaled_norm(compressed[:, :LAT], kv_gain).astype(jnp.bfloat16),
@@ -208,19 +222,6 @@
         ],
         axis=1,
     )
-
-    query_heads = query_rows.reshape(tok_rows, heads_here, NOPE + ROPE)
-    own_rope_q = rotate(query_heads[..., NOPE:].astype(jnp.float32), positions[:, None]).astype(
-        jnp.bfloat16
-    )
-    outgoing = jnp.concatenate(
-        [
-            query_heads[..., :NOPE].reshape(tok_rows, heads_here * NOPE),
-            own_rope_q.reshape(tok_rows, heads_here * ROPE),
-        ],
-        axis=1,
-    )
-    raw_all = gather_axis(outgoing, "wide")
     total_tokens = raw_all.shape[0] * tok_rows
     raw_all = raw_all.reshape(total_tokens, heads_here * (NOPE + ROPE))
     kvb_heads = kvb_full.reshape(LAT, heads_here, NOPE + VDIM)
@@ -295,15 +296,8 @@
     partial_out = jnp.einsum(
         "tk,wkc->twc", context, o_got, preferred_element_type=jnp.float32
     ).reshape(tok_rows, -1)
-    out_cols = partial_out.shape[1]
-    pieces = jnp.transpose(
-        partial_out.astype(jnp.bfloat16).reshape(tok_rows, narrow_count, out_cols // narrow_count),
-        (1, 0, 2),
-    )
-    got_pieces = lax.all_to_all(pieces, "narrow", 0, 0, tiled=True)
-    mine = jnp.sum(got_pieces.astype(jnp.float32), axis=0).astype(jnp.bfloat16)
-    all_pieces = gather_axis(mine, "narrow")
-    return jnp.transpose(all_pieces, (1, 0, 2)).reshape(tok_rows, out_cols)
+    got_parts = gather_axis(partial_out.astype(jnp.bfloat16), "narrow")
+    return jnp.sum(got_parts.astype(jnp.float32), axis=0).astype(jnp.bfloat16)
 
 
 def solution(mesh):

time: 448 us -> 445 us (level)
    all_to_all x1 -> x0, blocking collectives: 19.7 us -> none  [per_device(): got_pieces = lax.all_to_all(pieces, 'narrow', 0, 0, tiled=True)]
    all_to_all x1, blocking collectives: 12.7 us -> 31 us  [gather_axis(): lax.all_to_all(spread, axis_name, split_axis=0, concat_axis=0, tiled=True)]
    all_to_all x4, waiting for transfers between devices: 151 us -> 142 us  [gather_axis(): lax.all_to_all(spread, axis_name, split_axis=0, concat_axis=0, tiled=True)]
    all_to_all x1, waiting for transfers between devices: 48.5 us -> 56.5 us  [per_device(): lax.all_to_all(value_out.astype(jnp.bfloat16).reshape(heads_here, wide_co...]
    unnamed x21 -> x31, local copies, waits for them, and re-layouts: 13.1 us -> 13.8 us
  transfers between devices with their start and end apart: 7 -> 7, of which waited for: 5 -> 4; matrix products, arithmetic and copies ran while one was open for 14% -> 14% of each run, Pallas kernels for 17% -> 17%
where the time goes in v10:
time: 445 us; the launch traced here: 444 us
  waiting for transfers between devices  199 us (45%)
  Pallas kernels  76.8 us (17%)
  local copies, waits for them, and re-layouts  41.5 us (9%)
  starting transfers between devices  40 us (9%)
  blocking collectives  31 us (7%)
  matrix products  24.4 us (5%)
  other arithmetic  17.3 us (4%)
  between operations  13.8 us (3%)
    all_to_all x4, waiting for transfers between devices, gather_axis(): lax.all_to_all(spread, axis_name, split_axis=0, concat_axis=0, tiled=True)  142 us
    pallas_call x1, Pallas kernels, cache_attention(): pl.pallas_call(cache_kernel, grid_spec=grid_spec, out_shape=[jax.ShapeDty...  76.8 us
    all_to_all x1, waiting for transfers between devices, per_device(): lax.all_to_all(value_out.astype(jnp.bfloat16).reshape(heads_here, wide_co...  56.5 us
    all_to_all x1, blocking collectives, gather_axis(): lax.all_to_all(spread, axis_name, split_axis=0, concat_axis=0, tiled=True)  31 us
    all_to_all x4, starting transfers between devices, gather_axis(): lax.all_to_all(spread, axis_name, split_axis=0, concat_axis=0, tiled=True)  28 us
    unnamed x31, local copies, waits for them, and re-layouts  13.8 us
  transfers between devices with their start and end apart: 7, of which 4 were waited for; matrix products, arithmetic and copies ran while one was open for 14% of the time, Pallas kernels for 17%

profile of v10, /device:TPU:1, one launch (start us, length us, event | category | flops | bytes accessed | tf_op | source)
XLA Modules:
  0.0 443.7 jit_solution(12902652600219925572)
XLA Ops:
  6.5 0.9 copy-done
  7.5 0.9 pad_maximum_fusion.1
  8.4 2.5 broadcast_in_dim.24
  10.9 9.5 %all-to-all-start = ((bf16[32,64,912]{2,1,0:T(8,128)(2,1)}), bf16[32,64,912]{2,1,0:T(8,128)(2,1)}, u32[]{:S(2)}, u32[]{:S(2)}) async-start(bf16[32,64,912]{2,1,0:T(8,128)(2,1)} %broadcast_in_dim.24), calls=%async_computation | async-start | bytes 8388608 | tf_op jit(solution)/shard_map/all_to_all | solution.py:47
  20.5 0.7 fusion.53
  21.2 4.8 %fusion.48 = f32[128]{0:T(128)S(1)} fusion(s32[]{:T(128)} %bitcast.6, s32[]{:T(128)} %bitcast.7, s32[]{:T(128)} %bitcast.8, s32[]{:T(128)} %bitcast.9, s32[]{:T(128)} %bitcast.10, s32[]{:T(128)} %bitcast.12, s32[]{:T(128)} %bitcast.11, s32[]{:T(128)} %bitcast.5, s32[]{:T(128)S(6)} %mul.164), kind=kLoop, calls=%fused_computation.98 | loop fusion | flops 6016 | bytes 548 | tf_op jit(solution)/shard_map/convert_element_type | solution.py:22
  26.3 53.3 %all-to-all-done = bf16[32,64,912]{2,1,0:T(8,128)(2,1)} async-done(((bf16[32,64,912]{2,1,0:T(8,128)(2,1)}), bf16[32,64,912]{2,1,0:T(8,128)(2,1)}, u32[]{:S(2)}, u32[]{:S(2)}) %all-to-all-start) | async-done | bytes 3735584 | tf_op jit(solution)/shard_map/all_to_all | solution.py:47
  79.6 1.1 broadcast_in_dim.26
  80.7 5.3 %all-to-all-start.2 = ((bf16[32,16,1024]{2,1,0:T(8,128)(2,1)}), bf16[32,16,1024]{2,1,0:T(8,128)(2,1)S(1)}, u32[]{:S(2)}, u32[]{:S(2)}) async-start(bf16[32,16,1024]{2,1,0:T(8,128)(2,1)} %broadcast_in_dim.26), calls=%async_computation.2 | async-start | bytes 2097152 | tf_op jit(solution)/shard_map/all_to_all | solution.py:47
  86.0 3.9 fusion.23
  90.1 11.9 %all-to-all-done.2 = bf16[32,16,1024]{2,1,0:T(8,128)(2,1)S(1)} async-done(((bf16[32,16,1024]{2,1,0:T(8,128)(2,1)}), bf16[32,16,1024]{2,1,0:T(8,128)(2,1)S(1)}, u32[]{:S(2)}, u32[]{:S(2)}) %all-to-all-start.2) | async-done | bytes 1048608 | tf_op jit(solution)/shard_map/all_to_all | solution.py:47
  102.0 4.1 broadcast_in_dim.25
  106.1 5.0 %all-to-all-start.1 = ((bf16[32,128,768]{1,2,0:T(8,128)(2,1)}), bf16[32,128,768]{1,2,0:T(8,128)(2,1)}, u32[]{:S(2)}, u32[]{:S(2)}) async-start(bf16[32,128,768]{1,2,0:T(8,128)(2,1)} %broadcast_in_dim.25), calls=%async_computation.1 | async-start | bytes 12582912 | tf_op jit(solution)/shard_map/all_to_all | solution.py:47
  111.2 0.7 all-gather.3.cloned.1.call-update
  111.9 8.4 %copy.52.kv_ref = bf16[8,640,576]{2,1,0:T(8,128)(2,1)} copy(bf16[8,640,576]{1,2,0:T(8,128)(2,1)} %param.16) | data formatting | bytes 11796480 | tf_op args[7]
  120.5 0.8 reshape_reshape.3
  121.3 0.4 fusion.52
  121.6 0.8 copy-done.3
  122.4 0.9 copy.81
  123.3 76.4 %all-to-all-done.1 = bf16[32,128,768]{1,2,0:T(8,128)(2,1)} async-done(((bf16[32,128,768]{1,2,0:T(8,128)(2,1)}), bf16[32,128,768]{1,2,0:T(8,128)(2,1)}, u32[]{:S(2)}, u32[]{:S(2)}) %all-to-all-start.1) | async-done | bytes 6291488 | tf_op jit(solution)/shard_map/all_to_all | solution.py:47
  199.6 6.3 %copy_bitcast_fusion = bf16[4096,768]{0,1:T(8,128)(2,1)} fusion(bf16[32,128,768]{1,2,0:T(8,128)(2,1)} %all-to-all-done.1), kind=kLoop, calls=%fused_computation.2 | loop fusion | bytes 12582912 | tf_op jit(solution)/shard_map/reshape | solution.py:226
  206.0 0.7 broadcast_in_dim.28
  206.7 8.2 %all-to-all-start.3 = ((f32[4,128,144]{1,2,0:T(8,128)}), f32[4,128,144]{1,2,0:T(8,128)S(1)}, u32[]{:S(2)}, u32[]{:S(2)}) async-start(f32[4,128,144]{1,2,0:T(8,128)} %broadcast_in_dim.28), calls=%async_computation.3 | async-start | bytes 589824 | tf_op jit(solution)/shard_map/all_to_all | solution.py:47
  214.9 2.2 slice-done.2
  217.1 8.2 %convolution_convert_fusion.lat_ref = bf16[4,4096,512]{2,1,0:T(8,128)(2,1)} fusion(bf16[4096,4,128]{0,2,1:T(8,128)(2,1)S(1)} %bitcast.104, bf16[512,4,128]{2,1,0:T(4,128)(2,1)S(1)} %get-tuple-element.21), kind=kOutput, calls=%fused_computation | convolution fusion | flops 2155872256 | bytes 21495808 | tf_op jit(solution)/shard_map/thc,lhc->htl/dot_general | solution.py:232
  225.5 3.2 copy.50
  228.7 76.8 %shard_map.91 = (f32[4,8,8,512]{3,2,1,0:T(8,128)}, f32[4,4096,128]{2,1,0:T(8,128)}) custom-call(s32[8]{0:T(128)} %lens_ref.1, s32[1]{0:T(128)} %bitcast.base_ref, bf16[4,4096,512]{2,1,0:T(8,128)(2,1)} %convolution_convert_fusion.lat_ref, bf16[4,4096,64]{2,1,0:T(8,128)(2,1)} %bitcast.106, bf16[8,640,576]{2,1,0:T(8,128)(2,1)} %copy.52.kv_ref, ...), custom_call_target="tpu_custom_call" | custom-call | tf_op jit(solution)/shard_map/pallas_call | solution.py:153
  305.5 1.5 slice_reduce_fusion
  307.5 0.3 fusion.32
  307.8 2.5 select_reduce_fusion
  310.4 0.2 fusion.20
  310.6 2.8 fusion.21
  313.4 0.7 pad_maximum_fusion.3
  314.1 3.9 all-to-all-start.4
  318.0 3.1 fusion.17
  321.1 0.4 copy-done.2
  321.5 2.8 fusion.12
  324.2 3.9 convert_element_type.88
  328.2 2.3 copy.57
  330.4 8.1 %all-to-all-start.5 = ((bf16[4,32,128,128]{3,2,0,1:T(8,128)(2,1)}), bf16[4,32,128,128]{3,2,0,1:T(8,128)(2,1)}, u32[]{:S(2)}, u32[]{:S(2)}) async-start(bf16[4,32,128,128]{3,2,0,1:T(8,128)(2,1)} %copy.57), calls=%async_computation.5 | async-start | bytes 8388608 | tf_op jit(solution)/shard_map/all_to_all | solution.py:280
  338.6 2.4 copy.74
  340.9 1.2 copy.60
  342.2 56.5 %all-to-all-done.5 = bf16[4,32,128,128]{3,2,0,1:T(8,128)(2,1)} async-done(((bf16[4,32,128,128]{3,2,0,1:T(8,128)(2,1)}), bf16[4,32,128,128]{3,2,0,1:T(8,128)(2,1)}, u32[]{:S(2)}, u32[]{:S(2)}) %all-to-all-start.5) | async-done | bytes 4194336 | tf_op jit(solution)/shard_map/all_to_all | solution.py:280
  398.8 4.4 multiply_reduce_fusion
  403.5 0.8 convolution_convert_fusion.1
  404.3 0.2 broadcast_in_dim.31
  404.6 31.0 %all_to_all.35 = bf16[4,128,2048]{2,1,0:T(8,128)(2,1)S(1)} all-to-all(bf16[4,128,2048]{2,1,0:T(8,128)(2,1)S(1)} %broadcast_in_dim.31), channel_id=1, replica_groups=mesh['wide'=32,'narrow'=4] {'narrow'}, dimensions={0} | all-to-all | bytes 4194304 | tf_op jit(solution)/shard_map/all_to_all | solution.py:47
  435.6 1.3 reduce_sum.65
  (61 shorter events, 1.8 us)
Async XLA Ops:
  6.5 0.9 copy-start
  10.9 9.5 %copy-start.9 = (bf16[2048]{0:T(1024)(128)(2,1)S(1)}, bf16[2048]{0:T(1024)(128)(2,1)}, u32[]{:S(2)}) copy-start(bf16[2048]{0:T(1024)(128)(2,1)} %param.10) | copy-start | bytes 12292
  10.9 9.5 %copy-start.7 = (s32[8]{0:T(128)S(1)}, s32[8]{0:T(128)}, u32[]{:S(2)}) copy-start(s32[8]{0:T(128)} %lens_ref.1) | copy-start | bytes 100
  10.9 15.1 %copy-start.5 = (bf16[128,2048]{1,0:T(8,128)(2,1)S(1)}, bf16[128,2048]{1,0:T(8,128)(2,1)}, u32[]{:S(2)}) copy-start(bf16[128,2048]{1,0:T(8,128)(2,1)} %param.9) | copy-start | bytes 1572868
  10.9 68.7 %copy-start.8 = (bf16[16,1024]{1,0:T(8,128)(2,1)S(1)}, bf16[16,1024]{1,0:T(8,128)(2,1)}, u32[]{:S(2)}) copy-start(bf16[16,1024]{1,0:T(8,128)(2,1)} %param.14) | copy-start | bytes 98308
  10.9 68.7 %all-to-all-start = ((bf16[32,64,912]{2,1,0:T(8,128)(2,1)}), bf16[32,64,912]{2,1,0:T(8,128)(2,1)}, u32[]{:S(2)}, u32[]{:S(2)}) async-start(bf16[32,64,912]{2,1,0:T(8,128)(2,1)} %broadcast_in_dim.24), calls=%async_computation | async-start | bytes 8388608 | tf_op jit(solution)/shard_map/all_to_all | solution.py:47
  80.7 21.3 %all-to-all-start.2 = ((bf16[32,16,1024]{2,1,0:T(8,128)(2,1)}), bf16[32,16,1024]{2,1,0:T(8,128)(2,1)S(1)}, u32[]{:S(2)}, u32[]{:S(2)}) async-start(bf16[32,16,1024]{2,1,0:T(8,128)(2,1)} %broadcast_in_dim.26), calls=%async_computation.2 | async-start | bytes 2097152 | tf_op jit(solution)/shard_map/all_to_all | solution.py:47
  90.0 33.3 %copy-start.6 = (f32[128,912]{0,1:T(8,128)}, f32[128,912]{0,1:T(8,128)S(1)}, u32[]{:S(2)}) copy-start(f32[128,912]{0,1:T(8,128)S(1)} %fusion.23) | copy-start | bytes 1400836
  106.1 5.8 %copy-start.10 = (bf16[512]{0:T(512)(128)(2,1)S(1)}, bf16[512]{0:T(512)(128)(2,1)}, u32[]{:S(2)}) copy-start(bf16[512]{0:T(512)(128)(2,1)} %param.13) | copy-start | bytes 3076
  106.1 93.6 %all-to-all-start.1 = ((bf16[32,128,768]{1,2,0:T(8,128)(2,1)}), bf16[32,128,768]{1,2,0:T(8,128)(2,1)}, u32[]{:S(2)}, u32[]{:S(2)}) async-start(bf16[32,128,768]{1,2,0:T(8,128)(2,1)} %broadcast_in_dim.25), calls=%async_computation.1 | async-start | bytes 12582912 | tf_op jit(solution)/shard_map/all_to_all | solution.py:47
  111.1 227.5 %all-gather.3.cloned.1.call-start = ((), (), s32[]{:S(2)}) async-start(), calls=%async_computation.7 | async-start | bytes 2162688 | tf_op jit(solution)/shard_map/all_gather | solution.py:192
  121.6 0.8 copy-start.3
  123.3 82.7 %slice-start.3 = ((f32[128,912]{0,1:T(8,128)}), f32[128,144]{0,1:T(8,128)S(1)}, s32[]{:S(2)}) async-start(f32[128,912]{0,1:T(8,128)} %copy-done.6), calls=%async_computation.11 | async-start | bytes 147456 | tf_op jit(solution)/shard_map/slice | solution.py:197
  206.7 100.5 %all-to-all-start.3 = ((f32[4,128,144]{1,2,0:T(8,128)}), f32[4,128,144]{1,2,0:T(8,128)S(1)}, u32[]{:S(2)}, u32[]{:S(2)}) async-start(f32[4,128,144]{1,2,0:T(8,128)} %broadcast_in_dim.28), calls=%async_computation.3 | async-start | bytes 589824 | tf_op jit(solution)/shard_map/all_to_all | solution.py:47
  214.9 2.2 slice-start.2
  214.9 10.4 %slice-start = ((s8[6291456]{0:T(1024)(128)(4,1)}), s8[4194304]{0:T(1024)(128)(4,1)S(1)}, s32[]{:S(2)}) async-start(s8[6291456]{0:T(1024)(128)(4,1)} %bitcast.102), calls=%async_computation.8 | async-start | bytes 8388608
  217.1 8.2 %slice-start.1 = ((s8[6291456]{0:T(1024)(128)(4,1)}), s8[2097152]{0:T(1024)(128)(4,1)S(1)}, s32[]{:S(2)}) async-start(s8[6291456]{0:T(1024)(128)(4,1)} %bitcast.102), calls=%async_computation.9 | async-start | bytes 4194304
  310.4 7.6 %copy-start.4 = (bf16[512,4,128]{2,1,0:T(4,128)(2,1)S(1)}, bf16[512,4,128]{2,1,0:T(4,128)(2,1)}, u32[]{:S(2)}) copy-start(bf16[512,4,128]{2,1,0:T(4,128)(2,1)} %copy-done.3) | copy-start | bytes 1572868
  314.1 16.3 %all-to-all-start.4 = ((bf16[2,4,32,128]{3,1,0,2:T(4,128)(2,1)}), bf16[2,4,32,128]{3,1,0,2:T(4,128)(2,1)S(1)}, u32[]{:S(2)}, u32[]{:S(2)}) async-start(bf16[2,4,32,128]{3,1,0,2:T(4,128)(2,1)} %pad_maximum_fusion.3), calls=%async_computation.4 | async-start | bytes 131072 | tf_op jit(solution)/shard_map/all_to_all | solution.py:277
  318.0 3.5 copy-start.2
  330.4 68.3 %all-to-all-start.5 = ((bf16[4,32,128,128]{3,2,0,1:T(8,128)(2,1)}), bf16[4,32,128,128]{3,2,0,1:T(8,128)(2,1)}, u32[]{:S(2)}, u32[]{:S(2)}) async-start(bf16[4,32,128,128]{3,2,0,1:T(8,128)(2,1)} %copy.57), calls=%async_computation.5 | async-start | bytes 8388608 | tf_op jit(solution)/shard_map/all_to_all | solution.py:280
  403.5 33.4 %copy-start.1 = (bf16[64,576]{1,0:T(8,128)(2,1)S(1)}, bf16[64,576]{1,0:T(8,128)(2,1)}, u32[]{:S(2)}) copy-start(bf16[64,576]{1,0:T(8,128)(2,1)} %param.12) | copy-start | bytes 221188
Sparse Core Ops, SparseCore 0:
  113.6 186.7 all-gather.2

commit v11 on v10

--- a/solution.py
+++ b/solution.py
@@ -273,19 +273,17 @@
     total_hm = lax.dynamic_update_slice_in_dim(total_hm, joint[1], start_row, 1)
     value_out = lax.dynamic_update_slice_in_dim(value_out, joint[2], start_row, 1)
 
-    stats = jnp.stack([peak_hm, total_hm], axis=0).astype(jnp.bfloat16)
-    got_stats = lax.all_to_all(
-        stats.reshape(2, heads_here, wide_count, tok_rows), "wide", 2, 2, tiled=True
-    ).astype(jnp.float32)
-    got_value = lax.all_to_all(
-        value_out.astype(jnp.bfloat16).reshape(heads_here, wide_count, tok_rows, VDIM),
-        "wide",
-        1,
-        1,
-        tiled=True,
-    ).astype(jnp.float32)
-    got_peak = got_stats[0]
-    got_total = got_stats[1]
+    stats = jnp.stack(
+        [peak_hm.reshape(heads_here, wide_count, tok_rows), total_hm.reshape(heads_here, wide_count, tok_rows)],
+        axis=2,
+    )
+    sending = jnp.concatenate(
+        [value_out.reshape(heads_here, wide_count, tok_rows, VDIM), stats], axis=2
+    ).astype(jnp.bfloat16)
+    got_all = lax.all_to_all(sending, "wide", 1, 1, tiled=True).astype(jnp.float32)
+    got_value = got_all[:, :, :tok_rows, :]
+    got_peak = got_all[:, :, tok_rows, :]
+    got_total = got_all[:, :, tok_rows + 1, :]
     peak_value = jnp.max(got_peak, axis=1)
     factor = jnp.exp(got_peak - peak_value[:, None])
     denominator = jnp.sum(factor * got_total, axis=1)
@@ -296,8 +294,15 @@
     partial_out = jnp.einsum(
         "tk,wkc->twc", context, o_got, preferred_element_type=jnp.float32
     ).reshape(tok_rows, -1)
-    got_parts = gather_axis(partial_out.astype(jnp.bfloat16), "narrow")
-    return jnp.sum(got_parts.astype(jnp.float32), axis=0).astype(jnp.bfloat16)
+    out_cols = partial_out.shape[1]
+    pieces = jnp.transpose(
+        partial_out.astype(jnp.bfloat16).reshape(tok_rows, narrow_count, out_cols // narrow_count),
+        (1, 0, 2),
+    )
+    got_pieces = lax.all_to_all(pieces, "narrow", 0, 0, tiled=True)
+    mine = jnp.sum(got_pieces.astype(jnp.float32), axis=0).astype(jnp.bfloat16)
+    all_pieces = gather_axis(mine, "narrow")
+    return jnp.transpose(all_pieces, (1, 0, 2)).reshape(tok_rows, out_cols)
 
 
 def solution(mesh):

time: 445 us -> 571 us (1.28)
  waiting for transfers between devices: 199 us -> 304 us
  blocking collectives: 31 us -> 47 us
  local copies, waits for them, and re-layouts: 41.5 us -> 49.6 us
    all_gather x1, waiting for transfers between devices: 0.02 us -> 166 us  [per_device(): o_got = lax.all_gather(o_weight, 'wide', axis=0, tiled=False)]
    all_to_all x2 -> x1, waiting for transfers between devices: 56.5 us -> 0.01 us  [per_device(): lax.all_to_all(sending, 'wide', 1, 1, tiled=True).astype(jnp.float32)]
    all_to_all x0 -> x1, blocking collectives: none -> 34.2 us  [per_device(): got_pieces = lax.all_to_all(pieces, 'narrow', 0, 0, tiled=True)]
    all_to_all x1, blocking collectives: 31 us -> 12.7 us  [gather_axis(): lax.all_to_all(spread, axis_name, split_axis=0, concat_axis=0, tiled=True)]
    all_to_all x2 -> x1, starting transfers between devices: 12 us -> 5.98 us  [per_device(): lax.all_to_all(sending, 'wide', 1, 1, tiled=True).astype(jnp.float32)]
    unnamed x31 -> x29, local copies, waits for them, and re-layouts: 13.8 us -> 18 us
  transfers between devices with their start and end apart: 7 -> 6, of which waited for: 4 -> 4; matrix products, arithmetic and copies ran while one was open for 14% -> 7% of each run, Pallas kernels for 17% -> 14%
where the time goes in v11:
time: 571 us; the launch traced here: 569 us
  waiting for transfers between devices  304 us (53%)
  Pallas kernels  76.9 us (13%)
  local copies, waits for them, and re-layouts  49.6 us (9%)
  blocking collectives  47 us (8%)
  starting transfers between devices  34.5 us (6%)
  other arithmetic  21.4 us (4%)
  matrix products  21.3 us (4%)
  between operations  13.8 us (2%)
    all_gather x1, waiting for transfers between devices, per_device(): o_got = lax.all_gather(o_weight, 'wide', axis=0, tiled=False)  166 us
    all_to_all x4, waiting for transfers between devices, gather_axis(): lax.all_to_all(spread, axis_name, split_axis=0, concat_axis=0, tiled=True)  137 us
    pallas_call x1, Pallas kernels, cache_attention(): pl.pallas_call(cache_kernel, grid_spec=grid_spec, out_shape=[jax.ShapeDty...  76.9 us
    all_to_all x1, blocking collectives, per_device(): got_pieces = lax.all_to_all(pieces, 'narrow', 0, 0, tiled=True)  34.2 us
    all_to_all x4, starting transfers between devices, gather_axis(): lax.all_to_all(spread, axis_name, split_axis=0, concat_axis=0, tiled=True)  28.5 us
    unnamed x29, local copies, waits for them, and re-layouts  18 us
    all_to_all x1, blocking collectives, gather_axis(): lax.all_to_all(spread, axis_name, split_axis=0, concat_axis=0, tiled=True)  12.7 us
  transfers between devices with their start and end apart: 6, of which 4 were waited for; matrix products, arithmetic and copies ran while one was open for 7% of the time, Pallas kernels for 14%

profile of v11, /device:TPU:1, one launch (start us, length us, event | category | flops | bytes accessed | tf_op | source)
XLA Modules:
  0.0 568.9 jit_solution(9339321319743224881)
XLA Ops:
  6.5 0.9 copy-done
  7.5 0.9 pad_maximum_fusion.2
  8.4 2.5 broadcast_in_dim.24
  10.9 9.5 %all-to-all-start = ((bf16[32,64,912]{2,1,0:T(8,128)(2,1)}), bf16[32,64,912]{2,1,0:T(8,128)(2,1)}, u32[]{:S(2)}, u32[]{:S(2)}) async-start(bf16[32,64,912]{2,1,0:T(8,128)(2,1)} %broadcast_in_dim.24), calls=%async_computation | async-start | bytes 8388608 | tf_op jit(solution)/shard_map/all_to_all | solution.py:47
  20.5 0.7 fusion.55
  21.2 4.9 fusion.50
  26.4 53.2 %all-to-all-done = bf16[32,64,912]{2,1,0:T(8,128)(2,1)} async-done(((bf16[32,64,912]{2,1,0:T(8,128)(2,1)}), bf16[32,64,912]{2,1,0:T(8,128)(2,1)}, u32[]{:S(2)}, u32[]{:S(2)}) %all-to-all-start) | async-done | bytes 3735584 | tf_op jit(solution)/shard_map/all_to_all | solution.py:47
  79.6 1.1 broadcast_in_dim.26
  80.7 5.3 all-to-all-start.2
  86.0 3.9 fusion.24
  90.1 11.9 %all-to-all-done.2 = bf16[32,16,1024]{2,1,0:T(8,128)(2,1)S(1)} async-done(((bf16[32,16,1024]{2,1,0:T(8,128)(2,1)}), bf16[32,16,1024]{2,1,0:T(8,128)(2,1)S(1)}, u32[]{:S(2)}, u32[]{:S(2)}) %all-to-all-start.2) | async-done | bytes 1048608 | tf_op jit(solution)/shard_map/all_to_all | solution.py:47
  102.0 4.1 broadcast_in_dim.25
  106.0 4.9 all-to-all-start.1
  111.0 8.5 %copy.63.kv_ref = bf16[8,640,576]{2,1,0:T(8,128)(2,1)} copy(bf16[8,640,576]{1,2,0:T(8,128)(2,1)} %param.16) | data formatting | bytes 11796480 | tf_op args[7]
  119.6 0.8 reshape_reshape.3
  120.8 0.9 copy.106
  121.6 72.2 %all-to-all-done.1 = bf16[32,128,768]{1,2,0:T(8,128)(2,1)} async-done(((bf16[32,128,768]{1,2,0:T(8,128)(2,1)}), bf16[32,128,768]{1,2,0:T(8,128)(2,1)}, u32[]{:S(2)}, u32[]{:S(2)}) %all-to-all-start.1) | async-done | bytes 6291488 | tf_op jit(solution)/shard_map/all_to_all | solution.py:47
  193.9 3.7 copy_bitcast_fusion
  197.6 2.4 slice.91
  200.0 1.5 copy-done.3
  201.5 0.7 broadcast_in_dim.28
  202.2 8.8 %all-to-all-start.3 = ((f32[4,128,144]{1,2,0:T(8,128)}), f32[4,128,144]{1,2,0:T(8,128)S(1)}, u32[]{:S(2)}, u32[]{:S(2)}) async-start(f32[4,128,144]{1,2,0:T(8,128)} %broadcast_in_dim.28), calls=%async_computation.3 | async-start | bytes 589824 | tf_op jit(solution)/shard_map/all_to_all | solution.py:47
  211.0 10.5 %convolution_convert_fusion.lat_ref = bf16[4,4096,512]{2,1,0:T(8,128)(2,1)} fusion(bf16[4096,4,128]{0,2,1:T(8,128)(2,1)} %bitcast.109, bf16[512,4,128]{2,1,0:T(4,128)(2,1)S(1)} %get-tuple-element.21), kind=kOutput, calls=%fused_computation | convolution fusion | flops 2155872256 | bytes 21495808 | tf_op jit(solution)/shard_map/thc,lhc->htl/dot_general | solution.py:232
  221.5 1.7 slice.93
  223.2 3.2 copy.61
  226.4 76.9 %shard_map.91 = (f32[4,8,8,512]{3,2,1,0:T(8,128)}, f32[4,4096,128]{2,1,0:T(8,128)}) custom-call(s32[8]{0:T(128)} %lens_ref.1, s32[1]{0:T(128)} %bitcast.base_ref, bf16[4,4096,512]{2,1,0:T(8,128)(2,1)} %convolution_convert_fusion.lat_ref, bf16[4,4096,64]{2,1,0:T(8,128)(2,1)} %bitcast.110, bf16[8,640,576]{2,1,0:T(8,128)(2,1)} %copy.63.kv_ref, ...), custom_call_target="tpu_custom_call" | custom-call | tf_op jit(solution)/shard_map/pallas_call | solution.py:153
  303.3 1.5 slice_reduce_fusion.1
  305.5 2.7 select_reduce_fusion
  308.5 0.8 fusion.22
  309.3 0.7 fusion.18
  310.1 0.6 slice-done.1
  310.6 1.5 fusion.13
  312.2 0.5 convert.33
  312.7 4.0 copy.67
  316.7 4.4 pad_maximum_fusion
  321.1 6.0 %all-to-all-start.4 = ((bf16[4,32,130,128]{3,0,2,1:T(4,128)(2,1)}), bf16[4,32,130,128]{3,0,2,1:T(4,128)(2,1)}, u32[]{:S(2)}, u32[]{:S(2)}) async-start(bf16[4,32,130,128]{3,0,2,1:T(4,128)(2,1)} %pad_maximum_fusion), calls=%async_computation.4 | async-start | bytes 8519680 | tf_op jit(solution)/shard_map/all_to_all | solution.py:283
  327.1 0.7 all-gather.3.cloned.1.call-update
  327.8 166.4 %all-gather.3.cloned.1.call-done = bf16[16384,64]{0,1:T(8,128)(2,1)} async-done(((bf16[512,64]{0,1:T(8,128)(2,1)}), bf16[16384,64]{0,1:T(8,128)(2,1)}) %all-gather.3.cloned.1.call-update) | async-done | bytes 2097168 | tf_op jit(solution)/shard_map/all_gather | solution.py:192
  494.2 2.4 copy.92
  496.6 1.2 copy.74
  497.7 2.8 convert_element_type.80
  500.6 3.2 copy-done.2
  503.8 2.0 copy.71
  505.9 6.6 %fusion = f32[4,128,128]{2,0,1:T(4,128)S(1)} fusion(f32[4,32,130,128]{3,0,2,1:T(4,128)} %copy-done.2, f32[4,32,128]{0,2,1:T(8,128)} %copy.71), kind=kLoop, calls=%fused_computation.2 | loop fusion | flops 4128768 | bytes 8716288 | tf_op jit(solution)/shard_map/reduce_sum | solution.py:290
  512.8 0.8 convolution_convert_fusion.1
  513.7 34.2 %all_to_all.35 = bf16[4,128,512]{2,1,0:T(8,128)(2,1)S(1)} all-to-all(bf16[4,128,512]{2,1,0:T(8,128)(2,1)S(1)} %bitcast.123), channel_id=1, replica_groups=mesh['wide'=32,'narrow'=4] {'narrow'}, dimensions={0} | all-to-all | bytes 1048576 | tf_op jit(solution)/shard_map/all_to_all | solution.py:302
  548.0 12.7 %all_to_all.36 = bf16[4,128,512]{2,1,0:T(8,128)(2,1)S(1)} all-to-all(bf16[4,128,512]{2,1,0:T(8,128)(2,1)S(1)} %broadcast_in_dim.31), channel_id=1, replica_groups=mesh['wide'=32,'narrow'=4] {'narrow'}, dimensions={0} | all-to-all | bytes 1048576 | tf_op jit(solution)/shard_map/all_to_all | solution.py:47
  561.0 1.0 copy.77
  (59 shorter events, 2.8 us)
Async XLA Ops:
  6.5 0.9 copy-start
  10.9 9.5 %copy-start.8 = (bf16[2048]{0:T(1024)(128)(2,1)S(1)}, bf16[2048]{0:T(1024)(128)(2,1)}, u32[]{:S(2)}) copy-start(bf16[2048]{0:T(1024)(128)(2,1)} %param.10) | copy-start | bytes 12292
  10.9 9.5 %copy-start.6 = (s32[8]{0:T(128)S(1)}, s32[8]{0:T(128)}, u32[]{:S(2)}) copy-start(s32[8]{0:T(128)} %lens_ref.1) | copy-start | bytes 100
  10.9 15.1 %copy-start.4 = (bf16[128,2048]{1,0:T(8,128)(2,1)S(1)}, bf16[128,2048]{1,0:T(8,128)(2,1)}, u32[]{:S(2)}) copy-start(bf16[128,2048]{1,0:T(8,128)(2,1)} %param.9) | copy-start | bytes 1572868
  10.9 68.7 %copy-start.7 = (bf16[16,1024]{1,0:T(8,128)(2,1)S(1)}, bf16[16,1024]{1,0:T(8,128)(2,1)}, u32[]{:S(2)}) copy-start(bf16[16,1024]{1,0:T(8,128)(2,1)} %param.14) | copy-start | bytes 98308
  10.9 68.7 %all-to-all-start = ((bf16[32,64,912]{2,1,0:T(8,128)(2,1)}), bf16[32,64,912]{2,1,0:T(8,128)(2,1)}, u32[]{:S(2)}, u32[]{:S(2)}) async-start(bf16[32,64,912]{2,1,0:T(8,128)(2,1)} %broadcast_in_dim.24), calls=%async_computation | async-start | bytes 8388608 | tf_op jit(solution)/shard_map/all_to_all | solution.py:47
  80.7 21.3 %all-to-all-start.2 = ((bf16[32,16,1024]{2,1,0:T(8,128)(2,1)}), bf16[32,16,1024]{2,1,0:T(8,128)(2,1)S(1)}, u32[]{:S(2)}, u32[]{:S(2)}) async-start(bf16[32,16,1024]{2,1,0:T(8,128)(2,1)} %broadcast_in_dim.26), calls=%async_computation.2 | async-start | bytes 2097152 | tf_op jit(solution)/shard_map/all_to_all | solution.py:47
  89.9 31.7 %copy-start.5 = (f32[128,912]{0,1:T(8,128)}, f32[128,912]{0,1:T(8,128)S(1)}, u32[]{:S(2)}) copy-start(f32[128,912]{0,1:T(8,128)S(1)} %fusion.24) | copy-start | bytes 1400836
  106.0 87.8 %all-to-all-start.1 = ((bf16[32,128,768]{1,2,0:T(8,128)(2,1)}), bf16[32,128,768]{1,2,0:T(8,128)(2,1)}, u32[]{:S(2)}, u32[]{:S(2)}) async-start(bf16[32,128,768]{1,2,0:T(8,128)(2,1)} %broadcast_in_dim.25), calls=%async_computation.1 | async-start | bytes 12582912 | tf_op jit(solution)/shard_map/all_to_all | solution.py:47
  111.0 8.5 %copy-start.9 = (bf16[512]{0:T(512)(128)(2,1)S(1)}, bf16[512]{0:T(512)(128)(2,1)}, u32[]{:S(2)}) copy-start(bf16[512]{0:T(512)(128)(2,1)} %param.13) | copy-start | bytes 3076
  197.6 3.9 copy-start.3
  197.6 3.9 slice-start.2
  202.2 102.7 %all-to-all-start.3 = ((f32[4,128,144]{1,2,0:T(8,128)}), f32[4,128,144]{1,2,0:T(8,128)S(1)}, u32[]{:S(2)}, u32[]{:S(2)}) async-start(f32[4,128,144]{1,2,0:T(8,128)} %broadcast_in_dim.28), calls=%async_computation.3 | async-start | bytes 589824 | tf_op jit(solution)/shard_map/all_to_all | solution.py:47
  305.5 4.5 slice-start
  308.5 2.2 slice-start.1
  321.1 176.6 %all-to-all-start.4 = ((bf16[4,32,130,128]{3,0,2,1:T(4,128)(2,1)}), bf16[4,32,130,128]{3,0,2,1:T(4,128)(2,1)}, u32[]{:S(2)}, u32[]{:S(2)}) async-start(bf16[4,32,130,128]{3,0,2,1:T(4,128)(2,1)} %pad_maximum_fusion), calls=%async_computation.4 | async-start | bytes 8519680 | tf_op jit(solution)/shard_map/all_to_all | solution.py:283
  327.1 167.1 %all-gather.3.cloned.1.call-start = ((), (), s32[]{:S(2)}) async-start(), calls=%async_computation.7 | async-start | bytes 2162688 | tf_op jit(solution)/shard_map/all_gather | solution.py:192
  500.5 3.3 copy-start.2
  512.8 49.3 %copy-start.1 = (bf16[64,576]{1,0:T(8,128)(2,1)S(1)}, bf16[64,576]{1,0:T(8,128)(2,1)}, u32[]{:S(2)}) copy-start(bf16[64,576]{1,0:T(8,128)(2,1)} %param.12) | copy-start | bytes 221188
Sparse Core Ops, SparseCore 0:
  329.6 164.5 all-gather.2

commit v12 on v10

--- a/solution.py
+++ b/solution.py
@@ -296,8 +296,15 @@
     partial_out = jnp.einsum(
         "tk,wkc->twc", context, o_got, preferred_element_type=jnp.float32
     ).reshape(tok_rows, -1)
-    got_parts = gather_axis(partial_out.astype(jnp.bfloat16), "narrow")
-    return jnp.sum(got_parts.astype(jnp.float32), axis=0).astype(jnp.bfloat16)
+    out_cols = partial_out.shape[1]
+    pieces = jnp.transpose(
+        partial_out.astype(jnp.bfloat16).reshape(tok_rows, narrow_count, out_cols // narrow_count),
+        (1, 0, 2),
+    )
+    got_pieces = lax.all_to_all(pieces, "narrow", 0, 0, tiled=True)
+    mine = jnp.sum(got_pieces.astype(jnp.float32), axis=0).astype(jnp.bfloat16)
+    all_pieces = gather_axis(mine, "narrow")
+    return jnp.transpose(all_pieces, (1, 0, 2)).reshape(tok_rows, out_cols)
 
 
 def solution(mesh):

time: 445 us -> 441 us (level)
    all_to_all x1, blocking collectives: 31 us -> 12.7 us  [gather_axis(): lax.all_to_all(spread, axis_name, split_axis=0, concat_axis=0, tiled=True)]
    all_to_all x0 -> x1, blocking collectives: none -> 14.2 us  [per_device(): got_pieces = lax.all_to_all(pieces, 'narrow', 0, 0, tiled=True)]
where the time goes in v12:
time: 441 us; the launch traced here: 440 us
  waiting for transfers between devices  199 us (45%)
  Pallas kernels  76.8 us (17%)
  local copies, waits for them, and re-layouts  42.6 us (10%)
  starting transfers between devices  40 us (9%)
  blocking collectives  26.9 us (6%)
  matrix products  24.4 us (6%)
  other arithmetic  16.1 us (4%)
  between operations  13.8 us (3%)
    all_to_all x4, waiting for transfers between devices, gather_axis(): lax.all_to_all(spread, axis_name, split_axis=0, concat_axis=0, tiled=True)  142 us
    pallas_call x1, Pallas kernels, cache_attention(): pl.pallas_call(cache_kernel, grid_spec=grid_spec, out_shape=[jax.ShapeDty...  76.8 us
    all_to_all x1, waiting for transfers between devices, per_device(): lax.all_to_all(value_out.astype(jnp.bfloat16).reshape(heads_here, wide_co...  56.5 us
    all_to_all x4, starting transfers between devices, gather_axis(): lax.all_to_all(spread, axis_name, split_axis=0, concat_axis=0, tiled=True)  28 us
    all_to_all x1, blocking collectives, per_device(): got_pieces = lax.all_to_all(pieces, 'narrow', 0, 0, tiled=True)  14.2 us
    unnamed x31, local copies, waits for them, and re-layouts  13.8 us
    all_to_all x1, blocking collectives, gather_axis(): lax.all_to_all(spread, axis_name, split_axis=0, concat_axis=0, tiled=True)  12.7 us
  transfers between devices with their start and end apart: 7, of which 4 were waited for; matrix products, arithmetic and copies ran while one was open for 14% of the time, Pallas kernels for 17%

profile of v12, /device:TPU:1, one launch (start us, length us, event | category | flops | bytes accessed | tf_op | source)
XLA Modules:
  0.0 439.5 jit_solution(18150587991535041411)
XLA Ops:
  6.5 0.9 copy-done
  7.5 0.9 pad_maximum_fusion.1
  8.4 2.5 broadcast_in_dim.24
  10.9 9.5 %all-to-all-start = ((bf16[32,64,912]{2,1,0:T(8,128)(2,1)}), bf16[32,64,912]{2,1,0:T(8,128)(2,1)}, u32[]{:S(2)}, u32[]{:S(2)}) async-start(bf16[32,64,912]{2,1,0:T(8,128)(2,1)} %broadcast_in_dim.24), calls=%async_computation | async-start | bytes 8388608 | tf_op jit(solution)/shard_map/all_to_all | solution.py:47
  20.5 0.7 fusion.53
  21.2 4.8 %fusion.48 = f32[128]{0:T(128)S(1)} fusion(s32[]{:T(128)} %bitcast.6, s32[]{:T(128)} %bitcast.7, s32[]{:T(128)} %bitcast.8, s32[]{:T(128)} %bitcast.9, s32[]{:T(128)} %bitcast.10, s32[]{:T(128)} %bitcast.12, s32[]{:T(128)} %bitcast.11, s32[]{:T(128)} %bitcast.5, s32[]{:T(128)S(6)} %mul.164), kind=kLoop, calls=%fused_computation.99 | loop fusion | flops 6016 | bytes 548 | tf_op jit(solution)/shard_map/convert_element_type | solution.py:22
  26.3 53.3 %all-to-all-done = bf16[32,64,912]{2,1,0:T(8,128)(2,1)} async-done(((bf16[32,64,912]{2,1,0:T(8,128)(2,1)}), bf16[32,64,912]{2,1,0:T(8,128)(2,1)}, u32[]{:S(2)}, u32[]{:S(2)}) %all-to-all-start) | async-done | bytes 3735584 | tf_op jit(solution)/shard_map/all_to_all | solution.py:47
  79.6 1.1 broadcast_in_dim.26
  80.7 5.3 %all-to-all-start.2 = ((bf16[32,16,1024]{2,1,0:T(8,128)(2,1)}), bf16[32,16,1024]{2,1,0:T(8,128)(2,1)S(1)}, u32[]{:S(2)}, u32[]{:S(2)}) async-start(bf16[32,16,1024]{2,1,0:T(8,128)(2,1)} %broadcast_in_dim.26), calls=%async_computation.2 | async-start | bytes 2097152 | tf_op jit(solution)/shard_map/all_to_all | solution.py:47
  86.0 3.9 fusion.23
  90.1 11.9 %all-to-all-done.2 = bf16[32,16,1024]{2,1,0:T(8,128)(2,1)S(1)} async-done(((bf16[32,16,1024]{2,1,0:T(8,128)(2,1)}), bf16[32,16,1024]{2,1,0:T(8,128)(2,1)S(1)}, u32[]{:S(2)}, u32[]{:S(2)}) %all-to-all-start.2) | async-done | bytes 1048608 | tf_op jit(solution)/shard_map/all_to_all | solution.py:47
  102.0 4.1 broadcast_in_dim.25
  106.1 5.0 %all-to-all-start.1 = ((bf16[32,128,768]{1,2,0:T(8,128)(2,1)}), bf16[32,128,768]{1,2,0:T(8,128)(2,1)}, u32[]{:S(2)}, u32[]{:S(2)}) async-start(bf16[32,128,768]{1,2,0:T(8,128)(2,1)} %broadcast_in_dim.25), calls=%async_computation.1 | async-start | bytes 12582912 | tf_op jit(solution)/shard_map/all_to_all | solution.py:47
  111.2 0.7 all-gather.3.cloned.1.call-update
  111.9 8.4 %copy.53.kv_ref = bf16[8,640,576]{2,1,0:T(8,128)(2,1)} copy(bf16[8,640,576]{1,2,0:T(8,128)(2,1)} %param.16) | data formatting | bytes 11796480 | tf_op args[7]
  120.5 0.8 reshape_reshape.3
  121.3 0.4 fusion.52
  121.6 0.8 copy-done.3
  122.4 0.9 copy.88
  123.3 76.4 %all-to-all-done.1 = bf16[32,128,768]{1,2,0:T(8,128)(2,1)} async-done(((bf16[32,128,768]{1,2,0:T(8,128)(2,1)}), bf16[32,128,768]{1,2,0:T(8,128)(2,1)}, u32[]{:S(2)}, u32[]{:S(2)}) %all-to-all-start.1) | async-done | bytes 6291488 | tf_op jit(solution)/shard_map/all_to_all | solution.py:47
  199.6 6.3 %copy_bitcast_fusion = bf16[4096,768]{0,1:T(8,128)(2,1)} fusion(bf16[32,128,768]{1,2,0:T(8,128)(2,1)} %all-to-all-done.1), kind=kLoop, calls=%fused_computation.2 | loop fusion | bytes 12582912 | tf_op jit(solution)/shard_map/reshape | solution.py:226
  206.0 0.7 broadcast_in_dim.28
  206.7 8.2 %all-to-all-start.3 = ((f32[4,128,144]{1,2,0:T(8,128)}), f32[4,128,144]{1,2,0:T(8,128)S(1)}, u32[]{:S(2)}, u32[]{:S(2)}) async-start(f32[4,128,144]{1,2,0:T(8,128)} %broadcast_in_dim.28), calls=%async_computation.3 | async-start | bytes 589824 | tf_op jit(solution)/shard_map/all_to_all | solution.py:47
  214.9 2.2 slice-done.2
  217.1 8.2 %convolution_convert_fusion.lat_ref = bf16[4,4096,512]{2,1,0:T(8,128)(2,1)} fusion(bf16[4096,4,128]{0,2,1:T(8,128)(2,1)S(1)} %bitcast.114, bf16[512,4,128]{2,1,0:T(4,128)(2,1)S(1)} %get-tuple-element.21), kind=kOutput, calls=%fused_computation | convolution fusion | flops 2155872256 | bytes 21495808 | tf_op jit(solution)/shard_map/thc,lhc->htl/dot_general | solution.py:232
  225.5 3.2 copy.51
  228.7 76.8 %shard_map.91 = (f32[4,8,8,512]{3,2,1,0:T(8,128)}, f32[4,4096,128]{2,1,0:T(8,128)}) custom-call(s32[8]{0:T(128)} %lens_ref.1, s32[1]{0:T(128)} %bitcast.base_ref, bf16[4,4096,512]{2,1,0:T(8,128)(2,1)} %convolution_convert_fusion.lat_ref, bf16[4,4096,64]{2,1,0:T(8,128)(2,1)} %bitcast.116, bf16[8,640,576]{2,1,0:T(8,128)(2,1)} %copy.53.kv_ref, ...), custom_call_target="tpu_custom_call" | custom-call | tf_op jit(solution)/shard_map/pallas_call | solution.py:153
  305.5 1.5 slice_reduce_fusion
  307.5 0.3 fusion.32
  307.8 2.5 select_reduce_fusion
  310.6 2.8 fusion.21
  313.4 0.7 pad_maximum_fusion.3
  314.1 3.9 all-to-all-start.4
  318.0 3.1 fusion.17
  321.1 0.4 copy-done.2
  321.5 2.8 fusion.12
  324.2 3.9 convert_element_type.88
  328.2 2.3 copy.58
  330.4 8.1 %all-to-all-start.5 = ((bf16[4,32,128,128]{3,2,0,1:T(8,128)(2,1)}), bf16[4,32,128,128]{3,2,0,1:T(8,128)(2,1)}, u32[]{:S(2)}, u32[]{:S(2)}) async-start(bf16[4,32,128,128]{3,2,0,1:T(8,128)(2,1)} %copy.58), calls=%async_computation.5 | async-start | bytes 8388608 | tf_op jit(solution)/shard_map/all_to_all | solution.py:280
  338.6 2.4 copy.79
  340.9 1.2 copy.61
  342.2 56.5 %all-to-all-done.5 = bf16[4,32,128,128]{3,2,0,1:T(8,128)(2,1)} async-done(((bf16[4,32,128,128]{3,2,0,1:T(8,128)(2,1)}), bf16[4,32,128,128]{3,2,0,1:T(8,128)(2,1)}, u32[]{:S(2)}, u32[]{:S(2)}) %all-to-all-start.5) | async-done | bytes 4194336 | tf_op jit(solution)/shard_map/all_to_all | solution.py:280
  398.8 4.4 %multiply_reduce_fusion = f32[4,128,128]{2,1,0:T(8,128)S(1)} fusion(bf16[4,32,128,128]{3,2,0,1:T(8,128)(2,1)} %all-to-all-done.5, f32[4,32,128]{2,0,1:T(4,128)S(1)} %get-tuple-element.16), kind=kLoop, calls=%fused_computation.1 | loop fusion | flops 6225920 | bytes 4521984 | tf_op jit(solution)/shard_map/reduce_sum | solution.py:292
  403.5 0.8 convolution_convert_fusion.1
  404.4 14.2 %all_to_all.40 = bf16[4,128,512]{2,1,0:T(8,128)(2,1)S(1)} all-to-all(bf16[4,128,512]{2,1,0:T(8,128)(2,1)S(1)} %bitcast.127), channel_id=1, replica_groups=mesh['wide'=32,'narrow'=4] {'narrow'}, dimensions={0} | all-to-all | bytes 1048576 | tf_op jit(solution)/shard_map/all_to_all | solution.py:304
  418.7 12.7 %all_to_all.41 = bf16[4,128,512]{2,1,0:T(8,128)(2,1)S(1)} all-to-all(bf16[4,128,512]{2,1,0:T(8,128)(2,1)S(1)} %broadcast_in_dim.31), channel_id=1, replica_groups=mesh['wide'=32,'narrow'=4] {'narrow'}, dimensions={0} | all-to-all | bytes 1048576 | tf_op jit(solution)/shard_map/all_to_all | solution.py:47
  431.4 0.3 copy.63
  431.6 1.0 copy.64
  (65 shorter events, 2.1 us)
Async XLA Ops:
  6.5 0.9 copy-start
  10.9 9.5 %copy-start.9 = (bf16[2048]{0:T(1024)(128)(2,1)S(1)}, bf16[2048]{0:T(1024)(128)(2,1)}, u32[]{:S(2)}) copy-start(bf16[2048]{0:T(1024)(128)(2,1)} %param.10) | copy-start | bytes 12292
  10.9 9.5 %copy-start.7 = (s32[8]{0:T(128)S(1)}, s32[8]{0:T(128)}, u32[]{:S(2)}) copy-start(s32[8]{0:T(128)} %lens_ref.1) | copy-start | bytes 100
  10.9 15.1 %copy-start.5 = (bf16[128,2048]{1,0:T(8,128)(2,1)S(1)}, bf16[128,2048]{1,0:T(8,128)(2,1)}, u32[]{:S(2)}) copy-start(bf16[128,2048]{1,0:T(8,128)(2,1)} %param.9) | copy-start | bytes 1572868
  10.9 68.7 %copy-start.8 = (bf16[16,1024]{1,0:T(8,128)(2,1)S(1)}, bf16[16,1024]{1,0:T(8,128)(2,1)}, u32[]{:S(2)}) copy-start(bf16[16,1024]{1,0:T(8,128)(2,1)} %param.14) | copy-start | bytes 98308
  10.9 68.7 %all-to-all-start = ((bf16[32,64,912]{2,1,0:T(8,128)(2,1)}), bf16[32,64,912]{2,1,0:T(8,128)(2,1)}, u32[]{:S(2)}, u32[]{:S(2)}) async-start(bf16[32,64,912]{2,1,0:T(8,128)(2,1)} %broadcast_in_dim.24), calls=%async_computation | async-start | bytes 8388608 | tf_op jit(solution)/shard_map/all_to_all | solution.py:47
  80.7 21.3 %all-to-all-start.2 = ((bf16[32,16,1024]{2,1,0:T(8,128)(2,1)}), bf16[32,16,1024]{2,1,0:T(8,128)(2,1)S(1)}, u32[]{:S(2)}, u32[]{:S(2)}) async-start(bf16[32,16,1024]{2,1,0:T(8,128)(2,1)} %broadcast_in_dim.26), calls=%async_computation.2 | async-start | bytes 2097152 | tf_op jit(solution)/shard_map/all_to_all | solution.py:47
  90.0 33.3 %copy-start.6 = (f32[128,912]{0,1:T(8,128)}, f32[128,912]{0,1:T(8,128)S(1)}, u32[]{:S(2)}) copy-start(f32[128,912]{0,1:T(8,128)S(1)} %fusion.23) | copy-start | bytes 1400836
  106.1 5.8 %copy-start.10 = (bf16[512]{0:T(512)(128)(2,1)S(1)}, bf16[512]{0:T(512)(128)(2,1)}, u32[]{:S(2)}) copy-start(bf16[512]{0:T(512)(128)(2,1)} %param.13) | copy-start | bytes 3076
  106.1 93.6 %all-to-all-start.1 = ((bf16[32,128,768]{1,2,0:T(8,128)(2,1)}), bf16[32,128,768]{1,2,0:T(8,128)(2,1)}, u32[]{:S(2)}, u32[]{:S(2)}) async-start(bf16[32,128,768]{1,2,0:T(8,128)(2,1)} %broadcast_in_dim.25), calls=%async_computation.1 | async-start | bytes 12582912 | tf_op jit(solution)/shard_map/all_to_all | solution.py:47
  111.1 227.5 %all-gather.3.cloned.1.call-start = ((), (), s32[]{:S(2)}) async-start(), calls=%async_computation.8 | async-start | bytes 2162688 | tf_op jit(solution)/shard_map/all_gather | solution.py:192
  121.6 0.8 copy-start.3
  123.3 82.7 %slice-start.3 = ((f32[128,912]{0,1:T(8,128)}), f32[128,144]{0,1:T(8,128)S(1)}, s32[]{:S(2)}) async-start(f32[128,912]{0,1:T(8,128)} %copy-done.6), calls=%async_computation.12 | async-start | bytes 147456 | tf_op jit(solution)/shard_map/slice | solution.py:197
  206.7 100.5 %all-to-all-start.3 = ((f32[4,128,144]{1,2,0:T(8,128)}), f32[4,128,144]{1,2,0:T(8,128)S(1)}, u32[]{:S(2)}, u32[]{:S(2)}) async-start(f32[4,128,144]{1,2,0:T(8,128)} %broadcast_in_dim.28), calls=%async_computation.3 | async-start | bytes 589824 | tf_op jit(solution)/shard_map/all_to_all | solution.py:47
  214.9 2.2 slice-start.2
  214.9 10.4 %slice-start = ((s8[6291456]{0:T(1024)(128)(4,1)}), s8[4194304]{0:T(1024)(128)(4,1)S(1)}, s32[]{:S(2)}) async-start(s8[6291456]{0:T(1024)(128)(4,1)} %bitcast.112), calls=%async_computation.9 | async-start | bytes 8388608
  217.1 8.2 %slice-start.1 = ((s8[6291456]{0:T(1024)(128)(4,1)}), s8[2097152]{0:T(1024)(128)(4,1)S(1)}, s32[]{:S(2)}) async-start(s8[6291456]{0:T(1024)(128)(4,1)} %bitcast.112), calls=%async_computation.10 | async-start | bytes 4194304
  310.4 7.6 %copy-start.4 = (bf16[512,4,128]{2,1,0:T(4,128)(2,1)S(1)}, bf16[512,4,128]{2,1,0:T(4,128)(2,1)}, u32[]{:S(2)}) copy-start(bf16[512,4,128]{2,1,0:T(4,128)(2,1)} %copy-done.3) | copy-start | bytes 1572868
  314.1 16.3 %all-to-all-start.4 = ((bf16[2,4,32,128]{3,1,0,2:T(4,128)(2,1)}), bf16[2,4,32,128]{3,1,0,2:T(4,128)(2,1)S(1)}, u32[]{:S(2)}, u32[]{:S(2)}) async-start(bf16[2,4,32,128]{3,1,0,2:T(4,128)(2,1)} %pad_maximum_fusion.3), calls=%async_computation.4 | async-start | bytes 131072 | tf_op jit(solution)/shard_map/all_to_all | solution.py:277
  318.0 3.5 copy-start.2
  330.4 68.3 %all-to-all-start.5 = ((bf16[4,32,128,128]{3,2,0,1:T(8,128)(2,1)}), bf16[4,32,128,128]{3,2,0,1:T(8,128)(2,1)}, u32[]{:S(2)}, u32[]{:S(2)}) async-start(bf16[4,32,128,128]{3,2,0,1:T(8,128)(2,1)} %copy.58), calls=%async_computation.5 | async-start | bytes 8388608 | tf_op jit(solution)/shard_map/all_to_all | solution.py:280
  403.5 29.2 %copy-start.1 = (bf16[64,576]{1,0:T(8,128)(2,1)S(1)}, bf16[64,576]{1,0:T(8,128)(2,1)}, u32[]{:S(2)}) copy-start(bf16[64,576]{1,0:T(8,128)(2,1)} %param.12) | copy-start | bytes 221188
Sparse Core Ops, SparseCore 0:
  113.6 186.7 all-gather.2

commit v13 on v12

--- a/solution.py
+++ b/solution.py
@@ -185,10 +185,14 @@
     kva_cols = kva_weight.shape[1]
     kva_part = kva_cols // narrow_count
     kva_mine = lax.dynamic_slice_in_dim(kva_weight, narrow_place * kva_part, kva_part, 1)
-    packed = jnp.concatenate([q_weight, kva_mine], axis=1)
+    kvb_rows, kvb_cols = kvb_weight.shape
+    w_rows = q_weight.shape[0]
+    packed = jnp.concatenate(
+        [q_weight, kva_mine, kvb_weight.reshape(w_rows, kvb_rows * kvb_cols // w_rows)], axis=1
+    )
     got_weights = gather_axis(packed, "wide")
-    proj_full = got_weights.reshape(-1, q_cols + kva_part)
-    kvb_full = gather_axis(kvb_weight, "wide").reshape(-1, kvb_weight.shape[1])
+    proj_full = got_weights[:, :, : q_cols + kva_part].reshape(-1, q_cols + kva_part)
+    kvb_full = got_weights[:, :, q_cols + kva_part :].reshape(-1, kvb_cols)
     o_got = lax.all_gather(o_weight, "wide", axis=0, tiled=False)
 
     normed = scaled_norm(hidden.astype(jnp.float32), attn_gain).astype(jnp.bfloat16)

time: 441 us -> 445 us (level)
    slice x0 -> x2, local copies, waits for them, and re-layouts: none -> 4.48 us  [the longest x1 2.63 us: per_device(): got_weights[:, :, :q_cols + kva_part].reshape(-1, q_cols + kva_part)]
    unnamed x31 -> x29, local copies, waits for them, and re-layouts: 13.8 us -> 13.1 us
    all_to_all x4 -> x3, starting transfers between devices: 28 us -> 27.9 us  [gather_axis(): lax.all_to_all(spread, axis_name, split_axis=0, concat_axis=0, tiled=True)]
    all_to_all x4 -> x3, waiting for transfers between devices: 142 us -> 141 us  [gather_axis(): lax.all_to_all(spread, axis_name, split_axis=0, concat_axis=0, tiled=True)]
  transfers between devices with their start and end apart: 7 -> 6, of which waited for: 4 -> 3; matrix products, arithmetic and copies ran while one was open for 14% -> 14% of each run, Pallas kernels for 17% -> 17%
where the time goes in v13:
time: 445 us; the launch traced here: 444 us
  waiting for transfers between devices  198 us (44%)
  Pallas kernels  76.9 us (17%)
  local copies, waits for them, and re-layouts  46.9 us (11%)
  starting transfers between devices  43.4 us (10%)
  blocking collectives  27.6 us (6%)
  matrix products  22.3 us (5%)
  other arithmetic  15.4 us (3%)
  between operations  13.8 us (3%)
    all_to_all x3, waiting for transfers between devices, gather_axis(): lax.all_to_all(spread, axis_name, split_axis=0, concat_axis=0, tiled=True)  141 us
    pallas_call x1, Pallas kernels, cache_attention(): pl.pallas_call(cache_kernel, grid_spec=grid_spec, out_shape=[jax.ShapeDty...  76.9 us
    all_to_all x1, waiting for transfers between devices, per_device(): lax.all_to_all(value_out.astype(jnp.bfloat16).reshape(heads_here, wide_co...  55.5 us
    all_to_all x3, starting transfers between devices, gather_axis(): lax.all_to_all(spread, axis_name, split_axis=0, concat_axis=0, tiled=True)  27.9 us
    all_to_all x1, blocking collectives, per_device(): got_pieces = lax.all_to_all(pieces, 'narrow', 0, 0, tiled=True)  14.9 us
    unnamed x29, local copies, waits for them, and re-layouts  13.1 us
    all_to_all x1, blocking collectives, gather_axis(): lax.all_to_all(spread, axis_name, split_axis=0, concat_axis=0, tiled=True)  12.7 us
  transfers between devices with their start and end apart: 6, of which 3 were waited for; matrix products, arithmetic and copies ran while one was open for 14% of the time, Pallas kernels for 17%

profile of v13, /device:TPU:1, one launch (start us, length us, event | category | flops | bytes accessed | tf_op | source)
XLA Modules:
  0.0 444.0 jit_solution(2572831163163888548)
XLA Ops:
  6.5 0.8 reshape.283
  7.5 1.0 concatenate.16
  8.5 2.9 broadcast_in_dim.22
  11.4 9.5 %all-to-all-start = ((bf16[32,64,1168]{2,1,0:T(8,128)(2,1)}), bf16[32,64,1168]{2,1,0:T(8,128)(2,1)}, u32[]{:S(2)}, u32[]{:S(2)}) async-start(bf16[32,64,1168]{2,1,0:T(8,128)(2,1)} %broadcast_in_dim.22), calls=%async_computation | async-start | bytes 10485760 | tf_op jit(solution)/shard_map/all_to_all | solution.py:47
  20.9 0.7 fusion.53
  21.6 5.0 %fusion.48 = f32[128]{0:T(128)S(1)} fusion(s32[]{:T(128)} %bitcast.6, s32[]{:T(128)} %bitcast.7, s32[]{:T(128)} %bitcast.8, s32[]{:T(128)} %bitcast.9, s32[]{:T(128)} %bitcast.10, s32[]{:T(128)} %bitcast.12, s32[]{:T(128)} %bitcast.11, s32[]{:T(128)} %bitcast.5, s32[]{:T(128)S(6)} %mul.164), kind=kLoop, calls=%fused_computation.98 | loop fusion | flops 6016 | bytes 548 | tf_op jit(solution)/shard_map/convert_element_type | solution.py:22
  27.0 67.8 %all-to-all-done = bf16[32,64,1168]{2,1,0:T(8,128)(2,1)} async-done(((bf16[32,64,1168]{2,1,0:T(8,128)(2,1)}), bf16[32,64,1168]{2,1,0:T(8,128)(2,1)}, u32[]{:S(2)}, u32[]{:S(2)}) %all-to-all-start) | async-done | bytes 4784160 | tf_op jit(solution)/shard_map/all_to_all | solution.py:47
  94.8 2.6 slice.89
  97.4 1.8 fusion.23
  99.4 4.1 broadcast_in_dim.23
  103.4 9.6 %all-to-all-start.1 = ((bf16[32,128,768]{1,2,0:T(8,128)(2,1)}), bf16[32,128,768]{1,2,0:T(8,128)(2,1)}, u32[]{:S(2)}, u32[]{:S(2)}) async-start(bf16[32,128,768]{1,2,0:T(8,128)(2,1)} %broadcast_in_dim.23), calls=%async_computation.1 | async-start | bytes 12582912 | tf_op jit(solution)/shard_map/all_to_all | solution.py:47
  113.1 0.7 all-gather.3.cloned.1.call-update
  113.9 8.5 %copy.53.kv_ref = bf16[8,640,576]{2,1,0:T(8,128)(2,1)} copy(bf16[8,640,576]{1,2,0:T(8,128)(2,1)} %param.16) | data formatting | bytes 11796480 | tf_op args[7]
  122.5 1.8 slice.97
  124.3 0.3 reshape_reshape.3
  124.6 0.4 fusion.52
  125.0 0.8 copy-done.3
  125.8 0.9 copy.88
  126.6 73.6 %all-to-all-done.1 = bf16[32,128,768]{1,2,0:T(8,128)(2,1)} async-done(((bf16[32,128,768]{1,2,0:T(8,128)(2,1)}), bf16[32,128,768]{1,2,0:T(8,128)(2,1)}, u32[]{:S(2)}, u32[]{:S(2)}) %all-to-all-start.1) | async-done | bytes 6291488 | tf_op jit(solution)/shard_map/all_to_all | solution.py:47
  200.3 6.4 %copy_bitcast_fusion = bf16[4096,768]{0,1:T(8,128)(2,1)} fusion(bf16[32,128,768]{1,2,0:T(8,128)(2,1)} %all-to-all-done.1), kind=kLoop, calls=%fused_computation.2 | loop fusion | bytes 12582912 | tf_op jit(solution)/shard_map/reshape | solution.py:230
  206.6 0.7 broadcast_in_dim.25
  207.4 8.8 %all-to-all-start.2 = ((f32[4,128,144]{1,2,0:T(8,128)}), f32[4,128,144]{1,2,0:T(8,128)S(1)}, u32[]{:S(2)}, u32[]{:S(2)}) async-start(f32[4,128,144]{1,2,0:T(8,128)} %broadcast_in_dim.25), calls=%async_computation.2 | async-start | bytes 589824 | tf_op jit(solution)/shard_map/all_to_all | solution.py:47
  216.2 2.2 slice-done.2
  218.4 8.1 %convolution_convert_fusion.lat_ref = bf16[4,4096,512]{2,1,0:T(8,128)(2,1)} fusion(bf16[4096,4,128]{0,2,1:T(8,128)(2,1)S(1)} %bitcast.114, bf16[512,4,128]{2,1,0:T(4,128)(2,1)S(1)} %get-tuple-element.21), kind=kOutput, calls=%fused_computation | convolution fusion | flops 2155872256 | bytes 21495808 | tf_op jit(solution)/shard_map/thc,lhc->htl/dot_general | solution.py:236
  226.8 3.2 copy.51
  229.9 76.9 %shard_map.91 = (f32[4,8,8,512]{3,2,1,0:T(8,128)}, f32[4,4096,128]{2,1,0:T(8,128)}) custom-call(s32[8]{0:T(128)} %lens_ref.1, s32[1]{0:T(128)} %bitcast.base_ref, bf16[4,4096,512]{2,1,0:T(8,128)(2,1)} %convolution_convert_fusion.lat_ref, bf16[4,4096,64]{2,1,0:T(8,128)(2,1)} %bitcast.117, bf16[8,640,576]{2,1,0:T(8,128)(2,1)} %copy.53.kv_ref, ...), custom_call_target="tpu_custom_call" | custom-call | tf_op jit(solution)/shard_map/pallas_call | solution.py:153
  306.8 1.5 slice_reduce_fusion
  308.8 0.3 fusion.32
  309.1 2.6 select_reduce_fusion
  311.7 0.2 fusion.20
  311.9 2.8 fusion.21
  314.7 0.7 pad_maximum_fusion.2
  315.4 7.4 %all-to-all-start.3 = ((bf16[2,4,32,128]{3,1,0,2:T(4,128)(2,1)}), bf16[2,4,32,128]{3,1,0,2:T(4,128)(2,1)S(1)}, u32[]{:S(2)}, u32[]{:S(2)}) async-start(bf16[2,4,32,128]{3,1,0,2:T(4,128)(2,1)} %pad_maximum_fusion.2), calls=%async_computation.3 | async-start | bytes 131072 | tf_op jit(solution)/shard_map/all_to_all | solution.py:281
  322.8 3.0 fusion.17
  325.9 0.4 copy-done.2
  326.3 2.8 fusion.12
  329.0 3.9 convert_element_type.88
  333.0 2.3 copy.58
  335.3 8.1 %all-to-all-start.4 = ((bf16[4,32,128,128]{3,2,0,1:T(8,128)(2,1)}), bf16[4,32,128,128]{3,2,0,1:T(8,128)(2,1)}, u32[]{:S(2)}, u32[]{:S(2)}) async-start(bf16[4,32,128,128]{3,2,0,1:T(8,128)(2,1)} %copy.58), calls=%async_computation.4 | async-start | bytes 8388608 | tf_op jit(solution)/shard_map/all_to_all | solution.py:284
  343.4 2.4 copy.79
  345.7 1.2 copy.61
  347.0 55.5 %all-to-all-done.4 = bf16[4,32,128,128]{3,2,0,1:T(8,128)(2,1)} async-done(((bf16[4,32,128,128]{3,2,0,1:T(8,128)(2,1)}), bf16[4,32,128,128]{3,2,0,1:T(8,128)(2,1)}, u32[]{:S(2)}, u32[]{:S(2)}) %all-to-all-start.4) | async-done | bytes 4194336 | tf_op jit(solution)/shard_map/all_to_all | solution.py:284
  402.6 4.4 multiply_reduce_fusion
  407.3 0.8 convolution_convert_fusion.1
  408.1 14.9 %all_to_all.35 = bf16[4,128,512]{2,1,0:T(8,128)(2,1)S(1)} all-to-all(bf16[4,128,512]{2,1,0:T(8,128)(2,1)S(1)} %bitcast.128), channel_id=1, replica_groups=mesh['wide'=32,'narrow'=4] {'narrow'}, dimensions={0} | all-to-all | bytes 1048576 | tf_op jit(solution)/shard_map/all_to_all | solution.py:308
  423.1 12.7 %all_to_all.36 = bf16[4,128,512]{2,1,0:T(8,128)(2,1)S(1)} all-to-all(bf16[4,128,512]{2,1,0:T(8,128)(2,1)S(1)} %broadcast_in_dim.28), channel_id=1, replica_groups=mesh['wide'=32,'narrow'=4] {'narrow'}, dimensions={0} | all-to-all | bytes 1048576 | tf_op jit(solution)/shard_map/all_to_all | solution.py:47
  435.9 0.3 copy.63
  436.1 1.0 copy.64
  (63 shorter events, 2.0 us)
Async XLA Ops:
  6.5 0.9 copy-start
  11.4 9.5 %copy-start.8 = (bf16[2048]{0:T(1024)(128)(2,1)S(1)}, bf16[2048]{0:T(1024)(128)(2,1)}, u32[]{:S(2)}) copy-start(bf16[2048]{0:T(1024)(128)(2,1)} %param.10) | copy-start | bytes 12292
  11.4 9.5 %copy-start.7 = (s32[8]{0:T(128)S(1)}, s32[8]{0:T(128)}, u32[]{:S(2)}) copy-start(s32[8]{0:T(128)} %lens_ref.1) | copy-start | bytes 100
  11.4 15.2 %copy-start.5 = (bf16[128,2048]{1,0:T(8,128)(2,1)S(1)}, bf16[128,2048]{1,0:T(8,128)(2,1)}, u32[]{:S(2)}) copy-start(bf16[128,2048]{1,0:T(8,128)(2,1)} %param.9) | copy-start | bytes 1572868
  11.4 83.4 %all-to-all-start = ((bf16[32,64,1168]{2,1,0:T(8,128)(2,1)}), bf16[32,64,1168]{2,1,0:T(8,128)(2,1)}, u32[]{:S(2)}, u32[]{:S(2)}) async-start(bf16[32,64,1168]{2,1,0:T(8,128)(2,1)} %broadcast_in_dim.22), calls=%async_computation | async-start | bytes 10485760 | tf_op jit(solution)/shard_map/all_to_all | solution.py:47
  99.2 23.2 %copy-start.6 = (f32[128,912]{0,1:T(8,128)}, f32[128,912]{0,1:T(8,128)S(1)}, u32[]{:S(2)}) copy-start(f32[128,912]{0,1:T(8,128)S(1)} %fusion.23) | copy-start | bytes 1400836
  103.4 10.4 %copy-start.9 = (bf16[512]{0:T(512)(128)(2,1)S(1)}, bf16[512]{0:T(512)(128)(2,1)}, u32[]{:S(2)}) copy-start(bf16[512]{0:T(512)(128)(2,1)} %param.13) | copy-start | bytes 3076
  103.4 96.8 %all-to-all-start.1 = ((bf16[32,128,768]{1,2,0:T(8,128)(2,1)}), bf16[32,128,768]{1,2,0:T(8,128)(2,1)}, u32[]{:S(2)}, u32[]{:S(2)}) async-start(bf16[32,128,768]{1,2,0:T(8,128)(2,1)} %broadcast_in_dim.23), calls=%async_computation.1 | async-start | bytes 12582912 | tf_op jit(solution)/shard_map/all_to_all | solution.py:47
  113.1 230.3 %all-gather.3.cloned.1.call-start = ((), (), s32[]{:S(2)}) async-start(), calls=%async_computation.7 | async-start | bytes 2162688 | tf_op jit(solution)/shard_map/all_gather | solution.py:196
  125.0 0.8 copy-start.3
  126.6 80.0 %slice-start.3 = ((f32[128,912]{0,1:T(8,128)}), f32[128,144]{0,1:T(8,128)S(1)}, s32[]{:S(2)}) async-start(f32[128,912]{0,1:T(8,128)} %copy-done.6), calls=%async_computation.11 | async-start | bytes 147456 | tf_op jit(solution)/shard_map/slice | solution.py:201
  207.4 101.1 %all-to-all-start.2 = ((f32[4,128,144]{1,2,0:T(8,128)}), f32[4,128,144]{1,2,0:T(8,128)S(1)}, u32[]{:S(2)}, u32[]{:S(2)}) async-start(f32[4,128,144]{1,2,0:T(8,128)} %broadcast_in_dim.25), calls=%async_computation.2 | async-start | bytes 589824 | tf_op jit(solution)/shard_map/all_to_all | solution.py:47
  216.2 2.2 slice-start.2
  216.2 10.3 %slice-start = ((s8[6291456]{0:T(1024)(128)(4,1)}), s8[4194304]{0:T(1024)(128)(4,1)S(1)}, s32[]{:S(2)}) async-start(s8[6291456]{0:T(1024)(128)(4,1)} %bitcast.112), calls=%async_computation.8 | async-start | bytes 8388608
  218.4 8.2 %slice-start.1 = ((s8[6291456]{0:T(1024)(128)(4,1)}), s8[2097152]{0:T(1024)(128)(4,1)S(1)}, s32[]{:S(2)}) async-start(s8[6291456]{0:T(1024)(128)(4,1)} %bitcast.112), calls=%async_computation.9 | async-start | bytes 4194304
  311.7 11.1 %copy-start.4 = (bf16[512,4,128]{2,1,0:T(4,128)(2,1)S(1)}, bf16[512,4,128]{2,1,0:T(4,128)(2,1)}, u32[]{:S(2)}) copy-start(bf16[512,4,128]{2,1,0:T(4,128)(2,1)} %copy-done.3) | copy-start | bytes 1572868
  315.4 19.8 %all-to-all-start.3 = ((bf16[2,4,32,128]{3,1,0,2:T(4,128)(2,1)}), bf16[2,4,32,128]{3,1,0,2:T(4,128)(2,1)S(1)}, u32[]{:S(2)}, u32[]{:S(2)}) async-start(bf16[2,4,32,128]{3,1,0,2:T(4,128)(2,1)} %pad_maximum_fusion.2), calls=%async_computation.3 | async-start | bytes 131072 | tf_op jit(solution)/shard_map/all_to_all | solution.py:281
  322.8 3.5 copy-start.2
  335.3 67.3 %all-to-all-start.4 = ((bf16[4,32,128,128]{3,2,0,1:T(8,128)(2,1)}), bf16[4,32,128,128]{3,2,0,1:T(8,128)(2,1)}, u32[]{:S(2)}, u32[]{:S(2)}) async-start(bf16[4,32,128,128]{3,2,0,1:T(8,128)(2,1)} %copy.58), calls=%async_computation.4 | async-start | bytes 8388608 | tf_op jit(solution)/shard_map/all_to_all | solution.py:284
  407.3 29.9 %copy-start.1 = (bf16[64,576]{1,0:T(8,128)(2,1)S(1)}, bf16[64,576]{1,0:T(8,128)(2,1)}, u32[]{:S(2)}) copy-start(bf16[64,576]{1,0:T(8,128)(2,1)} %param.12) | copy-start | bytes 221188
Sparse Core Ops, SparseCore 0:
  115.5 188.7 all-gather.2

commit v14 on v12

--- a/solution.py
+++ b/solution.py
@@ -10,6 +10,7 @@
 VDIM = 128
 LAT = 512
 SPAN = 512
+HEADS_PER_STEP = 2
 
 
 eps = 1e-06
@@ -98,15 +99,14 @@
     base = base_ref[0]
     live_block = base < length_now
 
-    @pl.when(live_block)
-    def _():
+    def one_head(j):
         keys = kv_ref[0]
         key_lat = keys[:, :LAT]
         key_rope = keys[:, LAT:]
         nt = (((1,), (1,)), ((), ()))
         scores = (
-            lax.dot_general(lat_ref[0], key_lat, nt, preferred_element_type=jnp.float32)
-            + lax.dot_general(rope_ref[0], key_rope, nt, preferred_element_type=jnp.float32)
+            lax.dot_general(lat_ref[j], key_lat, nt, preferred_element_type=jnp.float32)
+            + lax.dot_general(rope_ref[j], key_rope, nt, preferred_element_type=jnp.float32)
         ) * score_scale
         slots = base + lax.broadcasted_iota(jnp.int32, scores.shape, 1)
         live = slots < length_now
@@ -115,14 +115,19 @@
         total = jnp.sum(weights, axis=-1, keepdims=True)
         lane = lax.broadcasted_iota(jnp.int32, (peak.shape[0], 128), 1)
         packed = jnp.where(lane == 0, peak, jnp.where(lane == 1, total, 0.0))
-        stats_ref[0, 0] = jnp.transpose(packed)[: stats_ref.shape[2]]
+        stats_ref[j, 0] = jnp.transpose(packed)[: stats_ref.shape[2]]
         mixed = jnp.dot(weights.astype(jnp.bfloat16), key_lat, preferred_element_type=jnp.float32)
-        value_map = vm_ref[0]
+        value_map = vm_ref[j]
         upper_part = mixed.astype(jnp.bfloat16)
         lower_part = (mixed - upper_part.astype(jnp.float32)).astype(jnp.bfloat16)
-        value_ref[0] = jnp.dot(upper_part, value_map, preferred_element_type=jnp.float32) + jnp.dot(
+        value_ref[j] = jnp.dot(upper_part, value_map, preferred_element_type=jnp.float32) + jnp.dot(
             lower_part, value_map, preferred_element_type=jnp.float32
         )
+
+    @pl.when(live_block)
+    def _():
+        for j in range(lat_ref.shape[0]):
+            one_head(j)
 
     @pl.when(jnp.logical_not(live_block))
     def _():
@@ -138,16 +143,16 @@
     vdim = value_hm.shape[2]
     grid_spec = pltpu.PrefetchScalarGridSpec(
         num_scalar_prefetch=2,
-        grid=(requests, heads_here),
+        grid=(requests, heads_here // HEADS_PER_STEP),
         in_specs=[
-            pl.BlockSpec((1, span, LAT), lambda r, h, lens, b: (h, r, 0)),
-            pl.BlockSpec((1, span, ROPE), lambda r, h, lens, b: (h, r, 0)),
+            pl.BlockSpec((HEADS_PER_STEP, span, LAT), lambda r, h, lens, b: (h, r, 0)),
+            pl.BlockSpec((HEADS_PER_STEP, span, ROPE), lambda r, h, lens, b: (h, r, 0)),
             pl.BlockSpec((1, cache_rows, width), lambda r, h, lens, b: (r, 0, 0)),
-            pl.BlockSpec((1, LAT, vdim), lambda r, h, lens, b: (h, 0, 0)),
+            pl.BlockSpec((HEADS_PER_STEP, LAT, vdim), lambda r, h, lens, b: (h, 0, 0)),
         ],
         out_specs=[
-            pl.BlockSpec((1, 1, 8, span), lambda r, h, lens, b: (h, r, 0, 0)),
-            pl.BlockSpec((1, span, vdim), lambda r, h, lens, b: (h, r, 0)),
+            pl.BlockSpec((HEADS_PER_STEP, 1, 8, span), lambda r, h, lens, b: (h, r, 0, 0)),
+            pl.BlockSpec((HEADS_PER_STEP, span, vdim), lambda r, h, lens, b: (h, r, 0)),
         ],
     )
     return pl.pallas_call(

time: 441 us -> 425 us (0.964)
  Pallas kernels: 76.8 us -> 61.2 us
    pallas_call x1, Pallas kernels: 76.8 us -> 61.2 us  [cache_attention(): pl.pallas_call(cache_kernel, grid_spec=grid_spec, out_shape=[jax.ShapeDty...]
  transfers between devices with their start and end apart: 7 -> 7, of which waited for: 4 -> 4; matrix products, arithmetic and copies ran while one was open for 14% -> 15% of each run, Pallas kernels for 17% -> 14%
where the time goes in v14:
time: 425 us; the launch traced here: 424 us
  waiting for transfers between devices  199 us (47%)
  Pallas kernels  61.2 us (14%)
  local copies, waits for them, and re-layouts  42.6 us (10%)
  starting transfers between devices  40 us (9%)
  blocking collectives  26.8 us (6%)
  matrix products  24.4 us (6%)
  other arithmetic  16.1 us (4%)
  between operations  13.8 us (3%)
    all_to_all x4, waiting for transfers between devices, gather_axis(): lax.all_to_all(spread, axis_name, split_axis=0, concat_axis=0, tiled=True)  142 us
    pallas_call x1, Pallas kernels, cache_attention(): pl.pallas_call(cache_kernel, grid_spec=grid_spec, out_shape=[jax.ShapeDty...  61.2 us
    all_to_all x1, waiting for transfers between devices, per_device(): lax.all_to_all(value_out.astype(jnp.bfloat16).reshape(heads_here, wide_co...  56.6 us
    all_to_all x4, starting transfers between devices, gather_axis(): lax.all_to_all(spread, axis_name, split_axis=0, concat_axis=0, tiled=True)  28 us
    all_to_all x1, blocking collectives, per_device(): got_pieces = lax.all_to_all(pieces, 'narrow', 0, 0, tiled=True)  14.1 us
    unnamed x31, local copies, waits for them, and re-layouts  13.9 us
    all_to_all x1, blocking collectives, gather_axis(): lax.all_to_all(spread, axis_name, split_axis=0, concat_axis=0, tiled=True)  12.7 us
  transfers between devices with their start and end apart: 7, of which 4 were waited for; matrix products, arithmetic and copies ran while one was open for 15% of the time, Pallas kernels for 14%

profile of v14, /device:TPU:1, one launch (start us, length us, event | category | flops | bytes accessed | tf_op | source)
XLA Modules:
  0.0 423.9 jit_solution(14260229910831241409)
XLA Ops:
  6.5 0.9 copy-done
  7.5 0.9 pad_maximum_fusion.1
  8.4 2.5 broadcast_in_dim.24
  10.9 9.5 %all-to-all-start = ((bf16[32,64,912]{2,1,0:T(8,128)(2,1)}), bf16[32,64,912]{2,1,0:T(8,128)(2,1)}, u32[]{:S(2)}, u32[]{:S(2)}) async-start(bf16[32,64,912]{2,1,0:T(8,128)(2,1)} %broadcast_in_dim.24), calls=%async_computation | async-start | bytes 8388608 | tf_op jit(solution)/shard_map/all_to_all | solution.py:48
  20.5 0.7 fusion.53
  21.2 4.8 %fusion.48 = f32[128]{0:T(128)S(1)} fusion(s32[]{:T(128)} %bitcast.6, s32[]{:T(128)} %bitcast.7, s32[]{:T(128)} %bitcast.8, s32[]{:T(128)} %bitcast.9, s32[]{:T(128)} %bitcast.10, s32[]{:T(128)} %bitcast.12, s32[]{:T(128)} %bitcast.11, s32[]{:T(128)} %bitcast.5, s32[]{:T(128)S(6)} %mul.164), kind=kLoop, calls=%fused_computation.99 | loop fusion | flops 6016 | bytes 548 | tf_op jit(solution)/shard_map/convert_element_type | solution.py:23
  26.3 53.3 %all-to-all-done = bf16[32,64,912]{2,1,0:T(8,128)(2,1)} async-done(((bf16[32,64,912]{2,1,0:T(8,128)(2,1)}), bf16[32,64,912]{2,1,0:T(8,128)(2,1)}, u32[]{:S(2)}, u32[]{:S(2)}) %all-to-all-start) | async-done | bytes 3735584 | tf_op jit(solution)/shard_map/all_to_all | solution.py:48
  79.6 1.1 broadcast_in_dim.26
  80.7 5.3 %all-to-all-start.2 = ((bf16[32,16,1024]{2,1,0:T(8,128)(2,1)}), bf16[32,16,1024]{2,1,0:T(8,128)(2,1)S(1)}, u32[]{:S(2)}, u32[]{:S(2)}) async-start(bf16[32,16,1024]{2,1,0:T(8,128)(2,1)} %broadcast_in_dim.26), calls=%async_computation.2 | async-start | bytes 2097152 | tf_op jit(solution)/shard_map/all_to_all | solution.py:48
  86.0 3.9 fusion.23
  90.1 11.9 %all-to-all-done.2 = bf16[32,16,1024]{2,1,0:T(8,128)(2,1)S(1)} async-done(((bf16[32,16,1024]{2,1,0:T(8,128)(2,1)}), bf16[32,16,1024]{2,1,0:T(8,128)(2,1)S(1)}, u32[]{:S(2)}, u32[]{:S(2)}) %all-to-all-start.2) | async-done | bytes 1048608 | tf_op jit(solution)/shard_map/all_to_all | solution.py:48
  102.0 4.1 broadcast_in_dim.25
  106.1 5.0 %all-to-all-start.1 = ((bf16[32,128,768]{1,2,0:T(8,128)(2,1)}), bf16[32,128,768]{1,2,0:T(8,128)(2,1)}, u32[]{:S(2)}, u32[]{:S(2)}) async-start(bf16[32,128,768]{1,2,0:T(8,128)(2,1)} %broadcast_in_dim.25), calls=%async_computation.1 | async-start | bytes 12582912 | tf_op jit(solution)/shard_map/all_to_all | solution.py:48
  111.2 0.7 all-gather.3.cloned.1.call-update
  111.9 8.4 %copy.53.kv_ref = bf16[8,640,576]{2,1,0:T(8,128)(2,1)} copy(bf16[8,640,576]{1,2,0:T(8,128)(2,1)} %param.16) | data formatting | bytes 11796480 | tf_op args[7]
  120.5 0.8 reshape_reshape.3
  121.3 0.4 fusion.52
  121.6 0.8 copy-done.3
  122.4 0.9 copy.88
  123.3 76.4 %all-to-all-done.1 = bf16[32,128,768]{1,2,0:T(8,128)(2,1)} async-done(((bf16[32,128,768]{1,2,0:T(8,128)(2,1)}), bf16[32,128,768]{1,2,0:T(8,128)(2,1)}, u32[]{:S(2)}, u32[]{:S(2)}) %all-to-all-start.1) | async-done | bytes 6291488 | tf_op jit(solution)/shard_map/all_to_all | solution.py:48
  199.6 6.3 %copy_bitcast_fusion = bf16[4096,768]{0,1:T(8,128)(2,1)} fusion(bf16[32,128,768]{1,2,0:T(8,128)(2,1)} %all-to-all-done.1), kind=kLoop, calls=%fused_computation.2 | loop fusion | bytes 12582912 | tf_op jit(solution)/shard_map/reshape | solution.py:231
  206.0 0.7 broadcast_in_dim.28
  206.7 8.2 %all-to-all-start.3 = ((f32[4,128,144]{1,2,0:T(8,128)}), f32[4,128,144]{1,2,0:T(8,128)S(1)}, u32[]{:S(2)}, u32[]{:S(2)}) async-start(f32[4,128,144]{1,2,0:T(8,128)} %broadcast_in_dim.28), calls=%async_computation.3 | async-start | bytes 589824 | tf_op jit(solution)/shard_map/all_to_all | solution.py:48
  214.9 2.2 slice-done.2
  217.1 8.2 %convolution_convert_fusion.lat_ref = bf16[4,4096,512]{2,1,0:T(8,128)(2,1)} fusion(bf16[4096,4,128]{0,2,1:T(8,128)(2,1)S(1)} %bitcast.114, bf16[512,4,128]{2,1,0:T(4,128)(2,1)S(1)} %get-tuple-element.21), kind=kOutput, calls=%fused_computation | convolution fusion | flops 2155872256 | bytes 21495808 | tf_op jit(solution)/shard_map/thc,lhc->htl/dot_general | solution.py:237
  225.5 3.2 copy.51
  228.7 61.2 %shard_map.91 = (f32[4,8,8,512]{3,2,1,0:T(8,128)}, f32[4,4096,128]{2,1,0:T(8,128)}) custom-call(s32[8]{0:T(128)} %lens_ref.1, s32[1]{0:T(128)} %bitcast.base_ref, bf16[4,4096,512]{2,1,0:T(8,128)(2,1)} %convolution_convert_fusion.lat_ref, bf16[4,4096,64]{2,1,0:T(8,128)(2,1)} %bitcast.116, bf16[8,640,576]{2,1,0:T(8,128)(2,1)} %copy.53.kv_ref, ...), custom_call_target="tpu_custom_call" | custom-call | tf_op jit(solution)/shard_map/pallas_call | solution.py:158
  289.9 1.5 slice_reduce_fusion
  291.8 0.3 fusion.32
  292.2 2.6 select_reduce_fusion
  295.0 2.8 fusion.21
  297.8 0.7 pad_maximum_fusion.3
  298.5 3.9 all-to-all-start.4
  302.4 3.0 fusion.17
  305.4 0.4 copy-done.2
  305.8 2.8 fusion.12
  308.6 3.9 convert_element_type.88
  312.5 2.3 copy.58
  314.8 8.1 %all-to-all-start.5 = ((bf16[4,32,128,128]{3,2,0,1:T(8,128)(2,1)}), bf16[4,32,128,128]{3,2,0,1:T(8,128)(2,1)}, u32[]{:S(2)}, u32[]{:S(2)}) async-start(bf16[4,32,128,128]{3,2,0,1:T(8,128)(2,1)} %copy.58), calls=%async_computation.5 | async-start | bytes 8388608 | tf_op jit(solution)/shard_map/all_to_all | solution.py:285
  322.9 2.4 copy.79
  325.3 1.2 copy.61
  326.6 56.6 %all-to-all-done.5 = bf16[4,32,128,128]{3,2,0,1:T(8,128)(2,1)} async-done(((bf16[4,32,128,128]{3,2,0,1:T(8,128)(2,1)}), bf16[4,32,128,128]{3,2,0,1:T(8,128)(2,1)}, u32[]{:S(2)}, u32[]{:S(2)}) %all-to-all-start.5) | async-done | bytes 4194336 | tf_op jit(solution)/shard_map/all_to_all | solution.py:285
  383.2 4.4 %multiply_reduce_fusion = f32[4,128,128]{2,1,0:T(8,128)S(1)} fusion(bf16[4,32,128,128]{3,2,0,1:T(8,128)(2,1)} %all-to-all-done.5, f32[4,32,128]{2,0,1:T(4,128)S(1)} %get-tuple-element.16), kind=kLoop, calls=%fused_computation.1 | loop fusion | flops 6225920 | bytes 4521984 | tf_op jit(solution)/shard_map/reduce_sum | solution.py:297
  387.9 0.8 convolution_convert_fusion.1
  388.8 14.1 %all_to_all.40 = bf16[4,128,512]{2,1,0:T(8,128)(2,1)S(1)} all-to-all(bf16[4,128,512]{2,1,0:T(8,128)(2,1)S(1)} %bitcast.127), channel_id=1, replica_groups=mesh['wide'=32,'narrow'=4] {'narrow'}, dimensions={0} | all-to-all | bytes 1048576 | tf_op jit(solution)/shard_map/all_to_all | solution.py:309
  403.0 12.7 %all_to_all.41 = bf16[4,128,512]{2,1,0:T(8,128)(2,1)S(1)} all-to-all(bf16[4,128,512]{2,1,0:T(8,128)(2,1)S(1)} %broadcast_in_dim.31), channel_id=1, replica_groups=mesh['wide'=32,'narrow'=4] {'narrow'}, dimensions={0} | all-to-all | bytes 1048576 | tf_op jit(solution)/shard_map/all_to_all | solution.py:48
  415.8 0.3 copy.63
  416.0 1.0 copy.64
  (65 shorter events, 2.1 us)
Async XLA Ops:
  6.5 0.9 copy-start
  10.9 9.5 %copy-start.9 = (bf16[2048]{0:T(1024)(128)(2,1)S(1)}, bf16[2048]{0:T(1024)(128)(2,1)}, u32[]{:S(2)}) copy-start(bf16[2048]{0:T(1024)(128)(2,1)} %param.10) | copy-start | bytes 12292
  10.9 9.5 %copy-start.7 = (s32[8]{0:T(128)S(1)}, s32[8]{0:T(128)}, u32[]{:S(2)}) copy-start(s32[8]{0:T(128)} %lens_ref.1) | copy-start | bytes 100
  10.9 15.1 %copy-start.5 = (bf16[128,2048]{1,0:T(8,128)(2,1)S(1)}, bf16[128,2048]{1,0:T(8,128)(2,1)}, u32[]{:S(2)}) copy-start(bf16[128,2048]{1,0:T(8,128)(2,1)} %param.9) | copy-start | bytes 1572868
  10.9 68.7 %copy-start.8 = (bf16[16,1024]{1,0:T(8,128)(2,1)S(1)}, bf16[16,1024]{1,0:T(8,128)(2,1)}, u32[]{:S(2)}) copy-start(bf16[16,1024]{1,0:T(8,128)(2,1)} %param.14) | copy-start | bytes 98308
  10.9 68.7 %all-to-all-start = ((bf16[32,64,912]{2,1,0:T(8,128)(2,1)}), bf16[32,64,912]{2,1,0:T(8,128)(2,1)}, u32[]{:S(2)}, u32[]{:S(2)}) async-start(bf16[32,64,912]{2,1,0:T(8,128)(2,1)} %broadcast_in_dim.24), calls=%async_computation | async-start | bytes 8388608 | tf_op jit(solution)/shard_map/all_to_all | solution.py:48
  80.7 21.3 %all-to-all-start.2 = ((bf16[32,16,1024]{2,1,0:T(8,128)(2,1)}), bf16[32,16,1024]{2,1,0:T(8,128)(2,1)S(1)}, u32[]{:S(2)}, u32[]{:S(2)}) async-start(bf16[32,16,1024]{2,1,0:T(8,128)(2,1)} %broadcast_in_dim.26), calls=%async_computation.2 | async-start | bytes 2097152 | tf_op jit(solution)/shard_map/all_to_all | solution.py:48
  90.0 33.3 %copy-start.6 = (f32[128,912]{0,1:T(8,128)}, f32[128,912]{0,1:T(8,128)S(1)}, u32[]{:S(2)}) copy-start(f32[128,912]{0,1:T(8,128)S(1)} %fusion.23) | copy-start | bytes 1400836
  106.1 5.8 %copy-start.10 = (bf16[512]{0:T(512)(128)(2,1)S(1)}, bf16[512]{0:T(512)(128)(2,1)}, u32[]{:S(2)}) copy-start(bf16[512]{0:T(512)(128)(2,1)} %param.13) | copy-start | bytes 3076
  106.1 93.6 %all-to-all-start.1 = ((bf16[32,128,768]{1,2,0:T(8,128)(2,1)}), bf16[32,128,768]{1,2,0:T(8,128)(2,1)}, u32[]{:S(2)}, u32[]{:S(2)}) async-start(bf16[32,128,768]{1,2,0:T(8,128)(2,1)} %broadcast_in_dim.25), calls=%async_computation.1 | async-start | bytes 12582912 | tf_op jit(solution)/shard_map/all_to_all | solution.py:48
  111.1 211.8 %all-gather.3.cloned.1.call-start = ((), (), s32[]{:S(2)}) async-start(), calls=%async_computation.8 | async-start | bytes 2162688 | tf_op jit(solution)/shard_map/all_gather | solution.py:197
  121.6 0.8 copy-start.3
  123.3 82.7 %slice-start.3 = ((f32[128,912]{0,1:T(8,128)}), f32[128,144]{0,1:T(8,128)S(1)}, s32[]{:S(2)}) async-start(f32[128,912]{0,1:T(8,128)} %copy-done.6), calls=%async_computation.12 | async-start | bytes 147456 | tf_op jit(solution)/shard_map/slice | solution.py:202
  206.7 84.9 %all-to-all-start.3 = ((f32[4,128,144]{1,2,0:T(8,128)}), f32[4,128,144]{1,2,0:T(8,128)S(1)}, u32[]{:S(2)}, u32[]{:S(2)}) async-start(f32[4,128,144]{1,2,0:T(8,128)} %broadcast_in_dim.28), calls=%async_computation.3 | async-start | bytes 589824 | tf_op jit(solution)/shard_map/all_to_all | solution.py:48
  214.9 2.2 slice-start.2
  214.9 10.4 %slice-start = ((s8[6291456]{0:T(1024)(128)(4,1)}), s8[4194304]{0:T(1024)(128)(4,1)S(1)}, s32[]{:S(2)}) async-start(s8[6291456]{0:T(1024)(128)(4,1)} %bitcast.112), calls=%async_computation.9 | async-start | bytes 8388608
  217.1 8.2 %slice-start.1 = ((s8[6291456]{0:T(1024)(128)(4,1)}), s8[2097152]{0:T(1024)(128)(4,1)S(1)}, s32[]{:S(2)}) async-start(s8[6291456]{0:T(1024)(128)(4,1)} %bitcast.112), calls=%async_computation.10 | async-start | bytes 4194304
  294.8 7.6 %copy-start.4 = (bf16[512,4,128]{2,1,0:T(4,128)(2,1)S(1)}, bf16[512,4,128]{2,1,0:T(4,128)(2,1)}, u32[]{:S(2)}) copy-start(bf16[512,4,128]{2,1,0:T(4,128)(2,1)} %copy-done.3) | copy-start | bytes 1572868
  298.5 16.3 %all-to-all-start.4 = ((bf16[2,4,32,128]{3,1,0,2:T(4,128)(2,1)}), bf16[2,4,32,128]{3,1,0,2:T(4,128)(2,1)S(1)}, u32[]{:S(2)}, u32[]{:S(2)}) async-start(bf16[2,4,32,128]{3,1,0,2:T(4,128)(2,1)} %pad_maximum_fusion.3), calls=%async_computation.4 | async-start | bytes 131072 | tf_op jit(solution)/shard_map/all_to_all | solution.py:282
  302.4 3.5 copy-start.2
  314.8 68.4 %all-to-all-start.5 = ((bf16[4,32,128,128]{3,2,0,1:T(8,128)(2,1)}), bf16[4,32,128,128]{3,2,0,1:T(8,128)(2,1)}, u32[]{:S(2)}, u32[]{:S(2)}) async-start(bf16[4,32,128,128]{3,2,0,1:T(8,128)(2,1)} %copy.58), calls=%async_computation.5 | async-start | bytes 8388608 | tf_op jit(solution)/shard_map/all_to_all | solution.py:285
  387.9 29.1 %copy-start.1 = (bf16[64,576]{1,0:T(8,128)(2,1)S(1)}, bf16[64,576]{1,0:T(8,128)(2,1)}, u32[]{:S(2)}) copy-start(bf16[64,576]{1,0:T(8,128)(2,1)} %param.12) | copy-start | bytes 221188
Sparse Core Ops, SparseCore 0:
  113.6 186.9 all-gather.2

commit v15 on v14

--- a/solution.py
+++ b/solution.py
@@ -10,7 +10,7 @@
 VDIM = 128
 LAT = 512
 SPAN = 512
-HEADS_PER_STEP = 2
+HEADS_PER_STEP = 4
 
 
 eps = 1e-06

time: 425 us -> 419 us (0.986)
  Pallas kernels: 61.2 us -> 55.4 us
    pallas_call x1, Pallas kernels: 61.2 us -> 55.4 us  [cache_attention(): pl.pallas_call(cache_kernel, grid_spec=grid_spec, out_shape=[jax.ShapeDty...]
  transfers between devices with their start and end apart: 7 -> 7, of which waited for: 4 -> 4; matrix products, arithmetic and copies ran while one was open for 15% -> 15% of each run, Pallas kernels for 14% -> 13%
where the time goes in v15:
time: 419 us; the launch traced here: 418 us
  waiting for transfers between devices  199 us (47%)
  Pallas kernels  55.4 us (13%)
  local copies, waits for them, and re-layouts  42.6 us (10%)
  starting transfers between devices  39.8 us (9%)
  blocking collectives  26.8 us (6%)
  matrix products  24.4 us (6%)
  other arithmetic  16.1 us (4%)
  between operations  13.8 us (3%)
    all_to_all x4, waiting for transfers between devices, gather_axis(): lax.all_to_all(spread, axis_name, split_axis=0, concat_axis=0, tiled=True)  142 us
    all_to_all x1, waiting for transfers between devices, per_device(): lax.all_to_all(value_out.astype(jnp.bfloat16).reshape(heads_here, wide_co...  56.7 us
    pallas_call x1, Pallas kernels, cache_attention(): pl.pallas_call(cache_kernel, grid_spec=grid_spec, out_shape=[jax.ShapeDty...  55.4 us
    all_to_all x4, starting transfers between devices, gather_axis(): lax.all_to_all(spread, axis_name, split_axis=0, concat_axis=0, tiled=True)  28 us
    all_to_all x1, blocking collectives, per_device(): got_pieces = lax.all_to_all(pieces, 'narrow', 0, 0, tiled=True)  14.1 us
    unnamed x31, local copies, waits for them, and re-layouts  13.9 us
    all_to_all x1, blocking collectives, gather_axis(): lax.all_to_all(spread, axis_name, split_axis=0, concat_axis=0, tiled=True)  12.7 us
    broadcast_in_dim x5, local copies, waits for them, and re-layouts, gather_axis(): spread = jnp.broadcast_to(x[None], (count,) + x.shape)  8.43 us
  transfers between devices with their start and end apart: 7, of which 4 were waited for; matrix products, arithmetic and copies ran while one was open for 15% of the time, Pallas kernels for 13%

profile of v15, /device:TPU:1, one launch (start us, length us, event | category | flops | bytes accessed | tf_op | source)
XLA Modules:
  0.0 418.0 jit_solution(13343860715033763684)
XLA Ops:
  6.5 0.9 copy-done
  7.5 0.9 pad_maximum_fusion.1
  8.4 2.5 broadcast_in_dim.24
  10.9 9.5 %all-to-all-start = ((bf16[32,64,912]{2,1,0:T(8,128)(2,1)}), bf16[32,64,912]{2,1,0:T(8,128)(2,1)}, u32[]{:S(2)}, u32[]{:S(2)}) async-start(bf16[32,64,912]{2,1,0:T(8,128)(2,1)} %broadcast_in_dim.24), calls=%async_computation | async-start | bytes 8388608 | tf_op jit(solution)/shard_map/all_to_all | solution.py:48
  20.5 0.7 fusion.53
  21.2 4.8 %fusion.48 = f32[128]{0:T(128)S(1)} fusion(s32[]{:T(128)} %bitcast.6, s32[]{:T(128)} %bitcast.7, s32[]{:T(128)} %bitcast.8, s32[]{:T(128)} %bitcast.9, s32[]{:T(128)} %bitcast.10, s32[]{:T(128)} %bitcast.12, s32[]{:T(128)} %bitcast.11, s32[]{:T(128)} %bitcast.5, s32[]{:T(128)S(6)} %mul.164), kind=kLoop, calls=%fused_computation.99 | loop fusion | flops 6016 | bytes 548 | tf_op jit(solution)/shard_map/convert_element_type | solution.py:23
  26.3 53.3 %all-to-all-done = bf16[32,64,912]{2,1,0:T(8,128)(2,1)} async-done(((bf16[32,64,912]{2,1,0:T(8,128)(2,1)}), bf16[32,64,912]{2,1,0:T(8,128)(2,1)}, u32[]{:S(2)}, u32[]{:S(2)}) %all-to-all-start) | async-done | bytes 3735584 | tf_op jit(solution)/shard_map/all_to_all | solution.py:48
  79.6 1.1 broadcast_in_dim.26
  80.7 5.3 %all-to-all-start.2 = ((bf16[32,16,1024]{2,1,0:T(8,128)(2,1)}), bf16[32,16,1024]{2,1,0:T(8,128)(2,1)S(1)}, u32[]{:S(2)}, u32[]{:S(2)}) async-start(bf16[32,16,1024]{2,1,0:T(8,128)(2,1)} %broadcast_in_dim.26), calls=%async_computation.2 | async-start | bytes 2097152 | tf_op jit(solution)/shard_map/all_to_all | solution.py:48
  86.0 3.9 fusion.23
  90.1 11.9 %all-to-all-done.2 = bf16[32,16,1024]{2,1,0:T(8,128)(2,1)S(1)} async-done(((bf16[32,16,1024]{2,1,0:T(8,128)(2,1)}), bf16[32,16,1024]{2,1,0:T(8,128)(2,1)S(1)}, u32[]{:S(2)}, u32[]{:S(2)}) %all-to-all-start.2) | async-done | bytes 1048608 | tf_op jit(solution)/shard_map/all_to_all | solution.py:48
  102.0 4.1 broadcast_in_dim.25
  106.1 5.0 %all-to-all-start.1 = ((bf16[32,128,768]{1,2,0:T(8,128)(2,1)}), bf16[32,128,768]{1,2,0:T(8,128)(2,1)}, u32[]{:S(2)}, u32[]{:S(2)}) async-start(bf16[32,128,768]{1,2,0:T(8,128)(2,1)} %broadcast_in_dim.25), calls=%async_computation.1 | async-start | bytes 12582912 | tf_op jit(solution)/shard_map/all_to_all | solution.py:48
  111.2 0.7 all-gather.3.cloned.1.call-update
  111.9 8.4 %copy.53.kv_ref = bf16[8,640,576]{2,1,0:T(8,128)(2,1)} copy(bf16[8,640,576]{1,2,0:T(8,128)(2,1)} %param.16) | data formatting | bytes 11796480 | tf_op args[7]
  120.5 0.8 reshape_reshape.3
  121.3 0.4 fusion.52
  121.6 0.8 copy-done.3
  122.4 0.9 copy.88
  123.3 76.4 %all-to-all-done.1 = bf16[32,128,768]{1,2,0:T(8,128)(2,1)} async-done(((bf16[32,128,768]{1,2,0:T(8,128)(2,1)}), bf16[32,128,768]{1,2,0:T(8,128)(2,1)}, u32[]{:S(2)}, u32[]{:S(2)}) %all-to-all-start.1) | async-done | bytes 6291488 | tf_op jit(solution)/shard_map/all_to_all | solution.py:48
  199.6 6.3 %copy_bitcast_fusion = bf16[4096,768]{0,1:T(8,128)(2,1)} fusion(bf16[32,128,768]{1,2,0:T(8,128)(2,1)} %all-to-all-done.1), kind=kLoop, calls=%fused_computation.2 | loop fusion | bytes 12582912 | tf_op jit(solution)/shard_map/reshape | solution.py:231
  206.0 0.7 broadcast_in_dim.28
  206.7 8.2 %all-to-all-start.3 = ((f32[4,128,144]{1,2,0:T(8,128)}), f32[4,128,144]{1,2,0:T(8,128)S(1)}, u32[]{:S(2)}, u32[]{:S(2)}) async-start(f32[4,128,144]{1,2,0:T(8,128)} %broadcast_in_dim.28), calls=%async_computation.3 | async-start | bytes 589824 | tf_op jit(solution)/shard_map/all_to_all | solution.py:48
  214.9 2.2 slice-done.2
  217.1 8.2 %convolution_convert_fusion.lat_ref = bf16[4,4096,512]{2,1,0:T(8,128)(2,1)} fusion(bf16[4096,4,128]{0,2,1:T(8,128)(2,1)S(1)} %bitcast.114, bf16[512,4,128]{2,1,0:T(4,128)(2,1)S(1)} %get-tuple-element.21), kind=kOutput, calls=%fused_computation | convolution fusion | flops 2155872256 | bytes 21495808 | tf_op jit(solution)/shard_map/thc,lhc->htl/dot_general | solution.py:237
  225.5 3.2 copy.51
  228.7 55.4 %shard_map.91 = (f32[4,8,8,512]{3,2,1,0:T(8,128)}, f32[4,4096,128]{2,1,0:T(8,128)}) custom-call(s32[8]{0:T(128)} %lens_ref.1, s32[1]{0:T(128)} %bitcast.base_ref, bf16[4,4096,512]{2,1,0:T(8,128)(2,1)} %convolution_convert_fusion.lat_ref, bf16[4,4096,64]{2,1,0:T(8,128)(2,1)} %bitcast.116, bf16[8,640,576]{2,1,0:T(8,128)(2,1)} %copy.53.kv_ref, ...), custom_call_target="tpu_custom_call" | custom-call | tf_op jit(solution)/shard_map/pallas_call | solution.py:158
  284.1 1.5 slice_reduce_fusion
  286.1 0.3 fusion.32
  286.4 2.6 select_reduce_fusion
  289.2 2.8 fusion.21
  292.0 0.7 pad_maximum_fusion.3
  292.7 4.1 all-to-all-start.4
  296.8 3.0 fusion.17
  299.9 0.4 copy-done.2
  300.3 2.8 fusion.12
  303.0 3.9 convert_element_type.88
  307.0 2.3 copy.58
  309.2 7.7 %all-to-all-start.5 = ((bf16[4,32,128,128]{3,2,0,1:T(8,128)(2,1)}), bf16[4,32,128,128]{3,2,0,1:T(8,128)(2,1)}, u32[]{:S(2)}, u32[]{:S(2)}) async-start(bf16[4,32,128,128]{3,2,0,1:T(8,128)(2,1)} %copy.58), calls=%async_computation.5 | async-start | bytes 8388608 | tf_op jit(solution)/shard_map/all_to_all | solution.py:285
  317.0 2.4 copy.79
  319.3 1.2 copy.61
  320.6 56.7 %all-to-all-done.5 = bf16[4,32,128,128]{3,2,0,1:T(8,128)(2,1)} async-done(((bf16[4,32,128,128]{3,2,0,1:T(8,128)(2,1)}), bf16[4,32,128,128]{3,2,0,1:T(8,128)(2,1)}, u32[]{:S(2)}, u32[]{:S(2)}) %all-to-all-start.5) | async-done | bytes 4194336 | tf_op jit(solution)/shard_map/all_to_all | solution.py:285
  377.3 4.4 %multiply_reduce_fusion = f32[4,128,128]{2,1,0:T(8,128)S(1)} fusion(bf16[4,32,128,128]{3,2,0,1:T(8,128)(2,1)} %all-to-all-done.5, f32[4,32,128]{2,0,1:T(4,128)S(1)} %get-tuple-element.16), kind=kLoop, calls=%fused_computation.1 | loop fusion | flops 6225920 | bytes 4521984 | tf_op jit(solution)/shard_map/reduce_sum | solution.py:297
  382.1 0.8 convolution_convert_fusion.1
  382.9 14.1 %all_to_all.40 = bf16[4,128,512]{2,1,0:T(8,128)(2,1)S(1)} all-to-all(bf16[4,128,512]{2,1,0:T(8,128)(2,1)S(1)} %bitcast.127), channel_id=1, replica_groups=mesh['wide'=32,'narrow'=4] {'narrow'}, dimensions={0} | all-to-all | bytes 1048576 | tf_op jit(solution)/shard_map/all_to_all | solution.py:309
  397.1 12.7 %all_to_all.41 = bf16[4,128,512]{2,1,0:T(8,128)(2,1)S(1)} all-to-all(bf16[4,128,512]{2,1,0:T(8,128)(2,1)S(1)} %broadcast_in_dim.31), channel_id=1, replica_groups=mesh['wide'=32,'narrow'=4] {'narrow'}, dimensions={0} | all-to-all | bytes 1048576 | tf_op jit(solution)/shard_map/all_to_all | solution.py:48
  409.8 0.3 copy.63
  410.1 1.0 copy.64
  (65 shorter events, 2.1 us)
Async XLA Ops:
  6.5 0.9 copy-start
  10.9 9.5 %copy-start.9 = (bf16[2048]{0:T(1024)(128)(2,1)S(1)}, bf16[2048]{0:T(1024)(128)(2,1)}, u32[]{:S(2)}) copy-start(bf16[2048]{0:T(1024)(128)(2,1)} %param.10) | copy-start | bytes 12292
  10.9 9.5 %copy-start.7 = (s32[8]{0:T(128)S(1)}, s32[8]{0:T(128)}, u32[]{:S(2)}) copy-start(s32[8]{0:T(128)} %lens_ref.1) | copy-start | bytes 100
  10.9 15.1 %copy-start.5 = (bf16[128,2048]{1,0:T(8,128)(2,1)S(1)}, bf16[128,2048]{1,0:T(8,128)(2,1)}, u32[]{:S(2)}) copy-start(bf16[128,2048]{1,0:T(8,128)(2,1)} %param.9) | copy-start | bytes 1572868
  10.9 68.7 %copy-start.8 = (bf16[16,1024]{1,0:T(8,128)(2,1)S(1)}, bf16[16,1024]{1,0:T(8,128)(2,1)}, u32[]{:S(2)}) copy-start(bf16[16,1024]{1,0:T(8,128)(2,1)} %param.14) | copy-start | bytes 98308
  10.9 68.7 %all-to-all-start = ((bf16[32,64,912]{2,1,0:T(8,128)(2,1)}), bf16[32,64,912]{2,1,0:T(8,128)(2,1)}, u32[]{:S(2)}, u32[]{:S(2)}) async-start(bf16[32,64,912]{2,1,0:T(8,128)(2,1)} %broadcast_in_dim.24), calls=%async_computation | async-start | bytes 8388608 | tf_op jit(solution)/shard_map/all_to_all | solution.py:48
  80.7 21.3 %all-to-all-start.2 = ((bf16[32,16,1024]{2,1,0:T(8,128)(2,1)}), bf16[32,16,1024]{2,1,0:T(8,128)(2,1)S(1)}, u32[]{:S(2)}, u32[]{:S(2)}) async-start(bf16[32,16,1024]{2,1,0:T(8,128)(2,1)} %broadcast_in_dim.26), calls=%async_computation.2 | async-start | bytes 2097152 | tf_op jit(solution)/shard_map/all_to_all | solution.py:48
  90.0 33.3 %copy-start.6 = (f32[128,912]{0,1:T(8,128)}, f32[128,912]{0,1:T(8,128)S(1)}, u32[]{:S(2)}) copy-start(f32[128,912]{0,1:T(8,128)S(1)} %fusion.23) | copy-start | bytes 1400836
  106.1 5.8 %copy-start.10 = (bf16[512]{0:T(512)(128)(2,1)S(1)}, bf16[512]{0:T(512)(128)(2,1)}, u32[]{:S(2)}) copy-start(bf16[512]{0:T(512)(128)(2,1)} %param.13) | copy-start | bytes 3076
  106.1 93.6 %all-to-all-start.1 = ((bf16[32,128,768]{1,2,0:T(8,128)(2,1)}), bf16[32,128,768]{1,2,0:T(8,128)(2,1)}, u32[]{:S(2)}, u32[]{:S(2)}) async-start(bf16[32,128,768]{1,2,0:T(8,128)(2,1)} %broadcast_in_dim.25), calls=%async_computation.1 | async-start | bytes 12582912 | tf_op jit(solution)/shard_map/all_to_all | solution.py:48
  111.1 205.8 %all-gather.3.cloned.1.call-start = ((), (), s32[]{:S(2)}) async-start(), calls=%async_computation.8 | async-start | bytes 2162688 | tf_op jit(solution)/shard_map/all_gather | solution.py:197
  121.6 0.8 copy-start.3
  123.3 82.7 %slice-start.3 = ((f32[128,912]{0,1:T(8,128)}), f32[128,144]{0,1:T(8,128)S(1)}, s32[]{:S(2)}) async-start(f32[128,912]{0,1:T(8,128)} %copy-done.6), calls=%async_computation.12 | async-start | bytes 147456 | tf_op jit(solution)/shard_map/slice | solution.py:202
  206.7 79.1 %all-to-all-start.3 = ((f32[4,128,144]{1,2,0:T(8,128)}), f32[4,128,144]{1,2,0:T(8,128)S(1)}, u32[]{:S(2)}, u32[]{:S(2)}) async-start(f32[4,128,144]{1,2,0:T(8,128)} %broadcast_in_dim.28), calls=%async_computation.3 | async-start | bytes 589824 | tf_op jit(solution)/shard_map/all_to_all | solution.py:48
  214.9 2.2 slice-start.2
  214.9 10.4 %slice-start = ((s8[6291456]{0:T(1024)(128)(4,1)}), s8[4194304]{0:T(1024)(128)(4,1)S(1)}, s32[]{:S(2)}) async-start(s8[6291456]{0:T(1024)(128)(4,1)} %bitcast.112), calls=%async_computation.9 | async-start | bytes 8388608
  217.1 8.2 %slice-start.1 = ((s8[6291456]{0:T(1024)(128)(4,1)}), s8[2097152]{0:T(1024)(128)(4,1)S(1)}, s32[]{:S(2)}) async-start(s8[6291456]{0:T(1024)(128)(4,1)} %bitcast.112), calls=%async_computation.10 | async-start | bytes 4194304
  289.0 7.8 %copy-start.4 = (bf16[512,4,128]{2,1,0:T(4,128)(2,1)S(1)}, bf16[512,4,128]{2,1,0:T(4,128)(2,1)}, u32[]{:S(2)}) copy-start(bf16[512,4,128]{2,1,0:T(4,128)(2,1)} %copy-done.3) | copy-start | bytes 1572868
  292.7 16.5 %all-to-all-start.4 = ((bf16[2,4,32,128]{3,1,0,2:T(4,128)(2,1)}), bf16[2,4,32,128]{3,1,0,2:T(4,128)(2,1)S(1)}, u32[]{:S(2)}, u32[]{:S(2)}) async-start(bf16[2,4,32,128]{3,1,0,2:T(4,128)(2,1)} %pad_maximum_fusion.3), calls=%async_computation.4 | async-start | bytes 131072 | tf_op jit(solution)/shard_map/all_to_all | solution.py:282
  296.8 3.5 copy-start.2
  309.2 68.1 %all-to-all-start.5 = ((bf16[4,32,128,128]{3,2,0,1:T(8,128)(2,1)}), bf16[4,32,128,128]{3,2,0,1:T(8,128)(2,1)}, u32[]{:S(2)}, u32[]{:S(2)}) async-start(bf16[4,32,128,128]{3,2,0,1:T(8,128)(2,1)} %copy.58), calls=%async_computation.5 | async-start | bytes 8388608 | tf_op jit(solution)/shard_map/all_to_all | solution.py:285
  382.0 29.1 %copy-start.1 = (bf16[64,576]{1,0:T(8,128)(2,1)S(1)}, bf16[64,576]{1,0:T(8,128)(2,1)}, u32[]{:S(2)}) copy-start(bf16[64,576]{1,0:T(8,128)(2,1)} %param.12) | copy-start | bytes 221188
Sparse Core Ops, SparseCore 0:
  113.6 186.9 all-gather.2

commit v16 on v15

--- a/solution.py
+++ b/solution.py
@@ -99,7 +99,7 @@
     base = base_ref[0]
     live_block = base < length_now
 
-    def one_head(j):
+    def one_head(j, masked):
         keys = kv_ref[0]
         key_lat = keys[:, :LAT]
         key_rope = keys[:, LAT:]
@@ -108,10 +108,14 @@
             lax.dot_general(lat_ref[j], key_lat, nt, preferred_element_type=jnp.float32)
             + lax.dot_general(rope_ref[j], key_rope, nt, preferred_element_type=jnp.float32)
         ) * score_scale
-        slots = base + lax.broadcasted_iota(jnp.int32, scores.shape, 1)
-        live = slots < length_now
-        peak = jnp.max(jnp.where(live, scores, -1e30), axis=-1, keepdims=True)
-        weights = jnp.where(live, jnp.exp(scores - peak), 0.0)
+        if masked:
+            slots = base + lax.broadcasted_iota(jnp.int32, scores.shape, 1)
+            live = slots < length_now
+            peak = jnp.max(jnp.where(live, scores, -1e30), axis=-1, keepdims=True)
+            weights = jnp.where(live, jnp.exp(scores - peak), 0.0)
+        else:
+            peak = jnp.max(scores, axis=-1, keepdims=True)
+            weights = jnp.exp(scores - peak)
         total = jnp.sum(weights, axis=-1, keepdims=True)
         lane = lax.broadcasted_iota(jnp.int32, (peak.shape[0], 128), 1)
         packed = jnp.where(lane == 0, peak, jnp.where(lane == 1, total, 0.0))
@@ -124,10 +128,17 @@
             lower_part, value_map, preferred_element_type=jnp.float32
         )
 
-    @pl.when(live_block)
+    whole_live = base + kv_ref.shape[1] <= length_now
+
+    @pl.when(whole_live)
     def _():
         for j in range(lat_ref.shape[0]):
-            one_head(j)
+            one_head(j, False)
+
+    @pl.when(jnp.logical_and(live_block, jnp.logical_not(whole_live)))
+    def _():
+        for j in range(lat_ref.shape[0]):
+            one_head(j, True)
 
     @pl.when(jnp.logical_not(live_block))
     def _():

time: 419 us -> 419 us (level)
  no operation moved by 1% of the time
where the time goes in v16:
time: 419 us
  waiting for transfers between devices  198 us (47%)
  Pallas kernels  55.1 us (13%)
  local copies, waits for them, and re-layouts  42.6 us (10%)
  starting transfers between devices  40.8 us (10%)
  blocking collectives  28 us (7%)
  matrix products  24.4 us (6%)
  other arithmetic  16.1 us (4%)
  between operations  13.8 us (3%)
    all_to_all x4, waiting for transfers between devices, gather_axis(): lax.all_to_all(spread, axis_name, split_axis=0, concat_axis=0, tiled=True)  142 us
    all_to_all x1, waiting for transfers between devices, per_device(): lax.all_to_all(value_out.astype(jnp.bfloat16).reshape(heads_here, wide_co...  55.7 us
    pallas_call x1, Pallas kernels, cache_attention(): pl.pallas_call(cache_kernel, grid_spec=grid_spec, out_shape=[jax.ShapeDty...  55.1 us
    all_to_all x4, starting transfers between devices, gather_axis(): lax.all_to_all(spread, axis_name, split_axis=0, concat_axis=0, tiled=True)  28 us
    all_to_all x1, blocking collectives, per_device(): got_pieces = lax.all_to_all(pieces, 'narrow', 0, 0, tiled=True)  15.3 us
    unnamed x31, local copies, waits for them, and re-layouts  13.9 us
    all_to_all x1, blocking collectives, gather_axis(): lax.all_to_all(spread, axis_name, split_axis=0, concat_axis=0, tiled=True)  12.7 us
    broadcast_in_dim x5, local copies, waits for them, and re-layouts, gather_axis(): spread = jnp.broadcast_to(x[None], (count,) + x.shape)  8.43 us
  transfers between devices with their start and end apart: 7, of which 4 were waited for; matrix products, arithmetic and copies ran while one was open for 15% of the time, Pallas kernels for 13%

profile of v16, /device:TPU:1, one launch (start us, length us, event | category | flops | bytes accessed | tf_op | source)
XLA Modules:
  0.0 418.9 jit_solution(9330931322034622443)
XLA Ops:
  6.5 0.9 copy-done
  7.5 0.9 pad_maximum_fusion.1
  8.4 2.5 broadcast_in_dim.24
  10.9 9.5 %all-to-all-start = ((bf16[32,64,912]{2,1,0:T(8,128)(2,1)}), bf16[32,64,912]{2,1,0:T(8,128)(2,1)}, u32[]{:S(2)}, u32[]{:S(2)}) async-start(bf16[32,64,912]{2,1,0:T(8,128)(2,1)} %broadcast_in_dim.24), calls=%async_computation | async-start | bytes 8388608 | tf_op jit(solution)/shard_map/all_to_all | solution.py:48
  20.5 0.7 fusion.53
  21.2 4.8 %fusion.48 = f32[128]{0:T(128)S(1)} fusion(s32[]{:T(128)} %bitcast.6, s32[]{:T(128)} %bitcast.7, s32[]{:T(128)} %bitcast.8, s32[]{:T(128)} %bitcast.9, s32[]{:T(128)} %bitcast.10, s32[]{:T(128)} %bitcast.12, s32[]{:T(128)} %bitcast.11, s32[]{:T(128)} %bitcast.5, s32[]{:T(128)S(6)} %mul.164), kind=kLoop, calls=%fused_computation.99 | loop fusion | flops 6016 | bytes 548 | tf_op jit(solution)/shard_map/convert_element_type | solution.py:23
  26.3 53.3 %all-to-all-done = bf16[32,64,912]{2,1,0:T(8,128)(2,1)} async-done(((bf16[32,64,912]{2,1,0:T(8,128)(2,1)}), bf16[32,64,912]{2,1,0:T(8,128)(2,1)}, u32[]{:S(2)}, u32[]{:S(2)}) %all-to-all-start) | async-done | bytes 3735584 | tf_op jit(solution)/shard_map/all_to_all | solution.py:48
  79.6 1.1 broadcast_in_dim.26
  80.7 5.3 %all-to-all-start.2 = ((bf16[32,16,1024]{2,1,0:T(8,128)(2,1)}), bf16[32,16,1024]{2,1,0:T(8,128)(2,1)S(1)}, u32[]{:S(2)}, u32[]{:S(2)}) async-start(bf16[32,16,1024]{2,1,0:T(8,128)(2,1)} %broadcast_in_dim.26), calls=%async_computation.2 | async-start | bytes 2097152 | tf_op jit(solution)/shard_map/all_to_all | solution.py:48
  86.0 3.9 fusion.23
  90.1 11.9 %all-to-all-done.2 = bf16[32,16,1024]{2,1,0:T(8,128)(2,1)S(1)} async-done(((bf16[32,16,1024]{2,1,0:T(8,128)(2,1)}), bf16[32,16,1024]{2,1,0:T(8,128)(2,1)S(1)}, u32[]{:S(2)}, u32[]{:S(2)}) %all-to-all-start.2) | async-done | bytes 1048608 | tf_op jit(solution)/shard_map/all_to_all | solution.py:48
  102.0 4.1 broadcast_in_dim.25
  106.1 5.0 %all-to-all-start.1 = ((bf16[32,128,768]{1,2,0:T(8,128)(2,1)}), bf16[32,128,768]{1,2,0:T(8,128)(2,1)}, u32[]{:S(2)}, u32[]{:S(2)}) async-start(bf16[32,128,768]{1,2,0:T(8,128)(2,1)} %broadcast_in_dim.25), calls=%async_computation.1 | async-start | bytes 12582912 | tf_op jit(solution)/shard_map/all_to_all | solution.py:48
  111.2 0.7 all-gather.3.cloned.1.call-update
  111.9 8.4 %copy.53.kv_ref = bf16[8,640,576]{2,1,0:T(8,128)(2,1)} copy(bf16[8,640,576]{1,2,0:T(8,128)(2,1)} %param.16) | data formatting | bytes 11796480 | tf_op args[7]
  120.5 0.8 reshape_reshape.3
  121.3 0.4 fusion.52
  121.6 0.8 copy-done.3
  122.4 0.9 copy.88
  123.3 76.4 %all-to-all-done.1 = bf16[32,128,768]{1,2,0:T(8,128)(2,1)} async-done(((bf16[32,128,768]{1,2,0:T(8,128)(2,1)}), bf16[32,128,768]{1,2,0:T(8,128)(2,1)}, u32[]{:S(2)}, u32[]{:S(2)}) %all-to-all-start.1) | async-done | bytes 6291488 | tf_op jit(solution)/shard_map/all_to_all | solution.py:48
  199.6 6.3 %copy_bitcast_fusion = bf16[4096,768]{0,1:T(8,128)(2,1)} fusion(bf16[32,128,768]{1,2,0:T(8,128)(2,1)} %all-to-all-done.1), kind=kLoop, calls=%fused_computation.2 | loop fusion | bytes 12582912 | tf_op jit(solution)/shard_map/reshape | solution.py:242
  206.0 0.7 broadcast_in_dim.28
  206.7 8.2 %all-to-all-start.3 = ((f32[4,128,144]{1,2,0:T(8,128)}), f32[4,128,144]{1,2,0:T(8,128)S(1)}, u32[]{:S(2)}, u32[]{:S(2)}) async-start(f32[4,128,144]{1,2,0:T(8,128)} %broadcast_in_dim.28), calls=%async_computation.3 | async-start | bytes 589824 | tf_op jit(solution)/shard_map/all_to_all | solution.py:48
  214.9 2.2 slice-done.2
  217.1 8.2 %convolution_convert_fusion.lat_ref = bf16[4,4096,512]{2,1,0:T(8,128)(2,1)} fusion(bf16[4096,4,128]{0,2,1:T(8,128)(2,1)S(1)} %bitcast.114, bf16[512,4,128]{2,1,0:T(4,128)(2,1)S(1)} %get-tuple-element.21), kind=kOutput, calls=%fused_computation | convolution fusion | flops 2155872256 | bytes 21495808 | tf_op jit(solution)/shard_map/thc,lhc->htl/dot_general | solution.py:248
  225.5 3.2 copy.51
  228.7 55.1 %shard_map.91 = (f32[4,8,8,512]{3,2,1,0:T(8,128)}, f32[4,4096,128]{2,1,0:T(8,128)}) custom-call(s32[8]{0:T(128)} %lens_ref.1, s32[1]{0:T(128)} %bitcast.base_ref, bf16[4,4096,512]{2,1,0:T(8,128)(2,1)} %convolution_convert_fusion.lat_ref, bf16[4,4096,64]{2,1,0:T(8,128)(2,1)} %bitcast.116, bf16[8,640,576]{2,1,0:T(8,128)(2,1)} %copy.53.kv_ref, ...), custom_call_target="tpu_custom_call" | custom-call | tf_op jit(solution)/shard_map/pallas_call | solution.py:169
  283.8 1.5 slice_reduce_fusion
  285.8 0.3 fusion.32
  286.1 2.5 select_reduce_fusion
  288.9 2.8 fusion.21
  291.7 0.7 pad_maximum_fusion.3
  292.4 4.9 %all-to-all-start.4 = ((bf16[2,4,32,128]{3,1,0,2:T(4,128)(2,1)}), bf16[2,4,32,128]{3,1,0,2:T(4,128)(2,1)S(1)}, u32[]{:S(2)}, u32[]{:S(2)}) async-start(bf16[2,4,32,128]{3,1,0,2:T(4,128)(2,1)} %pad_maximum_fusion.3), calls=%async_computation.4 | async-start | bytes 131072 | tf_op jit(solution)/shard_map/all_to_all | solution.py:293
  297.3 3.0 fusion.17
  300.3 0.4 copy-done.2
  300.7 2.8 fusion.12
  303.5 3.9 convert_element_type.88
  307.4 2.3 copy.58
  309.7 7.9 %all-to-all-start.5 = ((bf16[4,32,128,128]{3,2,0,1:T(8,128)(2,1)}), bf16[4,32,128,128]{3,2,0,1:T(8,128)(2,1)}, u32[]{:S(2)}, u32[]{:S(2)}) async-start(bf16[4,32,128,128]{3,2,0,1:T(8,128)(2,1)} %copy.58), calls=%async_computation.5 | async-start | bytes 8388608 | tf_op jit(solution)/shard_map/all_to_all | solution.py:296
  317.6 2.4 copy.79
  320.0 1.2 copy.61
  321.3 55.7 %all-to-all-done.5 = bf16[4,32,128,128]{3,2,0,1:T(8,128)(2,1)} async-done(((bf16[4,32,128,128]{3,2,0,1:T(8,128)(2,1)}), bf16[4,32,128,128]{3,2,0,1:T(8,128)(2,1)}, u32[]{:S(2)}, u32[]{:S(2)}) %all-to-all-start.5) | async-done | bytes 4194336 | tf_op jit(solution)/shard_map/all_to_all | solution.py:296
  377.0 4.4 %multiply_reduce_fusion = f32[4,128,128]{2,1,0:T(8,128)S(1)} fusion(bf16[4,32,128,128]{3,2,0,1:T(8,128)(2,1)} %all-to-all-done.5, f32[4,32,128]{2,0,1:T(4,128)S(1)} %get-tuple-element.16), kind=kLoop, calls=%fused_computation.1 | loop fusion | flops 6225920 | bytes 4521984 | tf_op jit(solution)/shard_map/reduce_sum | solution.py:308
  381.7 0.8 convolution_convert_fusion.1
  382.6 15.3 %all_to_all.40 = bf16[4,128,512]{2,1,0:T(8,128)(2,1)S(1)} all-to-all(bf16[4,128,512]{2,1,0:T(8,128)(2,1)S(1)} %bitcast.127), channel_id=1, replica_groups=mesh['wide'=32,'narrow'=4] {'narrow'}, dimensions={0} | all-to-all | bytes 1048576 | tf_op jit(solution)/shard_map/all_to_all | solution.py:320
  398.0 12.7 %all_to_all.41 = bf16[4,128,512]{2,1,0:T(8,128)(2,1)S(1)} all-to-all(bf16[4,128,512]{2,1,0:T(8,128)(2,1)S(1)} %broadcast_in_dim.31), channel_id=1, replica_groups=mesh['wide'=32,'narrow'=4] {'narrow'}, dimensions={0} | all-to-all | bytes 1048576 | tf_op jit(solution)/shard_map/all_to_all | solution.py:48
  410.7 0.3 copy.63
  411.0 1.0 copy.64
  (65 shorter events, 2.1 us)
Async XLA Ops:
  6.5 0.9 copy-start
  10.9 9.5 %copy-start.9 = (bf16[2048]{0:T(1024)(128)(2,1)S(1)}, bf16[2048]{0:T(1024)(128)(2,1)}, u32[]{:S(2)}) copy-start(bf16[2048]{0:T(1024)(128)(2,1)} %param.10) | copy-start | bytes 12292
  10.9 9.5 %copy-start.7 = (s32[8]{0:T(128)S(1)}, s32[8]{0:T(128)}, u32[]{:S(2)}) copy-start(s32[8]{0:T(128)} %lens_ref.1) | copy-start | bytes 100
  10.9 15.1 %copy-start.5 = (bf16[128,2048]{1,0:T(8,128)(2,1)S(1)}, bf16[128,2048]{1,0:T(8,128)(2,1)}, u32[]{:S(2)}) copy-start(bf16[128,2048]{1,0:T(8,128)(2,1)} %param.9) | copy-start | bytes 1572868
  10.9 68.7 %copy-start.8 = (bf16[16,1024]{1,0:T(8,128)(2,1)S(1)}, bf16[16,1024]{1,0:T(8,128)(2,1)}, u32[]{:S(2)}) copy-start(bf16[16,1024]{1,0:T(8,128)(2,1)} %param.14) | copy-start | bytes 98308
  10.9 68.7 %all-to-all-start = ((bf16[32,64,912]{2,1,0:T(8,128)(2,1)}), bf16[32,64,912]{2,1,0:T(8,128)(2,1)}, u32[]{:S(2)}, u32[]{:S(2)}) async-start(bf16[32,64,912]{2,1,0:T(8,128)(2,1)} %broadcast_in_dim.24), calls=%async_computation | async-start | bytes 8388608 | tf_op jit(solution)/shard_map/all_to_all | solution.py:48
  80.7 21.3 %all-to-all-start.2 = ((bf16[32,16,1024]{2,1,0:T(8,128)(2,1)}), bf16[32,16,1024]{2,1,0:T(8,128)(2,1)S(1)}, u32[]{:S(2)}, u32[]{:S(2)}) async-start(bf16[32,16,1024]{2,1,0:T(8,128)(2,1)} %broadcast_in_dim.26), calls=%async_computation.2 | async-start | bytes 2097152 | tf_op jit(solution)/shard_map/all_to_all | solution.py:48
  90.0 33.3 %copy-start.6 = (f32[128,912]{0,1:T(8,128)}, f32[128,912]{0,1:T(8,128)S(1)}, u32[]{:S(2)}) copy-start(f32[128,912]{0,1:T(8,128)S(1)} %fusion.23) | copy-start | bytes 1400836
  106.1 5.8 %copy-start.10 = (bf16[512]{0:T(512)(128)(2,1)S(1)}, bf16[512]{0:T(512)(128)(2,1)}, u32[]{:S(2)}) copy-start(bf16[512]{0:T(512)(128)(2,1)} %param.13) | copy-start | bytes 3076
  106.1 93.6 %all-to-all-start.1 = ((bf16[32,128,768]{1,2,0:T(8,128)(2,1)}), bf16[32,128,768]{1,2,0:T(8,128)(2,1)}, u32[]{:S(2)}, u32[]{:S(2)}) async-start(bf16[32,128,768]{1,2,0:T(8,128)(2,1)} %broadcast_in_dim.25), calls=%async_computation.1 | async-start | bytes 12582912 | tf_op jit(solution)/shard_map/all_to_all | solution.py:48
  111.1 206.5 %all-gather.3.cloned.1.call-start = ((), (), s32[]{:S(2)}) async-start(), calls=%async_computation.8 | async-start | bytes 2162688 | tf_op jit(solution)/shard_map/all_gather | solution.py:208
  121.6 0.8 copy-start.3
  123.3 82.7 %slice-start.3 = ((f32[128,912]{0,1:T(8,128)}), f32[128,144]{0,1:T(8,128)S(1)}, s32[]{:S(2)}) async-start(f32[128,912]{0,1:T(8,128)} %copy-done.6), calls=%async_computation.12 | async-start | bytes 147456 | tf_op jit(solution)/shard_map/slice | solution.py:213
  206.7 78.8 %all-to-all-start.3 = ((f32[4,128,144]{1,2,0:T(8,128)}), f32[4,128,144]{1,2,0:T(8,128)S(1)}, u32[]{:S(2)}, u32[]{:S(2)}) async-start(f32[4,128,144]{1,2,0:T(8,128)} %broadcast_in_dim.28), calls=%async_computation.3 | async-start | bytes 589824 | tf_op jit(solution)/shard_map/all_to_all | solution.py:48
  214.9 2.2 slice-start.2
  214.9 10.4 %slice-start = ((s8[6291456]{0:T(1024)(128)(4,1)}), s8[4194304]{0:T(1024)(128)(4,1)S(1)}, s32[]{:S(2)}) async-start(s8[6291456]{0:T(1024)(128)(4,1)} %bitcast.112), calls=%async_computation.9 | async-start | bytes 8388608
  217.1 8.2 %slice-start.1 = ((s8[6291456]{0:T(1024)(128)(4,1)}), s8[2097152]{0:T(1024)(128)(4,1)S(1)}, s32[]{:S(2)}) async-start(s8[6291456]{0:T(1024)(128)(4,1)} %bitcast.112), calls=%async_computation.10 | async-start | bytes 4194304
  288.7 8.6 %copy-start.4 = (bf16[512,4,128]{2,1,0:T(4,128)(2,1)S(1)}, bf16[512,4,128]{2,1,0:T(4,128)(2,1)}, u32[]{:S(2)}) copy-start(bf16[512,4,128]{2,1,0:T(4,128)(2,1)} %copy-done.3) | copy-start | bytes 1572868
  292.4 17.3 %all-to-all-start.4 = ((bf16[2,4,32,128]{3,1,0,2:T(4,128)(2,1)}), bf16[2,4,32,128]{3,1,0,2:T(4,128)(2,1)S(1)}, u32[]{:S(2)}, u32[]{:S(2)}) async-start(bf16[2,4,32,128]{3,1,0,2:T(4,128)(2,1)} %pad_maximum_fusion.3), calls=%async_computation.4 | async-start | bytes 131072 | tf_op jit(solution)/shard_map/all_to_all | solution.py:293
  297.3 3.5 copy-start.2
  309.7 67.3 %all-to-all-start.5 = ((bf16[4,32,128,128]{3,2,0,1:T(8,128)(2,1)}), bf16[4,32,128,128]{3,2,0,1:T(8,128)(2,1)}, u32[]{:S(2)}, u32[]{:S(2)}) async-start(bf16[4,32,128,128]{3,2,0,1:T(8,128)(2,1)} %copy.58), calls=%async_computation.5 | async-start | bytes 8388608 | tf_op jit(solution)/shard_map/all_to_all | solution.py:296
  381.7 30.3 %copy-start.1 = (bf16[64,576]{1,0:T(8,128)(2,1)S(1)}, bf16[64,576]{1,0:T(8,128)(2,1)}, u32[]{:S(2)}) copy-start(bf16[64,576]{1,0:T(8,128)(2,1)} %param.12) | copy-start | bytes 221188
Sparse Core Ops, SparseCore 0:
  113.6 187.0 all-gather.2

commit v17 on v15

--- a/solution.py
+++ b/solution.py
@@ -99,35 +99,40 @@
     base = base_ref[0]
     live_block = base < length_now
 
-    def one_head(j):
+    def all_heads():
         keys = kv_ref[0]
         key_lat = keys[:, :LAT]
         key_rope = keys[:, LAT:]
         nt = (((1,), (1,)), ((), ()))
+        heads_step, span = lat_ref.shape[0], lat_ref.shape[1]
+        q_lat = lat_ref[...].reshape(heads_step * span, LAT)
+        q_rope = rope_ref[...].reshape(heads_step * span, ROPE)
         scores = (
-            lax.dot_general(lat_ref[j], key_lat, nt, preferred_element_type=jnp.float32)
-            + lax.dot_general(rope_ref[j], key_rope, nt, preferred_element_type=jnp.float32)
+            lax.dot_general(q_lat, key_lat, nt, preferred_element_type=jnp.float32)
+            + lax.dot_general(q_rope, key_rope, nt, preferred_element_type=jnp.float32)
         ) * score_scale
         slots = base + lax.broadcasted_iota(jnp.int32, scores.shape, 1)
         live = slots < length_now
         peak = jnp.max(jnp.where(live, scores, -1e30), axis=-1, keepdims=True)
         weights = jnp.where(live, jnp.exp(scores - peak), 0.0)
         total = jnp.sum(weights, axis=-1, keepdims=True)
-        lane = lax.broadcasted_iota(jnp.int32, (peak.shape[0], 128), 1)
-        packed = jnp.where(lane == 0, peak, jnp.where(lane == 1, total, 0.0))
-        stats_ref[j, 0] = jnp.transpose(packed)[: stats_ref.shape[2]]
         mixed = jnp.dot(weights.astype(jnp.bfloat16), key_lat, preferred_element_type=jnp.float32)
-        value_map = vm_ref[j]
-        upper_part = mixed.astype(jnp.bfloat16)
-        lower_part = (mixed - upper_part.astype(jnp.float32)).astype(jnp.bfloat16)
-        value_ref[j] = jnp.dot(upper_part, value_map, preferred_element_type=jnp.float32) + jnp.dot(
-            lower_part, value_map, preferred_element_type=jnp.float32
-        )
+        for j in range(heads_step):
+            rows = slice(j * span, (j + 1) * span)
+            lane = lax.broadcasted_iota(jnp.int32, (span, 128), 1)
+            packed = jnp.where(lane == 0, peak[rows], jnp.where(lane == 1, total[rows], 0.0))
+            stats_ref[j, 0] = jnp.transpose(packed)[: stats_ref.shape[2]]
+            value_map = vm_ref[j]
+            head_mixed = mixed[rows]
+            upper_part = head_mixed.astype(jnp.bfloat16)
+            lower_part = (head_mixed - upper_part.astype(jnp.float32)).astype(jnp.bfloat16)
+            value_ref[j] = jnp.dot(
+                upper_part, value_map, preferred_element_type=jnp.float32
+            ) + jnp.dot(lower_part, value_map, preferred_element_type=jnp.float32)
 
     @pl.when(live_block)
     def _():
-        for j in range(lat_ref.shape[0]):
-            one_head(j)
+        all_heads()
 
     @pl.when(jnp.logical_not(live_block))
     def _():

time: 419 us -> 418 us (level)
  no operation moved by 1% of the time
where the time goes in v17:
time: 418 us; the launch traced here: 417 us
  waiting for transfers between devices  199 us (48%)
  Pallas kernels  54.2 us (13%)
  local copies, waits for them, and re-layouts  42.6 us (10%)
  starting transfers between devices  39.8 us (10%)
  blocking collectives  27.2 us (7%)
  matrix products  24.4 us (6%)
  other arithmetic  16.1 us (4%)
  between operations  13.8 us (3%)
    all_to_all x4, waiting for transfers between devices, gather_axis(): lax.all_to_all(spread, axis_name, split_axis=0, concat_axis=0, tiled=True)  142 us
    all_to_all x1, waiting for transfers between devices, per_device(): lax.all_to_all(value_out.astype(jnp.bfloat16).reshape(heads_here, wide_co...  56.5 us
    pallas_call x1, Pallas kernels, cache_attention(): pl.pallas_call(cache_kernel, grid_spec=grid_spec, out_shape=[jax.ShapeDty...  54.2 us
    all_to_all x4, starting transfers between devices, gather_axis(): lax.all_to_all(spread, axis_name, split_axis=0, concat_axis=0, tiled=True)  28 us
    all_to_all x1, blocking collectives, per_device(): got_pieces = lax.all_to_all(pieces, 'narrow', 0, 0, tiled=True)  14.5 us
    unnamed x31, local copies, waits for them, and re-layouts  13.9 us
    all_to_all x1, blocking collectives, gather_axis(): lax.all_to_all(spread, axis_name, split_axis=0, concat_axis=0, tiled=True)  12.7 us
    broadcast_in_dim x5, local copies, waits for them, and re-layouts, gather_axis(): spread = jnp.broadcast_to(x[None], (count,) + x.shape)  8.43 us
  transfers between devices with their start and end apart: 7, of which 4 were waited for; matrix products, arithmetic and copies ran while one was open for 15% of the time, Pallas kernels for 13%

profile of v17, /device:TPU:1, one launch (start us, length us, event | category | flops | bytes accessed | tf_op | source)
XLA Modules:
  0.0 417.0 jit_solution(8464199841619873138)
XLA Ops:
  6.5 0.9 copy-done
  7.5 0.9 pad_maximum_fusion.1
  8.4 2.5 broadcast_in_dim.24
  10.9 9.5 %all-to-all-start = ((bf16[32,64,912]{2,1,0:T(8,128)(2,1)}), bf16[32,64,912]{2,1,0:T(8,128)(2,1)}, u32[]{:S(2)}, u32[]{:S(2)}) async-start(bf16[32,64,912]{2,1,0:T(8,128)(2,1)} %broadcast_in_dim.24), calls=%async_computation | async-start | bytes 8388608 | tf_op jit(solution)/shard_map/all_to_all | solution.py:48
  20.5 0.7 fusion.53
  21.2 4.8 %fusion.48 = f32[128]{0:T(128)S(1)} fusion(s32[]{:T(128)} %bitcast.6, s32[]{:T(128)} %bitcast.7, s32[]{:T(128)} %bitcast.8, s32[]{:T(128)} %bitcast.9, s32[]{:T(128)} %bitcast.10, s32[]{:T(128)} %bitcast.12, s32[]{:T(128)} %bitcast.11, s32[]{:T(128)} %bitcast.5, s32[]{:T(128)S(6)} %mul.164), kind=kLoop, calls=%fused_computation.99 | loop fusion | flops 6016 | bytes 548 | tf_op jit(solution)/shard_map/convert_element_type | solution.py:23
  26.3 53.3 %all-to-all-done = bf16[32,64,912]{2,1,0:T(8,128)(2,1)} async-done(((bf16[32,64,912]{2,1,0:T(8,128)(2,1)}), bf16[32,64,912]{2,1,0:T(8,128)(2,1)}, u32[]{:S(2)}, u32[]{:S(2)}) %all-to-all-start) | async-done | bytes 3735584 | tf_op jit(solution)/shard_map/all_to_all | solution.py:48
  79.6 1.1 broadcast_in_dim.26
  80.7 5.3 %all-to-all-start.2 = ((bf16[32,16,1024]{2,1,0:T(8,128)(2,1)}), bf16[32,16,1024]{2,1,0:T(8,128)(2,1)S(1)}, u32[]{:S(2)}, u32[]{:S(2)}) async-start(bf16[32,16,1024]{2,1,0:T(8,128)(2,1)} %broadcast_in_dim.26), calls=%async_computation.2 | async-start | bytes 2097152 | tf_op jit(solution)/shard_map/all_to_all | solution.py:48
  86.0 3.9 fusion.23
  90.1 11.9 %all-to-all-done.2 = bf16[32,16,1024]{2,1,0:T(8,128)(2,1)S(1)} async-done(((bf16[32,16,1024]{2,1,0:T(8,128)(2,1)}), bf16[32,16,1024]{2,1,0:T(8,128)(2,1)S(1)}, u32[]{:S(2)}, u32[]{:S(2)}) %all-to-all-start.2) | async-done | bytes 1048608 | tf_op jit(solution)/shard_map/all_to_all | solution.py:48
  102.0 4.1 broadcast_in_dim.25
  106.1 5.0 %all-to-all-start.1 = ((bf16[32,128,768]{1,2,0:T(8,128)(2,1)}), bf16[32,128,768]{1,2,0:T(8,128)(2,1)}, u32[]{:S(2)}, u32[]{:S(2)}) async-start(bf16[32,128,768]{1,2,0:T(8,128)(2,1)} %broadcast_in_dim.25), calls=%async_computation.1 | async-start | bytes 12582912 | tf_op jit(solution)/shard_map/all_to_all | solution.py:48
  111.2 0.7 all-gather.3.cloned.1.call-update
  111.9 8.4 %copy.53.kv_ref = bf16[8,640,576]{2,1,0:T(8,128)(2,1)} copy(bf16[8,640,576]{1,2,0:T(8,128)(2,1)} %param.16) | data formatting | bytes 11796480 | tf_op args[7]
  120.5 0.8 reshape_reshape.3
  121.3 0.4 fusion.52
  121.6 0.8 copy-done.3
  122.4 0.9 copy.88
  123.3 76.4 %all-to-all-done.1 = bf16[32,128,768]{1,2,0:T(8,128)(2,1)} async-done(((bf16[32,128,768]{1,2,0:T(8,128)(2,1)}), bf16[32,128,768]{1,2,0:T(8,128)(2,1)}, u32[]{:S(2)}, u32[]{:S(2)}) %all-to-all-start.1) | async-done | bytes 6291488 | tf_op jit(solution)/shard_map/all_to_all | solution.py:48
  199.6 6.3 %copy_bitcast_fusion = bf16[4096,768]{0,1:T(8,128)(2,1)} fusion(bf16[32,128,768]{1,2,0:T(8,128)(2,1)} %all-to-all-done.1), kind=kLoop, calls=%fused_computation.2 | loop fusion | bytes 12582912 | tf_op jit(solution)/shard_map/reshape | solution.py:236
  206.0 0.7 broadcast_in_dim.28
  206.7 8.2 %all-to-all-start.3 = ((f32[4,128,144]{1,2,0:T(8,128)}), f32[4,128,144]{1,2,0:T(8,128)S(1)}, u32[]{:S(2)}, u32[]{:S(2)}) async-start(f32[4,128,144]{1,2,0:T(8,128)} %broadcast_in_dim.28), calls=%async_computation.3 | async-start | bytes 589824 | tf_op jit(solution)/shard_map/all_to_all | solution.py:48
  214.9 2.2 slice-done.2
  217.1 8.2 %convolution_convert_fusion.lat_ref = bf16[4,4096,512]{2,1,0:T(8,128)(2,1)} fusion(bf16[4096,4,128]{0,2,1:T(8,128)(2,1)S(1)} %bitcast.114, bf16[512,4,128]{2,1,0:T(4,128)(2,1)S(1)} %get-tuple-element.21), kind=kOutput, calls=%fused_computation | convolution fusion | flops 2155872256 | bytes 21495808 | tf_op jit(solution)/shard_map/thc,lhc->htl/dot_general | solution.py:242
  225.5 3.2 copy.51
  228.7 54.2 %shard_map.91 = (f32[4,8,8,512]{3,2,1,0:T(8,128)}, f32[4,4096,128]{2,1,0:T(8,128)}) custom-call(s32[8]{0:T(128)} %lens_ref.1, s32[1]{0:T(128)} %bitcast.base_ref, bf16[4,4096,512]{2,1,0:T(8,128)(2,1)} %convolution_convert_fusion.lat_ref, bf16[4,4096,64]{2,1,0:T(8,128)(2,1)} %bitcast.116, bf16[8,640,576]{2,1,0:T(8,128)(2,1)} %copy.53.kv_ref, ...), custom_call_target="tpu_custom_call" | custom-call | tf_op jit(solution)/shard_map/pallas_call | solution.py:163
  282.9 1.5 slice_reduce_fusion
  284.8 0.3 fusion.32
  285.2 2.6 select_reduce_fusion
  288.0 2.8 fusion.21
  290.8 0.7 pad_maximum_fusion.3
  291.5 4.1 all-to-all-start.4
  295.6 3.0 fusion.17
  298.6 0.4 copy-done.2
  299.0 2.8 fusion.12
  301.8 3.9 convert_element_type.88
  305.7 2.3 copy.58
  308.0 7.7 %all-to-all-start.5 = ((bf16[4,32,128,128]{3,2,0,1:T(8,128)(2,1)}), bf16[4,32,128,128]{3,2,0,1:T(8,128)(2,1)}, u32[]{:S(2)}, u32[]{:S(2)}) async-start(bf16[4,32,128,128]{3,2,0,1:T(8,128)(2,1)} %copy.58), calls=%async_computation.5 | async-start | bytes 8388608 | tf_op jit(solution)/shard_map/all_to_all | solution.py:290
  315.7 2.4 copy.79
  318.1 1.2 copy.61
  319.4 56.5 %all-to-all-done.5 = bf16[4,32,128,128]{3,2,0,1:T(8,128)(2,1)} async-done(((bf16[4,32,128,128]{3,2,0,1:T(8,128)(2,1)}), bf16[4,32,128,128]{3,2,0,1:T(8,128)(2,1)}, u32[]{:S(2)}, u32[]{:S(2)}) %all-to-all-start.5) | async-done | bytes 4194336 | tf_op jit(solution)/shard_map/all_to_all | solution.py:290
  375.9 4.4 %multiply_reduce_fusion = f32[4,128,128]{2,1,0:T(8,128)S(1)} fusion(bf16[4,32,128,128]{3,2,0,1:T(8,128)(2,1)} %all-to-all-done.5, f32[4,32,128]{2,0,1:T(4,128)S(1)} %get-tuple-element.16), kind=kLoop, calls=%fused_computation.1 | loop fusion | flops 6225920 | bytes 4521984 | tf_op jit(solution)/shard_map/reduce_sum | solution.py:302
  380.6 0.8 convolution_convert_fusion.1
  381.5 14.5 %all_to_all.40 = bf16[4,128,512]{2,1,0:T(8,128)(2,1)S(1)} all-to-all(bf16[4,128,512]{2,1,0:T(8,128)(2,1)S(1)} %bitcast.127), channel_id=1, replica_groups=mesh['wide'=32,'narrow'=4] {'narrow'}, dimensions={0} | all-to-all | bytes 1048576 | tf_op jit(solution)/shard_map/all_to_all | solution.py:314
  396.1 12.7 %all_to_all.41 = bf16[4,128,512]{2,1,0:T(8,128)(2,1)S(1)} all-to-all(bf16[4,128,512]{2,1,0:T(8,128)(2,1)S(1)} %broadcast_in_dim.31), channel_id=1, replica_groups=mesh['wide'=32,'narrow'=4] {'narrow'}, dimensions={0} | all-to-all | bytes 1048576 | tf_op jit(solution)/shard_map/all_to_all | solution.py:48
  408.9 0.3 copy.63
  409.1 1.0 copy.64
  (65 shorter events, 2.1 us)
Async XLA Ops:
  6.5 0.9 copy-start
  10.9 9.5 %copy-start.9 = (bf16[2048]{0:T(1024)(128)(2,1)S(1)}, bf16[2048]{0:T(1024)(128)(2,1)}, u32[]{:S(2)}) copy-start(bf16[2048]{0:T(1024)(128)(2,1)} %param.10) | copy-start | bytes 12292
  10.9 9.5 %copy-start.7 = (s32[8]{0:T(128)S(1)}, s32[8]{0:T(128)}, u32[]{:S(2)}) copy-start(s32[8]{0:T(128)} %lens_ref.1) | copy-start | bytes 100
  10.9 15.1 %copy-start.5 = (bf16[128,2048]{1,0:T(8,128)(2,1)S(1)}, bf16[128,2048]{1,0:T(8,128)(2,1)}, u32[]{:S(2)}) copy-start(bf16[128,2048]{1,0:T(8,128)(2,1)} %param.9) | copy-start | bytes 1572868
  10.9 68.7 %copy-start.8 = (bf16[16,1024]{1,0:T(8,128)(2,1)S(1)}, bf16[16,1024]{1,0:T(8,128)(2,1)}, u32[]{:S(2)}) copy-start(bf16[16,1024]{1,0:T(8,128)(2,1)} %param.14) | copy-start | bytes 98308
  10.9 68.7 %all-to-all-start = ((bf16[32,64,912]{2,1,0:T(8,128)(2,1)}), bf16[32,64,912]{2,1,0:T(8,128)(2,1)}, u32[]{:S(2)}, u32[]{:S(2)}) async-start(bf16[32,64,912]{2,1,0:T(8,128)(2,1)} %broadcast_in_dim.24), calls=%async_computation | async-start | bytes 8388608 | tf_op jit(solution)/shard_map/all_to_all | solution.py:48
  80.7 21.3 %all-to-all-start.2 = ((bf16[32,16,1024]{2,1,0:T(8,128)(2,1)}), bf16[32,16,1024]{2,1,0:T(8,128)(2,1)S(1)}, u32[]{:S(2)}, u32[]{:S(2)}) async-start(bf16[32,16,1024]{2,1,0:T(8,128)(2,1)} %broadcast_in_dim.26), calls=%async_computation.2 | async-start | bytes 2097152 | tf_op jit(solution)/shard_map/all_to_all | solution.py:48
  90.0 33.3 %copy-start.6 = (f32[128,912]{0,1:T(8,128)}, f32[128,912]{0,1:T(8,128)S(1)}, u32[]{:S(2)}) copy-start(f32[128,912]{0,1:T(8,128)S(1)} %fusion.23) | copy-start | bytes 1400836
  106.1 5.8 %copy-start.10 = (bf16[512]{0:T(512)(128)(2,1)S(1)}, bf16[512]{0:T(512)(128)(2,1)}, u32[]{:S(2)}) copy-start(bf16[512]{0:T(512)(128)(2,1)} %param.13) | copy-start | bytes 3076
  106.1 93.6 %all-to-all-start.1 = ((bf16[32,128,768]{1,2,0:T(8,128)(2,1)}), bf16[32,128,768]{1,2,0:T(8,128)(2,1)}, u32[]{:S(2)}, u32[]{:S(2)}) async-start(bf16[32,128,768]{1,2,0:T(8,128)(2,1)} %broadcast_in_dim.25), calls=%async_computation.1 | async-start | bytes 12582912 | tf_op jit(solution)/shard_map/all_to_all | solution.py:48
  111.1 204.6 %all-gather.3.cloned.1.call-start = ((), (), s32[]{:S(2)}) async-start(), calls=%async_computation.8 | async-start | bytes 2162688 | tf_op jit(solution)/shard_map/all_gather | solution.py:202
  121.6 0.8 copy-start.3
  123.3 82.7 %slice-start.3 = ((f32[128,912]{0,1:T(8,128)}), f32[128,144]{0,1:T(8,128)S(1)}, s32[]{:S(2)}) async-start(f32[128,912]{0,1:T(8,128)} %copy-done.6), calls=%async_computation.12 | async-start | bytes 147456 | tf_op jit(solution)/shard_map/slice | solution.py:207
  206.7 77.9 %all-to-all-start.3 = ((f32[4,128,144]{1,2,0:T(8,128)}), f32[4,128,144]{1,2,0:T(8,128)S(1)}, u32[]{:S(2)}, u32[]{:S(2)}) async-start(f32[4,128,144]{1,2,0:T(8,128)} %broadcast_in_dim.28), calls=%async_computation.3 | async-start | bytes 589824 | tf_op jit(solution)/shard_map/all_to_all | solution.py:48
  214.9 2.2 slice-start.2
  214.9 10.4 %slice-start = ((s8[6291456]{0:T(1024)(128)(4,1)}), s8[4194304]{0:T(1024)(128)(4,1)S(1)}, s32[]{:S(2)}) async-start(s8[6291456]{0:T(1024)(128)(4,1)} %bitcast.112), calls=%async_computation.9 | async-start | bytes 8388608
  217.1 8.2 %slice-start.1 = ((s8[6291456]{0:T(1024)(128)(4,1)}), s8[2097152]{0:T(1024)(128)(4,1)S(1)}, s32[]{:S(2)}) async-start(s8[6291456]{0:T(1024)(128)(4,1)} %bitcast.112), calls=%async_computation.10 | async-start | bytes 4194304
  287.7 7.8 %copy-start.4 = (bf16[512,4,128]{2,1,0:T(4,128)(2,1)S(1)}, bf16[512,4,128]{2,1,0:T(4,128)(2,1)}, u32[]{:S(2)}) copy-start(bf16[512,4,128]{2,1,0:T(4,128)(2,1)} %copy-done.3) | copy-start | bytes 1572868
  291.5 16.5 %all-to-all-start.4 = ((bf16[2,4,32,128]{3,1,0,2:T(4,128)(2,1)}), bf16[2,4,32,128]{3,1,0,2:T(4,128)(2,1)S(1)}, u32[]{:S(2)}, u32[]{:S(2)}) async-start(bf16[2,4,32,128]{3,1,0,2:T(4,128)(2,1)} %pad_maximum_fusion.3), calls=%async_computation.4 | async-start | bytes 131072 | tf_op jit(solution)/shard_map/all_to_all | solution.py:287
  295.6 3.5 copy-start.2
  308.0 67.9 %all-to-all-start.5 = ((bf16[4,32,128,128]{3,2,0,1:T(8,128)(2,1)}), bf16[4,32,128,128]{3,2,0,1:T(8,128)(2,1)}, u32[]{:S(2)}, u32[]{:S(2)}) async-start(bf16[4,32,128,128]{3,2,0,1:T(8,128)(2,1)} %copy.58), calls=%async_computation.5 | async-start | bytes 8388608 | tf_op jit(solution)/shard_map/all_to_all | solution.py:290
  380.6 29.5 %copy-start.1 = (bf16[64,576]{1,0:T(8,128)(2,1)S(1)}, bf16[64,576]{1,0:T(8,128)(2,1)}, u32[]{:S(2)}) copy-start(bf16[64,576]{1,0:T(8,128)(2,1)} %param.12) | copy-start | bytes 221188
Sparse Core Ops, SparseCore 0:
  113.6 186.9 all-gather.2
